TPU v7x, 512 devices: a whole 4x4x16 slice. The times are simulated.
512 devices in a mesh: section: 4 (over x), expert: 16 (over z), rep: 8 (over y, core).
Axes of the slice: x: 4, y: 4, z: 16, core: 2. Of those that a mesh axis runs over, the one named last changes fastest.
Arguments:
- tokens: bfloat16 [4, 2048, 4096], P('section', 'expert', 'rep'), may hold values from -6 to 6
- expert_ids: int32 [4, 2048, 2], P('section', 'expert'), may hold values from 0 to 15, all different within a row; in each aligned block of 128 rows (0 to 127, 128 to 255, ..., all dimensions but the last counted through in order) at most 20 rows name the same one
- route_weight: float32 [4, 2048, 2], P('section', 'expert'), may hold values from 0.05 to 0.5
- language: int32 [4, 2048], P('section', 'expert'), may hold values from 0 to 3
- capacity: int32 [4, 16], replicated, may hold values from 0 to 7
- spill_table: int32 [4, 16], P('section'), may hold values from 0 to 15, as said below
- w_gate: bfloat16 [4, 16, 4096, 1024], P('section', 'expert', None, 'rep'), may hold values from -0.09375 to 0.09375
- w_up: bfloat16 [4, 16, 4096, 1024], P('section', 'expert', None, 'rep'), may hold values from -0.09375 to 0.09375
- w_down: bfloat16 [4, 16, 1024, 4096], P('section', 'expert', None, 'rep'), may hold values from -0.1875 to 0.1875
Outputs:
- next_rows: bfloat16 [4, 2048, 4096], P('section', 'expert', 'rep')
Inputs may be any that keep to these rules, and one draw needn't show every extreme that they name: `expert_ids`: each token names 2 different experts. Among the tokens of one index of expert (aligned blocks of 128 rows, sections in order) no expert is named by more than 20 tokens, a bound that some block reaches. `spill_table`: in each section's row every expert names another expert, and every expert is named by exactly one; each row is one cycle through all 16.
All inputs are finite; a program needn't handle non-finite values.
Results may differ from a plain program's by a relative error of at most 0.0057.
Values may be sent and summed in bfloat16 or wider, within the bound.
No kernel may reach another device: no remote copies, remote signals or barrier semaphores. Data moves between devices by JAX's collectives and lax.ppermute only.
A program may use at most 64 MiB of HBM per device.

v0:
```python
import jax
import jax.numpy as jnp
from jax import lax
from jax.sharding import PartitionSpec as P


def passed_along(value, axis, steps):
    count = lax.axis_size(axis)
    pairs = [(source, (source + steps) % count) for source in range(count)]
    return lax.ppermute(value, axis, pairs)


def admission(chosen, language, capacity, experts):
    lang_count = capacity.shape[0]
    hit_table = jnp.sum(
        (chosen[:, :, None] == jnp.arange(experts, dtype=jnp.int32)[None, None, :]).astype(
            jnp.int32
        ),
        axis=1,
    )
    lang_hot = (language[:, None] == jnp.arange(lang_count, dtype=jnp.int32)[None, :]).astype(
        jnp.int32
    )
    lang_hits = lang_hot[:, :, None] * hit_table[:, None, :]
    before = jnp.cumsum(lang_hits, axis=0) - lang_hits
    place_rank = jnp.sum(before * lang_hot[:, :, None], axis=1)
    allowance = jnp.sum(lang_hot[:, :, None] * capacity[None, :, :], axis=1)
    admitted = hit_table * (place_rank < allowance).astype(jnp.int32)
    return (hit_table, admitted)


def slot_sources(markers, slot_table, slot_depth):
    tok_rows = markers.shape[0]
    selected = markers[:, :, None] * (
        slot_table[:, :, None] == jnp.arange(slot_depth, dtype=jnp.int32)[None, None, :]
    ).astype(jnp.int32)
    positions = jnp.arange(tok_rows, dtype=jnp.int32)[:, None, None]
    source = jnp.sum(selected * positions, axis=0)
    filled = jnp.sum(selected, axis=0)
    return jnp.where(filled > 0, source, tok_rows)


def local(tokens, expert_ids, route_weight, language, capacity, spill_table, w_gate, w_up, w_down):
    experts = lax.axis_size("expert")
    chosen = expert_ids[0]
    spill_row = spill_table[0]
    tok_rows, top_count = chosen.shape
    slot_depth = min(tok_rows, max(2, 5 * tok_rows * top_count // (4 * experts)))
    expert_iota = jnp.arange(experts, dtype=jnp.int32)
    hit_table, admitted = admission(chosen, language[0], capacity, experts)
    spilled = hit_table - admitted
    main_slot = jnp.cumsum(admitted, axis=0) - admitted
    spill_slot = jnp.cumsum(spilled, axis=0) - spilled
    spill_move = (spill_row[:, None] == expert_iota[None, :]).astype(jnp.int32)
    spill_marks = jnp.sum(spilled[:, :, None] * spill_move[None, :, :], axis=1)
    spill_places = jnp.sum((spill_slot * spilled)[:, :, None] * spill_move[None, :, :], axis=1)
    row_source = lax.all_gather(tokens[0], "rep", axis=1, tiled=True)
    with_blank = jnp.concatenate(
        [row_source, jnp.zeros((1, row_source.shape[1]), row_source.dtype)], axis=0
    )
    main_source = slot_sources(admitted, main_slot, slot_depth)
    spill_source = slot_sources(spill_marks, spill_places, slot_depth)
    outgoing = jnp.take(with_blank, jnp.stack([main_source, spill_source]), axis=0)
    arrived = jnp.stack(
        [
            lax.all_to_all(outgoing[0], "expert", split_axis=0, concat_axis=0, tiled=True),
            lax.all_to_all(outgoing[1], "expert", split_axis=0, concat_axis=0, tiled=True),
        ]
    )
    feat_width = arrived.shape[3]
    flattened = arrived.reshape(-1, feat_width)
    gate_proj = jnp.dot(flattened, w_gate[0, 0], preferred_element_type=jnp.float32)
    up_proj = jnp.dot(flattened, w_up[0, 0], preferred_element_type=jnp.float32)
    activated = (jax.nn.silu(gate_proj) * up_proj).astype(jnp.bfloat16)
    down_local = w_down[0, 0]
    produced = jnp.dot(
        lax.all_gather(activated, "rep", axis=1, tiled=True),
        down_local,
        preferred_element_type=jnp.float32,
    )
    produced = produced.astype(jnp.bfloat16).reshape(2, experts, slot_depth, down_local.shape[1])
    returned = jnp.stack(
        [
            lax.all_to_all(produced[0], "expert", split_axis=0, concat_axis=0, tiled=True),
            lax.all_to_all(produced[1], "expert", split_axis=0, concat_axis=0, tiled=True),
        ]
    )
    id_match = (chosen[:, :, None] == expert_iota[None, None, :]).astype(jnp.int32)
    row_kept = jnp.sum(id_match * admitted[:, None, :], axis=2)
    row_main = jnp.sum(id_match * main_slot[:, None, :], axis=2)
    row_spill = jnp.sum(id_match * spill_slot[:, None, :], axis=2)
    row_other = jnp.sum(id_match * spill_row[None, None, :], axis=2)
    target = jnp.where(row_kept > 0, chosen, row_other)
    slot_pick = jnp.where(row_kept > 0, row_main, row_spill)
    row_index = (1 - row_kept) * experts * slot_depth + target * slot_depth + slot_pick
    out_width = returned.shape[3]
    picked = jnp.take(returned.reshape(-1, out_width), row_index.reshape(-1), axis=0).reshape(
        tok_rows, top_count, out_width
    )
    combined = jnp.sum(route_weight[0][:, :, None] * picked.astype(jnp.float32), axis=1).astype(
        jnp.bfloat16
    )
    forwarded = passed_along(combined, "section", 1)
    return forwarded[None]


def solution(mesh):
    in_specs = (
        P("section", "expert", "rep"),
        P("section", "expert", None),
        P("section", "expert", None),
        P("section", "expert"),
        P(),
        P("section", None),
        P("section", "expert", None, "rep"),
        P("section", "expert", None, "rep"),
        P("section", "expert", None, "rep"),
    )
    out_specs = P("section", "expert", "rep")
    return jax.shard_map(local, mesh=mesh, in_specs=in_specs, out_specs=out_specs, check_vma=False)
```

profile of v0, /device:TPU:24, one launch (start us, length us, event | category | flops | bytes accessed | tf_op | source)
XLA Modules:
  0.0 495.8 jit_solution(13053874309466298952)
XLA Ops:
  6.5 0.7 all-gather.6.cloned.1.call-update
  7.3 0.7 convert_reduce_fusion
  8.1 0.7 fusion.13
  8.8 1.2 multiply_reduce_fusion.1
  10.1 0.2 reduce_window_sum.30
  10.3 0.2 reduce_window_sum.29
  10.7 0.7 fusion.14
  11.5 0.7 select_reduce_fusion
  12.3 0.8 select_reduce_fusion.1
  13.4 30.1 %all-gather.6.cloned.1.call-done = bf16[1,128,4096]{2,1,0:T(8,128)(2,1)} async-done(((bf16[1,128,512]{2,1,0:T(8,128)(2,1)}), bf16[1,128,4096]{2,1,0:T(8,128)(2,1)}) %all-gather.6.cloned.1.call-update) | async-done | bytes 1048592 | tf_op jit(solution)/shard_map/all_gather | solution.py:57
  43.5 1.3 concatenate.24
  44.8 5.4 %gather_fusion = bf16[640,4096]{1,0:T(8,128)(2,1)} fusion(bf16[129,4096]{1,0:T(8,128)(2,1)S(1)} %concatenate.24, s32[1024]{0:T(1024)S(1)} %pad_clamp_fusion.1), kind=kCustom, calls=%fused_computation | custom fusion | bytes 10488320 | tf_op jit(solution)/shard_map/jit(_take)/gather | solution.py:63
  50.2 7.7 %reshape.378 = bf16[2,16,20,4096]{3,2,1,0:T(8,128)(2,1)} reshape(bf16[640,4096]{1,0:T(8,128)(2,1)} %gather_fusion) | data formatting | bytes 10485760 | tf_op jit(solution)/shard_map/jit(_take)/gather | solution.py:63
  57.8 3.4 broadcast_select_fusion
  61.3 0.7 slice_bitcast_fusion.1
  62.0 153.5 %all_to_all.20 = bf16[16,20,4096]{2,1,0:T(8,128)(2,1)S(1)} all-to-all(bf16[16,20,4096]{2,1,0:T(8,128)(2,1)S(1)} %get-tuple-element.23), channel_id=1, replica_groups=mesh['section'=4,'expert'=16,'rep'=8] {'expert'}, dimensions={0} | all-to-all | bytes 5242880 | tf_op jit(solution)/shard_map/all_to_all | solution.py:66
  215.5 147.8 %all_to_all.21 = bf16[16,20,4096]{2,1,0:T(8,128)(2,1)S(1)} all-to-all(bf16[16,20,4096]{2,1,0:T(8,128)(2,1)S(1)} %get-tuple-element.24), channel_id=1, replica_groups=mesh['section'=4,'expert'=16,'rep'=8] {'expert'}, dimensions={0} | all-to-all | bytes 5242880 | tf_op jit(solution)/shard_map/all_to_all | solution.py:67
  363.3 3.4 pad_maximum_fusion
  366.7 7.9 %reshape.375 = bf16[640,4096]{1,0:T(8,128)(2,1)} reshape(bf16[2,16,20,4096]{3,2,1,0:T(8,128)(2,1)} %pad_maximum_fusion) | data formatting | bytes 10485760 | tf_op jit(solution)/shard_map/reshape | solution.py:71
  374.6 4.1 fusion.3
  378.8 0.2 copy-done.6
  378.9 2.2 fusion
  381.2 27.0 %all-gather.4.cloned.1.call-done = bf16[640,1024]{1,0:T(8,128)(2,1)} async-done(((bf16[640,128]{1,0:T(8,128)(2,1)}), bf16[640,1024]{1,0:T(8,128)(2,1)}) %all-gather.4.cloned.1.call-update) | async-done | bytes 1310736 | tf_op jit(solution)/shard_map/all_gather | solution.py:77
  408.2 2.2 convolution_convert_fusion
  410.4 0.8 squeeze.33
  411.2 12.3 %all-to-all-start.2 = ((bf16[16,20,512]{2,1,0:T(8,128)(2,1)}), bf16[16,20,512]{2,1,0:T(8,128)(2,1)S(1)}, u32[]{:S(2)}, u32[]{:S(2)}) async-start(bf16[16,20,512]{2,1,0:T(8,128)(2,1)} %squeeze.33), calls=%async_computation.2 | async-start | bytes 786432 | tf_op jit(solution)/shard_map/all_to_all | solution.py:84
  423.5 0.8 squeeze.34
  424.3 23.7 %all-to-all-done.2 = bf16[16,20,512]{2,1,0:T(8,128)(2,1)S(1)} async-done(((bf16[16,20,512]{2,1,0:T(8,128)(2,1)}), bf16[16,20,512]{2,1,0:T(8,128)(2,1)S(1)}, u32[]{:S(2)}, u32[]{:S(2)}) %all-to-all-start.2) | async-done | bytes 327712 | tf_op jit(solution)/shard_map/all_to_all | solution.py:84
  448.0 5.7 %all-to-all-start.3 = ((bf16[16,20,512]{2,1,0:T(8,128)(2,1)}), bf16[16,20,512]{2,1,0:T(8,128)(2,1)S(1)}, u32[]{:S(2)}, u32[]{:S(2)}) async-start(bf16[16,20,512]{2,1,0:T(8,128)(2,1)} %squeeze.34), calls=%async_computation.3 | async-start | bytes 786432 | tf_op jit(solution)/shard_map/all_to_all | solution.py:85
  453.7 0.1 copy.57
  454.0 0.1 copy.58
  454.3 0.1 copy.56
  454.5 0.1 gt.67
  454.6 0.1 copy.55
  454.7 0.1 mul.221
  454.9 0.1 reduce_sum.145
  455.0 0.1 reduce_sum.146
  455.2 0.1 reduce_sum.147
  455.3 0.1 squeeze.35
  455.5 0.1 copy.48
  455.6 0.1 copy.41
  455.7 22.1 %all-to-all-done.3 = bf16[16,20,512]{2,1,0:T(8,128)(2,1)S(1)} async-done(((bf16[16,20,512]{2,1,0:T(8,128)(2,1)}), bf16[16,20,512]{2,1,0:T(8,128)(2,1)S(1)}, u32[]{:S(2)}, u32[]{:S(2)}) %all-to-all-start.3) | async-done | bytes 327712 | tf_op jit(solution)/shard_map/all_to_all | solution.py:85
  477.9 0.1 reshape.376
  478.1 1.2 gather_fusion.1
  479.3 0.9 multiply_reduce_fusion
  480.2 3.4 collective-permute-start
  483.6 4.7 collective-permute-done
  488.3 0.7 copy.62
  (43 shorter events, 1.5 us)
Async XLA Ops:
  6.5 401.6 %copy-start = (bf16[1,1,1024,512]{3,2,1,0:T(8,128)(2,1)S(1)}, bf16[1,1,1024,512]{3,2,1,0:T(8,128)(2,1)}, u32[]{:S(2)}) copy-start(bf16[1,1,1024,512]{3,2,1,0:T(8,128)(2,1)} %param.17) | copy-start | bytes 3145732
  6.5 36.9 %all-gather.6.cloned.1.call-start = ((), (), s32[]{:S(2)}) async-start(), calls=%async_computation.5 | async-start | bytes 1179648 | tf_op jit(solution)/shard_map/all_gather | solution.py:57
  7.3 400.9 %all-gather.4.cloned.1.call-start = ((), (), s32[]{:S(2)}) async-start(), calls=%async_computation.4 | async-start | bytes 1474560 | tf_op jit(solution)/shard_map/all_gather | solution.py:77
  366.7 7.9 %copy-start.5 = (bf16[1,1,4096,128]{3,2,1,0:T(8,128)(2,1)S(1)}, bf16[1,1,4096,128]{3,2,1,0:T(8,128)(2,1)}, u32[]{:S(2)}) copy-start(bf16[1,1,4096,128]{3,2,1,0:T(8,128)(2,1)} %param.15) | copy-start | bytes 3145732
  374.6 4.2 copy-start.1
  374.6 4.3 copy-start.6
  381.1 72.6 %copy-start.2 = (s32[1,128,2]{1,2,0:T(2,128)S(1)}, s32[1,128,2]{1,2,0:T(2,128)}, u32[]{:S(2)}) copy-start(s32[1,128,2]{1,2,0:T(2,128)} %param.10) | copy-start | bytes 3076
  381.1 72.7 %copy-start.3 = (s32[1,16]{1,0:T(1,128)S(1)}, s32[1,16]{1,0:T(1,128)}, u32[]{:S(2)}) copy-start(s32[1,16]{1,0:T(1,128)} %param.14) | copy-start | bytes 196
  381.1 74.5 %copy-start.4 = (f32[1,128,2]{1,2,0:T(2,128)S(1)}, f32[1,128,2]{1,2,0:T(2,128)}, u32[]{:S(2)}) copy-start(f32[1,128,2]{1,2,0:T(2,128)} %param.11) | copy-start | bytes 3076
  411.2 36.8 %all-to-all-start.2 = ((bf16[16,20,512]{2,1,0:T(8,128)(2,1)}), bf16[16,20,512]{2,1,0:T(8,128)(2,1)S(1)}, u32[]{:S(2)}, u32[]{:S(2)}) async-start(bf16[16,20,512]{2,1,0:T(8,128)(2,1)} %squeeze.33), calls=%async_computation.2 | async-start | bytes 786432 | tf_op jit(solution)/shard_map/all_to_all | solution.py:84
  448.0 29.9 %all-to-all-start.3 = ((bf16[16,20,512]{2,1,0:T(8,128)(2,1)}), bf16[16,20,512]{2,1,0:T(8,128)(2,1)S(1)}, u32[]{:S(2)}, u32[]{:S(2)}) async-start(bf16[16,20,512]{2,1,0:T(8,128)(2,1)} %squeeze.34), calls=%async_computation.3 | async-start | bytes 786432 | tf_op jit(solution)/shard_map/all_to_all | solution.py:85
  480.2 8.1 %collective-permute-start = (bf16[128,512]{1,0:T(8,128)(2,1)S(1)}, bf16[128,512]{1,0:T(8,128)(2,1)S(1)}, u32[]{:S(2)}, u32[]{:S(2)}) collective-permute-start(bf16[128,512]{1,0:T(8,128)(2,1)S(1)} %multiply_reduce_fusion), channel_id=1, source_target_pairs={{0,128},{128,256},{256,384},{384,0},{1,129},{129,257},{257,385},{3... | collective-permute-start | bytes 393224 | tf_op jit(solution)/shard_map/ppermute | solution.py:10
Sparse Core Ops, SparseCore 0:
  9.5 33.9 all-gather.5
  381.3 26.8 all-gather.3
where the time goes:
time: 497 us; the launch traced here: 496 us
  blocking collectives  301 us (61%)
  waiting for transfers between devices  108 us (22%)
  local copies, waits for them, and re-layouts  29.4 us (6%)
  starting transfers between devices  21.4 us (4%)
  between operations  13.6 us (3%)
  other arithmetic  13.3 us (3%)
  matrix products  8.48 us (2%)
    all_to_all x1, blocking collectives, local(): lax.all_to_all(outgoing[0], 'expert', split_axis=0, concat_axis=0, tiled=...  154 us
    all_to_all x1, blocking collectives, local(): lax.all_to_all(outgoing[1], 'expert', split_axis=0, concat_axis=0, tiled=...  148 us
    all_gather x1, waiting for transfers between devices, local(): row_source = lax.all_gather(tokens[0], 'rep', axis=1, tiled=True)  30.1 us
    all_gather x1, waiting for transfers between devices, local(): lax.all_gather(activated, 'rep', axis=1, tiled=True)  27 us
    all_to_all x1, waiting for transfers between devices, local(): lax.all_to_all(produced[0], 'expert', split_axis=0, concat_axis=0, tiled=...  23.7 us
    all_to_all x1, waiting for transfers between devices, local(): lax.all_to_all(produced[1], 'expert', split_axis=0, concat_axis=0, tiled=...  22.1 us
    gather x2, local copies, waits for them, and re-layouts, local(): jnp.take(with_blank, jnp.stack([main_source, spill_source]), axis=0)  13.1 us
    all_to_all x1, starting transfers between devices, local(): lax.all_to_all(produced[0], 'expert', split_axis=0, concat_axis=0, tiled=...  12.3 us
  transfers between devices with their start and end apart: 5, of which 5 were waited for; matrix products, arithmetic and copies ran while one was open for 2% of the time, Pallas kernels for 0%

commit v1 on v0

--- a/solution.py
+++ b/solution.py
@@ -42,6 +42,7 @@
 
 def local(tokens, expert_ids, route_weight, language, capacity, spill_table, w_gate, w_up, w_down):
     experts = lax.axis_size("expert")
+    reps = lax.axis_size("rep")
     chosen = expert_ids[0]
     spill_row = spill_table[0]
     tok_rows, top_count = chosen.shape
@@ -54,46 +55,38 @@
     spill_move = (spill_row[:, None] == expert_iota[None, :]).astype(jnp.int32)
     spill_marks = jnp.sum(spilled[:, :, None] * spill_move[None, :, :], axis=1)
     spill_places = jnp.sum((spill_slot * spilled)[:, :, None] * spill_move[None, :, :], axis=1)
-    row_source = lax.all_gather(tokens[0], "rep", axis=1, tiled=True)
+    rows_local = tokens[0]
+    feat_width = rows_local.shape[1]
     with_blank = jnp.concatenate(
-        [row_source, jnp.zeros((1, row_source.shape[1]), row_source.dtype)], axis=0
+        [rows_local, jnp.zeros((1, feat_width), rows_local.dtype)], axis=0
     )
     main_source = slot_sources(admitted, main_slot, slot_depth)
     spill_source = slot_sources(spill_marks, spill_places, slot_depth)
-    outgoing = jnp.take(with_blank, jnp.stack([main_source, spill_source]), axis=0)
-    arrived = jnp.stack(
-        [
-            lax.all_to_all(outgoing[0], "expert", split_axis=0, concat_axis=0, tiled=True),
-            lax.all_to_all(outgoing[1], "expert", split_axis=0, concat_axis=0, tiled=True),
-        ]
-    )
-    feat_width = arrived.shape[3]
+    sources = jnp.concatenate([main_source, spill_source], axis=1)
+    outgoing = jnp.take(with_blank, sources, axis=0)
+    arrived = lax.all_to_all(outgoing, "expert", split_axis=0, concat_axis=0, tiled=True)
     flattened = arrived.reshape(-1, feat_width)
-    gate_proj = jnp.dot(flattened, w_gate[0, 0], preferred_element_type=jnp.float32)
-    up_proj = jnp.dot(flattened, w_up[0, 0], preferred_element_type=jnp.float32)
+    all_feats = lax.all_gather(flattened, "rep", axis=0)
+    gate_w = w_gate[0, 0].reshape(reps, feat_width, -1)
+    up_w = w_up[0, 0].reshape(reps, feat_width, -1)
+    dims = (((0, 2), (0, 1)), ((), ()))
+    gate_proj = lax.dot_general(all_feats, gate_w, dims, preferred_element_type=jnp.float32)
+    up_proj = lax.dot_general(all_feats, up_w, dims, preferred_element_type=jnp.float32)
     activated = (jax.nn.silu(gate_proj) * up_proj).astype(jnp.bfloat16)
-    down_local = w_down[0, 0]
-    produced = jnp.dot(
-        lax.all_gather(activated, "rep", axis=1, tiled=True),
-        down_local,
-        preferred_element_type=jnp.float32,
-    )
-    produced = produced.astype(jnp.bfloat16).reshape(2, experts, slot_depth, down_local.shape[1])
-    returned = jnp.stack(
-        [
-            lax.all_to_all(produced[0], "expert", split_axis=0, concat_axis=0, tiled=True),
-            lax.all_to_all(produced[1], "expert", split_axis=0, concat_axis=0, tiled=True),
-        ]
-    )
+    all_act = lax.all_gather(activated, "rep", axis=0)
+    down_w = w_down[0, 0].reshape(reps, activated.shape[1], -1)
+    produced = lax.dot_general(all_act, down_w, dims, preferred_element_type=jnp.float32)
+    out_width = down_w.shape[2]
+    produced = produced.astype(jnp.bfloat16).reshape(experts, 2 * slot_depth, out_width)
+    returned = lax.all_to_all(produced, "expert", split_axis=0, concat_axis=0, tiled=True)
     id_match = (chosen[:, :, None] == expert_iota[None, None, :]).astype(jnp.int32)
     row_kept = jnp.sum(id_match * admitted[:, None, :], axis=2)
     row_main = jnp.sum(id_match * main_slot[:, None, :], axis=2)
     row_spill = jnp.sum(id_match * spill_slot[:, None, :], axis=2)
     row_other = jnp.sum(id_match * spill_row[None, None, :], axis=2)
     target = jnp.where(row_kept > 0, chosen, row_other)
-    slot_pick = jnp.where(row_kept > 0, row_main, row_spill)
-    row_index = (1 - row_kept) * experts * slot_depth + target * slot_depth + slot_pick
-    out_width = returned.shape[3]
+    slot_pick = jnp.where(row_kept > 0, row_main, slot_depth + row_spill)
+    row_index = target * (2 * slot_depth) + slot_pick
     picked = jnp.take(returned.reshape(-1, out_width), row_index.reshape(-1), axis=0).reshape(
         tok_rows, top_count, out_width
     )

time: 497 us -> 213 us (0.43)
  blocking collectives: 301 us -> 51.7 us
  local copies, waits for them, and re-layouts: 29.4 us -> 7.95 us
  other arithmetic: 13.3 us -> 6.85 us
  starting transfers between devices: 21.4 us -> 15.5 us
    all_to_all x2 -> x1, blocking collectives: 301 us -> 51.7 us  [local(): lax.all_to_all(outgoing, 'expert', split_axis=0, concat_axis=0, tiled=True)]
    all_to_all x2 -> x1, waiting for transfers between devices: 45.8 us -> 32.6 us  [local(): lax.all_to_all(produced, 'expert', split_axis=0, concat_axis=0, tiled=True)]
    all_gather x2, waiting for transfers between devices: 57.1 us -> 68.2 us  [the longest x1 36 us: local(): all_feats = lax.all_gather(flattened, 'rep', axis=0)]
    gather x2 -> x1, local copies, waits for them, and re-layouts: 13.1 us -> 2.79 us  [local(): outgoing = jnp.take(with_blank, sources, axis=0)]
    reshape x2 -> x0, local copies, waits for them, and re-layouts: 8.06 us -> none  [the longest x1 7.92 us: local(): flattened = arrived.reshape(-1, feat_width)]
    all_to_all x2 -> x1, starting transfers between devices: 18 us -> 12.1 us  [local(): lax.all_to_all(produced, 'expert', split_axis=0, concat_axis=0, tiled=True)]
  transfers between devices with their start and end apart: 5 -> 4, of which waited for: 5 -> 4; matrix products, arithmetic and copies ran while one was open for 2% -> 1% of each run, Pallas kernels for 0% -> 0%
where the time goes in v1:
time: 213 us; the launch traced here: 211 us
  waiting for transfers between devices  106 us (50%)
  blocking collectives  51.7 us (24%)
  starting transfers between devices  15.5 us (7%)
  between operations  13.6 us (6%)
  matrix products  9.35 us (4%)
  local copies, waits for them, and re-layouts  7.95 us (4%)
  other arithmetic  6.85 us (3%)
    all_to_all x1, blocking collectives, local(): lax.all_to_all(outgoing, 'expert', split_axis=0, concat_axis=0, tiled=True)  51.7 us
    all_gather x1, waiting for transfers between devices, local(): all_feats = lax.all_gather(flattened, 'rep', axis=0)  36 us
    all_to_all x1, waiting for transfers between devices, local(): lax.all_to_all(produced, 'expert', split_axis=0, concat_axis=0, tiled=True)  32.6 us
    all_gather x1, waiting for transfers between devices, local(): all_act = lax.all_gather(activated, 'rep', axis=0)  32.2 us
    all_to_all x1, starting transfers between devices, local(): lax.all_to_all(produced, 'expert', split_axis=0, concat_axis=0, tiled=True)  12.1 us
    ppermute x1, waiting for transfers between devices, passed_along(): return lax.ppermute(value, axis, pairs)  4.69 us
  transfers between devices with their start and end apart: 4, of which 4 were waited for; matrix products, arithmetic and copies ran while one was open for 1% of the time, Pallas kernels for 0%

profile of v1, /device:TPU:24, one launch (start us, length us, event | category | flops | bytes accessed | tf_op | source)
XLA Modules:
  0.0 210.5 jit_solution(14522851581845692840)
XLA Ops:
  6.5 0.8 convert_reduce_fusion
  7.3 0.1 copy.67
  7.4 0.7 fusion.11
  8.2 1.2 multiply_reduce_fusion.1
  9.4 0.1 copy.69
  9.4 0.2 reduce_window_sum.29
  9.6 0.2 reduce_window_sum.30
  10.0 0.8 fusion.12
  10.8 0.1 multiply_reduce_fusion.4
  10.9 0.7 select_reduce_fusion
  11.7 0.1 copy.79
  11.8 0.7 select_reduce_fusion.1
  12.5 0.1 copy.78
  12.6 0.1 copy.81
  12.7 0.1 copy.80
  12.8 0.1 compare_select_fusion.1
  12.9 0.1 reshape.286
  13.0 0.1 compare_and_fusion
  13.0 0.9 concatenate.34
  14.0 2.8 %gather_fusion = bf16[640,512]{1,0:T(8,128)(2,1)S(1)} fusion(bf16[129,512]{1,0:T(8,128)(2,1)S(1)} %concatenate.34, s32[1024]{0:T(1024)S(1)} %pad_clamp_fusion.1), kind=kCustom, calls=%fused_computation | custom fusion | bytes 1313280 | tf_op jit(solution)/shard_map/jit(_take)/gather | solution.py:66
  16.8 0.2 broadcast_select_fusion
  16.9 51.7 %all_to_all.10 = bf16[16,40,512]{2,1,0:T(8,128)(2,1)} all-to-all(bf16[16,40,512]{2,1,0:T(8,128)(2,1)S(1)} %broadcast_select_fusion), channel_id=1, replica_groups=mesh['section'=4,'expert'=16,'rep'=8] {'expert'}, dimensions={0} | all-to-all | bytes 1310720 | tf_op jit(solution)/shard_map/all_to_all | solution.py:67
  68.7 36.0 %all-gather.4.cloned.1.call-done = bf16[8,640,512]{2,1,0:T(8,128)(2,1)} async-done(((bf16[1,640,512]{2,1,0:T(8,128)(2,1)}), bf16[8,640,512]{2,1,0:T(8,128)(2,1)}) %all-gather.4.cloned.1.call-update) | async-done | bytes 5242896 | tf_op jit(solution)/shard_map/all_gather | solution.py:69
  104.7 4.1 %convolution_bitcast_fusion.2 = f32[640,128]{1,0:T(8,128)S(1)} fusion(bf16[8,640,512]{2,1,0:T(8,128)(2,1)} %all-gather.4.cloned.1.call-done, bf16[8,512,128]{2,1,0:T(8,128)(2,1)S(1)} %bitcast.54), kind=kOutput, calls=%fused_computation.6 | convolution fusion | flops 671088640 | bytes 6619136 | tf_op jit(solution)/shard_map/dot_general | solution.py:73
  108.8 2.2 %fusion.2 = bf16[640,128]{1,0:T(8,128)(2,1)} fusion(bf16[8,640,512]{2,1,0:T(8,128)(2,1)S(1)} %copy-done.4, bf16[8,512,128]{2,1,0:T(8,128)(2,1)S(1)} %bitcast.55, f32[640,128]{1,0:T(8,128)S(1)} %convolution_bitcast_fusion.2), kind=kOutput, calls=%fused_computation.7 | convolution fusion | flops 671580160 | bytes 6782976 | tf_op jit(solution)/shard_map/dot_general | solution.py:74
  111.0 32.2 %all-gather.6.cloned.1.call-done = bf16[5120,128]{1,0:T(8,128)(2,1)} async-done(((bf16[640,128]{1,0:T(8,128)(2,1)}), bf16[5120,128]{1,0:T(8,128)(2,1)}) %all-gather.6.cloned.1.call-update) | async-done | bytes 1310736 | tf_op jit(solution)/shard_map/all_gather | solution.py:76
  143.3 3.0 %fusion = bf16[640,512]{1,0:T(8,128)(2,1)} fusion(bf16[8,640,128]{2,1,0:T(8,128)(2,1)} %bitcast.53, bf16[8,128,512]{2,1,0:T(8,128)(2,1)S(1)} %bitcast.38), kind=kOutput, calls=%fused_computation.3 | convolution fusion | flops 671416320 | bytes 3014656 | tf_op jit(solution)/shard_map/dot_general | solution.py:78
  146.3 12.1 %all-to-all-start.1 = ((bf16[16,40,512]{2,1,0:T(8,128)(2,1)}), bf16[16,40,512]{2,1,0:T(8,128)(2,1)S(1)}, u32[]{:S(2)}, u32[]{:S(2)}) async-start(bf16[16,40,512]{2,1,0:T(8,128)(2,1)} %bitcast.16), calls=%async_computation.1 | async-start | bytes 1310720 | tf_op jit(solution)/shard_map/all_to_all | solution.py:81
  158.4 0.1 copy.83
  158.6 0.1 select_reduce_fusion.4
  158.7 0.1 copy.84
  158.8 0.1 copy.85
  159.0 0.1 copy.82
  159.1 0.1 gt.51
  159.3 0.1 copy.86
  159.4 0.1 add.95
  159.5 0.1 reduce_sum.143
  159.7 0.1 reduce_sum.144
  159.8 0.1 squeeze.7
  159.9 0.1 copy.73
  160.1 0.1 copy.66
  160.2 32.6 %all-to-all-done.1 = bf16[16,40,512]{2,1,0:T(8,128)(2,1)S(1)} async-done(((bf16[16,40,512]{2,1,0:T(8,128)(2,1)}), bf16[16,40,512]{2,1,0:T(8,128)(2,1)S(1)}, u32[]{:S(2)}, u32[]{:S(2)}) %all-to-all-start.1) | async-done | bytes 655392 | tf_op jit(solution)/shard_map/all_to_all | solution.py:81
  192.8 1.2 gather_fusion.1
  194.0 0.1 gather.12
  194.1 0.9 multiply_reduce_fusion
  194.9 3.4 %collective-permute-start = (bf16[128,512]{1,0:T(8,128)(2,1)S(1)}, bf16[128,512]{1,0:T(8,128)(2,1)S(1)}, u32[]{:S(2)}, u32[]{:S(2)}) collective-permute-start(bf16[128,512]{1,0:T(8,128)(2,1)S(1)} %multiply_reduce_fusion), channel_id=1, source_target_pairs={{0,128},{128,256},{256,384},{384,0},{1,129},{129,257},{257,385},{3... | collective-permute-start | bytes 393224 | tf_op jit(solution)/shard_map/ppermute | solution.py:10
  198.3 4.7 %collective-permute-done = bf16[128,512]{1,0:T(8,128)(2,1)S(1)} collective-permute-done((bf16[128,512]{1,0:T(8,128)(2,1)S(1)}, bf16[128,512]{1,0:T(8,128)(2,1)S(1)}, u32[]{:S(2)}, u32[]{:S(2)}) %collective-permute-start) | collective-permute-done | bytes 131104 | tf_op jit(solution)/shard_map/ppermute | solution.py:10
  203.0 0.7 copy.88
  (32 shorter events, 0.4 us)
Async XLA Ops:
  6.5 136.8 %copy-start = (bf16[1,1,1024,512]{3,2,1,0:T(8,128)(2,1)S(1)}, bf16[1,1,1024,512]{3,2,1,0:T(8,128)(2,1)}, u32[]{:S(2)}) copy-start(bf16[1,1,1024,512]{3,2,1,0:T(8,128)(2,1)} %param.17) | copy-start | bytes 3145732
  6.5 98.1 %all-gather.4.cloned.1.call-start = ((), (), s32[]{:S(2)}) async-start(), calls=%async_computation.2 | async-start | bytes 5898240 | tf_op jit(solution)/shard_map/all_gather | solution.py:69
  9.8 94.9 %copy-start.5 = (bf16[1,1,4096,128]{3,2,1,0:T(8,128)(2,1)S(1)}, bf16[1,1,4096,128]{3,2,1,0:T(8,128)(2,1)}, u32[]{:S(2)}) copy-start(bf16[1,1,4096,128]{3,2,1,0:T(8,128)(2,1)} %param.15) | copy-start | bytes 3145732
  16.9 91.9 %copy-start.6 = (bf16[1,1,4096,128]{3,2,1,0:T(8,128)(2,1)S(1)}, bf16[1,1,4096,128]{3,2,1,0:T(8,128)(2,1)}, u32[]{:S(2)}) copy-start(bf16[1,1,4096,128]{3,2,1,0:T(8,128)(2,1)} %param.16) | copy-start | bytes 3145732
  68.6 74.7 %all-gather.6.cloned.1.call-start = ((), (), s32[]{:S(2)}) async-start(), calls=%async_computation.3 | async-start | bytes 1474560 | tf_op jit(solution)/shard_map/all_gather | solution.py:76
  104.7 4.2 %copy-start.4 = (bf16[8,640,512]{2,1,0:T(8,128)(2,1)S(1)}, bf16[8,640,512]{2,1,0:T(8,128)(2,1)}, u32[]{:S(2)}) copy-start(bf16[8,640,512]{2,1,0:T(8,128)(2,1)} %all-gather.4.cloned.1.call-done) | copy-start | bytes 15728644
  111.0 47.4 %copy-start.1 = (s32[1,128,2]{1,2,0:T(2,128)S(1)}, s32[1,128,2]{1,2,0:T(2,128)}, u32[]{:S(2)}) copy-start(s32[1,128,2]{1,2,0:T(2,128)} %param.10) | copy-start | bytes 3076
  111.0 47.6 %copy-start.2 = (s32[1,16]{1,0:T(1,128)S(1)}, s32[1,16]{1,0:T(1,128)}, u32[]{:S(2)}) copy-start(s32[1,16]{1,0:T(1,128)} %param.14) | copy-start | bytes 196
  111.0 49.1 %copy-start.3 = (f32[1,128,2]{1,2,0:T(2,128)S(1)}, f32[1,128,2]{1,2,0:T(2,128)}, u32[]{:S(2)}) copy-start(f32[1,128,2]{1,2,0:T(2,128)} %param.11) | copy-start | bytes 3076
  146.3 46.5 %all-to-all-start.1 = ((bf16[16,40,512]{2,1,0:T(8,128)(2,1)}), bf16[16,40,512]{2,1,0:T(8,128)(2,1)S(1)}, u32[]{:S(2)}, u32[]{:S(2)}) async-start(bf16[16,40,512]{2,1,0:T(8,128)(2,1)} %bitcast.16), calls=%async_computation.1 | async-start | bytes 1310720 | tf_op jit(solution)/shard_map/all_to_all | solution.py:81
  194.9 8.1 %collective-permute-start = (bf16[128,512]{1,0:T(8,128)(2,1)S(1)}, bf16[128,512]{1,0:T(8,128)(2,1)S(1)}, u32[]{:S(2)}, u32[]{:S(2)}) collective-permute-start(bf16[128,512]{1,0:T(8,128)(2,1)S(1)} %multiply_reduce_fusion), channel_id=1, source_target_pairs={{0,128},{128,256},{256,384},{384,0},{1,129},{129,257},{257,385},{3... | collective-permute-start | bytes 393224 | tf_op jit(solution)/shard_map/ppermute | solution.py:10
Sparse Core Ops, SparseCore 0:
  68.7 35.8 all-gather.3
  111.2 32.0 all-gather.5

commit v2 on v1

--- a/solution.py
+++ b/solution.py
@@ -8,6 +8,22 @@
     count = lax.axis_size(axis)
     pairs = [(source, (source + steps) % count) for source in range(count)]
     return lax.ppermute(value, axis, pairs)
+
+
+def gathered(value, axis):
+    count = lax.axis_size(axis)
+    pieces = [value]
+    for shift in range(1, count):
+        pairs = [(source, (source + shift) % count) for source in range(count)]
+        pieces.append(lax.ppermute(value, axis, pairs))
+    return jnp.stack(pieces)
+
+
+def arrival_order(weight, axis):
+    count = lax.axis_size(axis)
+    me = lax.axis_index(axis)
+    origin = (me - jnp.arange(count, dtype=jnp.int32)) % count
+    return jnp.take(weight, origin, axis=0)
 
 
 def admission(chosen, language, capacity, experts):
@@ -66,15 +82,15 @@
     outgoing = jnp.take(with_blank, sources, axis=0)
     arrived = lax.all_to_all(outgoing, "expert", split_axis=0, concat_axis=0, tiled=True)
     flattened = arrived.reshape(-1, feat_width)
-    all_feats = lax.all_gather(flattened, "rep", axis=0)
-    gate_w = w_gate[0, 0].reshape(reps, feat_width, -1)
-    up_w = w_up[0, 0].reshape(reps, feat_width, -1)
+    all_feats = gathered(flattened, "rep")
+    gate_w = arrival_order(w_gate[0, 0].reshape(reps, feat_width, -1), "rep")
+    up_w = arrival_order(w_up[0, 0].reshape(reps, feat_width, -1), "rep")
     dims = (((0, 2), (0, 1)), ((), ()))
     gate_proj = lax.dot_general(all_feats, gate_w, dims, preferred_element_type=jnp.float32)
     up_proj = lax.dot_general(all_feats, up_w, dims, preferred_element_type=jnp.float32)
     activated = (jax.nn.silu(gate_proj) * up_proj).astype(jnp.bfloat16)
-    all_act = lax.all_gather(activated, "rep", axis=0)
-    down_w = w_down[0, 0].reshape(reps, activated.shape[1], -1)
+    all_act = gathered(activated, "rep")
+    down_w = arrival_order(w_down[0, 0].reshape(reps, activated.shape[1], -1), "rep")
     produced = lax.dot_general(all_act, down_w, dims, preferred_element_type=jnp.float32)
     out_width = down_w.shape[2]
     produced = produced.astype(jnp.bfloat16).reshape(experts, 2 * slot_depth, out_width)

time: 213 us -> 211 us (level)
  starting transfers between devices: 15.5 us -> 50.7 us
  waiting for transfers between devices: 106 us -> 73.8 us
  between operations: 13.6 us -> 0.47 us
  local copies, waits for them, and re-layouts: 7.95 us -> 19.2 us
  matrix products: 9.35 us -> 7.01 us
    all_gather x2 -> x0, waiting for transfers between devices: 68.2 us -> none  [the longest x1 36 us: local(): all_feats = lax.all_gather(flattened, 'rep', axis=0)]
    ppermute x0 -> x14, starting transfers between devices: none -> 42.7 us  [gathered(): pieces.append(lax.ppermute(value, axis, pairs))]
    ppermute x0 -> x14, waiting for transfers between devices: none -> 36.3 us  [gathered(): pieces.append(lax.ppermute(value, axis, pairs))]
    all_to_all x1, starting transfers between devices: 12.1 us -> 4.59 us  [local(): lax.all_to_all(produced, 'expert', split_axis=0, concat_axis=0, tiled=True)]
    unnamed x16 -> x31, local copies, waits for them, and re-layouts: 0.8 us -> 7.32 us
    gather x0 -> x3, local copies, waits for them, and re-layouts: none -> 4 us  [arrival_order(): return jnp.take(weight, origin, axis=0)]
    dot_general x1, matrix products: 4.14 us -> 1.59 us  [local(): lax.dot_general(all_feats, gate_w, dims, preferred_element_type=jnp.float32)]
  transfers between devices with their start and end apart: 4 -> 16, of which waited for: 4 -> 8; matrix products, arithmetic and copies ran while one was open for 1% -> 6% of each run, Pallas kernels for 0% -> 0%
where the time goes in v2:
time: 211 us; the launch traced here: 209 us
  waiting for transfers between devices  73.8 us (35%)
  blocking collectives  51.4 us (24%)
  starting transfers between devices  50.7 us (24%)
  local copies, waits for them, and re-layouts  19.2 us (9%)
  matrix products  7.01 us (3%)
  other arithmetic  6.85 us (3%)
    all_to_all x1, blocking collectives, local(): lax.all_to_all(outgoing, 'expert', split_axis=0, concat_axis=0, tiled=True)  51.4 us
    ppermute x14, starting transfers between devices, gathered(): pieces.append(lax.ppermute(value, axis, pairs))  42.7 us
    ppermute x14, waiting for transfers between devices, gathered(): pieces.append(lax.ppermute(value, axis, pairs))  36.3 us
    all_to_all x1, waiting for transfers between devices, local(): lax.all_to_all(produced, 'expert', split_axis=0, concat_axis=0, tiled=True)  32.9 us
    unnamed x31, local copies, waits for them, and re-layouts  7.32 us
    ppermute x1, waiting for transfers between devices, passed_along(): return lax.ppermute(value, axis, pairs)  4.67 us
    all_to_all x1, starting transfers between devices, local(): lax.all_to_all(produced, 'expert', split_axis=0, concat_axis=0, tiled=True)  4.59 us
  transfers between devices with their start and end apart: 16, of which 8 were waited for; matrix products, arithmetic and copies ran while one was open for 6% of the time, Pallas kernels for 0%

profile of v2, /device:TPU:24, one launch (start us, length us, event | category | flops | bytes accessed | tf_op | source)
XLA Modules:
  0.0 209.4 jit_solution(6330985670988926205)
XLA Ops:
  0.0 0.8 convert_reduce_fusion
  0.9 0.7 fusion.18
  1.6 1.2 multiply_reduce_fusion.1
  3.4 0.7 fusion.19
  4.2 0.7 select_reduce_fusion
  5.1 0.8 select_reduce_fusion.1
  6.4 0.9 concatenate.34
  7.4 2.8 %gather_fusion = bf16[640,512]{1,0:T(8,128)(2,1)S(1)} fusion(bf16[129,512]{1,0:T(8,128)(2,1)S(1)} %concatenate.34, s32[1024]{0:T(1024)S(1)} %pad_clamp_fusion.3), kind=kCustom, calls=%fused_computation.2 | custom fusion | bytes 1313280 | tf_op jit(solution)/shard_map/jit(_take)/gather | solution.py:82
  10.3 51.4 %all_to_all.10 = bf16[16,40,512]{2,1,0:T(8,128)(2,1)S(1)} all-to-all(bf16[16,40,512]{2,1,0:T(8,128)(2,1)S(1)} %broadcast_select_fusion), channel_id=1, replica_groups=mesh['section'=4,'expert'=16,'rep'=8] {'expert'}, dimensions={0} | all-to-all | bytes 1310720 | tf_op jit(solution)/shard_map/all_to_all | solution.py:83
  61.7 2.1 %collective-permute-start.1 = (bf16[640,512]{1,0:T(8,128)(2,1)S(1)}, bf16[640,512]{1,0:T(8,128)(2,1)}, u32[]{:S(2)}, u32[]{:S(2)}) collective-permute-start(bf16[640,512]{1,0:T(8,128)(2,1)S(1)} %bitcast.70), channel_id=1, source_target_pairs={{0,2},{1,3},{2,4},{3,5},{4,6},{5,7},{6,0},{7,1},{8,10},{9,11},{10,... | collective-permute-start | bytes 1966088 | tf_op jit(solution)/shard_map/ppermute | solution.py:18
  63.9 4.5 %collective-permute-start.2 = (bf16[640,512]{1,0:T(8,128)(2,1)S(1)}, bf16[640,512]{1,0:T(8,128)(2,1)}, u32[]{:S(2)}, u32[]{:S(2)}) collective-permute-start(bf16[640,512]{1,0:T(8,128)(2,1)S(1)} %bitcast.71), channel_id=1, source_target_pairs={{0,3},{1,4},{2,5},{3,6},{4,7},{5,0},{6,1},{7,2},{8,11},{9,12},{10,... | collective-permute-start | bytes 1966088 | tf_op jit(solution)/shard_map/ppermute | solution.py:18
  68.4 1.7 gather_fusion.3
  70.2 1.7 gather_fusion.4
  71.8 2.9 %collective-permute-start.3 = (bf16[640,512]{1,0:T(8,128)(2,1)S(1)}, bf16[640,512]{1,0:T(8,128)(2,1)S(1)}, u32[]{:S(2)}, u32[]{:S(2)}) collective-permute-start(bf16[640,512]{1,0:T(8,128)(2,1)S(1)} %bitcast.72), channel_id=1, source_target_pairs={{0,4},{1,5},{2,6},{3,7},{4,0},{5,1},{6,2},{7,3},{8,12},{9,13},{10,... | collective-permute-start | bytes 1966088 | tf_op jit(solution)/shard_map/ppermute | solution.py:18
  74.7 3.9 %collective-permute-start.4 = (bf16[640,512]{1,0:T(8,128)(2,1)S(1)}, bf16[640,512]{1,0:T(8,128)(2,1)S(1)}, u32[]{:S(2)}, u32[]{:S(2)}) collective-permute-start(bf16[640,512]{1,0:T(8,128)(2,1)S(1)} %bitcast.73), channel_id=1, source_target_pairs={{0,5},{1,6},{2,7},{3,0},{4,1},{5,2},{6,3},{7,4},{8,13},{9,14},{10,... | collective-permute-start | bytes 1966088 | tf_op jit(solution)/shard_map/ppermute | solution.py:18
  78.7 2.1 collective-permute-start.5
  81.4 9.6 %collective-permute-start.6 = (bf16[640,512]{1,0:T(8,128)(2,1)S(1)}, bf16[640,512]{1,0:T(8,128)(2,1)S(1)}, u32[]{:S(2)}, u32[]{:S(2)}) collective-permute-start(bf16[640,512]{1,0:T(8,128)(2,1)S(1)} %bitcast.76), channel_id=1, source_target_pairs={{0,7},{1,0},{2,1},{3,2},{4,3},{5,4},{6,5},{7,6},{8,15},{9,8},{10,9... | collective-permute-start | bytes 1966088 | tf_op jit(solution)/shard_map/ppermute | solution.py:18
  91.0 1.1 bitcast_dynamic-update-slice_fusion.5
  92.1 1.1 bitcast_dynamic-update-slice_fusion.4
  93.3 19.6 %collective-permute-done.4 = bf16[640,512]{1,0:T(8,128)(2,1)S(1)} collective-permute-done((bf16[640,512]{1,0:T(8,128)(2,1)S(1)}, bf16[640,512]{1,0:T(8,128)(2,1)S(1)}, u32[]{:S(2)}, u32[]{:S(2)}) %collective-permute-start.4) | collective-permute-done | bytes 655392 | tf_op jit(solution)/shard_map/ppermute | solution.py:18
  113.0 5.1 %collective-permute-done.5 = bf16[640,512]{1,0:T(8,128)(2,1)S(1)} collective-permute-done((bf16[640,512]{1,0:T(8,128)(2,1)S(1)}, bf16[640,512]{1,0:T(8,128)(2,1)S(1)}, u32[]{:S(2)}, u32[]{:S(2)}) %collective-permute-start.5) | collective-permute-done | bytes 655392 | tf_op jit(solution)/shard_map/ppermute | solution.py:18
  118.1 7.0 %collective-permute-done.6 = bf16[640,512]{1,0:T(8,128)(2,1)S(1)} collective-permute-done((bf16[640,512]{1,0:T(8,128)(2,1)S(1)}, bf16[640,512]{1,0:T(8,128)(2,1)S(1)}, u32[]{:S(2)}, u32[]{:S(2)}) %collective-permute-start.6) | collective-permute-done | bytes 655392 | tf_op jit(solution)/shard_map/ppermute | solution.py:18
  125.2 1.6 convolution_bitcast_fusion.2
  126.8 2.3 %bitcast_dynamic-update-slice_fusion.15 = (bf16[8,640,128]{2,1,0:T(8,128)(2,1)}, bf16[640,128]{1,0:T(8,128)(2,1)}) fusion(bf16[8,640,512]{2,1,0:T(8,128)(2,1)S(1)} %bitcast_dynamic-update-slice_fusion, bf16[8,512,128]{2,1,0:T(8,128)(2,1)S(1)} %copy-done.3, pred[8]{0:T(512)(128)(4,1)S(1)} %compare_and_fusion.1, f32[640,128]{1,0:T(8,128)S(1)} %convolution_bitcast_fusion.2), kind=kOutput, calls=%fused_computation.48 | convolution fusion | flops 672104448 | bytes 6946824 | tf_op jit(solution)/shard_map/dot_general | solution.py:90
  129.1 1.8 collective-permute-start.7
  131.0 0.6 gather_fusion.1
  131.6 2.5 %collective-permute-start.8 = (bf16[640,128]{1,0:T(8,128)(2,1)}, bf16[640,128]{1,0:T(8,128)(2,1)S(1)}, u32[]{:S(2)}, u32[]{:S(2)}) collective-permute-start(bf16[640,128]{1,0:T(8,128)(2,1)} %get-tuple-element.25), channel_id=1, source_target_pairs={{0,2},{1,3},{2,4},{3,5},{4,6},{5,7},{6,0},{7,1},{8,10},{9,11},{10,... | collective-permute-start | bytes 491528 | tf_op jit(solution)/shard_map/ppermute | solution.py:18
  134.1 3.2 %collective-permute-start.9 = (bf16[640,128]{1,0:T(8,128)(2,1)}, bf16[640,128]{1,0:T(8,128)(2,1)S(1)}, u32[]{:S(2)}, u32[]{:S(2)}) collective-permute-start(bf16[640,128]{1,0:T(8,128)(2,1)} %get-tuple-element.25), channel_id=1, source_target_pairs={{0,3},{1,4},{2,5},{3,6},{4,7},{5,0},{6,1},{7,2},{8,11},{9,12},{10,... | collective-permute-start | bytes 491528 | tf_op jit(solution)/shard_map/ppermute | solution.py:18
  137.3 3.5 %collective-permute-start.10 = (bf16[640,128]{1,0:T(8,128)(2,1)}, bf16[640,128]{1,0:T(8,128)(2,1)S(1)}, u32[]{:S(2)}, u32[]{:S(2)}) collective-permute-start(bf16[640,128]{1,0:T(8,128)(2,1)} %get-tuple-element.25), channel_id=1, source_target_pairs={{0,4},{1,5},{2,6},{3,7},{4,0},{5,1},{6,2},{7,3},{8,12},{9,13},{10,... | collective-permute-start | bytes 491528 | tf_op jit(solution)/shard_map/ppermute | solution.py:18
  140.8 4.1 %collective-permute-start.11 = (bf16[640,128]{1,0:T(8,128)(2,1)}, bf16[640,128]{1,0:T(8,128)(2,1)S(1)}, u32[]{:S(2)}, u32[]{:S(2)}) collective-permute-start(bf16[640,128]{1,0:T(8,128)(2,1)} %get-tuple-element.25), channel_id=1, source_target_pairs={{0,5},{1,6},{2,7},{3,0},{4,1},{5,2},{6,3},{7,4},{8,13},{9,14},{10,... | collective-permute-start | bytes 491528 | tf_op jit(solution)/shard_map/ppermute | solution.py:18
  144.8 2.7 %collective-permute-start.12 = (bf16[640,128]{1,0:T(8,128)(2,1)}, bf16[640,128]{1,0:T(8,128)(2,1)S(1)}, u32[]{:S(2)}, u32[]{:S(2)}) collective-permute-start(bf16[640,128]{1,0:T(8,128)(2,1)} %get-tuple-element.25), channel_id=1, source_target_pairs={{0,6},{1,7},{2,0},{3,1},{4,2},{5,3},{6,4},{7,5},{8,14},{9,15},{10,... | collective-permute-start | bytes 491528 | tf_op jit(solution)/shard_map/ppermute | solution.py:18
  147.5 0.7 bitcast_dynamic-update-slice_fusion.14
  148.2 0.7 bitcast_dynamic-update-slice_fusion.13
  148.9 0.7 bitcast_dynamic-update-slice_fusion.12
  149.6 0.7 bitcast_dynamic-update-slice_fusion.11
  150.2 0.8 collective-permute-done.11
  151.0 0.7 bitcast_dynamic-update-slice_fusion.10
  151.7 3.1 %collective-permute-done.12 = bf16[640,128]{1,0:T(8,128)(2,1)S(1)} collective-permute-done((bf16[640,128]{1,0:T(8,128)(2,1)}, bf16[640,128]{1,0:T(8,128)(2,1)S(1)}, u32[]{:S(2)}, u32[]{:S(2)}) %collective-permute-start.12) | collective-permute-done | bytes 163872 | tf_op jit(solution)/shard_map/ppermute | solution.py:18
  154.9 0.7 bitcast_dynamic-update-slice_fusion.9
  155.5 0.7 bitcast_dynamic-update-slice_fusion.8
  156.2 3.1 %fusion = bf16[640,512]{1,0:T(8,128)(2,1)} fusion(bf16[8,640,128]{2,1,0:T(8,128)(2,1)} %bitcast_dynamic-update-slice_fusion.8, bf16[8,128,512]{2,1,0:T(8,128)(2,1)S(1)} %gather_fusion.1, pred[8]{0:T(512)(128)(4,1)S(1)} %compare_and_fusion.1), kind=kOutput, calls=%fused_computation.6 | convolution fusion | flops 671940608 | bytes 3014664 | tf_op jit(solution)/shard_map/dot_general | solution.py:94
  159.3 4.6 %all-to-all-start.1 = ((bf16[16,40,512]{2,1,0:T(8,128)(2,1)}), bf16[16,40,512]{2,1,0:T(8,128)(2,1)S(1)}, u32[]{:S(2)}, u32[]{:S(2)}) async-start(bf16[16,40,512]{2,1,0:T(8,128)(2,1)} %bitcast.32), calls=%async_computation.1 | async-start | bytes 1310720 | tf_op jit(solution)/shard_map/all_to_all | solution.py:97
  165.7 32.9 %all-to-all-done.1 = bf16[16,40,512]{2,1,0:T(8,128)(2,1)S(1)} async-done(((bf16[16,40,512]{2,1,0:T(8,128)(2,1)}), bf16[16,40,512]{2,1,0:T(8,128)(2,1)S(1)}, u32[]{:S(2)}, u32[]{:S(2)}) %all-to-all-start.1) | async-done | bytes 655392 | tf_op jit(solution)/shard_map/all_to_all | solution.py:97
  198.6 1.2 gather_fusion.2
  199.8 0.9 multiply_reduce_fusion
  200.7 3.4 %collective-permute-start.14 = (bf16[128,512]{1,0:T(8,128)(2,1)S(1)}, bf16[128,512]{1,0:T(8,128)(2,1)S(1)}, u32[]{:S(2)}, u32[]{:S(2)}) collective-permute-start(bf16[128,512]{1,0:T(8,128)(2,1)S(1)} %multiply_reduce_fusion), channel_id=1, source_target_pairs={{0,128},{128,256},{256,384},{384,0},{1,129},{129,257},{257,385},{3... | collective-permute-start | bytes 393224 | tf_op jit(solution)/shard_map/ppermute | solution.py:10
  204.1 4.7 %collective-permute-done.14 = bf16[128,512]{1,0:T(8,128)(2,1)S(1)} collective-permute-done((bf16[128,512]{1,0:T(8,128)(2,1)S(1)}, bf16[128,512]{1,0:T(8,128)(2,1)S(1)}, u32[]{:S(2)}, u32[]{:S(2)}) %collective-permute-start.14) | collective-permute-done | bytes 131104 | tf_op jit(solution)/shard_map/ppermute | solution.py:10
  208.8 0.7 copy.94
  (79 shorter events, 4.4 us)
Async XLA Ops:
  0.0 68.4 %copy-start = (bf16[1,1,4096,128]{3,2,1,0:T(8,128)(2,1)S(1)}, bf16[1,1,4096,128]{3,2,1,0:T(8,128)(2,1)}, u32[]{:S(2)}) copy-start(bf16[1,1,4096,128]{3,2,1,0:T(8,128)(2,1)} %param.17) | copy-start | bytes 3145732
  7.4 62.8 %copy-start.1 = (bf16[1,1,4096,128]{3,2,1,0:T(8,128)(2,1)S(1)}, bf16[1,1,4096,128]{3,2,1,0:T(8,128)(2,1)}, u32[]{:S(2)}) copy-start(bf16[1,1,4096,128]{3,2,1,0:T(8,128)(2,1)} %param.18) | copy-start | bytes 3145732
  61.7 16.9 %collective-permute-start = (bf16[640,512]{1,0:T(8,128)(2,1)S(1)}, bf16[640,512]{1,0:T(8,128)(2,1)S(1)}, u32[]{:S(2)}, u32[]{:S(2)}) collective-permute-start(bf16[640,512]{1,0:T(8,128)(2,1)S(1)} %bitcast.69), channel_id=1, source_target_pairs={{0,1},{1,2},{2,3},{3,4},{4,5},{5,6},{6,7},{7,0},{8,9},{9,10},{10,1... | collective-permute-start | bytes 1966088 | tf_op jit(solution)/shard_map/ppermute | solution.py:18
  61.7 19.7 %collective-permute-start.1 = (bf16[640,512]{1,0:T(8,128)(2,1)S(1)}, bf16[640,512]{1,0:T(8,128)(2,1)}, u32[]{:S(2)}, u32[]{:S(2)}) collective-permute-start(bf16[640,512]{1,0:T(8,128)(2,1)S(1)} %bitcast.70), channel_id=1, source_target_pairs={{0,2},{1,3},{2,4},{3,5},{4,6},{5,7},{6,0},{7,1},{8,10},{9,11},{10,... | collective-permute-start | bytes 1966088 | tf_op jit(solution)/shard_map/ppermute | solution.py:18
  63.9 28.2 %collective-permute-start.2 = (bf16[640,512]{1,0:T(8,128)(2,1)S(1)}, bf16[640,512]{1,0:T(8,128)(2,1)}, u32[]{:S(2)}, u32[]{:S(2)}) collective-permute-start(bf16[640,512]{1,0:T(8,128)(2,1)S(1)} %bitcast.71), channel_id=1, source_target_pairs={{0,3},{1,4},{2,5},{3,6},{4,7},{5,0},{6,1},{7,2},{8,11},{9,12},{10,... | collective-permute-start | bytes 1966088 | tf_op jit(solution)/shard_map/ppermute | solution.py:18
  71.8 21.4 %collective-permute-start.3 = (bf16[640,512]{1,0:T(8,128)(2,1)S(1)}, bf16[640,512]{1,0:T(8,128)(2,1)S(1)}, u32[]{:S(2)}, u32[]{:S(2)}) collective-permute-start(bf16[640,512]{1,0:T(8,128)(2,1)S(1)} %bitcast.72), channel_id=1, source_target_pairs={{0,4},{1,5},{2,6},{3,7},{4,0},{5,1},{6,2},{7,3},{8,12},{9,13},{10,... | collective-permute-start | bytes 1966088 | tf_op jit(solution)/shard_map/ppermute | solution.py:18
  74.7 38.2 %collective-permute-start.4 = (bf16[640,512]{1,0:T(8,128)(2,1)S(1)}, bf16[640,512]{1,0:T(8,128)(2,1)S(1)}, u32[]{:S(2)}, u32[]{:S(2)}) collective-permute-start(bf16[640,512]{1,0:T(8,128)(2,1)S(1)} %bitcast.73), channel_id=1, source_target_pairs={{0,5},{1,6},{2,7},{3,0},{4,1},{5,2},{6,3},{7,4},{8,13},{9,14},{10,... | collective-permute-start | bytes 1966088 | tf_op jit(solution)/shard_map/ppermute | solution.py:18
  78.6 46.5 %copy-start.4 = (bf16[8,512,128]{2,1,0:T(8,128)(2,1)S(1)}, bf16[8,512,128]{2,1,0:T(8,128)(2,1)}, u32[]{:S(2)}) copy-start(bf16[8,512,128]{2,1,0:T(8,128)(2,1)} %gather_fusion.3) | copy-start | bytes 3145732
  78.7 39.3 %collective-permute-start.5 = (bf16[640,512]{1,0:T(8,128)(2,1)S(1)}, bf16[640,512]{1,0:T(8,128)(2,1)S(1)}, u32[]{:S(2)}, u32[]{:S(2)}) collective-permute-start(bf16[640,512]{1,0:T(8,128)(2,1)S(1)} %bitcast.75), channel_id=1, source_target_pairs={{0,6},{1,7},{2,0},{3,1},{4,2},{5,3},{6,4},{7,5},{8,14},{9,15},{10,... | collective-permute-start | bytes 1966088 | tf_op jit(solution)/shard_map/ppermute | solution.py:18
  81.4 43.7 %collective-permute-start.6 = (bf16[640,512]{1,0:T(8,128)(2,1)S(1)}, bf16[640,512]{1,0:T(8,128)(2,1)S(1)}, u32[]{:S(2)}, u32[]{:S(2)}) collective-permute-start(bf16[640,512]{1,0:T(8,128)(2,1)S(1)} %bitcast.76), channel_id=1, source_target_pairs={{0,7},{1,0},{2,1},{3,2},{4,3},{5,4},{6,5},{7,6},{8,15},{9,8},{10,9... | collective-permute-start | bytes 1966088 | tf_op jit(solution)/shard_map/ppermute | solution.py:18
  118.1 8.7 %copy-start.3 = (bf16[8,512,128]{2,1,0:T(8,128)(2,1)S(1)}, bf16[8,512,128]{2,1,0:T(8,128)(2,1)}, u32[]{:S(2)}) copy-start(bf16[8,512,128]{2,1,0:T(8,128)(2,1)} %gather_fusion.4) | copy-start | bytes 3145732
  126.8 4.1 %copy-start.2 = (bf16[1,1,1024,512]{3,2,1,0:T(8,128)(2,1)S(1)}, bf16[1,1,1024,512]{3,2,1,0:T(8,128)(2,1)}, u32[]{:S(2)}) copy-start(bf16[1,1,1024,512]{3,2,1,0:T(8,128)(2,1)} %param.19) | copy-start | bytes 3145732
  129.1 34.8 %copy-start.5 = (s32[1,128,2]{1,2,0:T(2,128)S(1)}, s32[1,128,2]{1,2,0:T(2,128)}, u32[]{:S(2)}) copy-start(s32[1,128,2]{1,2,0:T(2,128)} %param.12) | copy-start | bytes 3076
  129.1 15.7 %collective-permute-start.7 = (bf16[640,128]{1,0:T(8,128)(2,1)}, bf16[640,128]{1,0:T(8,128)(2,1)S(1)}, u32[]{:S(2)}, u32[]{:S(2)}) collective-permute-start(bf16[640,128]{1,0:T(8,128)(2,1)} %get-tuple-element.25), channel_id=1, source_target_pairs={{0,1},{1,2},{2,3},{3,4},{4,5},{5,6},{6,7},{7,0},{8,9},{9,10},{10,1... | collective-permute-start | bytes 491528 | tf_op jit(solution)/shard_map/ppermute | solution.py:18
  130.9 33.1 %copy-start.6 = (s32[1,16]{1,0:T(1,128)S(1)}, s32[1,16]{1,0:T(1,128)}, u32[]{:S(2)}) copy-start(s32[1,16]{1,0:T(1,128)} %param.16) | copy-start | bytes 196
  130.9 34.6 %copy-start.7 = (f32[1,128,2]{1,2,0:T(2,128)S(1)}, f32[1,128,2]{1,2,0:T(2,128)}, u32[]{:S(2)}) copy-start(f32[1,128,2]{1,2,0:T(2,128)} %param.13) | copy-start | bytes 3076
  131.6 16.6 %collective-permute-start.8 = (bf16[640,128]{1,0:T(8,128)(2,1)}, bf16[640,128]{1,0:T(8,128)(2,1)S(1)}, u32[]{:S(2)}, u32[]{:S(2)}) collective-permute-start(bf16[640,128]{1,0:T(8,128)(2,1)} %get-tuple-element.25), channel_id=1, source_target_pairs={{0,2},{1,3},{2,4},{3,5},{4,6},{5,7},{6,0},{7,1},{8,10},{9,11},{10,... | collective-permute-start | bytes 491528 | tf_op jit(solution)/shard_map/ppermute | solution.py:18
  134.1 14.8 %collective-permute-start.9 = (bf16[640,128]{1,0:T(8,128)(2,1)}, bf16[640,128]{1,0:T(8,128)(2,1)S(1)}, u32[]{:S(2)}, u32[]{:S(2)}) collective-permute-start(bf16[640,128]{1,0:T(8,128)(2,1)} %get-tuple-element.25), channel_id=1, source_target_pairs={{0,3},{1,4},{2,5},{3,6},{4,7},{5,0},{6,1},{7,2},{8,11},{9,12},{10,... | collective-permute-start | bytes 491528 | tf_op jit(solution)/shard_map/ppermute | solution.py:18
  137.3 12.3 %collective-permute-start.10 = (bf16[640,128]{1,0:T(8,128)(2,1)}, bf16[640,128]{1,0:T(8,128)(2,1)S(1)}, u32[]{:S(2)}, u32[]{:S(2)}) collective-permute-start(bf16[640,128]{1,0:T(8,128)(2,1)} %get-tuple-element.25), channel_id=1, source_target_pairs={{0,4},{1,5},{2,6},{3,7},{4,0},{5,1},{6,2},{7,3},{8,12},{9,13},{10,... | collective-permute-start | bytes 491528 | tf_op jit(solution)/shard_map/ppermute | solution.py:18
  140.8 10.3 %collective-permute-start.11 = (bf16[640,128]{1,0:T(8,128)(2,1)}, bf16[640,128]{1,0:T(8,128)(2,1)S(1)}, u32[]{:S(2)}, u32[]{:S(2)}) collective-permute-start(bf16[640,128]{1,0:T(8,128)(2,1)} %get-tuple-element.25), channel_id=1, source_target_pairs={{0,5},{1,6},{2,7},{3,0},{4,1},{5,2},{6,3},{7,4},{8,13},{9,14},{10,... | collective-permute-start | bytes 491528 | tf_op jit(solution)/shard_map/ppermute | solution.py:18
  144.8 10.0 %collective-permute-start.12 = (bf16[640,128]{1,0:T(8,128)(2,1)}, bf16[640,128]{1,0:T(8,128)(2,1)S(1)}, u32[]{:S(2)}, u32[]{:S(2)}) collective-permute-start(bf16[640,128]{1,0:T(8,128)(2,1)} %get-tuple-element.25), channel_id=1, source_target_pairs={{0,6},{1,7},{2,0},{3,1},{4,2},{5,3},{6,4},{7,5},{8,14},{9,15},{10,... | collective-permute-start | bytes 491528 | tf_op jit(solution)/shard_map/ppermute | solution.py:18
  148.2 7.3 %collective-permute-start.13 = (bf16[640,128]{1,0:T(8,128)(2,1)}, bf16[640,128]{1,0:T(8,128)(2,1)S(1)}, u32[]{:S(2)}, u32[]{:S(2)}) collective-permute-start(bf16[640,128]{1,0:T(8,128)(2,1)} %get-tuple-element.25), channel_id=1, source_target_pairs={{0,7},{1,0},{2,1},{3,2},{4,3},{5,4},{6,5},{7,6},{8,15},{9,8},{10,9... | collective-permute-start | bytes 491528 | tf_op jit(solution)/shard_map/ppermute | solution.py:18
  159.3 39.2 %all-to-all-start.1 = ((bf16[16,40,512]{2,1,0:T(8,128)(2,1)}), bf16[16,40,512]{2,1,0:T(8,128)(2,1)S(1)}, u32[]{:S(2)}, u32[]{:S(2)}) async-start(bf16[16,40,512]{2,1,0:T(8,128)(2,1)} %bitcast.32), calls=%async_computation.1 | async-start | bytes 1310720 | tf_op jit(solution)/shard_map/all_to_all | solution.py:97
  200.7 8.1 %collective-permute-start.14 = (bf16[128,512]{1,0:T(8,128)(2,1)S(1)}, bf16[128,512]{1,0:T(8,128)(2,1)S(1)}, u32[]{:S(2)}, u32[]{:S(2)}) collective-permute-start(bf16[128,512]{1,0:T(8,128)(2,1)S(1)} %multiply_reduce_fusion), channel_id=1, source_target_pairs={{0,128},{128,256},{256,384},{384,0},{1,129},{129,257},{257,385},{3... | collective-permute-start | bytes 393224 | tf_op jit(solution)/shard_map/ppermute | solution.py:10

commit v3 on v2

--- a/solution.py
+++ b/solution.py
@@ -82,9 +82,9 @@
     outgoing = jnp.take(with_blank, sources, axis=0)
     arrived = lax.all_to_all(outgoing, "expert", split_axis=0, concat_axis=0, tiled=True)
     flattened = arrived.reshape(-1, feat_width)
-    all_feats = gathered(flattened, "rep")
-    gate_w = arrival_order(w_gate[0, 0].reshape(reps, feat_width, -1), "rep")
-    up_w = arrival_order(w_up[0, 0].reshape(reps, feat_width, -1), "rep")
+    all_feats = lax.all_gather(flattened, "rep", axis=0)
+    gate_w = w_gate[0, 0].reshape(reps, feat_width, -1)
+    up_w = w_up[0, 0].reshape(reps, feat_width, -1)
     dims = (((0, 2), (0, 1)), ((), ()))
     gate_proj = lax.dot_general(all_feats, gate_w, dims, preferred_element_type=jnp.float32)
     up_proj = lax.dot_general(all_feats, up_w, dims, preferred_element_type=jnp.float32)

time: 211 us -> 206 us (0.976)
  starting transfers between devices: 50.7 us -> 33.3 us
  between operations: 0.47 us -> 13.7 us
  local copies, waits for them, and re-layouts: 19.2 us -> 12.4 us
  waiting for transfers between devices: 73.8 us -> 77.9 us
  matrix products: 7.01 us -> 9.5 us
    all_gather x0 -> x1, waiting for transfers between devices: none -> 36 us  [local(): all_feats = lax.all_gather(flattened, 'rep', axis=0)]
    ppermute x14 -> x7, waiting for transfers between devices: 36.3 us -> 4.03 us  [gathered(): pieces.append(lax.ppermute(value, axis, pairs))]
    ppermute x14 -> x7, starting transfers between devices: 42.7 us -> 17.5 us  [gathered(): pieces.append(lax.ppermute(value, axis, pairs))]
    all_to_all x1, starting transfers between devices: 4.59 us -> 12.4 us  [local(): lax.all_to_all(produced, 'expert', split_axis=0, concat_axis=0, tiled=True)]
    gather x3 -> x1, local copies, waits for them, and re-layouts: 4 us -> 0.61 us  [arrival_order(): return jnp.take(weight, origin, axis=0)]
    dot_general x1, matrix products: 1.59 us -> 4.14 us  [local(): lax.dot_general(all_feats, gate_w, dims, preferred_element_type=jnp.float32)]
    unnamed x31 -> x24, local copies, waits for them, and re-layouts: 7.32 us -> 4.83 us
  transfers between devices with their start and end apart: 16 -> 10, of which waited for: 8 -> 5; matrix products, arithmetic and copies ran while one was open for 6% -> 3% of each run, Pallas kernels for 0% -> 0%
where the time goes in v3:
time: 206 us; the launch traced here: 205 us
  waiting for transfers between devices  77.9 us (38%)
  blocking collectives  51.7 us (25%)
  starting transfers between devices  33.3 us (16%)
  between operations  13.7 us (7%)
  local copies, waits for them, and re-layouts  12.4 us (6%)
  matrix products  9.5 us (5%)
  other arithmetic  6.18 us (3%)
    all_to_all x1, blocking collectives, local(): lax.all_to_all(outgoing, 'expert', split_axis=0, concat_axis=0, tiled=True)  51.7 us
    all_gather x1, waiting for transfers between devices, local(): all_feats = lax.all_gather(flattened, 'rep', axis=0)  36 us
    all_to_all x1, waiting for transfers between devices, local(): lax.all_to_all(produced, 'expert', split_axis=0, concat_axis=0, tiled=True)  33.1 us
    ppermute x7, starting transfers between devices, gathered(): pieces.append(lax.ppermute(value, axis, pairs))  17.5 us
    all_to_all x1, starting transfers between devices, local(): lax.all_to_all(produced, 'expert', split_axis=0, concat_axis=0, tiled=True)  12.4 us
    unnamed x24, local copies, waits for them, and re-layouts  4.83 us
    ppermute x1, waiting for transfers between devices, passed_along(): return lax.ppermute(value, axis, pairs)  4.68 us
    dot_general x1, matrix products, local(): lax.dot_general(all_feats, gate_w, dims, preferred_element_type=jnp.float32)  4.14 us
  transfers between devices with their start and end apart: 10, of which 5 were waited for; matrix products, arithmetic and copies ran while one was open for 3% of the time, Pallas kernels for 0%

profile of v3, /device:TPU:24, one launch (start us, length us, event | category | flops | bytes accessed | tf_op | source)
XLA Modules:
  0.0 204.6 jit_solution(10758804920488303382)
XLA Ops:
  6.5 0.8 convert_reduce_fusion
  7.4 0.7 fusion.14
  8.2 1.2 multiply_reduce_fusion.1
  9.4 0.2 reduce_window_sum.29
  9.6 0.2 reduce_window_sum.30
  10.1 0.1 multiply_reduce_fusion.4
  10.2 0.7 select_reduce_fusion
  11.1 0.7 select_reduce_fusion.1
  12.4 2.8 %gather_fusion = bf16[640,512]{1,0:T(8,128)(2,1)S(1)} fusion(bf16[129,512]{1,0:T(8,128)(2,1)S(1)} %concatenate.34, s32[1024]{0:T(1024)S(1)} %pad_clamp_fusion.2), kind=kCustom, calls=%fused_computation | custom fusion | bytes 1313280 | tf_op jit(solution)/shard_map/jit(_take)/gather | solution.py:82
  15.2 0.2 broadcast_select_fusion
  15.3 51.7 %all_to_all.10 = bf16[16,40,512]{2,1,0:T(8,128)(2,1)} all-to-all(bf16[16,40,512]{2,1,0:T(8,128)(2,1)S(1)} %broadcast_select_fusion), channel_id=1, replica_groups=mesh['section'=4,'expert'=16,'rep'=8] {'expert'}, dimensions={0} | all-to-all | bytes 1310720 | tf_op jit(solution)/shard_map/all_to_all | solution.py:83
  67.0 36.0 %all-gather.2.cloned.1.call-done = bf16[8,640,512]{2,1,0:T(8,128)(2,1)} async-done(((bf16[1,640,512]{2,1,0:T(8,128)(2,1)}), bf16[8,640,512]{2,1,0:T(8,128)(2,1)}) %all-gather.2.cloned.1.call-update) | async-done | bytes 5242896 | tf_op jit(solution)/shard_map/all_gather | solution.py:85
  103.1 4.1 %convolution_bitcast_fusion.2 = f32[640,128]{1,0:T(8,128)S(1)} fusion(bf16[8,640,512]{2,1,0:T(8,128)(2,1)} %all-gather.2.cloned.1.call-done, bf16[8,512,128]{2,1,0:T(8,128)(2,1)S(1)} %bitcast.70), kind=kOutput, calls=%fused_computation.7 | convolution fusion | flops 671088640 | bytes 6619136 | tf_op jit(solution)/shard_map/dot_general | solution.py:89
  107.2 2.2 %bitcast_dynamic-update-slice_fusion.7 = (bf16[8,640,128]{2,1,0:T(8,128)(2,1)}, bf16[640,128]{1,0:T(8,128)(2,1)}) fusion(bf16[8,640,512]{2,1,0:T(8,128)(2,1)S(1)} %copy-done.6, bf16[8,512,128]{2,1,0:T(8,128)(2,1)S(1)} %bitcast.54, f32[640,128]{1,0:T(8,128)S(1)} %convolution_bitcast_fusion.2), kind=kOutput, calls=%fused_computation.33 | convolution fusion | flops 671580160 | bytes 6946816 | tf_op jit(solution)/shard_map/dot_general | solution.py:90
  109.5 0.3 collective-permute-start
  109.8 0.6 gather_fusion.1
  110.4 4.3 %collective-permute-start.1 = (bf16[640,128]{1,0:T(8,128)(2,1)}, bf16[640,128]{1,0:T(8,128)(2,1)S(1)}, u32[]{:S(2)}, u32[]{:S(2)}) collective-permute-start(bf16[640,128]{1,0:T(8,128)(2,1)} %get-tuple-element.24), channel_id=1, source_target_pairs={{0,2},{1,3},{2,4},{3,5},{4,6},{5,7},{6,0},{7,1},{8,10},{9,11},{10,... | collective-permute-start | bytes 491528 | tf_op jit(solution)/shard_map/ppermute | solution.py:18
  114.7 2.8 %collective-permute-start.2 = (bf16[640,128]{1,0:T(8,128)(2,1)}, bf16[640,128]{1,0:T(8,128)(2,1)S(1)}, u32[]{:S(2)}, u32[]{:S(2)}) collective-permute-start(bf16[640,128]{1,0:T(8,128)(2,1)} %get-tuple-element.24), channel_id=1, source_target_pairs={{0,3},{1,4},{2,5},{3,6},{4,7},{5,0},{6,1},{7,2},{8,11},{9,12},{10,... | collective-permute-start | bytes 491528 | tf_op jit(solution)/shard_map/ppermute | solution.py:18
  117.5 4.3 %collective-permute-start.3 = (bf16[640,128]{1,0:T(8,128)(2,1)}, bf16[640,128]{1,0:T(8,128)(2,1)S(1)}, u32[]{:S(2)}, u32[]{:S(2)}) collective-permute-start(bf16[640,128]{1,0:T(8,128)(2,1)} %get-tuple-element.24), channel_id=1, source_target_pairs={{0,4},{1,5},{2,6},{3,7},{4,0},{5,1},{6,2},{7,3},{8,12},{9,13},{10,... | collective-permute-start | bytes 491528 | tf_op jit(solution)/shard_map/ppermute | solution.py:18
  121.8 2.7 %collective-permute-start.4 = (bf16[640,128]{1,0:T(8,128)(2,1)}, bf16[640,128]{1,0:T(8,128)(2,1)S(1)}, u32[]{:S(2)}, u32[]{:S(2)}) collective-permute-start(bf16[640,128]{1,0:T(8,128)(2,1)} %get-tuple-element.24), channel_id=1, source_target_pairs={{0,5},{1,6},{2,7},{3,0},{4,1},{5,2},{6,3},{7,4},{8,13},{9,14},{10,... | collective-permute-start | bytes 491528 | tf_op jit(solution)/shard_map/ppermute | solution.py:18
  124.6 2.3 %collective-permute-start.5 = (bf16[640,128]{1,0:T(8,128)(2,1)}, bf16[640,128]{1,0:T(8,128)(2,1)S(1)}, u32[]{:S(2)}, u32[]{:S(2)}) collective-permute-start(bf16[640,128]{1,0:T(8,128)(2,1)} %get-tuple-element.24), channel_id=1, source_target_pairs={{0,6},{1,7},{2,0},{3,1},{4,2},{5,3},{6,4},{7,5},{8,14},{9,15},{10,... | collective-permute-start | bytes 491528 | tf_op jit(solution)/shard_map/ppermute | solution.py:18
  126.9 0.7 bitcast_dynamic-update-slice_fusion.6
  127.5 0.8 collective-permute-start.6
  128.3 0.7 bitcast_dynamic-update-slice_fusion.5
  129.0 0.7 bitcast_dynamic-update-slice_fusion.4
  129.7 0.7 bitcast_dynamic-update-slice_fusion.3
  130.3 1.5 collective-permute-done.4
  131.8 0.7 bitcast_dynamic-update-slice_fusion.2
  132.5 2.5 %collective-permute-done.5 = bf16[640,128]{1,0:T(8,128)(2,1)S(1)} collective-permute-done((bf16[640,128]{1,0:T(8,128)(2,1)}, bf16[640,128]{1,0:T(8,128)(2,1)S(1)}, u32[]{:S(2)}, u32[]{:S(2)}) %collective-permute-start.5) | collective-permute-done | bytes 163872 | tf_op jit(solution)/shard_map/ppermute | solution.py:18
  135.0 0.7 bitcast_dynamic-update-slice_fusion.1
  135.7 0.7 bitcast_dynamic-update-slice_fusion
  136.4 3.1 %fusion = bf16[640,512]{1,0:T(8,128)(2,1)} fusion(bf16[8,640,128]{2,1,0:T(8,128)(2,1)} %bitcast_dynamic-update-slice_fusion, bf16[8,128,512]{2,1,0:T(8,128)(2,1)S(1)} %gather_fusion.1, pred[8]{0:T(512)(128)(4,1)S(1)} %compare_and_fusion.1), kind=kOutput, calls=%fused_computation.4 | convolution fusion | flops 671940608 | bytes 3014664 | tf_op jit(solution)/shard_map/dot_general | solution.py:94
  139.5 12.4 %all-to-all-start.1 = ((bf16[16,40,512]{2,1,0:T(8,128)(2,1)}), bf16[16,40,512]{2,1,0:T(8,128)(2,1)S(1)}, u32[]{:S(2)}, u32[]{:S(2)}) async-start(bf16[16,40,512]{2,1,0:T(8,128)(2,1)} %bitcast.24), calls=%async_computation.1 | async-start | bytes 1310720 | tf_op jit(solution)/shard_map/all_to_all | solution.py:97
  151.9 0.1 copy.83
  152.2 0.1 copy.84
  152.5 0.1 copy.82
  152.6 0.1 gt.51
  152.9 0.1 add.131
  153.0 0.1 reduce_sum.143
  153.2 0.1 reduce_sum.144
  153.3 0.1 squeeze.7
  153.4 0.1 copy.73
  153.7 33.1 %all-to-all-done.1 = bf16[16,40,512]{2,1,0:T(8,128)(2,1)S(1)} async-done(((bf16[16,40,512]{2,1,0:T(8,128)(2,1)}), bf16[16,40,512]{2,1,0:T(8,128)(2,1)S(1)}, u32[]{:S(2)}, u32[]{:S(2)}) %all-to-all-start.1) | async-done | bytes 655392 | tf_op jit(solution)/shard_map/all_to_all | solution.py:97
  186.9 1.2 gather_fusion.2
  188.1 0.9 multiply_reduce_fusion
  189.0 3.4 %collective-permute-start.7 = (bf16[128,512]{1,0:T(8,128)(2,1)S(1)}, bf16[128,512]{1,0:T(8,128)(2,1)S(1)}, u32[]{:S(2)}, u32[]{:S(2)}) collective-permute-start(bf16[128,512]{1,0:T(8,128)(2,1)S(1)} %multiply_reduce_fusion), channel_id=1, source_target_pairs={{0,128},{128,256},{256,384},{384,0},{1,129},{129,257},{257,385},{3... | collective-permute-start | bytes 393224 | tf_op jit(solution)/shard_map/ppermute | solution.py:10
  192.4 4.7 %collective-permute-done.7 = bf16[128,512]{1,0:T(8,128)(2,1)S(1)} collective-permute-done((bf16[128,512]{1,0:T(8,128)(2,1)S(1)}, bf16[128,512]{1,0:T(8,128)(2,1)S(1)}, u32[]{:S(2)}, u32[]{:S(2)}) %collective-permute-start.7) | collective-permute-done | bytes 131104 | tf_op jit(solution)/shard_map/ppermute | solution.py:10
  197.1 0.7 copy.95
  (56 shorter events, 1.8 us)
Async XLA Ops:
  6.5 100.7 %copy-start = (bf16[1,1,4096,128]{3,2,1,0:T(8,128)(2,1)S(1)}, bf16[1,1,4096,128]{3,2,1,0:T(8,128)(2,1)}, u32[]{:S(2)}) copy-start(bf16[1,1,4096,128]{3,2,1,0:T(8,128)(2,1)} %param.16) | copy-start | bytes 3145732
  6.5 3.5 %copy-start.4 = (s32[1,16]{1,0:T(1,128)S(1)}, s32[1,16]{1,0:T(1,128)}, u32[]{:S(2)}) copy-start(s32[1,16]{1,0:T(1,128)} %param.14) | copy-start | bytes 196
  6.5 5.8 %copy-start.2 = (bf16[1,128,512]{2,1,0:T(8,128)(2,1)S(1)}, bf16[1,128,512]{2,1,0:T(8,128)(2,1)}, u32[]{:S(2)}) copy-start(bf16[1,128,512]{2,1,0:T(8,128)(2,1)} %param.9) | copy-start | bytes 393220
  6.5 96.5 %all-gather.2.cloned.1.call-start = ((), (), s32[]{:S(2)}) async-start(), calls=%async_computation.2 | async-start | bytes 5898240 | tf_op jit(solution)/shard_map/all_gather | solution.py:85
  15.3 87.7 %copy-start.7 = (bf16[1,1,4096,128]{3,2,1,0:T(8,128)(2,1)S(1)}, bf16[1,1,4096,128]{3,2,1,0:T(8,128)(2,1)}, u32[]{:S(2)}) copy-start(bf16[1,1,4096,128]{3,2,1,0:T(8,128)(2,1)} %param.15) | copy-start | bytes 3145732
  103.1 4.2 %copy-start.6 = (bf16[8,640,512]{2,1,0:T(8,128)(2,1)S(1)}, bf16[8,640,512]{2,1,0:T(8,128)(2,1)}, u32[]{:S(2)}) copy-start(bf16[8,640,512]{2,1,0:T(8,128)(2,1)} %all-gather.2.cloned.1.call-done) | copy-start | bytes 15728644
  107.2 2.5 %copy-start.1 = (bf16[1,1,1024,512]{3,2,1,0:T(8,128)(2,1)S(1)}, bf16[1,1,1024,512]{3,2,1,0:T(8,128)(2,1)}, u32[]{:S(2)}) copy-start(bf16[1,1,1024,512]{3,2,1,0:T(8,128)(2,1)} %param.17) | copy-start | bytes 3145732
  109.5 15.1 %collective-permute-start = (bf16[640,128]{1,0:T(8,128)(2,1)}, bf16[640,128]{1,0:T(8,128)(2,1)S(1)}, u32[]{:S(2)}, u32[]{:S(2)}) collective-permute-start(bf16[640,128]{1,0:T(8,128)(2,1)} %get-tuple-element.24), channel_id=1, source_target_pairs={{0,1},{1,2},{2,3},{3,4},{4,5},{5,6},{6,7},{7,0},{8,9},{9,10},{10,1... | collective-permute-start | bytes 491528 | tf_op jit(solution)/shard_map/ppermute | solution.py:18
  110.4 17.1 %collective-permute-start.1 = (bf16[640,128]{1,0:T(8,128)(2,1)}, bf16[640,128]{1,0:T(8,128)(2,1)S(1)}, u32[]{:S(2)}, u32[]{:S(2)}) collective-permute-start(bf16[640,128]{1,0:T(8,128)(2,1)} %get-tuple-element.24), channel_id=1, source_target_pairs={{0,2},{1,3},{2,4},{3,5},{4,6},{5,7},{6,0},{7,1},{8,10},{9,11},{10,... | collective-permute-start | bytes 491528 | tf_op jit(solution)/shard_map/ppermute | solution.py:18
  114.7 14.3 %collective-permute-start.2 = (bf16[640,128]{1,0:T(8,128)(2,1)}, bf16[640,128]{1,0:T(8,128)(2,1)S(1)}, u32[]{:S(2)}, u32[]{:S(2)}) collective-permute-start(bf16[640,128]{1,0:T(8,128)(2,1)} %get-tuple-element.24), channel_id=1, source_target_pairs={{0,3},{1,4},{2,5},{3,6},{4,7},{5,0},{6,1},{7,2},{8,11},{9,12},{10,... | collective-permute-start | bytes 491528 | tf_op jit(solution)/shard_map/ppermute | solution.py:18
  117.5 12.1 %collective-permute-start.3 = (bf16[640,128]{1,0:T(8,128)(2,1)}, bf16[640,128]{1,0:T(8,128)(2,1)S(1)}, u32[]{:S(2)}, u32[]{:S(2)}) collective-permute-start(bf16[640,128]{1,0:T(8,128)(2,1)} %get-tuple-element.24), channel_id=1, source_target_pairs={{0,4},{1,5},{2,6},{3,7},{4,0},{5,1},{6,2},{7,3},{8,12},{9,13},{10,... | collective-permute-start | bytes 491528 | tf_op jit(solution)/shard_map/ppermute | solution.py:18
  121.8 10.0 %collective-permute-start.4 = (bf16[640,128]{1,0:T(8,128)(2,1)}, bf16[640,128]{1,0:T(8,128)(2,1)S(1)}, u32[]{:S(2)}, u32[]{:S(2)}) collective-permute-start(bf16[640,128]{1,0:T(8,128)(2,1)} %get-tuple-element.24), channel_id=1, source_target_pairs={{0,5},{1,6},{2,7},{3,0},{4,1},{5,2},{6,3},{7,4},{8,13},{9,14},{10,... | collective-permute-start | bytes 491528 | tf_op jit(solution)/shard_map/ppermute | solution.py:18
  124.6 10.5 %collective-permute-start.5 = (bf16[640,128]{1,0:T(8,128)(2,1)}, bf16[640,128]{1,0:T(8,128)(2,1)S(1)}, u32[]{:S(2)}, u32[]{:S(2)}) collective-permute-start(bf16[640,128]{1,0:T(8,128)(2,1)} %get-tuple-element.24), channel_id=1, source_target_pairs={{0,6},{1,7},{2,0},{3,1},{4,2},{5,3},{6,4},{7,5},{8,14},{9,15},{10,... | collective-permute-start | bytes 491528 | tf_op jit(solution)/shard_map/ppermute | solution.py:18
  127.5 8.2 %collective-permute-start.6 = (bf16[640,128]{1,0:T(8,128)(2,1)}, bf16[640,128]{1,0:T(8,128)(2,1)S(1)}, u32[]{:S(2)}, u32[]{:S(2)}) collective-permute-start(bf16[640,128]{1,0:T(8,128)(2,1)} %get-tuple-element.24), channel_id=1, source_target_pairs={{0,7},{1,0},{2,1},{3,2},{4,3},{5,4},{6,5},{7,6},{8,15},{9,8},{10,9... | collective-permute-start | bytes 491528 | tf_op jit(solution)/shard_map/ppermute | solution.py:18
  139.5 12.4 %copy-start.3 = (s32[1,128,2]{1,2,0:T(2,128)S(1)}, s32[1,128,2]{1,2,0:T(2,128)}, u32[]{:S(2)}) copy-start(s32[1,128,2]{1,2,0:T(2,128)} %param.10) | copy-start | bytes 3076
  139.5 14.1 %copy-start.5 = (f32[1,128,2]{1,2,0:T(2,128)S(1)}, f32[1,128,2]{1,2,0:T(2,128)}, u32[]{:S(2)}) copy-start(f32[1,128,2]{1,2,0:T(2,128)} %param.11) | copy-start | bytes 3076
  139.5 47.4 %all-to-all-start.1 = ((bf16[16,40,512]{2,1,0:T(8,128)(2,1)}), bf16[16,40,512]{2,1,0:T(8,128)(2,1)S(1)}, u32[]{:S(2)}, u32[]{:S(2)}) async-start(bf16[16,40,512]{2,1,0:T(8,128)(2,1)} %bitcast.24), calls=%async_computation.1 | async-start | bytes 1310720 | tf_op jit(solution)/shard_map/all_to_all | solution.py:97
  189.0 8.1 %collective-permute-start.7 = (bf16[128,512]{1,0:T(8,128)(2,1)S(1)}, bf16[128,512]{1,0:T(8,128)(2,1)S(1)}, u32[]{:S(2)}, u32[]{:S(2)}) collective-permute-start(bf16[128,512]{1,0:T(8,128)(2,1)S(1)} %multiply_reduce_fusion), channel_id=1, source_target_pairs={{0,128},{128,256},{256,384},{384,0},{1,129},{129,257},{257,385},{3... | collective-permute-start | bytes 393224 | tf_op jit(solution)/shard_map/ppermute | solution.py:10
Sparse Core Ops, SparseCore 0:
  67.1 35.8 all-gather.1

commit v4 on v3

--- a/solution.py
+++ b/solution.py
@@ -78,23 +78,27 @@
     )
     main_source = slot_sources(admitted, main_slot, slot_depth)
     spill_source = slot_sources(spill_marks, spill_places, slot_depth)
-    sources = jnp.concatenate([main_source, spill_source], axis=1)
-    outgoing = jnp.take(with_blank, sources, axis=0)
-    arrived = lax.all_to_all(outgoing, "expert", split_axis=0, concat_axis=0, tiled=True)
-    flattened = arrived.reshape(-1, feat_width)
-    all_feats = lax.all_gather(flattened, "rep", axis=0)
     gate_w = w_gate[0, 0].reshape(reps, feat_width, -1)
     up_w = w_up[0, 0].reshape(reps, feat_width, -1)
+    down_local = w_down[0, 0]
     dims = (((0, 2), (0, 1)), ((), ()))
-    gate_proj = lax.dot_general(all_feats, gate_w, dims, preferred_element_type=jnp.float32)
-    up_proj = lax.dot_general(all_feats, up_w, dims, preferred_element_type=jnp.float32)
-    activated = (jax.nn.silu(gate_proj) * up_proj).astype(jnp.bfloat16)
-    all_act = gathered(activated, "rep")
-    down_w = arrival_order(w_down[0, 0].reshape(reps, activated.shape[1], -1), "rep")
-    produced = lax.dot_general(all_act, down_w, dims, preferred_element_type=jnp.float32)
-    out_width = down_w.shape[2]
-    produced = produced.astype(jnp.bfloat16).reshape(experts, 2 * slot_depth, out_width)
-    returned = lax.all_to_all(produced, "expert", split_axis=0, concat_axis=0, tiled=True)
+
+    def stream(sources):
+        outgoing = jnp.take(with_blank, sources, axis=0)
+        arrived = lax.all_to_all(outgoing, "expert", split_axis=0, concat_axis=0, tiled=True)
+        flattened = arrived.reshape(-1, feat_width)
+        all_feats = lax.all_gather(flattened, "rep", axis=0)
+        gate_proj = lax.dot_general(all_feats, gate_w, dims, preferred_element_type=jnp.float32)
+        up_proj = lax.dot_general(all_feats, up_w, dims, preferred_element_type=jnp.float32)
+        activated = (jax.nn.silu(gate_proj) * up_proj).astype(jnp.bfloat16)
+        all_act = gathered(activated, "rep")
+        down_w = arrival_order(down_local.reshape(reps, activated.shape[1], -1), "rep")
+        produced = lax.dot_general(all_act, down_w, dims, preferred_element_type=jnp.float32)
+        produced = produced.astype(jnp.bfloat16).reshape(experts, slot_depth, -1)
+        return lax.all_to_all(produced, "expert", split_axis=0, concat_axis=0, tiled=True)
+
+    returned = jnp.concatenate([stream(main_source), stream(spill_source)], axis=1)
+    out_width = returned.shape[2]
     id_match = (chosen[:, :, None] == expert_iota[None, None, :]).astype(jnp.int32)
     row_kept = jnp.sum(id_match * admitted[:, None, :], axis=2)
     row_main = jnp.sum(id_match * main_slot[:, None, :], axis=2)

time: 206 us -> 266 us (1.29)
  starting transfers between devices: 33.3 us -> 54.5 us
  blocking collectives: 51.7 us -> 67.7 us
  waiting for transfers between devices: 77.9 us -> 90.5 us
  local copies, waits for them, and re-layouts: 12.4 us -> 19.4 us
    ppermute x7 -> x14, waiting for transfers between devices: 4.03 us -> 26.9 us  [gathered(): pieces.append(lax.ppermute(value, axis, pairs))]
    all_to_all x1 -> x2, blocking collectives: 51.7 us -> 67.7 us  [stream(): lax.all_to_all(outgoing, 'expert', split_axis=0, concat_axis=0, tiled=True)]
    ppermute x7 -> x14, starting transfers between devices: 17.5 us -> 33 us  [gathered(): pieces.append(lax.ppermute(value, axis, pairs))]
    all_gather x1 -> x2, waiting for transfers between devices: 36 us -> 25.1 us  [stream(): all_feats = lax.all_gather(flattened, 'rep', axis=0)]
    all_to_all x1 -> x2, starting transfers between devices: 12.4 us -> 18.1 us  [stream(): lax.all_to_all(produced, 'expert', split_axis=0, concat_axis=0, tiled=True)]
    dot_general x3 -> x6, matrix products: 9.5 us -> 10.6 us  [the longest x2 5.44 us: stream(): lax.dot_general(all_feats, gate_w, dims, preferred_element_type=jnp.float32)]
    all_to_all x1 -> x2, waiting for transfers between devices: 33.1 us -> 33.7 us  [stream(): lax.all_to_all(produced, 'expert', split_axis=0, concat_axis=0, tiled=True)]
  transfers between devices with their start and end apart: 10 -> 19, of which waited for: 5 -> 11; matrix products, arithmetic and copies ran while one was open for 3% -> 9% of each run, Pallas kernels for 0% -> 0%
where the time goes in v4:
time: 266 us; the launch traced here: 265 us
  waiting for transfers between devices  90.5 us (34%)
  blocking collectives  67.7 us (25%)
  starting transfers between devices  54.5 us (20%)
  local copies, waits for them, and re-layouts  19.4 us (7%)
  between operations  13.9 us (5%)
  matrix products  10.6 us (4%)
  other arithmetic  8.31 us (3%)
    all_to_all x2, blocking collectives, stream(): lax.all_to_all(outgoing, 'expert', split_axis=0, concat_axis=0, tiled=True)  67.7 us
    all_to_all x2, waiting for transfers between devices, stream(): lax.all_to_all(produced, 'expert', split_axis=0, concat_axis=0, tiled=True)  33.7 us
    ppermute x14, starting transfers between devices, gathered(): pieces.append(lax.ppermute(value, axis, pairs))  33 us
    ppermute x14, waiting for transfers between devices, gathered(): pieces.append(lax.ppermute(value, axis, pairs))  26.9 us
    all_gather x2, waiting for transfers between devices, stream(): all_feats = lax.all_gather(flattened, 'rep', axis=0)  25.1 us
    all_to_all x2, starting transfers between devices, stream(): lax.all_to_all(produced, 'expert', split_axis=0, concat_axis=0, tiled=True)  18.1 us
    dot_general x2, matrix products, stream(): lax.dot_general(all_feats, gate_w, dims, preferred_element_type=jnp.float32)  5.44 us
  transfers between devices with their start and end apart: 19, of which 11 were waited for; matrix products, arithmetic and copies ran while one was open for 9% of the time, Pallas kernels for 0%

profile of v4, /device:TPU:24, one launch (start us, length us, event | category | flops | bytes accessed | tf_op | source)
XLA Modules:
  0.0 265.0 jit_solution(12584977853264097388)
XLA Ops:
  6.5 0.8 convert_reduce_fusion
  7.4 0.7 fusion.14
  8.2 1.2 multiply_reduce_fusion.1
  11.4 0.7 select_reduce_fusion
  12.4 0.8 select_reduce_fusion.1
  13.5 0.9 concatenate.6
  14.4 2.0 gather_fusion.1
  16.6 38.8 %all_to_all.20 = bf16[16,20,512]{2,1,0:T(8,128)(2,1)S(1)} all-to-all(bf16[16,20,512]{2,1,0:T(8,128)(2,1)S(1)} %broadcast_select_fusion.5), channel_id=1, replica_groups=mesh['section'=4,'expert'=16,'rep'=8] {'expert'}, dimensions={0} | all-to-all | bytes 655360 | tf_op jit(solution)/shard_map/all_to_all | solution.py:88
  55.4 0.8 all_gather_reshape.6
  56.9 2.0 gather_fusion.3
  59.1 0.9 broadcast_select_fusion.4
  60.0 28.9 %all_to_all.21 = bf16[16,20,512]{2,1,0:T(8,128)(2,1)S(1)} all-to-all(bf16[16,20,512]{2,1,0:T(8,128)(2,1)S(1)} %broadcast_select_fusion.4), channel_id=1, replica_groups=mesh['section'=4,'expert'=16,'rep'=8] {'expert'}, dimensions={0} | all-to-all | bytes 655360 | tf_op jit(solution)/shard_map/all_to_all | solution.py:88
  88.9 0.8 all_gather_reshape.7
  89.8 1.6 gather_fusion.2
  91.5 2.7 %convolution_bitcast_fusion.5 = f32[320,128]{1,0:T(8,128)S(1)} fusion(bf16[8,320,512]{2,1,0:T(8,128)(2,1)} %all-gather.3.cloned.1.call-done, bf16[8,512,128]{2,1,0:T(8,128)(2,1)S(1)} %bitcast.81), kind=kOutput, calls=%fused_computation.13 | convolution fusion | flops 335544320 | bytes 3833856 | tf_op jit(solution)/shard_map/dot_general | solution.py:91
  94.2 1.5 bitcast_dynamic-update-slice_fusion.15
  95.7 25.1 %all-gather.5.cloned.1.call-done = bf16[8,320,512]{2,1,0:T(8,128)(2,1)} async-done(((bf16[1,320,512]{2,1,0:T(8,128)(2,1)}), bf16[8,320,512]{2,1,0:T(8,128)(2,1)}) %all-gather.5.cloned.1.call-update) | async-done | bytes 2621456 | tf_op jit(solution)/shard_map/all_gather | solution.py:90
  120.8 2.7 %convolution_bitcast_fusion.3 = f32[320,128]{1,0:T(8,128)S(1)} fusion(bf16[8,320,512]{2,1,0:T(8,128)(2,1)} %all-gather.5.cloned.1.call-done, bf16[8,512,128]{2,1,0:T(8,128)(2,1)S(1)} %bitcast.82), kind=kOutput, calls=%fused_computation.10 | convolution fusion | flops 335544320 | bytes 3833856 | tf_op jit(solution)/shard_map/dot_general | solution.py:91
  123.5 1.5 bitcast_dynamic-update-slice_fusion.7
  125.0 3.0 %collective-permute-start.12 = (bf16[320,128]{1,0:T(8,128)(2,1)S(1)}, bf16[320,128]{1,0:T(8,128)(2,1)S(1)}, u32[]{:S(2)}, u32[]{:S(2)}) collective-permute-start(bf16[320,128]{1,0:T(8,128)(2,1)S(1)} %get-tuple-element.30), channel_id=1, source_target_pairs={{0,6},{1,7},{2,0},{3,1},{4,2},{5,3},{6,4},{7,5},{8,14},{9,15},{10,... | collective-permute-start | bytes 245768 | tf_op jit(solution)/shard_map/ppermute | solution.py:18
  128.0 3.4 %collective-permute-start.11 = (bf16[320,128]{1,0:T(8,128)(2,1)S(1)}, bf16[320,128]{1,0:T(8,128)(2,1)S(1)}, u32[]{:S(2)}, u32[]{:S(2)}) collective-permute-start(bf16[320,128]{1,0:T(8,128)(2,1)S(1)} %get-tuple-element.30), channel_id=1, source_target_pairs={{0,5},{1,6},{2,7},{3,0},{4,1},{5,2},{6,3},{7,4},{8,13},{9,14},{10,... | collective-permute-start | bytes 245768 | tf_op jit(solution)/shard_map/ppermute | solution.py:18
  131.4 3.6 %collective-permute-start.10 = (bf16[320,128]{1,0:T(8,128)(2,1)S(1)}, bf16[320,128]{1,0:T(8,128)(2,1)S(1)}, u32[]{:S(2)}, u32[]{:S(2)}) collective-permute-start(bf16[320,128]{1,0:T(8,128)(2,1)S(1)} %get-tuple-element.30), channel_id=1, source_target_pairs={{0,4},{1,5},{2,6},{3,7},{4,0},{5,1},{6,2},{7,3},{8,12},{9,13},{10,... | collective-permute-start | bytes 245768 | tf_op jit(solution)/shard_map/ppermute | solution.py:18
  134.9 2.8 %collective-permute-start.9 = (bf16[320,128]{1,0:T(8,128)(2,1)S(1)}, bf16[320,128]{1,0:T(8,128)(2,1)S(1)}, u32[]{:S(2)}, u32[]{:S(2)}) collective-permute-start(bf16[320,128]{1,0:T(8,128)(2,1)S(1)} %get-tuple-element.30), channel_id=1, source_target_pairs={{0,3},{1,4},{2,5},{3,6},{4,7},{5,0},{6,1},{7,2},{8,11},{9,12},{10,... | collective-permute-start | bytes 245768 | tf_op jit(solution)/shard_map/ppermute | solution.py:18
  137.7 3.2 %collective-permute-start.1 = (bf16[320,128]{1,0:T(8,128)(2,1)S(1)}, bf16[320,128]{1,0:T(8,128)(2,1)S(1)}, u32[]{:S(2)}, u32[]{:S(2)}) collective-permute-start(bf16[320,128]{1,0:T(8,128)(2,1)S(1)} %get-tuple-element.32), channel_id=1, source_target_pairs={{0,2},{1,3},{2,4},{3,5},{4,6},{5,7},{6,0},{7,1},{8,10},{9,11},{10,... | collective-permute-start | bytes 245768 | tf_op jit(solution)/shard_map/ppermute | solution.py:18
  140.9 3.8 %collective-permute-done.1 = bf16[320,128]{1,0:T(8,128)(2,1)S(1)} collective-permute-done((bf16[320,128]{1,0:T(8,128)(2,1)S(1)}, bf16[320,128]{1,0:T(8,128)(2,1)S(1)}, u32[]{:S(2)}, u32[]{:S(2)}) %collective-permute-start.1) | collective-permute-done | bytes 81952 | tf_op jit(solution)/shard_map/ppermute | solution.py:18
  144.7 4.3 %collective-permute-start.2 = (bf16[320,128]{1,0:T(8,128)(2,1)S(1)}, bf16[320,128]{1,0:T(8,128)(2,1)S(1)}, u32[]{:S(2)}, u32[]{:S(2)}) collective-permute-start(bf16[320,128]{1,0:T(8,128)(2,1)S(1)} %get-tuple-element.32), channel_id=1, source_target_pairs={{0,3},{1,4},{2,5},{3,6},{4,7},{5,0},{6,1},{7,2},{8,11},{9,12},{10,... | collective-permute-start | bytes 245768 | tf_op jit(solution)/shard_map/ppermute | solution.py:18
  149.0 3.0 %collective-permute-done.2 = bf16[320,128]{1,0:T(8,128)(2,1)S(1)} collective-permute-done((bf16[320,128]{1,0:T(8,128)(2,1)S(1)}, bf16[320,128]{1,0:T(8,128)(2,1)S(1)}, u32[]{:S(2)}, u32[]{:S(2)}) %collective-permute-start.2) | collective-permute-done | bytes 81952 | tf_op jit(solution)/shard_map/ppermute | solution.py:18
  152.0 3.6 %collective-permute-start.3 = (bf16[320,128]{1,0:T(8,128)(2,1)S(1)}, bf16[320,128]{1,0:T(8,128)(2,1)S(1)}, u32[]{:S(2)}, u32[]{:S(2)}) collective-permute-start(bf16[320,128]{1,0:T(8,128)(2,1)S(1)} %get-tuple-element.32), channel_id=1, source_target_pairs={{0,4},{1,5},{2,6},{3,7},{4,0},{5,1},{6,2},{7,3},{8,12},{9,13},{10,... | collective-permute-start | bytes 245768 | tf_op jit(solution)/shard_map/ppermute | solution.py:18
  155.6 4.2 %collective-permute-done.3 = bf16[320,128]{1,0:T(8,128)(2,1)S(1)} collective-permute-done((bf16[320,128]{1,0:T(8,128)(2,1)S(1)}, bf16[320,128]{1,0:T(8,128)(2,1)S(1)}, u32[]{:S(2)}, u32[]{:S(2)}) %collective-permute-start.3) | collective-permute-done | bytes 81952 | tf_op jit(solution)/shard_map/ppermute | solution.py:18
  159.8 2.0 collective-permute-start.4
  161.8 4.9 %collective-permute-done.4 = bf16[320,128]{1,0:T(8,128)(2,1)S(1)} collective-permute-done((bf16[320,128]{1,0:T(8,128)(2,1)S(1)}, bf16[320,128]{1,0:T(8,128)(2,1)S(1)}, u32[]{:S(2)}, u32[]{:S(2)}) %collective-permute-start.4) | collective-permute-done | bytes 81952 | tf_op jit(solution)/shard_map/ppermute | solution.py:18
  166.8 2.4 collective-permute-start.5
  169.2 5.4 %collective-permute-done.5 = bf16[320,128]{1,0:T(8,128)(2,1)S(1)} collective-permute-done((bf16[320,128]{1,0:T(8,128)(2,1)S(1)}, bf16[320,128]{1,0:T(8,128)(2,1)S(1)}, u32[]{:S(2)}, u32[]{:S(2)}) %collective-permute-start.5) | collective-permute-done | bytes 81952 | tf_op jit(solution)/shard_map/ppermute | solution.py:18
  174.7 2.0 collective-permute-done.6
  176.7 2.7 %collective-permute-start.7 = (bf16[320,128]{1,0:T(8,128)(2,1)S(1)}, bf16[320,128]{1,0:T(8,128)(2,1)S(1)}, u32[]{:S(2)}, u32[]{:S(2)}) collective-permute-start(bf16[320,128]{1,0:T(8,128)(2,1)S(1)} %get-tuple-element.30), channel_id=1, source_target_pairs={{0,1},{1,2},{2,3},{3,4},{4,5},{5,6},{6,7},{7,0},{8,9},{9,10},{10,1... | collective-permute-start | bytes 245768 | tf_op jit(solution)/shard_map/ppermute | solution.py:18
  180.0 0.8 reshape.226
  180.8 12.3 %all-to-all-start.1 = ((bf16[16,20,512]{2,1,0:T(8,128)(2,1)}), bf16[16,20,512]{2,1,0:T(8,128)(2,1)S(1)}, u32[]{:S(2)}, u32[]{:S(2)}) async-start(bf16[16,20,512]{2,1,0:T(8,128)(2,1)} %reshape.226), calls=%async_computation.1 | async-start | bytes 786432 | tf_op jit(solution)/shard_map/all_to_all | solution.py:98
  193.1 2.2 collective-permute-start.8
  196.0 3.5 %collective-permute-done.8 = bf16[320,128]{1,0:T(8,128)(2,1)S(1)} collective-permute-done((bf16[320,128]{1,0:T(8,128)(2,1)S(1)}, bf16[320,128]{1,0:T(8,128)(2,1)S(1)}, u32[]{:S(2)}, u32[]{:S(2)}) %collective-permute-start.8) | collective-permute-done | bytes 81952 | tf_op jit(solution)/shard_map/ppermute | solution.py:18
  203.3 1.7 fusion.1
  205.0 0.8 reshape.227
  205.8 11.5 %all-to-all-done.1 = bf16[16,20,512]{2,1,0:T(8,128)(2,1)S(1)} async-done(((bf16[16,20,512]{2,1,0:T(8,128)(2,1)}), bf16[16,20,512]{2,1,0:T(8,128)(2,1)S(1)}, u32[]{:S(2)}, u32[]{:S(2)}) %all-to-all-start.1) | async-done | bytes 327712 | tf_op jit(solution)/shard_map/all_to_all | solution.py:98
  217.3 5.8 %all-to-all-start.3 = ((bf16[16,20,512]{2,1,0:T(8,128)(2,1)}), bf16[16,20,512]{2,1,0:T(8,128)(2,1)S(1)}, u32[]{:S(2)}, u32[]{:S(2)}) async-start(bf16[16,20,512]{2,1,0:T(8,128)(2,1)} %reshape.227), calls=%async_computation.3 | async-start | bytes 786432 | tf_op jit(solution)/shard_map/all_to_all | solution.py:98
  224.9 22.2 %all-to-all-done.3 = bf16[16,20,512]{2,1,0:T(8,128)(2,1)S(1)} async-done(((bf16[16,20,512]{2,1,0:T(8,128)(2,1)}), bf16[16,20,512]{2,1,0:T(8,128)(2,1)S(1)}, u32[]{:S(2)}, u32[]{:S(2)}) %all-to-all-start.3) | async-done | bytes 327712 | tf_op jit(solution)/shard_map/all_to_all | solution.py:98
  247.3 1.2 gather_fusion
  248.5 0.9 multiply_reduce_fusion
  249.4 3.4 %collective-permute-start.14 = (bf16[128,512]{1,0:T(8,128)(2,1)S(1)}, bf16[128,512]{1,0:T(8,128)(2,1)S(1)}, u32[]{:S(2)}, u32[]{:S(2)}) collective-permute-start(bf16[128,512]{1,0:T(8,128)(2,1)S(1)} %multiply_reduce_fusion), channel_id=1, source_target_pairs={{0,128},{128,256},{256,384},{384,0},{1,129},{129,257},{257,385},{3... | collective-permute-start | bytes 393224 | tf_op jit(solution)/shard_map/ppermute | solution.py:10
  252.8 4.7 %collective-permute-done.14 = bf16[128,512]{1,0:T(8,128)(2,1)S(1)} collective-permute-done((bf16[128,512]{1,0:T(8,128)(2,1)S(1)}, bf16[128,512]{1,0:T(8,128)(2,1)S(1)}, u32[]{:S(2)}, u32[]{:S(2)}) %collective-permute-start.14) | collective-permute-done | bytes 131104 | tf_op jit(solution)/shard_map/ppermute | solution.py:10
  (100 shorter events, 11.5 us)
Async XLA Ops:
  6.5 87.7 %copy-start = (bf16[1,1,4096,128]{3,2,1,0:T(8,128)(2,1)S(1)}, bf16[1,1,4096,128]{3,2,1,0:T(8,128)(2,1)}, u32[]{:S(2)}) copy-start(bf16[1,1,4096,128]{3,2,1,0:T(8,128)(2,1)} %param.20) | copy-start | bytes 3145732
  6.5 84.9 %all-gather.3.cloned.1.call-start = ((), (), s32[]{:S(2)}) async-start(), calls=%async_computation.4 | async-start | bytes 2949120 | tf_op jit(solution)/shard_map/all_gather | solution.py:90
  56.2 64.5 %all-gather.5.cloned.1.call-start = ((), (), s32[]{:S(2)}) async-start(), calls=%async_computation.5 | async-start | bytes 2949120 | tf_op jit(solution)/shard_map/all_gather | solution.py:90
  59.0 32.5 %copy-start.1 = (bf16[1,1,4096,128]{3,2,1,0:T(8,128)(2,1)S(1)}, bf16[1,1,4096,128]{3,2,1,0:T(8,128)(2,1)}, u32[]{:S(2)}) copy-start(bf16[1,1,4096,128]{3,2,1,0:T(8,128)(2,1)} %param.19) | copy-start | bytes 3145732
  59.1 30.7 %copy-start.4 = (bf16[1,1,1024,512]{3,2,1,0:T(8,128)(2,1)S(1)}, bf16[1,1,1024,512]{3,2,1,0:T(8,128)(2,1)}, u32[]{:S(2)}) copy-start(bf16[1,1,1024,512]{3,2,1,0:T(8,128)(2,1)} %param.21) | copy-start | bytes 3145732
  91.5 2.8 %copy-start.2 = (bf16[8,320,512]{2,1,0:T(8,128)(2,1)S(1)}, bf16[8,320,512]{2,1,0:T(8,128)(2,1)}, u32[]{:S(2)}) copy-start(bf16[8,320,512]{2,1,0:T(8,128)(2,1)} %all-gather.3.cloned.1.call-done) | copy-start | bytes 7864324
  95.7 42.0 %collective-permute-start = (bf16[320,128]{1,0:T(8,128)(2,1)S(1)}, bf16[320,128]{1,0:T(8,128)(2,1)S(1)}, u32[]{:S(2)}, u32[]{:S(2)}) collective-permute-start(bf16[320,128]{1,0:T(8,128)(2,1)S(1)} %get-tuple-element.32), channel_id=1, source_target_pairs={{0,1},{1,2},{2,3},{3,4},{4,5},{5,6},{6,7},{7,0},{8,9},{9,10},{10,1... | collective-permute-start | bytes 245768 | tf_op jit(solution)/shard_map/ppermute | solution.py:18
  120.8 2.7 %copy-start.3 = (bf16[8,320,512]{2,1,0:T(8,128)(2,1)S(1)}, bf16[8,320,512]{2,1,0:T(8,128)(2,1)}, u32[]{:S(2)}) copy-start(bf16[8,320,512]{2,1,0:T(8,128)(2,1)} %all-gather.5.cloned.1.call-done) | copy-start | bytes 7864324
  123.5 17.4 %copy-start.10 = (bf16[8,320,128]{2,1,0:T(8,128)(2,1)S(1)}, bf16[8,320,128]{2,1,0:T(8,128)(2,1)}, u32[]{:S(2)}) copy-start(bf16[8,320,128]{2,1,0:T(8,128)(2,1)} %get-tuple-element.31) | copy-start | bytes 1966084
  123.5 55.9 %copy-start.5 = (bf16[8,128,512]{2,1,0:T(8,128)(2,1)S(1)}, bf16[8,128,512]{2,1,0:T(8,128)(2,1)}, u32[]{:S(2)}) copy-start(bf16[8,128,512]{2,1,0:T(8,128)(2,1)} %gather_fusion.2) | copy-start | bytes 3145732
  125.0 77.0 %collective-permute-start.12 = (bf16[320,128]{1,0:T(8,128)(2,1)S(1)}, bf16[320,128]{1,0:T(8,128)(2,1)S(1)}, u32[]{:S(2)}, u32[]{:S(2)}) collective-permute-start(bf16[320,128]{1,0:T(8,128)(2,1)S(1)} %get-tuple-element.30), channel_id=1, source_target_pairs={{0,6},{1,7},{2,0},{3,1},{4,2},{5,3},{6,4},{7,5},{8,14},{9,15},{10,... | collective-permute-start | bytes 245768 | tf_op jit(solution)/shard_map/ppermute | solution.py:18
  128.0 73.4 %collective-permute-start.11 = (bf16[320,128]{1,0:T(8,128)(2,1)S(1)}, bf16[320,128]{1,0:T(8,128)(2,1)S(1)}, u32[]{:S(2)}, u32[]{:S(2)}) collective-permute-start(bf16[320,128]{1,0:T(8,128)(2,1)S(1)} %get-tuple-element.30), channel_id=1, source_target_pairs={{0,5},{1,6},{2,7},{3,0},{4,1},{5,2},{6,3},{7,4},{8,13},{9,14},{10,... | collective-permute-start | bytes 245768 | tf_op jit(solution)/shard_map/ppermute | solution.py:18
  131.4 69.4 %collective-permute-start.10 = (bf16[320,128]{1,0:T(8,128)(2,1)S(1)}, bf16[320,128]{1,0:T(8,128)(2,1)S(1)}, u32[]{:S(2)}, u32[]{:S(2)}) collective-permute-start(bf16[320,128]{1,0:T(8,128)(2,1)S(1)} %get-tuple-element.30), channel_id=1, source_target_pairs={{0,4},{1,5},{2,6},{3,7},{4,0},{5,1},{6,2},{7,3},{8,12},{9,13},{10,... | collective-permute-start | bytes 245768 | tf_op jit(solution)/shard_map/ppermute | solution.py:18
  134.9 65.2 %collective-permute-start.9 = (bf16[320,128]{1,0:T(8,128)(2,1)S(1)}, bf16[320,128]{1,0:T(8,128)(2,1)S(1)}, u32[]{:S(2)}, u32[]{:S(2)}) collective-permute-start(bf16[320,128]{1,0:T(8,128)(2,1)S(1)} %get-tuple-element.30), channel_id=1, source_target_pairs={{0,3},{1,4},{2,5},{3,6},{4,7},{5,0},{6,1},{7,2},{8,11},{9,12},{10,... | collective-permute-start | bytes 245768 | tf_op jit(solution)/shard_map/ppermute | solution.py:18
  137.7 7.0 %collective-permute-start.1 = (bf16[320,128]{1,0:T(8,128)(2,1)S(1)}, bf16[320,128]{1,0:T(8,128)(2,1)S(1)}, u32[]{:S(2)}, u32[]{:S(2)}) collective-permute-start(bf16[320,128]{1,0:T(8,128)(2,1)S(1)} %get-tuple-element.32), channel_id=1, source_target_pairs={{0,2},{1,3},{2,4},{3,5},{4,6},{5,7},{6,0},{7,1},{8,10},{9,11},{10,... | collective-permute-start | bytes 245768 | tf_op jit(solution)/shard_map/ppermute | solution.py:18
  144.7 7.3 %collective-permute-start.2 = (bf16[320,128]{1,0:T(8,128)(2,1)S(1)}, bf16[320,128]{1,0:T(8,128)(2,1)S(1)}, u32[]{:S(2)}, u32[]{:S(2)}) collective-permute-start(bf16[320,128]{1,0:T(8,128)(2,1)S(1)} %get-tuple-element.32), channel_id=1, source_target_pairs={{0,3},{1,4},{2,5},{3,6},{4,7},{5,0},{6,1},{7,2},{8,11},{9,12},{10,... | collective-permute-start | bytes 245768 | tf_op jit(solution)/shard_map/ppermute | solution.py:18
  152.0 7.8 %collective-permute-start.3 = (bf16[320,128]{1,0:T(8,128)(2,1)S(1)}, bf16[320,128]{1,0:T(8,128)(2,1)S(1)}, u32[]{:S(2)}, u32[]{:S(2)}) collective-permute-start(bf16[320,128]{1,0:T(8,128)(2,1)S(1)} %get-tuple-element.32), channel_id=1, source_target_pairs={{0,4},{1,5},{2,6},{3,7},{4,0},{5,1},{6,2},{7,3},{8,12},{9,13},{10,... | collective-permute-start | bytes 245768 | tf_op jit(solution)/shard_map/ppermute | solution.py:18
  159.8 7.0 %collective-permute-start.4 = (bf16[320,128]{1,0:T(8,128)(2,1)S(1)}, bf16[320,128]{1,0:T(8,128)(2,1)S(1)}, u32[]{:S(2)}, u32[]{:S(2)}) collective-permute-start(bf16[320,128]{1,0:T(8,128)(2,1)S(1)} %get-tuple-element.32), channel_id=1, source_target_pairs={{0,5},{1,6},{2,7},{3,0},{4,1},{5,2},{6,3},{7,4},{8,13},{9,14},{10,... | collective-permute-start | bytes 245768 | tf_op jit(solution)/shard_map/ppermute | solution.py:18
  166.8 7.9 %collective-permute-start.5 = (bf16[320,128]{1,0:T(8,128)(2,1)S(1)}, bf16[320,128]{1,0:T(8,128)(2,1)S(1)}, u32[]{:S(2)}, u32[]{:S(2)}) collective-permute-start(bf16[320,128]{1,0:T(8,128)(2,1)S(1)} %get-tuple-element.32), channel_id=1, source_target_pairs={{0,6},{1,7},{2,0},{3,1},{4,2},{5,3},{6,4},{7,5},{8,14},{9,15},{10,... | collective-permute-start | bytes 245768 | tf_op jit(solution)/shard_map/ppermute | solution.py:18
  174.7 2.1 collective-permute-start.6
  176.7 16.4 %collective-permute-start.7 = (bf16[320,128]{1,0:T(8,128)(2,1)S(1)}, bf16[320,128]{1,0:T(8,128)(2,1)S(1)}, u32[]{:S(2)}, u32[]{:S(2)}) collective-permute-start(bf16[320,128]{1,0:T(8,128)(2,1)S(1)} %get-tuple-element.30), channel_id=1, source_target_pairs={{0,1},{1,2},{2,3},{3,4},{4,5},{5,6},{6,7},{7,0},{8,9},{9,10},{10,1... | collective-permute-start | bytes 245768 | tf_op jit(solution)/shard_map/ppermute | solution.py:18
  180.8 36.5 %all-to-all-start.1 = ((bf16[16,20,512]{2,1,0:T(8,128)(2,1)}), bf16[16,20,512]{2,1,0:T(8,128)(2,1)S(1)}, u32[]{:S(2)}, u32[]{:S(2)}) async-start(bf16[16,20,512]{2,1,0:T(8,128)(2,1)} %reshape.226), calls=%async_computation.1 | async-start | bytes 786432 | tf_op jit(solution)/shard_map/all_to_all | solution.py:98
  193.1 6.3 %collective-permute-start.8 = (bf16[320,128]{1,0:T(8,128)(2,1)S(1)}, bf16[320,128]{1,0:T(8,128)(2,1)S(1)}, u32[]{:S(2)}, u32[]{:S(2)}) collective-permute-start(bf16[320,128]{1,0:T(8,128)(2,1)S(1)} %get-tuple-element.30), channel_id=1, source_target_pairs={{0,2},{1,3},{2,4},{3,5},{4,6},{5,7},{6,0},{7,1},{8,10},{9,11},{10,... | collective-permute-start | bytes 245768 | tf_op jit(solution)/shard_map/ppermute | solution.py:18
  199.5 3.2 %collective-permute-start.13 = (bf16[320,128]{1,0:T(8,128)(2,1)S(1)}, bf16[320,128]{1,0:T(8,128)(2,1)S(1)}, u32[]{:S(2)}, u32[]{:S(2)}) collective-permute-start(bf16[320,128]{1,0:T(8,128)(2,1)S(1)} %get-tuple-element.30), channel_id=1, source_target_pairs={{0,7},{1,0},{2,1},{3,2},{4,3},{5,4},{6,5},{7,6},{8,15},{9,8},{10,9... | collective-permute-start | bytes 245768 | tf_op jit(solution)/shard_map/ppermute | solution.py:18
  200.7 22.3 %copy-start.7 = (s32[1,128,2]{1,2,0:T(2,128)S(1)}, s32[1,128,2]{1,2,0:T(2,128)}, u32[]{:S(2)}) copy-start(s32[1,128,2]{1,2,0:T(2,128)} %param.14) | copy-start | bytes 3076
  201.4 21.8 %copy-start.9 = (f32[1,128,2]{1,2,0:T(2,128)S(1)}, f32[1,128,2]{1,2,0:T(2,128)}, u32[]{:S(2)}) copy-start(f32[1,128,2]{1,2,0:T(2,128)} %param.15) | copy-start | bytes 3076
  201.4 22.1 %copy-start.6 = (s32[128,16]{1,0:T(8,128)S(1)}, s32[128,16]{1,0:T(8,128)}, u32[]{:S(2)}) copy-start(s32[128,16]{1,0:T(8,128)} %get-tuple-element.26) | copy-start | bytes 24580
  202.0 21.5 %copy-start.8 = (s32[1,16]{1,0:T(1,128)S(1)}, s32[1,16]{1,0:T(1,128)}, u32[]{:S(2)}) copy-start(s32[1,16]{1,0:T(1,128)} %param.18) | copy-start | bytes 196
  217.3 29.9 %all-to-all-start.3 = ((bf16[16,20,512]{2,1,0:T(8,128)(2,1)}), bf16[16,20,512]{2,1,0:T(8,128)(2,1)S(1)}, u32[]{:S(2)}, u32[]{:S(2)}) async-start(bf16[16,20,512]{2,1,0:T(8,128)(2,1)} %reshape.227), calls=%async_computation.3 | async-start | bytes 786432 | tf_op jit(solution)/shard_map/all_to_all | solution.py:98
  249.4 8.1 %collective-permute-start.14 = (bf16[128,512]{1,0:T(8,128)(2,1)S(1)}, bf16[128,512]{1,0:T(8,128)(2,1)S(1)}, u32[]{:S(2)}, u32[]{:S(2)}) collective-permute-start(bf16[128,512]{1,0:T(8,128)(2,1)S(1)} %multiply_reduce_fusion), channel_id=1, source_target_pairs={{0,128},{128,256},{256,384},{384,0},{1,129},{129,257},{257,385},{3... | collective-permute-start | bytes 393224 | tf_op jit(solution)/shard_map/ppermute | solution.py:10
Sparse Core Ops, SparseCore 0:
  56.3 27.8 all-gather.2
  89.9 30.8 all-gather.4

commit v5 on v3

--- a/solution.py
+++ b/solution.py
@@ -73,14 +73,31 @@
     spill_places = jnp.sum((spill_slot * spilled)[:, :, None] * spill_move[None, :, :], axis=1)
     rows_local = tokens[0]
     feat_width = rows_local.shape[1]
-    with_blank = jnp.concatenate(
-        [rows_local, jnp.zeros((1, feat_width), rows_local.dtype)], axis=0
-    )
-    main_source = slot_sources(admitted, main_slot, slot_depth)
-    spill_source = slot_sources(spill_marks, spill_places, slot_depth)
-    sources = jnp.concatenate([main_source, spill_source], axis=1)
-    outgoing = jnp.take(with_blank, sources, axis=0)
-    arrived = lax.all_to_all(outgoing, "expert", split_axis=0, concat_axis=0, tiled=True)
+    routing = jnp.concatenate([chosen, language[0][:, None]], axis=1)
+    all_routing = lax.all_gather(routing, "expert", axis=0)
+    all_rows = lax.all_gather(rows_local, "expert", axis=0)
+    me = lax.axis_index("expert")
+    mine = (expert_iota == me).astype(jnp.int32)
+    spill_mine = (spill_row == me).astype(jnp.int32)
+
+    def block_pick(block_routing):
+        block_hits, block_admitted = admission(
+            block_routing[:, :top_count], block_routing[:, top_count], capacity, experts
+        )
+        block_spilled = block_hits - block_admitted
+        marks = jnp.stack(
+            [block_admitted @ mine, block_spilled @ spill_mine], axis=1
+        )
+        places = jnp.cumsum(marks, axis=0) - marks
+        sources = slot_sources(marks, places, slot_depth).reshape(-1)
+        return (sources[:, None] == jnp.arange(tok_rows, dtype=jnp.int32)[None, :]).astype(
+            rows_local.dtype
+        )
+
+    picks = jax.vmap(block_pick)(all_routing)
+    arrived = jnp.einsum(
+        "bjt,btf->bjf", picks, all_rows, preferred_element_type=jnp.float32
+    ).astype(rows_local.dtype)
     flattened = arrived.reshape(-1, feat_width)
     all_feats = lax.all_gather(flattened, "rep", axis=0)
     gate_w = w_gate[0, 0].reshape(reps, feat_width, -1)

time: 206 us -> 231 us (1.12)
  other arithmetic: 6.18 us -> 31.6 us
  blocking collectives: 51.7 us -> 35.6 us
  waiting for transfers between devices: 77.9 us -> 90.6 us
  matrix products: 9.5 us -> 12.7 us
    all_to_all x1 -> x0, blocking collectives: 51.7 us -> none  [local(): lax.all_to_all(outgoing, 'expert', split_axis=0, concat_axis=0, tiled=True)]
    all_gather x0 -> x1, blocking collectives: none -> 35.6 us  [local(): all_routing = lax.all_gather(routing, 'expert', axis=0)]
    another operation x0 -> x2, other arithmetic: none -> 23.3 us  [the longest x1 23.3 us: block_pick(): places = jnp.cumsum(marks, axis=0) - marks]
    all_gather x0 -> x1, waiting for transfers between devices: none -> 10.4 us  [local(): all_rows = lax.all_gather(rows_local, 'expert', axis=0)]
    dot_general x0 -> x3, matrix products: none -> 3.28 us  [the longest x1 2.9 us: local(): jnp.einsum('bjt,btf->bjf', picks, all_rows, preferred_element_type=jnp.fl...]
    another operation x1 -> x2, other arithmetic: 1.18 us -> 4.42 us  [admission(): before = jnp.cumsum(lang_hits, axis=0) - lang_hits]
    all_gather x1, waiting for transfers between devices: 36 us -> 39.1 us  [local(): all_feats = lax.all_gather(flattened, 'rep', axis=0)]
    gather x1 -> x0, local copies, waits for them, and re-layouts: 2.79 us -> none  [local(): outgoing = jnp.take(with_blank, sources, axis=0)]
  transfers between devices with their start and end apart: 10 -> 11, of which waited for: 5 -> 6; matrix products, arithmetic and copies ran while one was open for 3% -> 18% of each run, Pallas kernels for 0% -> 0%
where the time goes in v5:
time: 231 us; the launch traced here: 230 us
  waiting for transfers between devices  90.6 us (39%)
  blocking collectives  35.6 us (15%)
  starting transfers between devices  33.3 us (14%)
  other arithmetic  31.6 us (14%)
  between operations  13.7 us (6%)
  local copies, waits for them, and re-layouts  12.8 us (6%)
  matrix products  12.7 us (5%)
    all_gather x1, waiting for transfers between devices, local(): all_feats = lax.all_gather(flattened, 'rep', axis=0)  39.1 us
    all_gather x1, blocking collectives, local(): all_routing = lax.all_gather(routing, 'expert', axis=0)  35.6 us
    all_to_all x1, waiting for transfers between devices, local(): lax.all_to_all(produced, 'expert', split_axis=0, concat_axis=0, tiled=True)  31.9 us
    another operation x1, other arithmetic, block_pick(): places = jnp.cumsum(marks, axis=0) - marks  23.3 us
    ppermute x7, starting transfers between devices, gathered(): pieces.append(lax.ppermute(value, axis, pairs))  17.5 us
    all_to_all x1, starting transfers between devices, local(): lax.all_to_all(produced, 'expert', split_axis=0, concat_axis=0, tiled=True)  12.4 us
    all_gather x1, waiting for transfers between devices, local(): all_rows = lax.all_gather(rows_local, 'expert', axis=0)  10.4 us
    unnamed x27, local copies, waits for them, and re-layouts  4.84 us
  transfers between devices with their start and end apart: 11, of which 6 were waited for; matrix products, arithmetic and copies ran while one was open for 18% of the time, Pallas kernels for 0%

profile of v5, /device:TPU:24, one launch (start us, length us, event | category | flops | bytes accessed | tf_op | source)
XLA Modules:
  0.0 230.3 jit_solution(7464108518543431792)
XLA Ops:
  6.5 0.7 all-gather.4.cloned.1.call-update
  7.3 0.7 pad_add_fusion.1
  8.0 35.6 %all-gather = s32[2048,3]{0,1:T(4,128)S(1)} all-gather(s32[128,3]{0,1:T(4,128)S(1)} %pad_add_fusion.1), channel_id=2, replica_groups=mesh['section'=4,'expert'=16,'rep'=8] {'expert'}, dimensions={0}, use_global_device_ids=true | all-gather | bytes 26112 | tf_op jit(solution)/shard_map/all_gather | solution.py:77
  43.7 0.5 copy.95
  44.3 3.9 %multiply_reduce_fusion = (s32[16,128,16]{2,0,1:T(8,128)S(1)}, s32[16,128,16]{2,0,1:T(8,128)}) fusion(s32[4,16]{1,0:T(4,128)S(1)} %copy-done.3, s32[16,128,4]{0,1,2:T(8,128)S(1)} %fusion.17, s32[16,128,16]{2,0,1:T(8,128)S(1)} %copy.95), kind=kOutput, calls=%fused_computation.7 | output fusion | flops 17498112 | bytes 426240 | tf_op jit(solution)/shard_map/vmap(jit(cumsum))/reduce_window_sum | solution.py:41
  48.2 1.6 copy.96
  49.8 0.4 copy.97
  50.2 0.2 fusion.18
  50.4 0.2 fusion.21
  50.7 0.5 copy.98
  51.2 23.3 %fusion.42 = s32[16,128,2]{2,0,1:T(8,128)S(1)} fusion(s32[16,128,2]{2,0,1:T(8,128)S(1)} %copy.98), kind=kOutput, calls=%fused_computation.98 | output fusion | flops 520192 | bytes 32768 | tf_op jit(solution)/shard_map/vmap(jit(cumsum))/reduce_window_sum | solution.py:91
  74.6 0.4 copy.100
  75.1 1.4 select_reduce_fusion
  76.7 10.4 %all-gather.4.cloned.1.call-done = bf16[16,128,512]{2,1,0:T(8,128)(2,1)} async-done(((bf16[1,128,512]{2,1,0:T(8,128)(2,1)}), bf16[16,128,512]{2,1,0:T(8,128)(2,1)}) %all-gather.4.cloned.1.call-update) | async-done | bytes 2097168 | tf_op jit(solution)/shard_map/all_gather | solution.py:78
  87.1 2.9 %convolution_convert_fusion = bf16[16,40,512]{2,1,0:T(8,128)(2,1)} fusion(bf16[16,128,512]{2,1,0:T(8,128)(2,1)} %all-gather.4.cloned.1.call-done, s32[16,40]{1,0:T(8,128)S(1)} %select_n.108), kind=kOutput, calls=%fused_computation.11 | convolution fusion | flops 84295680 | bytes 2755072 | tf_op jit(solution)/shard_map/bjt,btf->bjf/dot_general | solution.py:98
  90.0 39.1 %all-gather.6.cloned.1.call-done = bf16[8,640,512]{2,1,0:T(8,128)(2,1)} async-done(((bf16[1,640,512]{2,1,0:T(8,128)(2,1)}), bf16[8,640,512]{2,1,0:T(8,128)(2,1)}) %all-gather.6.cloned.1.call-update) | async-done | bytes 5242896 | tf_op jit(solution)/shard_map/all_gather | solution.py:102
  129.1 4.1 %convolution_bitcast_fusion.2 = f32[640,128]{1,0:T(8,128)S(1)} fusion(bf16[8,640,512]{2,1,0:T(8,128)(2,1)} %all-gather.6.cloned.1.call-done, bf16[8,512,128]{2,1,0:T(8,128)(2,1)S(1)} %bitcast.93), kind=kOutput, calls=%fused_computation.15 | convolution fusion | flops 671088640 | bytes 6619136 | tf_op jit(solution)/shard_map/dot_general | solution.py:106
  133.3 2.2 bitcast_dynamic-update-slice_fusion.7
  135.5 0.2 collective-permute-start
  135.8 0.6 gather_fusion
  136.4 4.3 %collective-permute-start.1 = (bf16[640,128]{1,0:T(8,128)(2,1)S(1)}, bf16[640,128]{1,0:T(8,128)(2,1)S(1)}, u32[]{:S(2)}, u32[]{:S(2)}) collective-permute-start(bf16[640,128]{1,0:T(8,128)(2,1)S(1)} %get-tuple-element.20), channel_id=1, source_target_pairs={{0,2},{1,3},{2,4},{3,5},{4,6},{5,7},{6,0},{7,1},{8,10},{9,11},{10,... | collective-permute-start | bytes 491528 | tf_op jit(solution)/shard_map/ppermute | solution.py:18
  140.7 2.8 %collective-permute-start.2 = (bf16[640,128]{1,0:T(8,128)(2,1)S(1)}, bf16[640,128]{1,0:T(8,128)(2,1)S(1)}, u32[]{:S(2)}, u32[]{:S(2)}) collective-permute-start(bf16[640,128]{1,0:T(8,128)(2,1)S(1)} %get-tuple-element.20), channel_id=1, source_target_pairs={{0,3},{1,4},{2,5},{3,6},{4,7},{5,0},{6,1},{7,2},{8,11},{9,12},{10,... | collective-permute-start | bytes 491528 | tf_op jit(solution)/shard_map/ppermute | solution.py:18
  143.5 4.3 %collective-permute-start.3 = (bf16[640,128]{1,0:T(8,128)(2,1)S(1)}, bf16[640,128]{1,0:T(8,128)(2,1)S(1)}, u32[]{:S(2)}, u32[]{:S(2)}) collective-permute-start(bf16[640,128]{1,0:T(8,128)(2,1)S(1)} %get-tuple-element.20), channel_id=1, source_target_pairs={{0,4},{1,5},{2,6},{3,7},{4,0},{5,1},{6,2},{7,3},{8,12},{9,13},{10,... | collective-permute-start | bytes 491528 | tf_op jit(solution)/shard_map/ppermute | solution.py:18
  147.8 2.7 %collective-permute-start.4 = (bf16[640,128]{1,0:T(8,128)(2,1)S(1)}, bf16[640,128]{1,0:T(8,128)(2,1)S(1)}, u32[]{:S(2)}, u32[]{:S(2)}) collective-permute-start(bf16[640,128]{1,0:T(8,128)(2,1)S(1)} %get-tuple-element.20), channel_id=1, source_target_pairs={{0,5},{1,6},{2,7},{3,0},{4,1},{5,2},{6,3},{7,4},{8,13},{9,14},{10,... | collective-permute-start | bytes 491528 | tf_op jit(solution)/shard_map/ppermute | solution.py:18
  150.6 2.3 collective-permute-start.5
  152.9 0.7 bitcast_dynamic-update-slice_fusion.6
  153.5 0.8 collective-permute-start.6
  154.3 0.7 bitcast_dynamic-update-slice_fusion.5
  155.0 0.7 bitcast_dynamic-update-slice_fusion.4
  155.7 0.7 bitcast_dynamic-update-slice_fusion.3
  156.3 1.3 collective-permute-done.4
  157.6 0.7 bitcast_dynamic-update-slice_fusion.2
  158.3 2.6 %collective-permute-done.5 = bf16[640,128]{1,0:T(8,128)(2,1)S(1)} collective-permute-done((bf16[640,128]{1,0:T(8,128)(2,1)S(1)}, bf16[640,128]{1,0:T(8,128)(2,1)S(1)}, u32[]{:S(2)}, u32[]{:S(2)}) %collective-permute-start.5) | collective-permute-done | bytes 163872 | tf_op jit(solution)/shard_map/ppermute | solution.py:18
  160.8 0.7 bitcast_dynamic-update-slice_fusion.1
  161.5 0.7 bitcast_dynamic-update-slice_fusion
  162.2 3.1 %fusion.6 = bf16[640,512]{1,0:T(8,128)(2,1)} fusion(bf16[8,640,128]{2,1,0:T(8,128)(2,1)} %bitcast_dynamic-update-slice_fusion, bf16[8,128,512]{2,1,0:T(8,128)(2,1)S(1)} %gather_fusion, pred[8]{0:T(512)(128)(4,1)S(1)} %compare_and_fusion), kind=kOutput, calls=%fused_computation.12 | convolution fusion | flops 671940608 | bytes 3014664 | tf_op jit(solution)/shard_map/dot_general | solution.py:111
  165.3 12.4 %all-to-all-start = ((bf16[16,40,512]{2,1,0:T(8,128)(2,1)}), bf16[16,40,512]{2,1,0:T(8,128)(2,1)S(1)}, u32[]{:S(2)}, u32[]{:S(2)}) async-start(bf16[16,40,512]{2,1,0:T(8,128)(2,1)} %bitcast.30), calls=%async_computation | async-start | bytes 1310720 | tf_op jit(solution)/shard_map/all_to_all | solution.py:114
  178.1 0.5 multiply_reduce_fusion.2
  178.6 0.2 reduce_window_sum.51
  178.9 0.2 reduce_window_sum.52
  179.6 0.1 gt.32
  179.8 0.1 reduce_sum.134
  180.8 31.9 %all-to-all-done = bf16[16,40,512]{2,1,0:T(8,128)(2,1)S(1)} async-done(((bf16[16,40,512]{2,1,0:T(8,128)(2,1)}), bf16[16,40,512]{2,1,0:T(8,128)(2,1)S(1)}, u32[]{:S(2)}, u32[]{:S(2)}) %all-to-all-start) | async-done | bytes 655392 | tf_op jit(solution)/shard_map/all_to_all | solution.py:114
  212.7 1.2 gather_fusion.1
  213.9 0.9 multiply_reduce_fusion.1
  214.8 3.4 %collective-permute-start.7 = (bf16[128,512]{1,0:T(8,128)(2,1)S(1)}, bf16[128,512]{1,0:T(8,128)(2,1)S(1)}, u32[]{:S(2)}, u32[]{:S(2)}) collective-permute-start(bf16[128,512]{1,0:T(8,128)(2,1)S(1)} %multiply_reduce_fusion.1), channel_id=1, source_target_pairs={{0,128},{128,256},{256,384},{384,0},{1,129},{129,257},{257,385},{3... | collective-permute-start | bytes 393224 | tf_op jit(solution)/shard_map/ppermute | solution.py:10
  218.2 4.7 %collective-permute-done.7 = bf16[128,512]{1,0:T(8,128)(2,1)S(1)} collective-permute-done((bf16[128,512]{1,0:T(8,128)(2,1)S(1)}, bf16[128,512]{1,0:T(8,128)(2,1)S(1)}, u32[]{:S(2)}, u32[]{:S(2)}) %collective-permute-start.7) | collective-permute-done | bytes 131104 | tf_op jit(solution)/shard_map/ppermute | solution.py:10
  222.9 0.7 copy.120
  (67 shorter events, 2.5 us)
Async XLA Ops:
  6.5 126.7 %copy-start = (bf16[1,1,4096,128]{3,2,1,0:T(8,128)(2,1)S(1)}, bf16[1,1,4096,128]{3,2,1,0:T(8,128)(2,1)}, u32[]{:S(2)}) copy-start(bf16[1,1,4096,128]{3,2,1,0:T(8,128)(2,1)} %param.16) | copy-start | bytes 3145732
  6.5 37.7 %copy-start.3 = (s32[4,16]{1,0:T(4,128)S(1)}, s32[4,16]{1,0:T(4,128)}, u32[]{:S(2)}) copy-start(s32[4,16]{1,0:T(4,128)} %param.13) | copy-start | bytes 772
  6.5 80.5 %all-gather.4.cloned.1.call-start = ((), (), s32[]{:S(2)}) async-start(), calls=%async_computation.1 | async-start | bytes 2228224 | tf_op jit(solution)/shard_map/all_gather | solution.py:78
  7.3 121.9 %all-gather.6.cloned.1.call-start = ((), (), s32[]{:S(2)}) async-start(), calls=%async_computation.2 | async-start | bytes 5898240 | tf_op jit(solution)/shard_map/all_gather | solution.py:102
  48.2 2.2 copy-start.4
  76.7 52.4 %copy-start.8 = (bf16[1,1,4096,128]{3,2,1,0:T(8,128)(2,1)S(1)}, bf16[1,1,4096,128]{3,2,1,0:T(8,128)(2,1)}, u32[]{:S(2)}) copy-start(bf16[1,1,4096,128]{3,2,1,0:T(8,128)(2,1)} %param.15) | copy-start | bytes 3145732
  129.1 4.2 %copy-start.7 = (bf16[8,640,512]{2,1,0:T(8,128)(2,1)S(1)}, bf16[8,640,512]{2,1,0:T(8,128)(2,1)}, u32[]{:S(2)}) copy-start(bf16[8,640,512]{2,1,0:T(8,128)(2,1)} %all-gather.6.cloned.1.call-done) | copy-start | bytes 15728644
  133.3 2.4 %copy-start.1 = (bf16[1,1,1024,512]{3,2,1,0:T(8,128)(2,1)S(1)}, bf16[1,1,1024,512]{3,2,1,0:T(8,128)(2,1)}, u32[]{:S(2)}) copy-start(bf16[1,1,1024,512]{3,2,1,0:T(8,128)(2,1)} %param.17) | copy-start | bytes 3145732
  135.5 15.1 %collective-permute-start = (bf16[640,128]{1,0:T(8,128)(2,1)S(1)}, bf16[640,128]{1,0:T(8,128)(2,1)S(1)}, u32[]{:S(2)}, u32[]{:S(2)}) collective-permute-start(bf16[640,128]{1,0:T(8,128)(2,1)S(1)} %get-tuple-element.20), channel_id=1, source_target_pairs={{0,1},{1,2},{2,3},{3,4},{4,5},{5,6},{6,7},{7,0},{8,9},{9,10},{10,1... | collective-permute-start | bytes 491528 | tf_op jit(solution)/shard_map/ppermute | solution.py:18
  136.4 17.1 %collective-permute-start.1 = (bf16[640,128]{1,0:T(8,128)(2,1)S(1)}, bf16[640,128]{1,0:T(8,128)(2,1)S(1)}, u32[]{:S(2)}, u32[]{:S(2)}) collective-permute-start(bf16[640,128]{1,0:T(8,128)(2,1)S(1)} %get-tuple-element.20), channel_id=1, source_target_pairs={{0,2},{1,3},{2,4},{3,5},{4,6},{5,7},{6,0},{7,1},{8,10},{9,11},{10,... | collective-permute-start | bytes 491528 | tf_op jit(solution)/shard_map/ppermute | solution.py:18
  140.7 14.3 %collective-permute-start.2 = (bf16[640,128]{1,0:T(8,128)(2,1)S(1)}, bf16[640,128]{1,0:T(8,128)(2,1)S(1)}, u32[]{:S(2)}, u32[]{:S(2)}) collective-permute-start(bf16[640,128]{1,0:T(8,128)(2,1)S(1)} %get-tuple-element.20), channel_id=1, source_target_pairs={{0,3},{1,4},{2,5},{3,6},{4,7},{5,0},{6,1},{7,2},{8,11},{9,12},{10,... | collective-permute-start | bytes 491528 | tf_op jit(solution)/shard_map/ppermute | solution.py:18
  143.5 12.1 %collective-permute-start.3 = (bf16[640,128]{1,0:T(8,128)(2,1)S(1)}, bf16[640,128]{1,0:T(8,128)(2,1)S(1)}, u32[]{:S(2)}, u32[]{:S(2)}) collective-permute-start(bf16[640,128]{1,0:T(8,128)(2,1)S(1)} %get-tuple-element.20), channel_id=1, source_target_pairs={{0,4},{1,5},{2,6},{3,7},{4,0},{5,1},{6,2},{7,3},{8,12},{9,13},{10,... | collective-permute-start | bytes 491528 | tf_op jit(solution)/shard_map/ppermute | solution.py:18
  147.8 9.7 %collective-permute-start.4 = (bf16[640,128]{1,0:T(8,128)(2,1)S(1)}, bf16[640,128]{1,0:T(8,128)(2,1)S(1)}, u32[]{:S(2)}, u32[]{:S(2)}) collective-permute-start(bf16[640,128]{1,0:T(8,128)(2,1)S(1)} %get-tuple-element.20), channel_id=1, source_target_pairs={{0,5},{1,6},{2,7},{3,0},{4,1},{5,2},{6,3},{7,4},{8,13},{9,14},{10,... | collective-permute-start | bytes 491528 | tf_op jit(solution)/shard_map/ppermute | solution.py:18
  150.6 10.2 %collective-permute-start.5 = (bf16[640,128]{1,0:T(8,128)(2,1)S(1)}, bf16[640,128]{1,0:T(8,128)(2,1)S(1)}, u32[]{:S(2)}, u32[]{:S(2)}) collective-permute-start(bf16[640,128]{1,0:T(8,128)(2,1)S(1)} %get-tuple-element.20), channel_id=1, source_target_pairs={{0,6},{1,7},{2,0},{3,1},{4,2},{5,3},{6,4},{7,5},{8,14},{9,15},{10,... | collective-permute-start | bytes 491528 | tf_op jit(solution)/shard_map/ppermute | solution.py:18
  153.5 8.0 %collective-permute-start.6 = (bf16[640,128]{1,0:T(8,128)(2,1)S(1)}, bf16[640,128]{1,0:T(8,128)(2,1)S(1)}, u32[]{:S(2)}, u32[]{:S(2)}) collective-permute-start(bf16[640,128]{1,0:T(8,128)(2,1)S(1)} %get-tuple-element.20), channel_id=1, source_target_pairs={{0,7},{1,0},{2,1},{3,2},{4,3},{5,4},{6,5},{7,6},{8,15},{9,8},{10,9... | collective-permute-start | bytes 491528 | tf_op jit(solution)/shard_map/ppermute | solution.py:18
  165.3 12.4 %copy-start.2 = (s32[1,128,2]{1,2,0:T(2,128)S(1)}, s32[1,128,2]{1,2,0:T(2,128)}, u32[]{:S(2)}) copy-start(s32[1,128,2]{1,2,0:T(2,128)} %param.10) | copy-start | bytes 3076
  165.3 12.7 %copy-start.5 = (s32[1,128]{1,0:T(1,128)S(1)}, s32[1,128]{1,0:T(1,128)}, u32[]{:S(2)}) copy-start(s32[1,128]{1,0:T(1,128)} %param.12) | copy-start | bytes 1540
  165.3 47.4 %all-to-all-start = ((bf16[16,40,512]{2,1,0:T(8,128)(2,1)}), bf16[16,40,512]{2,1,0:T(8,128)(2,1)S(1)}, u32[]{:S(2)}, u32[]{:S(2)}) async-start(bf16[16,40,512]{2,1,0:T(8,128)(2,1)} %bitcast.30), calls=%async_computation | async-start | bytes 1310720 | tf_op jit(solution)/shard_map/all_to_all | solution.py:114
  177.7 2.9 %copy-start.6 = (f32[1,128,2]{1,2,0:T(2,128)S(1)}, f32[1,128,2]{1,2,0:T(2,128)}, u32[]{:S(2)}) copy-start(f32[1,128,2]{1,2,0:T(2,128)} %param.11) | copy-start | bytes 3076
  214.8 8.1 %collective-permute-start.7 = (bf16[128,512]{1,0:T(8,128)(2,1)S(1)}, bf16[128,512]{1,0:T(8,128)(2,1)S(1)}, u32[]{:S(2)}, u32[]{:S(2)}) collective-permute-start(bf16[128,512]{1,0:T(8,128)(2,1)S(1)} %multiply_reduce_fusion.1), channel_id=1, source_target_pairs={{0,128},{128,256},{256,384},{384,0},{1,129},{129,257},{257,385},{3... | collective-permute-start | bytes 393224 | tf_op jit(solution)/shard_map/ppermute | solution.py:10
Sparse Core Ops, SparseCore 0:
  9.4 77.5 all-gather.3
  90.1 38.9 all-gather.5

commit v6 on v3

--- a/solution.py
+++ b/solution.py
@@ -16,7 +16,7 @@
     for shift in range(1, count):
         pairs = [(source, (source + shift) % count) for source in range(count)]
         pieces.append(lax.ppermute(value, axis, pairs))
-    return jnp.stack(pieces)
+    return pieces
 
 
 def arrival_order(weight, axis):
@@ -91,7 +91,11 @@
     activated = (jax.nn.silu(gate_proj) * up_proj).astype(jnp.bfloat16)
     all_act = gathered(activated, "rep")
     down_w = arrival_order(w_down[0, 0].reshape(reps, activated.shape[1], -1), "rep")
-    produced = lax.dot_general(all_act, down_w, dims, preferred_element_type=jnp.float32)
+    produced = jnp.dot(all_act[0], down_w[0], preferred_element_type=jnp.float32)
+    for shift in range(1, reps):
+        produced = produced + jnp.dot(
+            all_act[shift], down_w[shift], preferred_element_type=jnp.float32
+        )
     out_width = down_w.shape[2]
     produced = produced.astype(jnp.bfloat16).reshape(experts, 2 * slot_depth, out_width)
     returned = lax.all_to_all(produced, "expert", split_axis=0, concat_axis=0, tiled=True)

time: 206 us -> 200 us (0.971)
  the two profiles are of different devices: /device:TPU:24 before, /device:TPU:48 now
where the time goes in v6:
time: 200 us
  waiting for transfers between devices  75 us (38%)
  blocking collectives  51.8 us (26%)
  starting transfers between devices  35.5 us (18%)
  between operations  13.8 us (7%)
  matrix products  9.51 us (5%)
  local copies, waits for them, and re-layouts  7.84 us (4%)
  other arithmetic  6.35 us (3%)
    all_to_all x1, blocking collectives, local(): lax.all_to_all(outgoing, 'expert', split_axis=0, concat_axis=0, tiled=True)  51.8 us
    all_gather x1, waiting for transfers between devices, local(): all_feats = lax.all_gather(flattened, 'rep', axis=0)  35.3 us
    all_to_all x1, waiting for transfers between devices, local(): lax.all_to_all(produced, 'expert', split_axis=0, concat_axis=0, tiled=True)  32.1 us
    ppermute x7, starting transfers between devices, gathered(): pieces.append(lax.ppermute(value, axis, pairs))  19.3 us
    all_to_all x1, starting transfers between devices, local(): lax.all_to_all(produced, 'expert', split_axis=0, concat_axis=0, tiled=True)  12.8 us
    ppermute x1, waiting for transfers between devices, passed_along(): return lax.ppermute(value, axis, pairs)  4.69 us
    dot_general x1, matrix products, local(): lax.dot_general(all_feats, gate_w, dims, preferred_element_type=jnp.float32)  4.43 us
  transfers between devices with their start and end apart: 10, of which 4 were waited for; matrix products, arithmetic and copies ran while one was open for 2% of the time, Pallas kernels for 0%

profile of v6, /device:TPU:48, one launch (start us, length us, event | category | flops | bytes accessed | tf_op | source)
XLA Modules:
  0.0 199.7 jit_solution(4161085440450039494)
XLA Ops:
  6.5 0.8 convert_reduce_fusion
  7.4 0.7 fusion.22
  8.2 1.2 multiply_reduce_fusion.1
  9.4 0.2 reduce_window_sum.29
  9.6 0.2 reduce_window_sum.30
  10.1 0.1 multiply_reduce_fusion.4
  10.2 0.7 select_reduce_fusion
  11.1 0.7 select_reduce_fusion.1
  12.4 2.8 %gather_fusion = bf16[640,512]{1,0:T(8,128)(2,1)S(1)} fusion(bf16[129,512]{1,0:T(8,128)(2,1)S(1)} %concatenate.34, s32[1024]{0:T(1024)S(1)} %pad_clamp_fusion.2), kind=kCustom, calls=%fused_computation | custom fusion | bytes 1313280 | tf_op jit(solution)/shard_map/jit(_take)/gather | solution.py:82
  15.2 0.2 broadcast_select_fusion.1
  15.3 51.8 %all_to_all.10 = bf16[16,40,512]{2,1,0:T(8,128)(2,1)} all-to-all(bf16[16,40,512]{2,1,0:T(8,128)(2,1)S(1)} %broadcast_select_fusion.1), channel_id=1, replica_groups=mesh['section'=4,'expert'=16,'rep'=8] {'expert'}, dimensions={0} | all-to-all | bytes 1310720 | tf_op jit(solution)/shard_map/all_to_all | solution.py:83
  67.2 0.6 gather_fusion.1
  67.8 0.2 broadcast_select_fusion
  68.0 35.3 %all-gather.2.cloned.1.call-done = bf16[8,640,512]{2,1,0:T(8,128)(2,1)} async-done(((bf16[1,640,512]{2,1,0:T(8,128)(2,1)}), bf16[8,640,512]{2,1,0:T(8,128)(2,1)}) %all-gather.2.cloned.1.call-update) | async-done | bytes 5242896 | tf_op jit(solution)/shard_map/all_gather | solution.py:85
  103.3 4.4 %convolution_bitcast_fusion.1 = f32[640,128]{1,0:T(8,128)S(1)} fusion(bf16[8,640,512]{2,1,0:T(8,128)(2,1)} %all-gather.2.cloned.1.call-done, bf16[8,512,128]{2,1,0:T(8,128)(2,1)} %bitcast.80), kind=kOutput, calls=%fused_computation.13 | convolution fusion | flops 671088640 | bytes 6619136 | tf_op jit(solution)/shard_map/dot_general | solution.py:89
  107.7 0.2 copy-done.6
  107.9 1.5 fusion.7
  109.4 0.3 collective-permute-start
  109.7 2.7 %collective-permute-start.5 = (bf16[640,128]{1,0:T(8,128)(2,1)S(1)}, bf16[640,128]{1,0:T(8,128)(2,1)S(1)}, u32[]{:S(2)}, u32[]{:S(2)}) collective-permute-start(bf16[640,128]{1,0:T(8,128)(2,1)S(1)} %fusion.7), channel_id=1, source_target_pairs={{0,6},{1,7},{2,0},{3,1},{4,2},{5,3},{6,4},{7,5},{8,14},{9,15},{10,... | collective-permute-start | bytes 491528 | tf_op jit(solution)/shard_map/ppermute | solution.py:18
  112.4 5.3 %collective-permute-start.4 = (bf16[640,128]{1,0:T(8,128)(2,1)S(1)}, bf16[640,128]{1,0:T(8,128)(2,1)S(1)}, u32[]{:S(2)}, u32[]{:S(2)}) collective-permute-start(bf16[640,128]{1,0:T(8,128)(2,1)S(1)} %fusion.7), channel_id=1, source_target_pairs={{0,5},{1,6},{2,7},{3,0},{4,1},{5,2},{6,3},{7,4},{8,13},{9,14},{10,... | collective-permute-start | bytes 491528 | tf_op jit(solution)/shard_map/ppermute | solution.py:18
  117.7 2.4 %collective-permute-start.3 = (bf16[640,128]{1,0:T(8,128)(2,1)S(1)}, bf16[640,128]{1,0:T(8,128)(2,1)S(1)}, u32[]{:S(2)}, u32[]{:S(2)}) collective-permute-start(bf16[640,128]{1,0:T(8,128)(2,1)S(1)} %fusion.7), channel_id=1, source_target_pairs={{0,4},{1,5},{2,6},{3,7},{4,0},{5,1},{6,2},{7,3},{8,12},{9,13},{10,... | collective-permute-start | bytes 491528 | tf_op jit(solution)/shard_map/ppermute | solution.py:18
  120.2 1.9 collective-permute-start.2
  122.1 0.3 fusion.19
  122.4 2.4 %collective-permute-start.6 = (bf16[640,128]{1,0:T(8,128)(2,1)S(1)}, bf16[640,128]{1,0:T(8,128)(2,1)S(1)}, u32[]{:S(2)}, u32[]{:S(2)}) collective-permute-start(bf16[640,128]{1,0:T(8,128)(2,1)S(1)} %fusion.7), channel_id=1, source_target_pairs={{0,7},{1,0},{2,1},{3,2},{4,3},{5,4},{6,5},{7,6},{8,15},{9,8},{10,9... | collective-permute-start | bytes 491528 | tf_op jit(solution)/shard_map/ppermute | solution.py:18
  124.8 0.3 convolution_add_fusion.1
  125.2 4.3 %collective-permute-start.1 = (bf16[640,128]{1,0:T(8,128)(2,1)S(1)}, bf16[640,128]{1,0:T(8,128)(2,1)S(1)}, u32[]{:S(2)}, u32[]{:S(2)}) collective-permute-start(bf16[640,128]{1,0:T(8,128)(2,1)S(1)} %fusion.7), channel_id=1, source_target_pairs={{0,2},{1,3},{2,4},{3,5},{4,6},{5,7},{6,0},{7,1},{8,10},{9,11},{10,... | collective-permute-start | bytes 491528 | tf_op jit(solution)/shard_map/ppermute | solution.py:18
  129.4 0.3 fusion.15
  129.7 0.3 fusion.16
  130.1 0.3 fusion.17
  130.4 0.3 fusion.18
  130.7 0.3 fusion.14
  131.0 2.9 %collective-permute-done.1 = bf16[640,128]{1,0:T(8,128)(2,1)S(1)} collective-permute-done((bf16[640,128]{1,0:T(8,128)(2,1)S(1)}, bf16[640,128]{1,0:T(8,128)(2,1)S(1)}, u32[]{:S(2)}, u32[]{:S(2)}) %collective-permute-start.1) | collective-permute-done | bytes 163872 | tf_op jit(solution)/shard_map/ppermute | solution.py:18
  133.9 1.4 fusion.5
  135.3 12.8 %all-to-all-start.1 = ((bf16[16,40,512]{2,1,0:T(8,128)(2,1)}), bf16[16,40,512]{2,1,0:T(8,128)(2,1)S(1)}, u32[]{:S(2)}, u32[]{:S(2)}) async-start(bf16[16,40,512]{2,1,0:T(8,128)(2,1)} %bitcast.23), calls=%async_computation.1 | async-start | bytes 1310720 | tf_op jit(solution)/shard_map/all_to_all | solution.py:101
  148.4 0.1 copy.84
  148.6 0.1 copy.82
  148.8 0.1 gt.51
  149.0 0.1 add.159
  149.2 0.1 reduce_sum.143
  149.3 0.1 reduce_sum.144
  149.4 0.1 squeeze.39
  149.6 0.1 copy.73
  149.9 32.1 %all-to-all-done.1 = bf16[16,40,512]{2,1,0:T(8,128)(2,1)S(1)} async-done(((bf16[16,40,512]{2,1,0:T(8,128)(2,1)}), bf16[16,40,512]{2,1,0:T(8,128)(2,1)S(1)}, u32[]{:S(2)}, u32[]{:S(2)}) %all-to-all-start.1) | async-done | bytes 655392 | tf_op jit(solution)/shard_map/all_to_all | solution.py:101
  182.0 1.2 gather_fusion.2
  183.2 0.9 multiply_reduce_fusion
  184.1 3.4 %collective-permute-start.7 = (bf16[128,512]{1,0:T(8,128)(2,1)S(1)}, bf16[128,512]{1,0:T(8,128)(2,1)S(1)}, u32[]{:S(2)}, u32[]{:S(2)}) collective-permute-start(bf16[128,512]{1,0:T(8,128)(2,1)S(1)} %multiply_reduce_fusion), channel_id=1, source_target_pairs={{0,128},{128,256},{256,384},{384,0},{1,129},{129,257},{257,385},{3... | collective-permute-start | bytes 393224 | tf_op jit(solution)/shard_map/ppermute | solution.py:10
  187.5 4.7 %collective-permute-done.7 = bf16[128,512]{1,0:T(8,128)(2,1)S(1)} collective-permute-done((bf16[128,512]{1,0:T(8,128)(2,1)S(1)}, bf16[128,512]{1,0:T(8,128)(2,1)S(1)}, u32[]{:S(2)}, u32[]{:S(2)}) %collective-permute-start.7) | collective-permute-done | bytes 131104 | tf_op jit(solution)/shard_map/ppermute | solution.py:10
  192.2 0.7 copy.88
  (55 shorter events, 1.9 us)
Async XLA Ops:
  6.5 60.6 %copy-start = (bf16[1,1,1024,512]{3,2,1,0:T(8,128)(2,1)S(1)}, bf16[1,1,1024,512]{3,2,1,0:T(8,128)(2,1)}, u32[]{:S(2)}) copy-start(bf16[1,1,1024,512]{3,2,1,0:T(8,128)(2,1)} %param.17) | copy-start | bytes 3145732
  6.5 3.5 %copy-start.3 = (s32[1,16]{1,0:T(1,128)S(1)}, s32[1,16]{1,0:T(1,128)}, u32[]{:S(2)}) copy-start(s32[1,16]{1,0:T(1,128)} %param.14) | copy-start | bytes 196
  6.5 5.8 %copy-start.1 = (bf16[1,128,512]{2,1,0:T(8,128)(2,1)S(1)}, bf16[1,128,512]{2,1,0:T(8,128)(2,1)}, u32[]{:S(2)}) copy-start(bf16[1,128,512]{2,1,0:T(8,128)(2,1)} %param.9) | copy-start | bytes 393220
  6.5 96.7 %all-gather.2.cloned.1.call-start = ((), (), s32[]{:S(2)}) async-start(), calls=%async_computation.2 | async-start | bytes 5898240 | tf_op jit(solution)/shard_map/all_gather | solution.py:85
  103.3 4.4 %copy-start.5 = (bf16[8,640,512]{2,1,0:T(8,128)(2,1)S(1)}, bf16[8,640,512]{2,1,0:T(8,128)(2,1)}, u32[]{:S(2)}) copy-start(bf16[8,640,512]{2,1,0:T(8,128)(2,1)} %all-gather.2.cloned.1.call-done) | copy-start | bytes 15728644
  103.3 4.6 %copy-start.6 = (bf16[1,1,4096,128]{3,2,1,0:T(8,128)(2,1)S(1)}, bf16[1,1,4096,128]{3,2,1,0:T(8,128)(2,1)}, u32[]{:S(2)}) copy-start(bf16[1,1,4096,128]{3,2,1,0:T(8,128)(2,1)} %param.16) | copy-start | bytes 3145732
  109.4 13.0 %collective-permute-start = (bf16[640,128]{1,0:T(8,128)(2,1)S(1)}, bf16[640,128]{1,0:T(8,128)(2,1)S(1)}, u32[]{:S(2)}, u32[]{:S(2)}) collective-permute-start(bf16[640,128]{1,0:T(8,128)(2,1)S(1)} %fusion.7), channel_id=1, source_target_pairs={{0,1},{1,2},{2,3},{3,4},{4,5},{5,6},{6,7},{7,0},{8,9},{9,10},{10,1... | collective-permute-start | bytes 491528 | tf_op jit(solution)/shard_map/ppermute | solution.py:18
  109.7 15.5 %collective-permute-start.5 = (bf16[640,128]{1,0:T(8,128)(2,1)S(1)}, bf16[640,128]{1,0:T(8,128)(2,1)S(1)}, u32[]{:S(2)}, u32[]{:S(2)}) collective-permute-start(bf16[640,128]{1,0:T(8,128)(2,1)S(1)} %fusion.7), channel_id=1, source_target_pairs={{0,6},{1,7},{2,0},{3,1},{4,2},{5,3},{6,4},{7,5},{8,14},{9,15},{10,... | collective-permute-start | bytes 491528 | tf_op jit(solution)/shard_map/ppermute | solution.py:18
  112.4 17.3 %collective-permute-start.4 = (bf16[640,128]{1,0:T(8,128)(2,1)S(1)}, bf16[640,128]{1,0:T(8,128)(2,1)S(1)}, u32[]{:S(2)}, u32[]{:S(2)}) collective-permute-start(bf16[640,128]{1,0:T(8,128)(2,1)S(1)} %fusion.7), channel_id=1, source_target_pairs={{0,5},{1,6},{2,7},{3,0},{4,1},{5,2},{6,3},{7,4},{8,13},{9,14},{10,... | collective-permute-start | bytes 491528 | tf_op jit(solution)/shard_map/ppermute | solution.py:18
  117.7 12.3 %collective-permute-start.3 = (bf16[640,128]{1,0:T(8,128)(2,1)S(1)}, bf16[640,128]{1,0:T(8,128)(2,1)S(1)}, u32[]{:S(2)}, u32[]{:S(2)}) collective-permute-start(bf16[640,128]{1,0:T(8,128)(2,1)S(1)} %fusion.7), channel_id=1, source_target_pairs={{0,4},{1,5},{2,6},{3,7},{4,0},{5,1},{6,2},{7,3},{8,12},{9,13},{10,... | collective-permute-start | bytes 491528 | tf_op jit(solution)/shard_map/ppermute | solution.py:18
  120.2 10.2 %collective-permute-start.2 = (bf16[640,128]{1,0:T(8,128)(2,1)S(1)}, bf16[640,128]{1,0:T(8,128)(2,1)S(1)}, u32[]{:S(2)}, u32[]{:S(2)}) collective-permute-start(bf16[640,128]{1,0:T(8,128)(2,1)S(1)} %fusion.7), channel_id=1, source_target_pairs={{0,3},{1,4},{2,5},{3,6},{4,7},{5,0},{6,1},{7,2},{8,11},{9,12},{10,... | collective-permute-start | bytes 491528 | tf_op jit(solution)/shard_map/ppermute | solution.py:18
  122.4 8.3 %collective-permute-start.6 = (bf16[640,128]{1,0:T(8,128)(2,1)S(1)}, bf16[640,128]{1,0:T(8,128)(2,1)S(1)}, u32[]{:S(2)}, u32[]{:S(2)}) collective-permute-start(bf16[640,128]{1,0:T(8,128)(2,1)S(1)} %fusion.7), channel_id=1, source_target_pairs={{0,7},{1,0},{2,1},{3,2},{4,3},{5,4},{6,5},{7,6},{8,15},{9,8},{10,9... | collective-permute-start | bytes 491528 | tf_op jit(solution)/shard_map/ppermute | solution.py:18
  125.2 8.7 %collective-permute-start.1 = (bf16[640,128]{1,0:T(8,128)(2,1)S(1)}, bf16[640,128]{1,0:T(8,128)(2,1)S(1)}, u32[]{:S(2)}, u32[]{:S(2)}) collective-permute-start(bf16[640,128]{1,0:T(8,128)(2,1)S(1)} %fusion.7), channel_id=1, source_target_pairs={{0,2},{1,3},{2,4},{3,5},{4,6},{5,7},{6,0},{7,1},{8,10},{9,11},{10,... | collective-permute-start | bytes 491528 | tf_op jit(solution)/shard_map/ppermute | solution.py:18
  135.3 12.8 %copy-start.2 = (s32[1,128,2]{1,2,0:T(2,128)S(1)}, s32[1,128,2]{1,2,0:T(2,128)}, u32[]{:S(2)}) copy-start(s32[1,128,2]{1,2,0:T(2,128)} %param.10) | copy-start | bytes 3076
  135.3 14.4 %copy-start.4 = (f32[1,128,2]{1,2,0:T(2,128)S(1)}, f32[1,128,2]{1,2,0:T(2,128)}, u32[]{:S(2)}) copy-start(f32[1,128,2]{1,2,0:T(2,128)} %param.11) | copy-start | bytes 3076
  135.3 46.7 %all-to-all-start.1 = ((bf16[16,40,512]{2,1,0:T(8,128)(2,1)}), bf16[16,40,512]{2,1,0:T(8,128)(2,1)S(1)}, u32[]{:S(2)}, u32[]{:S(2)}) async-start(bf16[16,40,512]{2,1,0:T(8,128)(2,1)} %bitcast.23), calls=%async_computation.1 | async-start | bytes 1310720 | tf_op jit(solution)/shard_map/all_to_all | solution.py:101
  184.1 8.1 %collective-permute-start.7 = (bf16[128,512]{1,0:T(8,128)(2,1)S(1)}, bf16[128,512]{1,0:T(8,128)(2,1)S(1)}, u32[]{:S(2)}, u32[]{:S(2)}) collective-permute-start(bf16[128,512]{1,0:T(8,128)(2,1)S(1)} %multiply_reduce_fusion), channel_id=1, source_target_pairs={{0,128},{128,256},{256,384},{384,0},{1,129},{129,257},{257,385},{3... | collective-permute-start | bytes 393224 | tf_op jit(solution)/shard_map/ppermute | solution.py:10
Sparse Core Ops, SparseCore 0:
  67.2 36.0 all-gather.1

commit v7 on v6

--- a/solution.py
+++ b/solution.py
@@ -17,6 +17,22 @@
         pairs = [(source, (source + shift) % count) for source in range(count)]
         pieces.append(lax.ppermute(value, axis, pairs))
     return pieces
+
+
+def paired_gather(value, axis):
+    count = lax.axis_size(axis)
+    me = lax.axis_index(axis)
+    partner = lax.ppermute(value, axis, [(source, source ^ 1) for source in range(count)])
+    pair = jnp.stack([value, partner])
+    pieces = [value, partner]
+    origins = [me, me ^ 1]
+    for shift in range(2, count, 2):
+        pairs = [(source, (source + shift) % count) for source in range(count)]
+        moved = lax.ppermute(pair, axis, pairs)
+        origin = (me - shift) % count
+        pieces.extend([moved[0], moved[1]])
+        origins.extend([origin, origin ^ 1])
+    return pieces, jnp.stack(origins)
 
 
 def arrival_order(weight, axis):
@@ -73,13 +89,15 @@
     spill_places = jnp.sum((spill_slot * spilled)[:, :, None] * spill_move[None, :, :], axis=1)
     rows_local = tokens[0]
     feat_width = rows_local.shape[1]
-    with_blank = jnp.concatenate(
-        [rows_local, jnp.zeros((1, feat_width), rows_local.dtype)], axis=0
-    )
     main_source = slot_sources(admitted, main_slot, slot_depth)
     spill_source = slot_sources(spill_marks, spill_places, slot_depth)
     sources = jnp.concatenate([main_source, spill_source], axis=1)
-    outgoing = jnp.take(with_blank, sources, axis=0)
+    picks = (sources[:, :, None] == jnp.arange(tok_rows, dtype=jnp.int32)[None, None, :]).astype(
+        rows_local.dtype
+    )
+    outgoing = jnp.einsum(
+        "xjt,tf->xjf", picks, rows_local, preferred_element_type=jnp.float32
+    ).astype(rows_local.dtype)
     arrived = lax.all_to_all(outgoing, "expert", split_axis=0, concat_axis=0, tiled=True)
     flattened = arrived.reshape(-1, feat_width)
     all_feats = lax.all_gather(flattened, "rep", axis=0)
@@ -89,8 +107,8 @@
     gate_proj = lax.dot_general(all_feats, gate_w, dims, preferred_element_type=jnp.float32)
     up_proj = lax.dot_general(all_feats, up_w, dims, preferred_element_type=jnp.float32)
     activated = (jax.nn.silu(gate_proj) * up_proj).astype(jnp.bfloat16)
-    all_act = gathered(activated, "rep")
-    down_w = arrival_order(w_down[0, 0].reshape(reps, activated.shape[1], -1), "rep")
+    all_act, act_origins = paired_gather(activated, "rep")
+    down_w = jnp.take(w_down[0, 0].reshape(reps, activated.shape[1], -1), act_origins, axis=0)
     produced = jnp.dot(all_act[0], down_w[0], preferred_element_type=jnp.float32)
     for shift in range(1, reps):
         produced = produced + jnp.dot(

time: 200 us -> 198 us (0.990)
  the two profiles are of different devices: /device:TPU:48 before, /device:TPU:24 now
where the time goes in v7:
time: 198 us; the launch traced here: 196 us
  waiting for transfers between devices  80.6 us (41%)
  blocking collectives  51.5 us (26%)
  starting transfers between devices  29.3 us (15%)
  between operations  13.7 us (7%)
  matrix products  9.62 us (5%)
  other arithmetic  6.13 us (3%)
  local copies, waits for them, and re-layouts  4.97 us (3%)
    all_to_all x1, blocking collectives, local(): lax.all_to_all(outgoing, 'expert', split_axis=0, concat_axis=0, tiled=True)  51.5 us
    all_gather x1, waiting for transfers between devices, local(): all_feats = lax.all_gather(flattened, 'rep', axis=0)  35.2 us
    all_to_all x1, waiting for transfers between devices, local(): lax.all_to_all(produced, 'expert', split_axis=0, concat_axis=0, tiled=True)  32.2 us
    all_to_all x1, starting transfers between devices, local(): lax.all_to_all(produced, 'expert', split_axis=0, concat_axis=0, tiled=True)  12.4 us
    ppermute x3, starting transfers between devices, paired_gather(): moved = lax.ppermute(pair, axis, pairs)  11.3 us
    ppermute x3, waiting for transfers between devices, paired_gather(): moved = lax.ppermute(pair, axis, pairs)  7.7 us
    ppermute x1, waiting for transfers between devices, passed_along(): return lax.ppermute(value, axis, pairs)  4.65 us
    dot_general x1, matrix products, local(): lax.dot_general(all_feats, gate_w, dims, preferred_element_type=jnp.float32)  4.15 us
  transfers between devices with their start and end apart: 7, of which 6 were waited for; matrix products, arithmetic and copies ran while one was open for 2% of the time, Pallas kernels for 0%

profile of v7, /device:TPU:24, one launch (start us, length us, event | category | flops | bytes accessed | tf_op | source)
XLA Modules:
  0.0 195.9 jit_solution(17119627878195895439)
XLA Ops:
  6.5 0.8 convert_reduce_fusion
  7.4 0.7 fusion.24
  8.2 1.2 multiply_reduce_fusion.1
  9.4 0.2 reduce_window_sum.30
  9.6 0.2 reduce_window_sum.29
  10.0 0.1 multiply_reduce_fusion.4
  10.1 0.7 select_reduce_fusion
  11.1 0.8 select_reduce_fusion.1
  12.0 0.4 convolution_convert_fusion
  12.4 51.5 %all_to_all.10 = bf16[16,40,512]{2,1,0:T(8,128)(2,1)} all-to-all(bf16[16,40,512]{2,1,0:T(8,128)(2,1)S(1)} %convolution_convert_fusion), channel_id=1, replica_groups=mesh['section'=4,'expert'=16,'rep'=8] {'expert'}, dimensions={0} | all-to-all | bytes 1310720 | tf_op jit(solution)/shard_map/all_to_all | solution.py:101
  64.1 0.6 gather_fusion
  64.8 35.2 %all-gather.2.cloned.1.call-done = bf16[8,640,512]{2,1,0:T(8,128)(2,1)} async-done(((bf16[1,640,512]{2,1,0:T(8,128)(2,1)}), bf16[8,640,512]{2,1,0:T(8,128)(2,1)}) %all-gather.2.cloned.1.call-update) | async-done | bytes 5242896 | tf_op jit(solution)/shard_map/all_gather | solution.py:103
  100.0 4.2 %convolution_bitcast_fusion.1 = f32[640,128]{1,0:T(8,128)S(1)} fusion(bf16[8,640,512]{2,1,0:T(8,128)(2,1)} %all-gather.2.cloned.1.call-done, bf16[8,512,128]{2,1,0:T(8,128)(2,1)S(1)} %bitcast.106), kind=kOutput, calls=%fused_computation.13 | convolution fusion | flops 671088640 | bytes 6619136 | tf_op jit(solution)/shard_map/dot_general | solution.py:107
  104.2 0.2 copy-done.7
  104.4 1.5 fusion.7
  105.9 2.2 %collective-permute-start = (bf16[640,128]{1,0:T(8,128)(2,1)S(1)}, bf16[640,128]{1,0:T(8,128)(2,1)S(1)}, u32[]{:S(2)}, u32[]{:S(2)}) collective-permute-start(bf16[640,128]{1,0:T(8,128)(2,1)S(1)} %fusion.7), channel_id=1, source_target_pairs={{0,1},{1,0},{2,3},{3,2},{4,5},{5,4},{6,7},{7,6},{8,9},{9,8},{10,11... | collective-permute-start | bytes 491528 | tf_op jit(solution)/shard_map/ppermute | solution.py:25
  108.0 0.2 broadcast_select_fusion
  108.2 0.9 collective-permute-done
  109.2 4.3 %collective-permute-start.2 = (bf16[2,640,128]{2,1,0:T(8,128)(2,1)S(1)}, bf16[2,640,128]{2,1,0:T(8,128)(2,1)S(1)}, u32[]{:S(2)}, u32[]{:S(2)}) collective-permute-start(bf16[2,640,128]{2,1,0:T(8,128)(2,1)S(1)} %pad_maximum_fusion), channel_id=1, source_target_pairs={{0,4},{1,5},{2,6},{3,7},{4,0},{5,1},{6,2},{7,3},{8,12},{9,13},{10,... | collective-permute-start | bytes 983048 | tf_op jit(solution)/shard_map/ppermute | solution.py:31
  113.5 0.3 fusion.20
  113.8 2.8 %collective-permute-start.3 = (bf16[2,640,128]{2,1,0:T(8,128)(2,1)S(1)}, bf16[2,640,128]{2,1,0:T(8,128)(2,1)S(1)}, u32[]{:S(2)}, u32[]{:S(2)}) collective-permute-start(bf16[2,640,128]{2,1,0:T(8,128)(2,1)S(1)} %pad_maximum_fusion), channel_id=1, source_target_pairs={{0,6},{1,7},{2,0},{3,1},{4,2},{5,3},{6,4},{7,5},{8,14},{9,15},{10,... | collective-permute-start | bytes 983048 | tf_op jit(solution)/shard_map/ppermute | solution.py:31
  116.6 4.2 %collective-permute-start.1 = (bf16[2,640,128]{2,1,0:T(8,128)(2,1)S(1)}, bf16[2,640,128]{2,1,0:T(8,128)(2,1)S(1)}, u32[]{:S(2)}, u32[]{:S(2)}) collective-permute-start(bf16[2,640,128]{2,1,0:T(8,128)(2,1)S(1)} %pad_maximum_fusion), channel_id=1, source_target_pairs={{0,2},{1,3},{2,4},{3,5},{4,6},{5,7},{6,0},{7,1},{8,10},{9,11},{10,... | collective-permute-start | bytes 983048 | tf_op jit(solution)/shard_map/ppermute | solution.py:31
  120.9 0.3 convolution_add_fusion.1
  121.2 2.0 %collective-permute-done.2 = bf16[2,640,128]{2,1,0:T(8,128)(2,1)S(1)} collective-permute-done((bf16[2,640,128]{2,1,0:T(8,128)(2,1)S(1)}, bf16[2,640,128]{2,1,0:T(8,128)(2,1)S(1)}, u32[]{:S(2)}, u32[]{:S(2)}) %collective-permute-start.2) | collective-permute-done | bytes 327712 | tf_op jit(solution)/shard_map/ppermute | solution.py:31
  123.2 0.3 fusion.16
  123.5 0.3 fusion.17
  123.8 5.7 %collective-permute-done.3 = bf16[2,640,128]{2,1,0:T(8,128)(2,1)S(1)} collective-permute-done((bf16[2,640,128]{2,1,0:T(8,128)(2,1)S(1)}, bf16[2,640,128]{2,1,0:T(8,128)(2,1)S(1)}, u32[]{:S(2)}, u32[]{:S(2)}) %collective-permute-start.3) | collective-permute-done | bytes 327712 | tf_op jit(solution)/shard_map/ppermute | solution.py:31
  129.5 0.3 fusion.15
  129.8 0.3 fusion.14
  130.1 0.3 fusion.18
  130.4 1.4 fusion.5
  131.8 12.4 %all-to-all-start.1 = ((bf16[16,40,512]{2,1,0:T(8,128)(2,1)}), bf16[16,40,512]{2,1,0:T(8,128)(2,1)S(1)}, u32[]{:S(2)}, u32[]{:S(2)}) async-start(bf16[16,40,512]{2,1,0:T(8,128)(2,1)} %bitcast.45), calls=%async_computation.1 | async-start | bytes 1310720 | tf_op jit(solution)/shard_map/all_to_all | solution.py:119
  144.3 0.1 copy.62
  144.6 0.1 copy.63
  144.8 0.1 copy.61
  144.9 0.1 gt.27
  145.1 0.1 copy.65
  145.2 0.1 add.129
  145.4 0.1 reduce_sum.143
  145.5 0.1 reduce_sum.144
  145.6 0.1 squeeze.63
  145.8 0.1 copy.54
  146.1 32.2 %all-to-all-done.1 = bf16[16,40,512]{2,1,0:T(8,128)(2,1)S(1)} async-done(((bf16[16,40,512]{2,1,0:T(8,128)(2,1)}), bf16[16,40,512]{2,1,0:T(8,128)(2,1)S(1)}, u32[]{:S(2)}, u32[]{:S(2)}) %all-to-all-start.1) | async-done | bytes 655392 | tf_op jit(solution)/shard_map/all_to_all | solution.py:119
  178.2 1.2 gather_fusion.1
  179.5 0.9 multiply_reduce_fusion
  180.4 3.4 %collective-permute-start.4 = (bf16[128,512]{1,0:T(8,128)(2,1)S(1)}, bf16[128,512]{1,0:T(8,128)(2,1)S(1)}, u32[]{:S(2)}, u32[]{:S(2)}) collective-permute-start(bf16[128,512]{1,0:T(8,128)(2,1)S(1)} %multiply_reduce_fusion), channel_id=1, source_target_pairs={{0,128},{128,256},{256,384},{384,0},{1,129},{129,257},{257,385},{3... | collective-permute-start | bytes 393224 | tf_op jit(solution)/shard_map/ppermute | solution.py:10
  183.8 4.6 %collective-permute-done.4 = bf16[128,512]{1,0:T(8,128)(2,1)S(1)} collective-permute-done((bf16[128,512]{1,0:T(8,128)(2,1)S(1)}, bf16[128,512]{1,0:T(8,128)(2,1)S(1)}, u32[]{:S(2)}, u32[]{:S(2)}) %collective-permute-start.4) | collective-permute-done | bytes 131104 | tf_op jit(solution)/shard_map/ppermute | solution.py:10
  188.4 0.7 copy.67
  (47 shorter events, 1.5 us)
Async XLA Ops:
  6.5 57.6 %copy-start = (bf16[1,1,1024,512]{3,2,1,0:T(8,128)(2,1)S(1)}, bf16[1,1,1024,512]{3,2,1,0:T(8,128)(2,1)}, u32[]{:S(2)}) copy-start(bf16[1,1,1024,512]{3,2,1,0:T(8,128)(2,1)} %param.17) | copy-start | bytes 3145732
  6.5 3.4 %copy-start.3 = (s32[1,16]{1,0:T(1,128)S(1)}, s32[1,16]{1,0:T(1,128)}, u32[]{:S(2)}) copy-start(s32[1,16]{1,0:T(1,128)} %param.14) | copy-start | bytes 196
  6.5 5.5 %copy-start.1 = (bf16[1,128,512]{2,1,0:T(8,128)(2,1)S(1)}, bf16[1,128,512]{2,1,0:T(8,128)(2,1)}, u32[]{:S(2)}) copy-start(bf16[1,128,512]{2,1,0:T(8,128)(2,1)} %param.9) | copy-start | bytes 393220
  6.5 93.5 %all-gather.2.cloned.1.call-start = ((), (), s32[]{:S(2)}) async-start(), calls=%async_computation.2 | async-start | bytes 5898240 | tf_op jit(solution)/shard_map/all_gather | solution.py:103
  63.9 36.1 %copy-start.6 = (bf16[1,1,4096,128]{3,2,1,0:T(8,128)(2,1)S(1)}, bf16[1,1,4096,128]{3,2,1,0:T(8,128)(2,1)}, u32[]{:S(2)}) copy-start(bf16[1,1,4096,128]{3,2,1,0:T(8,128)(2,1)} %param.15) | copy-start | bytes 3145732
  100.0 4.2 %copy-start.5 = (bf16[8,640,512]{2,1,0:T(8,128)(2,1)S(1)}, bf16[8,640,512]{2,1,0:T(8,128)(2,1)}, u32[]{:S(2)}) copy-start(bf16[8,640,512]{2,1,0:T(8,128)(2,1)} %all-gather.2.cloned.1.call-done) | copy-start | bytes 15728644
  100.0 4.3 %copy-start.7 = (bf16[1,1,4096,128]{3,2,1,0:T(8,128)(2,1)S(1)}, bf16[1,1,4096,128]{3,2,1,0:T(8,128)(2,1)}, u32[]{:S(2)}) copy-start(bf16[1,1,4096,128]{3,2,1,0:T(8,128)(2,1)} %param.16) | copy-start | bytes 3145732
  105.9 3.3 %collective-permute-start = (bf16[640,128]{1,0:T(8,128)(2,1)S(1)}, bf16[640,128]{1,0:T(8,128)(2,1)S(1)}, u32[]{:S(2)}, u32[]{:S(2)}) collective-permute-start(bf16[640,128]{1,0:T(8,128)(2,1)S(1)} %fusion.7), channel_id=1, source_target_pairs={{0,1},{1,0},{2,3},{3,2},{4,5},{5,4},{6,7},{7,6},{8,9},{9,8},{10,11... | collective-permute-start | bytes 491528 | tf_op jit(solution)/shard_map/ppermute | solution.py:25
  109.2 14.0 %collective-permute-start.2 = (bf16[2,640,128]{2,1,0:T(8,128)(2,1)S(1)}, bf16[2,640,128]{2,1,0:T(8,128)(2,1)S(1)}, u32[]{:S(2)}, u32[]{:S(2)}) collective-permute-start(bf16[2,640,128]{2,1,0:T(8,128)(2,1)S(1)} %pad_maximum_fusion), channel_id=1, source_target_pairs={{0,4},{1,5},{2,6},{3,7},{4,0},{5,1},{6,2},{7,3},{8,12},{9,13},{10,... | collective-permute-start | bytes 983048 | tf_op jit(solution)/shard_map/ppermute | solution.py:31
  113.8 15.7 %collective-permute-start.3 = (bf16[2,640,128]{2,1,0:T(8,128)(2,1)S(1)}, bf16[2,640,128]{2,1,0:T(8,128)(2,1)S(1)}, u32[]{:S(2)}, u32[]{:S(2)}) collective-permute-start(bf16[2,640,128]{2,1,0:T(8,128)(2,1)S(1)} %pad_maximum_fusion), channel_id=1, source_target_pairs={{0,6},{1,7},{2,0},{3,1},{4,2},{5,3},{6,4},{7,5},{8,14},{9,15},{10,... | collective-permute-start | bytes 983048 | tf_op jit(solution)/shard_map/ppermute | solution.py:31
  116.6 13.5 %collective-permute-start.1 = (bf16[2,640,128]{2,1,0:T(8,128)(2,1)S(1)}, bf16[2,640,128]{2,1,0:T(8,128)(2,1)S(1)}, u32[]{:S(2)}, u32[]{:S(2)}) collective-permute-start(bf16[2,640,128]{2,1,0:T(8,128)(2,1)S(1)} %pad_maximum_fusion), channel_id=1, source_target_pairs={{0,2},{1,3},{2,4},{3,5},{4,6},{5,7},{6,0},{7,1},{8,10},{9,11},{10,... | collective-permute-start | bytes 983048 | tf_op jit(solution)/shard_map/ppermute | solution.py:31
  131.8 12.4 %copy-start.2 = (s32[1,128,2]{1,2,0:T(2,128)S(1)}, s32[1,128,2]{1,2,0:T(2,128)}, u32[]{:S(2)}) copy-start(s32[1,128,2]{1,2,0:T(2,128)} %param.10) | copy-start | bytes 3076
  131.8 14.1 %copy-start.4 = (f32[1,128,2]{1,2,0:T(2,128)S(1)}, f32[1,128,2]{1,2,0:T(2,128)}, u32[]{:S(2)}) copy-start(f32[1,128,2]{1,2,0:T(2,128)} %param.11) | copy-start | bytes 3076
  131.8 46.4 %all-to-all-start.1 = ((bf16[16,40,512]{2,1,0:T(8,128)(2,1)}), bf16[16,40,512]{2,1,0:T(8,128)(2,1)S(1)}, u32[]{:S(2)}, u32[]{:S(2)}) async-start(bf16[16,40,512]{2,1,0:T(8,128)(2,1)} %bitcast.45), calls=%async_computation.1 | async-start | bytes 1310720 | tf_op jit(solution)/shard_map/all_to_all | solution.py:119
  180.4 8.1 %collective-permute-start.4 = (bf16[128,512]{1,0:T(8,128)(2,1)S(1)}, bf16[128,512]{1,0:T(8,128)(2,1)S(1)}, u32[]{:S(2)}, u32[]{:S(2)}) collective-permute-start(bf16[128,512]{1,0:T(8,128)(2,1)S(1)} %multiply_reduce_fusion), channel_id=1, source_target_pairs={{0,128},{128,256},{256,384},{384,0},{1,129},{129,257},{257,385},{3... | collective-permute-start | bytes 393224 | tf_op jit(solution)/shard_map/ppermute | solution.py:10
Sparse Core Ops, SparseCore 0:
  64.1 35.9 all-gather.1

commit v8 on v7

--- a/solution.py
+++ b/solution.py
@@ -17,6 +17,21 @@
         pairs = [(source, (source + shift) % count) for source in range(count)]
         pieces.append(lax.ppermute(value, axis, pairs))
     return pieces
+
+
+def chips_then_core(value, axis):
+    count = lax.axis_size(axis)
+    me = lax.axis_index(axis)
+    pieces = [value]
+    origins = [me]
+    for shift in range(2, count, 2):
+        pairs = [(source, (source + shift) % count) for source in range(count)]
+        pieces.append(lax.ppermute(value, axis, pairs))
+        origins.append((me - shift) % count)
+    bundle = jnp.stack(pieces)
+    swapped = lax.ppermute(bundle, axis, [(source, source ^ 1) for source in range(count)])
+    origins = jnp.stack(origins)
+    return bundle, swapped, origins, origins ^ 1
 
 
 def paired_gather(value, axis):
@@ -100,20 +115,35 @@
     ).astype(rows_local.dtype)
     arrived = lax.all_to_all(outgoing, "expert", split_axis=0, concat_axis=0, tiled=True)
     flattened = arrived.reshape(-1, feat_width)
-    all_feats = lax.all_gather(flattened, "rep", axis=0)
-    gate_w = w_gate[0, 0].reshape(reps, feat_width, -1)
-    up_w = w_up[0, 0].reshape(reps, feat_width, -1)
+    own_feats, partner_feats, own_from, partner_from = chips_then_core(flattened, "rep")
+    gate_all = w_gate[0, 0].reshape(reps, feat_width, -1)
+    up_all = w_up[0, 0].reshape(reps, feat_width, -1)
     dims = (((0, 2), (0, 1)), ((), ()))
-    gate_proj = lax.dot_general(all_feats, gate_w, dims, preferred_element_type=jnp.float32)
-    up_proj = lax.dot_general(all_feats, up_w, dims, preferred_element_type=jnp.float32)
+
+    def project(weights):
+        own = lax.dot_general(
+            own_feats, jnp.take(weights, own_from, axis=0), dims,
+            preferred_element_type=jnp.float32,
+        )
+        partner = lax.dot_general(
+            partner_feats, jnp.take(weights, partner_from, axis=0), dims,
+            preferred_element_type=jnp.float32,
+        )
+        return own + partner
+
+    gate_proj = project(gate_all)
+    up_proj = project(up_all)
     activated = (jax.nn.silu(gate_proj) * up_proj).astype(jnp.bfloat16)
-    all_act, act_origins = paired_gather(activated, "rep")
-    down_w = jnp.take(w_down[0, 0].reshape(reps, activated.shape[1], -1), act_origins, axis=0)
-    produced = jnp.dot(all_act[0], down_w[0], preferred_element_type=jnp.float32)
-    for shift in range(1, reps):
-        produced = produced + jnp.dot(
-            all_act[shift], down_w[shift], preferred_element_type=jnp.float32
-        )
+    own_act, partner_act, act_own_from, act_partner_from = chips_then_core(activated, "rep")
+    down_all = w_down[0, 0].reshape(reps, activated.shape[1], -1)
+    produced = lax.dot_general(
+        own_act, jnp.take(down_all, act_own_from, axis=0), dims,
+        preferred_element_type=jnp.float32,
+    ) + lax.dot_general(
+        partner_act, jnp.take(down_all, act_partner_from, axis=0), dims,
+        preferred_element_type=jnp.float32,
+    )
+    down_w = down_all
     out_width = down_w.shape[2]
     produced = produced.astype(jnp.bfloat16).reshape(experts, 2 * slot_depth, out_width)
     returned = lax.all_to_all(produced, "expert", split_axis=0, concat_axis=0, tiled=True)

time: 198 us -> 191 us (0.965)
  between operations: 13.7 us -> 0.44 us
  waiting for transfers between devices: 80.6 us -> 69.8 us
  matrix products: 9.62 us -> 16.5 us
  local copies, waits for them, and re-layouts: 4.97 us -> 10.1 us
  starting transfers between devices: 29.3 us -> 33.6 us
  other arithmetic: 6.13 us -> 8.57 us
    all_gather x1 -> x0, waiting for transfers between devices: 35.2 us -> none  [local(): all_feats = lax.all_gather(flattened, 'rep', axis=0)]
    ppermute x4 -> x8, waiting for transfers between devices: 8.65 us -> 32.3 us  [the longest x6 31.3 us: chips_then_core(): pieces.append(lax.ppermute(value, axis, pairs))]
    ppermute x4 -> x8, starting transfers between devices: 13.5 us -> 23 us  [the longest x6 19.2 us: chips_then_core(): pieces.append(lax.ppermute(value, axis, pairs))]
    dot_general x10 -> x6, matrix products: 9.23 us -> 15.2 us  [the longest x2 5.46 us: project(): lax.dot_general(own_feats, jnp.take(weights, own_from, axis=0), dims, pre...]
    gather x1 -> x6, local copies, waits for them, and re-layouts: 0.61 us -> 6.09 us  [the longest x2 2.84 us: project(): jnp.take(weights, partner_from, axis=0)]
    all_to_all x1, starting transfers between devices: 12.4 us -> 7.15 us  [local(): lax.all_to_all(produced, 'expert', split_axis=0, concat_axis=0, tiled=True)]
  transfers between devices with their start and end apart: 7 -> 10, of which waited for: 6 -> 9; matrix products, arithmetic and copies ran while one was open for 2% -> 4% of each run, Pallas kernels for 0% -> 0%
where the time goes in v8:
time: 191 us; the launch traced here: 190 us
  waiting for transfers between devices  69.8 us (37%)
  blocking collectives  51.4 us (27%)
  starting transfers between devices  33.6 us (18%)
  matrix products  16.5 us (9%)
  local copies, waits for them, and re-layouts  10.1 us (5%)
  other arithmetic  8.57 us (4%)
    all_to_all x1, blocking collectives, local(): lax.all_to_all(outgoing, 'expert', split_axis=0, concat_axis=0, tiled=True)  51.4 us
    all_to_all x1, waiting for transfers between devices, local(): lax.all_to_all(produced, 'expert', split_axis=0, concat_axis=0, tiled=True)  32.8 us
    ppermute x6, waiting for transfers between devices, chips_then_core(): pieces.append(lax.ppermute(value, axis, pairs))  31.3 us
    ppermute x6, starting transfers between devices, chips_then_core(): pieces.append(lax.ppermute(value, axis, pairs))  19.2 us
    all_to_all x1, starting transfers between devices, local(): lax.all_to_all(produced, 'expert', split_axis=0, concat_axis=0, tiled=True)  7.15 us
    dot_general x2, matrix products, project(): lax.dot_general(own_feats, jnp.take(weights, own_from, axis=0), dims, pre...  5.46 us
    dot_general x2, matrix products, project(): lax.dot_general(partner_feats, jnp.take(weights, partner_from, axis=0), d...  5.4 us
    ppermute x1, waiting for transfers between devices, passed_along(): return lax.ppermute(value, axis, pairs)  4.66 us
  transfers between devices with their start and end apart: 10, of which 9 were waited for; matrix products, arithmetic and copies ran while one was open for 4% of the time, Pallas kernels for 0%

profile of v8, /device:TPU:24, one launch (start us, length us, event | category | flops | bytes accessed | tf_op | source)
XLA Modules:
  0.0 190.4 jit_solution(8239089408246973414)
XLA Ops:
  0.0 0.8 convert_reduce_fusion
  0.9 0.7 fusion.34
  1.6 1.2 multiply_reduce_fusion.1
  2.9 0.2 reduce_window_sum.30
  3.1 0.2 reduce_window_sum.29
  3.4 0.7 fusion.35
  4.2 0.7 select_reduce_fusion
  5.1 0.8 select_reduce_fusion.1
  6.1 1.3 convolution_convert_fusion
  7.4 51.4 %all_to_all.10 = bf16[16,40,512]{2,1,0:T(8,128)(2,1)S(1)} all-to-all(bf16[16,40,512]{2,1,0:T(8,128)(2,1)S(1)} %convolution_convert_fusion), channel_id=1, replica_groups=mesh['section'=4,'expert'=16,'rep'=8] {'expert'}, dimensions={0} | all-to-all | bytes 1310720 | tf_op jit(solution)/shard_map/all_to_all | solution.py:116
  58.8 2.6 %collective-permute-start.2 = (bf16[640,512]{1,0:T(8,128)(2,1)S(1)}, bf16[640,512]{1,0:T(8,128)(2,1)S(1)}, u32[]{:S(2)}, u32[]{:S(2)}) collective-permute-start(bf16[640,512]{1,0:T(8,128)(2,1)S(1)} %bitcast.59), channel_id=1, source_target_pairs={{0,6},{1,7},{2,0},{3,1},{4,2},{5,3},{6,4},{7,5},{8,14},{9,15},{10,... | collective-permute-start | bytes 1966088 | tf_op jit(solution)/shard_map/ppermute | solution.py:29
  61.4 4.4 %collective-permute-start = (bf16[640,512]{1,0:T(8,128)(2,1)S(1)}, bf16[640,512]{1,0:T(8,128)(2,1)S(1)}, u32[]{:S(2)}, u32[]{:S(2)}) collective-permute-start(bf16[640,512]{1,0:T(8,128)(2,1)S(1)} %bitcast.60), channel_id=1, source_target_pairs={{0,2},{1,3},{2,4},{3,5},{4,6},{5,7},{6,0},{7,1},{8,10},{9,11},{10,... | collective-permute-start | bytes 1966088 | tf_op jit(solution)/shard_map/ppermute | solution.py:29
  65.9 1.9 %collective-permute-start.1 = (bf16[640,512]{1,0:T(8,128)(2,1)S(1)}, bf16[640,512]{1,0:T(8,128)(2,1)S(1)}, u32[]{:S(2)}, u32[]{:S(2)}) collective-permute-start(bf16[640,512]{1,0:T(8,128)(2,1)S(1)} %bitcast.61), channel_id=1, source_target_pairs={{0,4},{1,5},{2,6},{3,7},{4,0},{5,1},{6,2},{7,3},{8,12},{9,13},{10,... | collective-permute-start | bytes 1966088 | tf_op jit(solution)/shard_map/ppermute | solution.py:29
  67.8 21.9 %collective-permute-done.2 = bf16[640,512]{1,0:T(8,128)(2,1)S(1)} collective-permute-done((bf16[640,512]{1,0:T(8,128)(2,1)S(1)}, bf16[640,512]{1,0:T(8,128)(2,1)S(1)}, u32[]{:S(2)}, u32[]{:S(2)}) %collective-permute-start.2) | collective-permute-done | bytes 655392 | tf_op jit(solution)/shard_map/ppermute | solution.py:29
  89.7 1.2 collective-permute-done
  90.9 1.8 pad_maximum_fusion
  92.7 1.9 %collective-permute-start.3 = (bf16[4,640,512]{2,1,0:T(8,128)(2,1)}, bf16[4,640,512]{2,1,0:T(8,128)(2,1)}, u32[]{:S(2)}, u32[]{:S(2)}) collective-permute-start(bf16[4,640,512]{2,1,0:T(8,128)(2,1)} %pad_maximum_fusion), channel_id=1, source_target_pairs={{0,1},{1,0},{2,3},{3,2},{4,5},{5,4},{6,7},{7,6},{8,9},{9,8},{10,11... | collective-permute-start | bytes 7864328 | tf_op jit(solution)/shard_map/ppermute | solution.py:32
  94.8 1.4 gather_fusion.2
  96.2 0.6 gather_fusion.1
  96.9 1.4 gather_fusion.4
  98.3 0.6 gather_fusion.3
  99.0 0.9 collective-permute-done.3
  99.9 2.7 %convolution_bitcast_fusion.4 = f32[640,128]{1,0:T(8,128)S(1)} fusion(bf16[4,640,512]{2,1,0:T(8,128)(2,1)} %collective-permute-done.3, bf16[4,512,128]{2,1,0:T(8,128)(2,1)} %gather_fusion.2, pred[4]{0:T(512)(128)(4,1)S(1)} %get-tuple-element.23), kind=kOutput, calls=%fused_computation.15 | convolution fusion | flops 335806464 | bytes 3473412 | tf_op jit(solution)/shard_map/dot_general | solution.py:128
  102.6 2.7 %fusion.2 = f32[640,128]{1,0:T(8,128)S(1)} fusion(f32[640,128]{1,0:T(8,128)S(1)} %convolution_bitcast_fusion.4, bf16[4,640,512]{2,1,0:T(8,128)(2,1)} %pad_maximum_fusion, bf16[4,512,128]{2,1,0:T(8,128)(2,1)S(1)} %gather_fusion.1, pred[4]{0:T(512)(128)(4,1)S(1)} %get-tuple-element.21), kind=kOutput, calls=%fused_computation.17 | convolution fusion | flops 335888384 | bytes 3801092 | tf_op jit(solution)/shard_map/dot_general | solution.py:124
  105.4 2.7 %convolution_bitcast_fusion.2 = f32[640,128]{1,0:T(8,128)S(1)} fusion(bf16[4,640,512]{2,1,0:T(8,128)(2,1)} %collective-permute-done.3, bf16[4,512,128]{2,1,0:T(8,128)(2,1)S(1)} %copy-done.3, pred[4]{0:T(512)(128)(4,1)S(1)} %get-tuple-element.23), kind=kOutput, calls=%fused_computation.13 | convolution fusion | flops 335806464 | bytes 3473412 | tf_op jit(solution)/shard_map/dot_general | solution.py:128
  108.0 2.7 %multiply_convert_fusion = bf16[640,128]{1,0:T(8,128)(2,1)S(1)} fusion(f32[640,128]{1,0:T(8,128)S(1)} %fusion.2, f32[640,128]{1,0:T(8,128)S(1)} %convolution_bitcast_fusion.2, bf16[4,640,512]{2,1,0:T(8,128)(2,1)} %pad_maximum_fusion, bf16[4,512,128]{2,1,0:T(8,128)(2,1)S(1)} %gather_fusion.3, pred[4]{0:T(512)(128)(4,1)S(1)} %get-tuple-element.21), kind=kOutput, calls=%fused_computation.37 | convolution fusion | flops 336379904 | bytes 3964932 | tf_op jit(solution)/shard_map/dot_general | solution.py:124
  110.8 5.6 %collective-permute-start.4 = (bf16[640,128]{1,0:T(8,128)(2,1)S(1)}, bf16[640,128]{1,0:T(8,128)(2,1)S(1)}, u32[]{:S(2)}, u32[]{:S(2)}) collective-permute-start(bf16[640,128]{1,0:T(8,128)(2,1)S(1)} %multiply_convert_fusion), channel_id=1, source_target_pairs={{0,2},{1,3},{2,4},{3,5},{4,6},{5,7},{6,0},{7,1},{8,10},{9,11},{10,... | collective-permute-start | bytes 491528 | tf_op jit(solution)/shard_map/ppermute | solution.py:29
  116.3 1.9 %collective-permute-start.5 = (bf16[640,128]{1,0:T(8,128)(2,1)S(1)}, bf16[640,128]{1,0:T(8,128)(2,1)S(1)}, u32[]{:S(2)}, u32[]{:S(2)}) collective-permute-start(bf16[640,128]{1,0:T(8,128)(2,1)S(1)} %multiply_convert_fusion), channel_id=1, source_target_pairs={{0,4},{1,5},{2,6},{3,7},{4,0},{5,1},{6,2},{7,3},{8,12},{9,13},{10,... | collective-permute-start | bytes 491528 | tf_op jit(solution)/shard_map/ppermute | solution.py:29
  118.3 2.8 %collective-permute-start.6 = (bf16[640,128]{1,0:T(8,128)(2,1)S(1)}, bf16[640,128]{1,0:T(8,128)(2,1)S(1)}, u32[]{:S(2)}, u32[]{:S(2)}) collective-permute-start(bf16[640,128]{1,0:T(8,128)(2,1)S(1)} %multiply_convert_fusion), channel_id=1, source_target_pairs={{0,6},{1,7},{2,0},{3,1},{4,2},{5,3},{6,4},{7,5},{8,14},{9,15},{10,... | collective-permute-start | bytes 491528 | tf_op jit(solution)/shard_map/ppermute | solution.py:29
  121.1 2.6 %collective-permute-done.4 = bf16[640,128]{1,0:T(8,128)(2,1)S(1)} collective-permute-done((bf16[640,128]{1,0:T(8,128)(2,1)S(1)}, bf16[640,128]{1,0:T(8,128)(2,1)S(1)}, u32[]{:S(2)}, u32[]{:S(2)}) %collective-permute-start.4) | collective-permute-done | bytes 163872 | tf_op jit(solution)/shard_map/ppermute | solution.py:29
  123.6 3.2 %collective-permute-done.5 = bf16[640,128]{1,0:T(8,128)(2,1)S(1)} collective-permute-done((bf16[640,128]{1,0:T(8,128)(2,1)S(1)}, bf16[640,128]{1,0:T(8,128)(2,1)S(1)}, u32[]{:S(2)}, u32[]{:S(2)}) %collective-permute-start.5) | collective-permute-done | bytes 163872 | tf_op jit(solution)/shard_map/ppermute | solution.py:29
  126.8 2.4 %collective-permute-done.6 = bf16[640,128]{1,0:T(8,128)(2,1)S(1)} collective-permute-done((bf16[640,128]{1,0:T(8,128)(2,1)S(1)}, bf16[640,128]{1,0:T(8,128)(2,1)S(1)}, u32[]{:S(2)}, u32[]{:S(2)}) %collective-permute-start.6) | collective-permute-done | bytes 163872 | tf_op jit(solution)/shard_map/ppermute | solution.py:29
  129.3 1.9 %collective-permute-start.7 = (bf16[4,640,128]{2,1,0:T(8,128)(2,1)S(1)}, bf16[4,640,128]{2,1,0:T(8,128)(2,1)}, u32[]{:S(2)}, u32[]{:S(2)}) collective-permute-start(bf16[4,640,128]{2,1,0:T(8,128)(2,1)S(1)} %pad_maximum_fusion.1), channel_id=1, source_target_pairs={{0,1},{1,0},{2,3},{3,2},{4,5},{5,4},{6,7},{7,6},{8,9},{9,8},{10,11... | collective-permute-start | bytes 1966088 | tf_op jit(solution)/shard_map/ppermute | solution.py:32
  131.3 0.6 gather_fusion.6
  131.9 1.4 gather_fusion.5
  133.3 0.2 collective-permute-done.7
  133.4 1.7 convolution_bitcast_fusion
  135.2 2.7 %fusion.1 = bf16[640,512]{1,0:T(8,128)(2,1)} fusion(f32[640,512]{1,0:T(8,128)S(1)} %convolution_bitcast_fusion, bf16[4,128,512]{2,1,0:T(8,128)(2,1)} %gather_fusion.5, pred[4]{0:T(512)(128)(4,1)S(1)} %get-tuple-element.21, bf16[1,640,128]{2,1,0:T(8,128)(2,1)} %bitcast.77, bf16[1,640,128]{2,1,0:T(8,128)(2,1)} %bitcast.75, bf16[1,640,128]{2,1,0:T(8,128)(2,1)} %bitcast.73, ...), kind=kOutput, calls=%fused_computation.12 | convolution fusion | flops 337444864 | bytes 3145732 | tf_op jit(solution)/shard_map/dot_general | solution.py:139
  137.9 7.2 %all-to-all-start.1 = ((bf16[16,40,512]{2,1,0:T(8,128)(2,1)}), bf16[16,40,512]{2,1,0:T(8,128)(2,1)S(1)}, u32[]{:S(2)}, u32[]{:S(2)}) async-start(bf16[16,40,512]{2,1,0:T(8,128)(2,1)} %bitcast.28), calls=%async_computation.1 | async-start | bytes 1310720 | tf_op jit(solution)/shard_map/all_to_all | solution.py:149
  145.7 0.1 gt.27
  146.3 0.1 reduce_sum.144
  146.4 0.1 squeeze.7
  146.8 32.8 %all-to-all-done.1 = bf16[16,40,512]{2,1,0:T(8,128)(2,1)S(1)} async-done(((bf16[16,40,512]{2,1,0:T(8,128)(2,1)}), bf16[16,40,512]{2,1,0:T(8,128)(2,1)S(1)}, u32[]{:S(2)}, u32[]{:S(2)}) %all-to-all-start.1) | async-done | bytes 655392 | tf_op jit(solution)/shard_map/all_to_all | solution.py:149
  179.6 1.2 gather_fusion
  180.8 0.9 multiply_reduce_fusion
  181.7 3.4 %collective-permute-start.8 = (bf16[128,512]{1,0:T(8,128)(2,1)S(1)}, bf16[128,512]{1,0:T(8,128)(2,1)S(1)}, u32[]{:S(2)}, u32[]{:S(2)}) collective-permute-start(bf16[128,512]{1,0:T(8,128)(2,1)S(1)} %multiply_reduce_fusion), channel_id=1, source_target_pairs={{0,128},{128,256},{256,384},{384,0},{1,129},{129,257},{257,385},{3... | collective-permute-start | bytes 393224 | tf_op jit(solution)/shard_map/ppermute | solution.py:10
  185.1 4.7 %collective-permute-done.8 = bf16[128,512]{1,0:T(8,128)(2,1)S(1)} collective-permute-done((bf16[128,512]{1,0:T(8,128)(2,1)S(1)}, bf16[128,512]{1,0:T(8,128)(2,1)S(1)}, u32[]{:S(2)}, u32[]{:S(2)}) %collective-permute-start.8) | collective-permute-done | bytes 131104 | tf_op jit(solution)/shard_map/ppermute | solution.py:10
  189.8 0.7 copy.59
  (57 shorter events, 2.4 us)
Async XLA Ops:
  0.0 94.8 %copy-start = (bf16[1,1,4096,128]{3,2,1,0:T(8,128)(2,1)S(1)}, bf16[1,1,4096,128]{3,2,1,0:T(8,128)(2,1)}, u32[]{:S(2)}) copy-start(bf16[1,1,4096,128]{3,2,1,0:T(8,128)(2,1)} %param.19) | copy-start | bytes 3145732
  58.8 30.9 %collective-permute-start.2 = (bf16[640,512]{1,0:T(8,128)(2,1)S(1)}, bf16[640,512]{1,0:T(8,128)(2,1)S(1)}, u32[]{:S(2)}, u32[]{:S(2)}) collective-permute-start(bf16[640,512]{1,0:T(8,128)(2,1)S(1)} %bitcast.59), channel_id=1, source_target_pairs={{0,6},{1,7},{2,0},{3,1},{4,2},{5,3},{6,4},{7,5},{8,14},{9,15},{10,... | collective-permute-start | bytes 1966088 | tf_op jit(solution)/shard_map/ppermute | solution.py:29
  61.4 29.4 %collective-permute-start = (bf16[640,512]{1,0:T(8,128)(2,1)S(1)}, bf16[640,512]{1,0:T(8,128)(2,1)S(1)}, u32[]{:S(2)}, u32[]{:S(2)}) collective-permute-start(bf16[640,512]{1,0:T(8,128)(2,1)S(1)} %bitcast.60), channel_id=1, source_target_pairs={{0,2},{1,3},{2,4},{3,5},{4,6},{5,7},{6,0},{7,1},{8,10},{9,11},{10,... | collective-permute-start | bytes 1966088 | tf_op jit(solution)/shard_map/ppermute | solution.py:29
  65.9 25.0 %collective-permute-start.1 = (bf16[640,512]{1,0:T(8,128)(2,1)S(1)}, bf16[640,512]{1,0:T(8,128)(2,1)S(1)}, u32[]{:S(2)}, u32[]{:S(2)}) collective-permute-start(bf16[640,512]{1,0:T(8,128)(2,1)S(1)} %bitcast.61), channel_id=1, source_target_pairs={{0,4},{1,5},{2,6},{3,7},{4,0},{5,1},{6,2},{7,3},{8,12},{9,13},{10,... | collective-permute-start | bytes 1966088 | tf_op jit(solution)/shard_map/ppermute | solution.py:29
  90.9 6.0 %copy-start.1 = (bf16[1,1,4096,128]{3,2,1,0:T(8,128)(2,1)S(1)}, bf16[1,1,4096,128]{3,2,1,0:T(8,128)(2,1)}, u32[]{:S(2)}) copy-start(bf16[1,1,4096,128]{3,2,1,0:T(8,128)(2,1)} %param.20) | copy-start | bytes 3145732
  92.7 7.1 %collective-permute-start.3 = (bf16[4,640,512]{2,1,0:T(8,128)(2,1)}, bf16[4,640,512]{2,1,0:T(8,128)(2,1)}, u32[]{:S(2)}, u32[]{:S(2)}) collective-permute-start(bf16[4,640,512]{2,1,0:T(8,128)(2,1)} %pad_maximum_fusion), channel_id=1, source_target_pairs={{0,1},{1,0},{2,3},{3,2},{4,5},{5,4},{6,7},{7,6},{8,9},{9,8},{10,11... | collective-permute-start | bytes 7864328 | tf_op jit(solution)/shard_map/ppermute | solution.py:32
  102.6 2.7 %copy-start.3 = (bf16[4,512,128]{2,1,0:T(8,128)(2,1)S(1)}, bf16[4,512,128]{2,1,0:T(8,128)(2,1)}, u32[]{:S(2)}) copy-start(bf16[4,512,128]{2,1,0:T(8,128)(2,1)} %gather_fusion.4) | copy-start | bytes 1572868
  108.0 23.3 %copy-start.2 = (bf16[1,1,1024,512]{3,2,1,0:T(8,128)(2,1)S(1)}, bf16[1,1,1024,512]{3,2,1,0:T(8,128)(2,1)}, u32[]{:S(2)}) copy-start(bf16[1,1,1024,512]{3,2,1,0:T(8,128)(2,1)} %param.21) | copy-start | bytes 3145732
  110.8 12.9 %collective-permute-start.4 = (bf16[640,128]{1,0:T(8,128)(2,1)S(1)}, bf16[640,128]{1,0:T(8,128)(2,1)S(1)}, u32[]{:S(2)}, u32[]{:S(2)}) collective-permute-start(bf16[640,128]{1,0:T(8,128)(2,1)S(1)} %multiply_convert_fusion), channel_id=1, source_target_pairs={{0,2},{1,3},{2,4},{3,5},{4,6},{5,7},{6,0},{7,1},{8,10},{9,11},{10,... | collective-permute-start | bytes 491528 | tf_op jit(solution)/shard_map/ppermute | solution.py:29
  116.3 10.5 %collective-permute-start.5 = (bf16[640,128]{1,0:T(8,128)(2,1)S(1)}, bf16[640,128]{1,0:T(8,128)(2,1)S(1)}, u32[]{:S(2)}, u32[]{:S(2)}) collective-permute-start(bf16[640,128]{1,0:T(8,128)(2,1)S(1)} %multiply_convert_fusion), channel_id=1, source_target_pairs={{0,4},{1,5},{2,6},{3,7},{4,0},{5,1},{6,2},{7,3},{8,12},{9,13},{10,... | collective-permute-start | bytes 491528 | tf_op jit(solution)/shard_map/ppermute | solution.py:29
  118.3 11.0 %collective-permute-start.6 = (bf16[640,128]{1,0:T(8,128)(2,1)S(1)}, bf16[640,128]{1,0:T(8,128)(2,1)S(1)}, u32[]{:S(2)}, u32[]{:S(2)}) collective-permute-start(bf16[640,128]{1,0:T(8,128)(2,1)S(1)} %multiply_convert_fusion), channel_id=1, source_target_pairs={{0,6},{1,7},{2,0},{3,1},{4,2},{5,3},{6,4},{7,5},{8,14},{9,15},{10,... | collective-permute-start | bytes 491528 | tf_op jit(solution)/shard_map/ppermute | solution.py:29
  123.6 7.6 %copy-start.4 = (bf16[640,128]{1,0:T(8,128)(2,1)}, bf16[640,128]{1,0:T(8,128)(2,1)S(1)}, u32[]{:S(2)}) copy-start(bf16[640,128]{1,0:T(8,128)(2,1)S(1)} %collective-permute-done.4) | copy-start | bytes 491524
  126.8 4.4 %copy-start.5 = (bf16[640,128]{1,0:T(8,128)(2,1)}, bf16[640,128]{1,0:T(8,128)(2,1)S(1)}, u32[]{:S(2)}) copy-start(bf16[640,128]{1,0:T(8,128)(2,1)S(1)} %collective-permute-done.5) | copy-start | bytes 491524
  129.2 2.0 %copy-start.6 = (bf16[640,128]{1,0:T(8,128)(2,1)}, bf16[640,128]{1,0:T(8,128)(2,1)S(1)}, u32[]{:S(2)}) copy-start(bf16[640,128]{1,0:T(8,128)(2,1)S(1)} %collective-permute-done.6) | copy-start | bytes 491524
  129.3 4.1 %collective-permute-start.7 = (bf16[4,640,128]{2,1,0:T(8,128)(2,1)S(1)}, bf16[4,640,128]{2,1,0:T(8,128)(2,1)}, u32[]{:S(2)}, u32[]{:S(2)}) collective-permute-start(bf16[4,640,128]{2,1,0:T(8,128)(2,1)S(1)} %pad_maximum_fusion.1), channel_id=1, source_target_pairs={{0,1},{1,0},{2,3},{3,2},{4,5},{5,4},{6,7},{7,6},{8,9},{9,8},{10,11... | collective-permute-start | bytes 1966088 | tf_op jit(solution)/shard_map/ppermute | solution.py:32
  135.1 9.9 %copy-start.7 = (s32[1,128,2]{1,2,0:T(2,128)S(1)}, s32[1,128,2]{1,2,0:T(2,128)}, u32[]{:S(2)}) copy-start(s32[1,128,2]{1,2,0:T(2,128)} %param.14) | copy-start | bytes 3076
  135.1 10.1 %copy-start.8 = (s32[1,16]{1,0:T(1,128)S(1)}, s32[1,16]{1,0:T(1,128)}, u32[]{:S(2)}) copy-start(s32[1,16]{1,0:T(1,128)} %param.18) | copy-start | bytes 196
  135.1 11.5 %copy-start.9 = (f32[1,128,2]{1,2,0:T(2,128)S(1)}, f32[1,128,2]{1,2,0:T(2,128)}, u32[]{:S(2)}) copy-start(f32[1,128,2]{1,2,0:T(2,128)} %param.15) | copy-start | bytes 3076
  137.9 41.7 %all-to-all-start.1 = ((bf16[16,40,512]{2,1,0:T(8,128)(2,1)}), bf16[16,40,512]{2,1,0:T(8,128)(2,1)S(1)}, u32[]{:S(2)}, u32[]{:S(2)}) async-start(bf16[16,40,512]{2,1,0:T(8,128)(2,1)} %bitcast.28), calls=%async_computation.1 | async-start | bytes 1310720 | tf_op jit(solution)/shard_map/all_to_all | solution.py:149
  181.7 8.1 %collective-permute-start.8 = (bf16[128,512]{1,0:T(8,128)(2,1)S(1)}, bf16[128,512]{1,0:T(8,128)(2,1)S(1)}, u32[]{:S(2)}, u32[]{:S(2)}) collective-permute-start(bf16[128,512]{1,0:T(8,128)(2,1)S(1)} %multiply_reduce_fusion), channel_id=1, source_target_pairs={{0,128},{128,256},{256,384},{384,0},{1,129},{129,257},{257,385},{3... | collective-permute-start | bytes 393224 | tf_op jit(solution)/shard_map/ppermute | solution.py:10

commit v9 on v8

--- a/solution.py
+++ b/solution.py
@@ -31,6 +31,23 @@
     bundle = jnp.stack(pieces)
     swapped = lax.ppermute(bundle, axis, [(source, source ^ 1) for source in range(count)])
     origins = jnp.stack(origins)
+    return bundle, swapped, origins, origins ^ 1
+
+
+def relayed_chips_then_core(value, axis):
+    count = lax.axis_size(axis)
+    me = lax.axis_index(axis)
+    up_pairs = [(source, (source + 2) % count) for source in range(count)]
+    down_pairs = [(source, (source - 2) % count) for source in range(count)]
+    from_below = lax.ppermute(value, axis, up_pairs)
+    from_above = lax.ppermute(value, axis, down_pairs)
+    half = value.shape[0] // 2
+    far_low = lax.ppermute(from_below[:half], axis, up_pairs)
+    far_high = lax.ppermute(from_above[half:], axis, down_pairs)
+    far = jnp.concatenate([far_low, far_high], axis=0)
+    bundle = jnp.stack([value, from_below, from_above, far])
+    swapped = lax.ppermute(bundle, axis, [(source, source ^ 1) for source in range(count)])
+    origins = jnp.stack([me, (me - 2) % count, (me + 2) % count, (me + 4) % count])
     return bundle, swapped, origins, origins ^ 1
 
 
@@ -115,7 +132,7 @@
     ).astype(rows_local.dtype)
     arrived = lax.all_to_all(outgoing, "expert", split_axis=0, concat_axis=0, tiled=True)
     flattened = arrived.reshape(-1, feat_width)
-    own_feats, partner_feats, own_from, partner_from = chips_then_core(flattened, "rep")
+    own_feats, partner_feats, own_from, partner_from = relayed_chips_then_core(flattened, "rep")
     gate_all = w_gate[0, 0].reshape(reps, feat_width, -1)
     up_all = w_up[0, 0].reshape(reps, feat_width, -1)
     dims = (((0, 2), (0, 1)), ((), ()))

time: 191 us -> 187 us (0.979)
  waiting for transfers between devices: 69.8 us -> 63.3 us
    ppermute x6 -> x3, waiting for transfers between devices: 31.3 us -> 7.16 us  [chips_then_core(): pieces.append(lax.ppermute(value, axis, pairs))]
    ppermute x0 -> x5, waiting for transfers between devices: none -> 18.4 us  [the longest x1 9.78 us: relayed_chips_then_core(): from_below = lax.ppermute(value, axis, up_pairs)]
    ppermute x0 -> x5, starting transfers between devices: none -> 13.6 us  [the longest x1 3.71 us: relayed_chips_then_core(): from_above = lax.ppermute(value, axis, down_pairs)]
    ppermute x6 -> x3, starting transfers between devices: 19.2 us -> 7.76 us  [chips_then_core(): pieces.append(lax.ppermute(value, axis, pairs))]
    ppermute x2 -> x1, starting transfers between devices: 3.83 us -> 1.92 us  [chips_then_core(): lax.ppermute(bundle, axis, [(source, source ^ 1) for source in range(coun...]
  transfers between devices with their start and end apart: 10 -> 11, of which waited for: 9 -> 10; matrix products, arithmetic and copies ran while one was open for 4% -> 4% of each run, Pallas kernels for 0% -> 0%
where the time goes in v9:
time: 187 us; the launch traced here: 186 us
  waiting for transfers between devices  63.3 us (34%)
  blocking collectives  51.4 us (27%)
  starting transfers between devices  35.2 us (19%)
  matrix products  16.5 us (9%)
  local copies, waits for them, and re-layouts  10.2 us (5%)
  other arithmetic  8.73 us (5%)
    all_to_all x1, blocking collectives, local(): lax.all_to_all(outgoing, 'expert', split_axis=0, concat_axis=0, tiled=True)  51.4 us
    all_to_all x1, waiting for transfers between devices, local(): lax.all_to_all(produced, 'expert', split_axis=0, concat_axis=0, tiled=True)  32.9 us
    ppermute x1, waiting for transfers between devices, relayed_chips_then_core(): from_below = lax.ppermute(value, axis, up_pairs)  9.78 us
    all_to_all x1, starting transfers between devices, local(): lax.all_to_all(produced, 'expert', split_axis=0, concat_axis=0, tiled=True)  8.53 us
    ppermute x3, starting transfers between devices, chips_then_core(): pieces.append(lax.ppermute(value, axis, pairs))  7.76 us
    ppermute x3, waiting for transfers between devices, chips_then_core(): pieces.append(lax.ppermute(value, axis, pairs))  7.16 us
    dot_general x2, matrix products, project(): lax.dot_general(own_feats, jnp.take(weights, own_from, axis=0), dims, pre...  5.47 us
    dot_general x2, matrix products, project(): lax.dot_general(partner_feats, jnp.take(weights, partner_from, axis=0), d...  5.4 us
  transfers between devices with their start and end apart: 11, of which 10 were waited for; matrix products, arithmetic and copies ran while one was open for 4% of the time, Pallas kernels for 0%

profile of v9, /device:TPU:24, one launch (start us, length us, event | category | flops | bytes accessed | tf_op | source)
XLA Modules:
  0.0 185.8 jit_solution(10907606418287737206)
XLA Ops:
  0.0 0.8 convert_reduce_fusion
  0.9 0.7 fusion.34
  1.6 1.2 multiply_reduce_fusion.1
  2.9 0.2 reduce_window_sum.30
  3.1 0.2 reduce_window_sum.29
  3.4 0.7 fusion.35
  4.2 0.7 select_reduce_fusion
  5.1 0.8 select_reduce_fusion.1
  6.1 1.3 convolution_convert_fusion
  7.4 51.4 %all_to_all.10 = bf16[16,40,512]{2,1,0:T(8,128)(2,1)S(1)} all-to-all(bf16[16,40,512]{2,1,0:T(8,128)(2,1)S(1)} %convolution_convert_fusion), channel_id=1, replica_groups=mesh['section'=4,'expert'=16,'rep'=8] {'expert'}, dimensions={0} | all-to-all | bytes 1310720 | tf_op jit(solution)/shard_map/all_to_all | solution.py:133
  58.8 2.1 %collective-permute-start = (bf16[640,512]{1,0:T(8,128)(2,1)S(1)}, bf16[640,512]{1,0:T(8,128)(2,1)S(1)}, u32[]{:S(2)}, u32[]{:S(2)}) collective-permute-start(bf16[640,512]{1,0:T(8,128)(2,1)S(1)} %bitcast.62), channel_id=1, source_target_pairs={{0,2},{1,3},{2,4},{3,5},{4,6},{5,7},{6,0},{7,1},{8,10},{9,11},{10,... | collective-permute-start | bytes 1966088 | tf_op jit(solution)/shard_map/ppermute | solution.py:42
  60.9 3.7 %collective-permute-start.1 = (bf16[640,512]{1,0:T(8,128)(2,1)S(1)}, bf16[640,512]{1,0:T(8,128)(2,1)S(1)}, u32[]{:S(2)}, u32[]{:S(2)}) collective-permute-start(bf16[640,512]{1,0:T(8,128)(2,1)S(1)} %bitcast.63), channel_id=1, source_target_pairs={{0,6},{1,7},{2,0},{3,1},{4,2},{5,3},{6,4},{7,5},{8,14},{9,15},{10,... | collective-permute-start | bytes 1966088 | tf_op jit(solution)/shard_map/ppermute | solution.py:43
  64.6 9.8 %collective-permute-done = bf16[640,512]{1,0:T(8,128)(2,1)S(1)} collective-permute-done((bf16[640,512]{1,0:T(8,128)(2,1)S(1)}, bf16[640,512]{1,0:T(8,128)(2,1)S(1)}, u32[]{:S(2)}, u32[]{:S(2)}) %collective-permute-start) | collective-permute-done | bytes 655392 | tf_op jit(solution)/shard_map/ppermute | solution.py:42
  74.4 3.4 %collective-permute-start.2 = (bf16[320,512]{1,0:T(8,128)(2,1)S(1)}, bf16[320,512]{1,0:T(8,128)(2,1)S(1)}, u32[]{:S(2)}, u32[]{:S(2)}) collective-permute-start(bf16[320,512]{1,0:T(8,128)(2,1)S(1)} %slice.22), channel_id=1, source_target_pairs={{0,2},{1,3},{2,4},{3,5},{4,6},{5,7},{6,0},{7,1},{8,10},{9,11},{10,... | collective-permute-start | bytes 983048 | tf_op jit(solution)/shard_map/ppermute | solution.py:45
  77.9 2.4 %collective-permute-start.3 = (bf16[320,512]{1,0:T(8,128)(2,1)S(1)}, bf16[320,512]{1,0:T(8,128)(2,1)S(1)}, u32[]{:S(2)}, u32[]{:S(2)}) collective-permute-start(bf16[320,512]{1,0:T(8,128)(2,1)S(1)} %slice.23), channel_id=1, source_target_pairs={{0,6},{1,7},{2,0},{3,1},{4,2},{5,3},{6,4},{7,5},{8,14},{9,15},{10,... | collective-permute-start | bytes 983048 | tf_op jit(solution)/shard_map/ppermute | solution.py:46
  80.3 3.1 %collective-permute-done.2 = bf16[320,512]{1,0:T(8,128)(2,1)S(1)} collective-permute-done((bf16[320,512]{1,0:T(8,128)(2,1)S(1)}, bf16[320,512]{1,0:T(8,128)(2,1)S(1)}, u32[]{:S(2)}, u32[]{:S(2)}) %collective-permute-start.2) | collective-permute-done | bytes 327712 | tf_op jit(solution)/shard_map/ppermute | solution.py:45
  83.4 4.7 %collective-permute-done.3 = bf16[320,512]{1,0:T(8,128)(2,1)S(1)} collective-permute-done((bf16[320,512]{1,0:T(8,128)(2,1)S(1)}, bf16[320,512]{1,0:T(8,128)(2,1)S(1)}, u32[]{:S(2)}, u32[]{:S(2)}) %collective-permute-start.3) | collective-permute-done | bytes 327712 | tf_op jit(solution)/shard_map/ppermute | solution.py:46
  88.1 1.8 pad_maximum_fusion
  90.0 1.9 %collective-permute-start.4 = (bf16[4,640,512]{2,1,0:T(8,128)(2,1)}, bf16[4,640,512]{2,1,0:T(8,128)(2,1)}, u32[]{:S(2)}, u32[]{:S(2)}) collective-permute-start(bf16[4,640,512]{2,1,0:T(8,128)(2,1)} %pad_maximum_fusion), channel_id=1, source_target_pairs={{0,1},{1,0},{2,3},{3,2},{4,5},{5,4},{6,7},{7,6},{8,9},{9,8},{10,11... | collective-permute-start | bytes 7864328 | tf_op jit(solution)/shard_map/ppermute | solution.py:49
  92.1 1.4 gather_fusion.2
  93.5 0.6 gather_fusion.1
  94.1 1.4 gather_fusion.4
  95.6 0.6 gather_fusion.3
  96.2 0.9 collective-permute-done.4
  97.1 2.7 %convolution_bitcast_fusion.4 = f32[640,128]{1,0:T(8,128)S(1)} fusion(bf16[4,640,512]{2,1,0:T(8,128)(2,1)} %collective-permute-done.4, bf16[4,512,128]{2,1,0:T(8,128)(2,1)} %gather_fusion.2, pred[4]{0:T(512)(128)(4,1)S(1)} %get-tuple-element.27), kind=kOutput, calls=%fused_computation.15 | convolution fusion | flops 335806464 | bytes 3473412 | tf_op jit(solution)/shard_map/dot_general | solution.py:145
  99.9 2.7 %fusion.2 = f32[640,128]{1,0:T(8,128)S(1)} fusion(f32[640,128]{1,0:T(8,128)S(1)} %convolution_bitcast_fusion.4, bf16[4,640,512]{2,1,0:T(8,128)(2,1)} %pad_maximum_fusion, bf16[4,512,128]{2,1,0:T(8,128)(2,1)S(1)} %gather_fusion.1, pred[4]{0:T(512)(128)(4,1)S(1)} %get-tuple-element.25), kind=kOutput, calls=%fused_computation.17 | convolution fusion | flops 335888384 | bytes 3801092 | tf_op jit(solution)/shard_map/dot_general | solution.py:141
  102.6 2.7 %convolution_bitcast_fusion.2 = f32[640,128]{1,0:T(8,128)S(1)} fusion(bf16[4,640,512]{2,1,0:T(8,128)(2,1)} %collective-permute-done.4, bf16[4,512,128]{2,1,0:T(8,128)(2,1)S(1)} %copy-done.3, pred[4]{0:T(512)(128)(4,1)S(1)} %get-tuple-element.27), kind=kOutput, calls=%fused_computation.13 | convolution fusion | flops 335806464 | bytes 3473412 | tf_op jit(solution)/shard_map/dot_general | solution.py:145
  105.3 2.7 %multiply_convert_fusion = bf16[640,128]{1,0:T(8,128)(2,1)S(1)} fusion(f32[640,128]{1,0:T(8,128)S(1)} %fusion.2, f32[640,128]{1,0:T(8,128)S(1)} %convolution_bitcast_fusion.2, bf16[4,640,512]{2,1,0:T(8,128)(2,1)} %pad_maximum_fusion, bf16[4,512,128]{2,1,0:T(8,128)(2,1)S(1)} %gather_fusion.3, pred[4]{0:T(512)(128)(4,1)S(1)} %get-tuple-element.25), kind=kOutput, calls=%fused_computation.38 | convolution fusion | flops 336379904 | bytes 3964932 | tf_op jit(solution)/shard_map/dot_general | solution.py:141
  108.0 1.9 %collective-permute-start.5 = (bf16[640,128]{1,0:T(8,128)(2,1)S(1)}, bf16[640,128]{1,0:T(8,128)(2,1)S(1)}, u32[]{:S(2)}, u32[]{:S(2)}) collective-permute-start(bf16[640,128]{1,0:T(8,128)(2,1)S(1)} %multiply_convert_fusion), channel_id=1, source_target_pairs={{0,2},{1,3},{2,4},{3,5},{4,6},{5,7},{6,0},{7,1},{8,10},{9,11},{10,... | collective-permute-start | bytes 491528 | tf_op jit(solution)/shard_map/ppermute | solution.py:29
  110.0 3.3 %collective-permute-start.6 = (bf16[640,128]{1,0:T(8,128)(2,1)S(1)}, bf16[640,128]{1,0:T(8,128)(2,1)S(1)}, u32[]{:S(2)}, u32[]{:S(2)}) collective-permute-start(bf16[640,128]{1,0:T(8,128)(2,1)S(1)} %multiply_convert_fusion), channel_id=1, source_target_pairs={{0,4},{1,5},{2,6},{3,7},{4,0},{5,1},{6,2},{7,3},{8,12},{9,13},{10,... | collective-permute-start | bytes 491528 | tf_op jit(solution)/shard_map/ppermute | solution.py:29
  113.3 2.6 %collective-permute-start.7 = (bf16[640,128]{1,0:T(8,128)(2,1)S(1)}, bf16[640,128]{1,0:T(8,128)(2,1)S(1)}, u32[]{:S(2)}, u32[]{:S(2)}) collective-permute-start(bf16[640,128]{1,0:T(8,128)(2,1)S(1)} %multiply_convert_fusion), channel_id=1, source_target_pairs={{0,6},{1,7},{2,0},{3,1},{4,2},{5,3},{6,4},{7,5},{8,14},{9,15},{10,... | collective-permute-start | bytes 491528 | tf_op jit(solution)/shard_map/ppermute | solution.py:29
  115.9 1.0 collective-permute-done.5
  117.0 2.7 %collective-permute-done.6 = bf16[640,128]{1,0:T(8,128)(2,1)S(1)} collective-permute-done((bf16[640,128]{1,0:T(8,128)(2,1)S(1)}, bf16[640,128]{1,0:T(8,128)(2,1)S(1)}, u32[]{:S(2)}, u32[]{:S(2)}) %collective-permute-start.6) | collective-permute-done | bytes 163872 | tf_op jit(solution)/shard_map/ppermute | solution.py:29
  119.7 3.4 %collective-permute-done.7 = bf16[640,128]{1,0:T(8,128)(2,1)S(1)} collective-permute-done((bf16[640,128]{1,0:T(8,128)(2,1)S(1)}, bf16[640,128]{1,0:T(8,128)(2,1)S(1)}, u32[]{:S(2)}, u32[]{:S(2)}) %collective-permute-start.7) | collective-permute-done | bytes 163872 | tf_op jit(solution)/shard_map/ppermute | solution.py:29
  123.2 1.9 %collective-permute-start.8 = (bf16[4,640,128]{2,1,0:T(8,128)(2,1)S(1)}, bf16[4,640,128]{2,1,0:T(8,128)(2,1)}, u32[]{:S(2)}, u32[]{:S(2)}) collective-permute-start(bf16[4,640,128]{2,1,0:T(8,128)(2,1)S(1)} %pad_maximum_fusion.1), channel_id=1, source_target_pairs={{0,1},{1,0},{2,3},{3,2},{4,5},{5,4},{6,7},{7,6},{8,9},{9,8},{10,11... | collective-permute-start | bytes 1966088 | tf_op jit(solution)/shard_map/ppermute | solution.py:32
  125.2 0.6 gather_fusion.6
  125.8 1.4 gather_fusion.5
  127.2 0.1 collective-permute-done.8
  127.3 1.7 convolution_bitcast_fusion
  129.0 2.7 %fusion.1 = bf16[640,512]{1,0:T(8,128)(2,1)} fusion(f32[640,512]{1,0:T(8,128)S(1)} %convolution_bitcast_fusion, bf16[4,128,512]{2,1,0:T(8,128)(2,1)} %gather_fusion.5, pred[4]{0:T(512)(128)(4,1)S(1)} %get-tuple-element.21, bf16[1,640,128]{2,1,0:T(8,128)(2,1)} %bitcast.78, bf16[1,640,128]{2,1,0:T(8,128)(2,1)} %bitcast.76, bf16[1,640,128]{2,1,0:T(8,128)(2,1)} %bitcast.74, ...), kind=kOutput, calls=%fused_computation.12 | convolution fusion | flops 337444864 | bytes 3145732 | tf_op jit(solution)/shard_map/dot_general | solution.py:156
  131.7 8.5 %all-to-all-start.1 = ((bf16[16,40,512]{2,1,0:T(8,128)(2,1)}), bf16[16,40,512]{2,1,0:T(8,128)(2,1)S(1)}, u32[]{:S(2)}, u32[]{:S(2)}) async-start(bf16[16,40,512]{2,1,0:T(8,128)(2,1)} %bitcast.30), calls=%async_computation.1 | async-start | bytes 1310720 | tf_op jit(solution)/shard_map/all_to_all | solution.py:166
  140.9 0.1 gt.27
  142.1 32.9 %all-to-all-done.1 = bf16[16,40,512]{2,1,0:T(8,128)(2,1)S(1)} async-done(((bf16[16,40,512]{2,1,0:T(8,128)(2,1)}), bf16[16,40,512]{2,1,0:T(8,128)(2,1)S(1)}, u32[]{:S(2)}, u32[]{:S(2)}) %all-to-all-start.1) | async-done | bytes 655392 | tf_op jit(solution)/shard_map/all_to_all | solution.py:166
  175.0 1.2 gather_fusion
  176.2 0.9 multiply_reduce_fusion
  177.1 3.4 %collective-permute-start.9 = (bf16[128,512]{1,0:T(8,128)(2,1)S(1)}, bf16[128,512]{1,0:T(8,128)(2,1)S(1)}, u32[]{:S(2)}, u32[]{:S(2)}) collective-permute-start(bf16[128,512]{1,0:T(8,128)(2,1)S(1)} %multiply_reduce_fusion), channel_id=1, source_target_pairs={{0,128},{128,256},{256,384},{384,0},{1,129},{129,257},{257,385},{3... | collective-permute-start | bytes 393224 | tf_op jit(solution)/shard_map/ppermute | solution.py:10
  180.5 4.7 %collective-permute-done.9 = bf16[128,512]{1,0:T(8,128)(2,1)S(1)} collective-permute-done((bf16[128,512]{1,0:T(8,128)(2,1)S(1)}, bf16[128,512]{1,0:T(8,128)(2,1)S(1)}, u32[]{:S(2)}, u32[]{:S(2)}) %collective-permute-start.9) | collective-permute-done | bytes 131104 | tf_op jit(solution)/shard_map/ppermute | solution.py:10
  185.2 0.7 copy.59
  (67 shorter events, 2.8 us)
Async XLA Ops:
  0.0 92.0 %copy-start = (bf16[1,1,4096,128]{3,2,1,0:T(8,128)(2,1)S(1)}, bf16[1,1,4096,128]{3,2,1,0:T(8,128)(2,1)}, u32[]{:S(2)}) copy-start(bf16[1,1,4096,128]{3,2,1,0:T(8,128)(2,1)} %param.19) | copy-start | bytes 3145732
  58.8 15.6 %collective-permute-start = (bf16[640,512]{1,0:T(8,128)(2,1)S(1)}, bf16[640,512]{1,0:T(8,128)(2,1)S(1)}, u32[]{:S(2)}, u32[]{:S(2)}) collective-permute-start(bf16[640,512]{1,0:T(8,128)(2,1)S(1)} %bitcast.62), channel_id=1, source_target_pairs={{0,2},{1,3},{2,4},{3,5},{4,6},{5,7},{6,0},{7,1},{8,10},{9,11},{10,... | collective-permute-start | bytes 1966088 | tf_op jit(solution)/shard_map/ppermute | solution.py:42
  60.9 16.9 %collective-permute-start.1 = (bf16[640,512]{1,0:T(8,128)(2,1)S(1)}, bf16[640,512]{1,0:T(8,128)(2,1)S(1)}, u32[]{:S(2)}, u32[]{:S(2)}) collective-permute-start(bf16[640,512]{1,0:T(8,128)(2,1)S(1)} %bitcast.63), channel_id=1, source_target_pairs={{0,6},{1,7},{2,0},{3,1},{4,2},{5,3},{6,4},{7,5},{8,14},{9,15},{10,... | collective-permute-start | bytes 1966088 | tf_op jit(solution)/shard_map/ppermute | solution.py:43
  74.4 9.0 %collective-permute-start.2 = (bf16[320,512]{1,0:T(8,128)(2,1)S(1)}, bf16[320,512]{1,0:T(8,128)(2,1)S(1)}, u32[]{:S(2)}, u32[]{:S(2)}) collective-permute-start(bf16[320,512]{1,0:T(8,128)(2,1)S(1)} %slice.22), channel_id=1, source_target_pairs={{0,2},{1,3},{2,4},{3,5},{4,6},{5,7},{6,0},{7,1},{8,10},{9,11},{10,... | collective-permute-start | bytes 983048 | tf_op jit(solution)/shard_map/ppermute | solution.py:45
  77.9 10.2 %collective-permute-start.3 = (bf16[320,512]{1,0:T(8,128)(2,1)S(1)}, bf16[320,512]{1,0:T(8,128)(2,1)S(1)}, u32[]{:S(2)}, u32[]{:S(2)}) collective-permute-start(bf16[320,512]{1,0:T(8,128)(2,1)S(1)} %slice.23), channel_id=1, source_target_pairs={{0,6},{1,7},{2,0},{3,1},{4,2},{5,3},{6,4},{7,5},{8,14},{9,15},{10,... | collective-permute-start | bytes 983048 | tf_op jit(solution)/shard_map/ppermute | solution.py:46
  88.1 6.0 %copy-start.1 = (bf16[1,1,4096,128]{3,2,1,0:T(8,128)(2,1)S(1)}, bf16[1,1,4096,128]{3,2,1,0:T(8,128)(2,1)}, u32[]{:S(2)}) copy-start(bf16[1,1,4096,128]{3,2,1,0:T(8,128)(2,1)} %param.20) | copy-start | bytes 3145732
  90.0 7.1 %collective-permute-start.4 = (bf16[4,640,512]{2,1,0:T(8,128)(2,1)}, bf16[4,640,512]{2,1,0:T(8,128)(2,1)}, u32[]{:S(2)}, u32[]{:S(2)}) collective-permute-start(bf16[4,640,512]{2,1,0:T(8,128)(2,1)} %pad_maximum_fusion), channel_id=1, source_target_pairs={{0,1},{1,0},{2,3},{3,2},{4,5},{5,4},{6,7},{7,6},{8,9},{9,8},{10,11... | collective-permute-start | bytes 7864328 | tf_op jit(solution)/shard_map/ppermute | solution.py:49
  99.9 2.7 %copy-start.3 = (bf16[4,512,128]{2,1,0:T(8,128)(2,1)S(1)}, bf16[4,512,128]{2,1,0:T(8,128)(2,1)}, u32[]{:S(2)}) copy-start(bf16[4,512,128]{2,1,0:T(8,128)(2,1)} %gather_fusion.4) | copy-start | bytes 1572868
  105.3 19.9 %copy-start.2 = (bf16[1,1,1024,512]{3,2,1,0:T(8,128)(2,1)S(1)}, bf16[1,1,1024,512]{3,2,1,0:T(8,128)(2,1)}, u32[]{:S(2)}) copy-start(bf16[1,1,1024,512]{3,2,1,0:T(8,128)(2,1)} %param.21) | copy-start | bytes 3145732
  108.0 8.9 %collective-permute-start.5 = (bf16[640,128]{1,0:T(8,128)(2,1)S(1)}, bf16[640,128]{1,0:T(8,128)(2,1)S(1)}, u32[]{:S(2)}, u32[]{:S(2)}) collective-permute-start(bf16[640,128]{1,0:T(8,128)(2,1)S(1)} %multiply_convert_fusion), channel_id=1, source_target_pairs={{0,2},{1,3},{2,4},{3,5},{4,6},{5,7},{6,0},{7,1},{8,10},{9,11},{10,... | collective-permute-start | bytes 491528 | tf_op jit(solution)/shard_map/ppermute | solution.py:29
  110.0 9.7 %collective-permute-start.6 = (bf16[640,128]{1,0:T(8,128)(2,1)S(1)}, bf16[640,128]{1,0:T(8,128)(2,1)S(1)}, u32[]{:S(2)}, u32[]{:S(2)}) collective-permute-start(bf16[640,128]{1,0:T(8,128)(2,1)S(1)} %multiply_convert_fusion), channel_id=1, source_target_pairs={{0,4},{1,5},{2,6},{3,7},{4,0},{5,1},{6,2},{7,3},{8,12},{9,13},{10,... | collective-permute-start | bytes 491528 | tf_op jit(solution)/shard_map/ppermute | solution.py:29
  113.3 9.9 %collective-permute-start.7 = (bf16[640,128]{1,0:T(8,128)(2,1)S(1)}, bf16[640,128]{1,0:T(8,128)(2,1)S(1)}, u32[]{:S(2)}, u32[]{:S(2)}) collective-permute-start(bf16[640,128]{1,0:T(8,128)(2,1)S(1)} %multiply_convert_fusion), channel_id=1, source_target_pairs={{0,6},{1,7},{2,0},{3,1},{4,2},{5,3},{6,4},{7,5},{8,14},{9,15},{10,... | collective-permute-start | bytes 491528 | tf_op jit(solution)/shard_map/ppermute | solution.py:29
  117.0 8.2 %copy-start.4 = (bf16[640,128]{1,0:T(8,128)(2,1)}, bf16[640,128]{1,0:T(8,128)(2,1)S(1)}, u32[]{:S(2)}) copy-start(bf16[640,128]{1,0:T(8,128)(2,1)S(1)} %collective-permute-done.5) | copy-start | bytes 491524
  119.7 5.5 %copy-start.5 = (bf16[640,128]{1,0:T(8,128)(2,1)}, bf16[640,128]{1,0:T(8,128)(2,1)S(1)}, u32[]{:S(2)}) copy-start(bf16[640,128]{1,0:T(8,128)(2,1)S(1)} %collective-permute-done.6) | copy-start | bytes 491524
  123.1 2.1 %copy-start.6 = (bf16[640,128]{1,0:T(8,128)(2,1)}, bf16[640,128]{1,0:T(8,128)(2,1)S(1)}, u32[]{:S(2)}) copy-start(bf16[640,128]{1,0:T(8,128)(2,1)S(1)} %collective-permute-done.7) | copy-start | bytes 491524
  123.2 4.1 %collective-permute-start.8 = (bf16[4,640,128]{2,1,0:T(8,128)(2,1)S(1)}, bf16[4,640,128]{2,1,0:T(8,128)(2,1)}, u32[]{:S(2)}, u32[]{:S(2)}) collective-permute-start(bf16[4,640,128]{2,1,0:T(8,128)(2,1)S(1)} %pad_maximum_fusion.1), channel_id=1, source_target_pairs={{0,1},{1,0},{2,3},{3,2},{4,5},{5,4},{6,7},{7,6},{8,9},{9,8},{10,11... | collective-permute-start | bytes 1966088 | tf_op jit(solution)/shard_map/ppermute | solution.py:32
  129.0 11.3 %copy-start.7 = (s32[1,128,2]{1,2,0:T(2,128)S(1)}, s32[1,128,2]{1,2,0:T(2,128)}, u32[]{:S(2)}) copy-start(s32[1,128,2]{1,2,0:T(2,128)} %param.14) | copy-start | bytes 3076
  129.0 11.5 %copy-start.8 = (s32[1,16]{1,0:T(1,128)S(1)}, s32[1,16]{1,0:T(1,128)}, u32[]{:S(2)}) copy-start(s32[1,16]{1,0:T(1,128)} %param.18) | copy-start | bytes 196
  129.0 12.9 %copy-start.9 = (f32[1,128,2]{1,2,0:T(2,128)S(1)}, f32[1,128,2]{1,2,0:T(2,128)}, u32[]{:S(2)}) copy-start(f32[1,128,2]{1,2,0:T(2,128)} %param.15) | copy-start | bytes 3076
  131.7 43.2 %all-to-all-start.1 = ((bf16[16,40,512]{2,1,0:T(8,128)(2,1)}), bf16[16,40,512]{2,1,0:T(8,128)(2,1)S(1)}, u32[]{:S(2)}, u32[]{:S(2)}) async-start(bf16[16,40,512]{2,1,0:T(8,128)(2,1)} %bitcast.30), calls=%async_computation.1 | async-start | bytes 1310720 | tf_op jit(solution)/shard_map/all_to_all | solution.py:166
  177.1 8.1 %collective-permute-start.9 = (bf16[128,512]{1,0:T(8,128)(2,1)S(1)}, bf16[128,512]{1,0:T(8,128)(2,1)S(1)}, u32[]{:S(2)}, u32[]{:S(2)}) collective-permute-start(bf16[128,512]{1,0:T(8,128)(2,1)S(1)} %multiply_reduce_fusion), channel_id=1, source_target_pairs={{0,128},{128,256},{256,384},{384,0},{1,129},{129,257},{257,385},{3... | collective-permute-start | bytes 393224 | tf_op jit(solution)/shard_map/ppermute | solution.py:10

commit v10 on v9

--- a/solution.py
+++ b/solution.py
@@ -133,23 +133,21 @@
     arrived = lax.all_to_all(outgoing, "expert", split_axis=0, concat_axis=0, tiled=True)
     flattened = arrived.reshape(-1, feat_width)
     own_feats, partner_feats, own_from, partner_from = relayed_chips_then_core(flattened, "rep")
-    gate_all = w_gate[0, 0].reshape(reps, feat_width, -1)
-    up_all = w_up[0, 0].reshape(reps, feat_width, -1)
+    hidden = w_gate.shape[3]
+    gate_up = jnp.concatenate(
+        [w_gate[0, 0].reshape(reps, feat_width, -1), w_up[0, 0].reshape(reps, feat_width, -1)],
+        axis=2,
+    )
     dims = (((0, 2), (0, 1)), ((), ()))
-
-    def project(weights):
-        own = lax.dot_general(
-            own_feats, jnp.take(weights, own_from, axis=0), dims,
-            preferred_element_type=jnp.float32,
-        )
-        partner = lax.dot_general(
-            partner_feats, jnp.take(weights, partner_from, axis=0), dims,
-            preferred_element_type=jnp.float32,
-        )
-        return own + partner
-
-    gate_proj = project(gate_all)
-    up_proj = project(up_all)
+    both = lax.dot_general(
+        own_feats, jnp.take(gate_up, own_from, axis=0), dims,
+        preferred_element_type=jnp.float32,
+    ) + lax.dot_general(
+        partner_feats, jnp.take(gate_up, partner_from, axis=0), dims,
+        preferred_element_type=jnp.float32,
+    )
+    gate_proj = both[:, :hidden]
+    up_proj = both[:, hidden:]
     activated = (jax.nn.silu(gate_proj) * up_proj).astype(jnp.bfloat16)
     own_act, partner_act, act_own_from, act_partner_from = chips_then_core(activated, "rep")
     down_all = w_down[0, 0].reshape(reps, activated.shape[1], -1)

time: 187 us -> 180 us (0.963)
  matrix products: 16.5 us -> 8.43 us
  other arithmetic: 8.73 us -> 10.7 us
    dot_general x4 -> x2, matrix products: 10.9 us -> 4.01 us  [the longest x1 3.08 us: local(): lax.dot_general(partner_feats, jnp.take(gate_up, partner_from, axis=0), d...]
    gather x4 -> x2, local copies, waits for them, and re-layouts: 4.14 us -> 3.25 us  [the longest x1 1.63 us: local(): jnp.take(gate_up, own_from, axis=0)]
  transfers between devices with their start and end apart: 11 -> 11, of which waited for: 10 -> 8; matrix products, arithmetic and copies ran while one was open for 4% -> 5% of each run, Pallas kernels for 0% -> 0%
where the time goes in v10:
time: 180 us; the launch traced here: 179 us
  waiting for transfers between devices  63.7 us (35%)
  blocking collectives  51.4 us (29%)
  starting transfers between devices  35.2 us (20%)
  other arithmetic  10.7 us (6%)
  local copies, waits for them, and re-layouts  9.28 us (5%)
  matrix products  8.43 us (5%)
    all_to_all x1, blocking collectives, local(): lax.all_to_all(outgoing, 'expert', split_axis=0, concat_axis=0, tiled=True)  51.4 us
    all_to_all x1, waiting for transfers between devices, local(): lax.all_to_all(produced, 'expert', split_axis=0, concat_axis=0, tiled=True)  34 us
    ppermute x1, waiting for transfers between devices, relayed_chips_then_core(): from_below = lax.ppermute(value, axis, up_pairs)  9.78 us
    all_to_all x1, starting transfers between devices, local(): lax.all_to_all(produced, 'expert', split_axis=0, concat_axis=0, tiled=True)  8.51 us
    ppermute x3, starting transfers between devices, chips_then_core(): pieces.append(lax.ppermute(value, axis, pairs))  7.76 us
    ppermute x3, waiting for transfers between devices, chips_then_core(): pieces.append(lax.ppermute(value, axis, pairs))  7.55 us
    ppermute x1, waiting for transfers between devices, relayed_chips_then_core(): far_high = lax.ppermute(from_above[half:], axis, down_pairs)  4.68 us
    ppermute x1, waiting for transfers between devices, passed_along(): return lax.ppermute(value, axis, pairs)  4.65 us
  transfers between devices with their start and end apart: 11, of which 8 were waited for; matrix products, arithmetic and copies ran while one was open for 5% of the time, Pallas kernels for 0%

profile of v10, /device:TPU:24, one launch (start us, length us, event | category | flops | bytes accessed | tf_op | source)
XLA Modules:
  0.0 179.3 jit_solution(5445611719920155311)
XLA Ops:
  0.0 0.8 convert_reduce_fusion
  0.9 0.7 fusion.26
  1.6 1.2 multiply_reduce_fusion.1
  2.9 0.2 reduce_window_sum.30
  3.1 0.2 reduce_window_sum.29
  3.4 0.7 fusion.27
  4.2 0.7 select_reduce_fusion
  5.1 0.8 select_reduce_fusion.1
  6.1 1.3 convolution_convert_fusion
  7.4 51.4 %all_to_all.10 = bf16[16,40,512]{2,1,0:T(8,128)(2,1)S(1)} all-to-all(bf16[16,40,512]{2,1,0:T(8,128)(2,1)S(1)} %convolution_convert_fusion), channel_id=1, replica_groups=mesh['section'=4,'expert'=16,'rep'=8] {'expert'}, dimensions={0} | all-to-all | bytes 1310720 | tf_op jit(solution)/shard_map/all_to_all | solution.py:133
  58.8 2.1 %collective-permute-start = (bf16[640,512]{1,0:T(8,128)(2,1)S(1)}, bf16[640,512]{1,0:T(8,128)(2,1)S(1)}, u32[]{:S(2)}, u32[]{:S(2)}) collective-permute-start(bf16[640,512]{1,0:T(8,128)(2,1)S(1)} %bitcast.52), channel_id=1, source_target_pairs={{0,2},{1,3},{2,4},{3,5},{4,6},{5,7},{6,0},{7,1},{8,10},{9,11},{10,... | collective-permute-start | bytes 1966088 | tf_op jit(solution)/shard_map/ppermute | solution.py:42
  60.9 3.7 %collective-permute-start.1 = (bf16[640,512]{1,0:T(8,128)(2,1)S(1)}, bf16[640,512]{1,0:T(8,128)(2,1)S(1)}, u32[]{:S(2)}, u32[]{:S(2)}) collective-permute-start(bf16[640,512]{1,0:T(8,128)(2,1)S(1)} %bitcast.53), channel_id=1, source_target_pairs={{0,6},{1,7},{2,0},{3,1},{4,2},{5,3},{6,4},{7,5},{8,14},{9,15},{10,... | collective-permute-start | bytes 1966088 | tf_op jit(solution)/shard_map/ppermute | solution.py:43
  64.6 9.8 %collective-permute-done = bf16[640,512]{1,0:T(8,128)(2,1)S(1)} collective-permute-done((bf16[640,512]{1,0:T(8,128)(2,1)S(1)}, bf16[640,512]{1,0:T(8,128)(2,1)S(1)}, u32[]{:S(2)}, u32[]{:S(2)}) %collective-permute-start) | collective-permute-done | bytes 655392 | tf_op jit(solution)/shard_map/ppermute | solution.py:42
  74.5 3.4 %collective-permute-start.2 = (bf16[320,512]{1,0:T(8,128)(2,1)S(1)}, bf16[320,512]{1,0:T(8,128)(2,1)S(1)}, u32[]{:S(2)}, u32[]{:S(2)}) collective-permute-start(bf16[320,512]{1,0:T(8,128)(2,1)S(1)} %slice.26), channel_id=1, source_target_pairs={{0,2},{1,3},{2,4},{3,5},{4,6},{5,7},{6,0},{7,1},{8,10},{9,11},{10,... | collective-permute-start | bytes 983048 | tf_op jit(solution)/shard_map/ppermute | solution.py:45
  77.9 2.4 %collective-permute-start.3 = (bf16[320,512]{1,0:T(8,128)(2,1)S(1)}, bf16[320,512]{1,0:T(8,128)(2,1)S(1)}, u32[]{:S(2)}, u32[]{:S(2)}) collective-permute-start(bf16[320,512]{1,0:T(8,128)(2,1)S(1)} %slice.27), channel_id=1, source_target_pairs={{0,6},{1,7},{2,0},{3,1},{4,2},{5,3},{6,4},{7,5},{8,14},{9,15},{10,... | collective-permute-start | bytes 983048 | tf_op jit(solution)/shard_map/ppermute | solution.py:46
  80.4 3.1 %collective-permute-done.2 = bf16[320,512]{1,0:T(8,128)(2,1)S(1)} collective-permute-done((bf16[320,512]{1,0:T(8,128)(2,1)S(1)}, bf16[320,512]{1,0:T(8,128)(2,1)S(1)}, u32[]{:S(2)}, u32[]{:S(2)}) %collective-permute-start.2) | collective-permute-done | bytes 327712 | tf_op jit(solution)/shard_map/ppermute | solution.py:45
  83.4 4.7 %collective-permute-done.3 = bf16[320,512]{1,0:T(8,128)(2,1)S(1)} collective-permute-done((bf16[320,512]{1,0:T(8,128)(2,1)S(1)}, bf16[320,512]{1,0:T(8,128)(2,1)S(1)}, u32[]{:S(2)}, u32[]{:S(2)}) %collective-permute-start.3) | collective-permute-done | bytes 327712 | tf_op jit(solution)/shard_map/ppermute | solution.py:46
  88.2 1.8 %pad_maximum_fusion = bf16[4,640,512]{2,1,0:T(8,128)(2,1)} fusion(bf16[1,640,512]{2,1,0:T(8,128)(2,1)S(1)} %maximum_bitcast_fusion, bf16[1,640,512]{2,1,0:T(8,128)(2,1)S(1)} %bitcast.58, bf16[1,640,512]{2,1,0:T(8,128)(2,1)S(1)} %bitcast.56, bf16[1,640,512]{2,1,0:T(8,128)(2,1)S(1)} %bitcast.54), kind=kLoop, calls=%fused_computation.5 | loop fusion | flops 3932160 | bytes 5242880 | tf_op jit(solution)/shard_map/stack | solution.py:48
  90.0 1.9 %collective-permute-start.4 = (bf16[4,640,512]{2,1,0:T(8,128)(2,1)}, bf16[4,640,512]{2,1,0:T(8,128)(2,1)}, u32[]{:S(2)}, u32[]{:S(2)}) collective-permute-start(bf16[4,640,512]{2,1,0:T(8,128)(2,1)} %pad_maximum_fusion), channel_id=1, source_target_pairs={{0,1},{1,0},{2,3},{3,2},{4,5},{5,4},{6,7},{7,6},{8,9},{9,8},{10,11... | collective-permute-start | bytes 7864328 | tf_op jit(solution)/shard_map/ppermute | solution.py:49
  92.1 1.8 pad_maximum_fusion.1
  93.9 1.6 gather_fusion.2
  95.5 1.6 gather_fusion.1
  97.3 3.1 %convolution_bitcast_fusion.2 = f32[640,256]{1,0:T(8,128)S(1)} fusion(bf16[4,640,512]{2,1,0:T(8,128)(2,1)} %collective-permute-done.4, bf16[4,512,256]{2,1,0:T(8,128)(2,1)} %gather_fusion.2, pred[4]{0:T(512)(128)(4,1)S(1)} %get-tuple-element.27), kind=kOutput, calls=%fused_computation.12 | convolution fusion | flops 671612928 | bytes 4325380 | tf_op jit(solution)/shard_map/dot_general | solution.py:145
  100.4 0.9 fusion.2
  101.5 1.9 %collective-permute-start.5 = (bf16[640,128]{1,0:T(8,128)(2,1)S(1)}, bf16[640,128]{1,0:T(8,128)(2,1)S(1)}, u32[]{:S(2)}, u32[]{:S(2)}) collective-permute-start(bf16[640,128]{1,0:T(8,128)(2,1)S(1)} %fusion.17), channel_id=1, source_target_pairs={{0,2},{1,3},{2,4},{3,5},{4,6},{5,7},{6,0},{7,1},{8,10},{9,11},{10,... | collective-permute-start | bytes 491528 | tf_op jit(solution)/shard_map/ppermute | solution.py:29
  103.4 3.3 %collective-permute-start.6 = (bf16[640,128]{1,0:T(8,128)(2,1)S(1)}, bf16[640,128]{1,0:T(8,128)(2,1)S(1)}, u32[]{:S(2)}, u32[]{:S(2)}) collective-permute-start(bf16[640,128]{1,0:T(8,128)(2,1)S(1)} %fusion.17), channel_id=1, source_target_pairs={{0,4},{1,5},{2,6},{3,7},{4,0},{5,1},{6,2},{7,3},{8,12},{9,13},{10,... | collective-permute-start | bytes 491528 | tf_op jit(solution)/shard_map/ppermute | solution.py:29
  106.7 2.6 %collective-permute-start.7 = (bf16[640,128]{1,0:T(8,128)(2,1)S(1)}, bf16[640,128]{1,0:T(8,128)(2,1)S(1)}, u32[]{:S(2)}, u32[]{:S(2)}) collective-permute-start(bf16[640,128]{1,0:T(8,128)(2,1)S(1)} %fusion.17), channel_id=1, source_target_pairs={{0,6},{1,7},{2,0},{3,1},{4,2},{5,3},{6,4},{7,5},{8,14},{9,15},{10,... | collective-permute-start | bytes 491528 | tf_op jit(solution)/shard_map/ppermute | solution.py:29
  109.4 1.0 collective-permute-done.5
  110.4 3.1 %collective-permute-done.6 = bf16[640,128]{1,0:T(8,128)(2,1)S(1)} collective-permute-done((bf16[640,128]{1,0:T(8,128)(2,1)S(1)}, bf16[640,128]{1,0:T(8,128)(2,1)S(1)}, u32[]{:S(2)}, u32[]{:S(2)}) %collective-permute-start.6) | collective-permute-done | bytes 163872 | tf_op jit(solution)/shard_map/ppermute | solution.py:29
  113.5 3.4 %collective-permute-done.7 = bf16[640,128]{1,0:T(8,128)(2,1)S(1)} collective-permute-done((bf16[640,128]{1,0:T(8,128)(2,1)S(1)}, bf16[640,128]{1,0:T(8,128)(2,1)S(1)}, u32[]{:S(2)}, u32[]{:S(2)}) %collective-permute-start.7) | collective-permute-done | bytes 163872 | tf_op jit(solution)/shard_map/ppermute | solution.py:29
  117.0 2.0 %collective-permute-start.8 = (bf16[4,640,128]{2,1,0:T(8,128)(2,1)S(1)}, bf16[4,640,128]{2,1,0:T(8,128)(2,1)S(1)}, u32[]{:S(2)}, u32[]{:S(2)}) collective-permute-start(bf16[4,640,128]{2,1,0:T(8,128)(2,1)S(1)} %pad_maximum_fusion.2), channel_id=1, source_target_pairs={{0,1},{1,0},{2,3},{3,2},{4,5},{5,4},{6,7},{7,6},{8,9},{9,8},{10,11... | collective-permute-start | bytes 1966088 | tf_op jit(solution)/shard_map/ppermute | solution.py:32
  119.0 0.6 gather_fusion.4
  119.6 1.4 gather_fusion.3
  121.0 0.6 convolution_bitcast_fusion
  121.6 2.6 %fusion.1 = bf16[640,512]{1,0:T(8,128)(2,1)} fusion(f32[640,512]{1,0:T(8,128)S(1)} %convolution_bitcast_fusion, bf16[4,128,512]{2,1,0:T(8,128)(2,1)} %gather_fusion.3, pred[4]{0:T(512)(128)(4,1)S(1)} %get-tuple-element.21, bf16[1,640,128]{2,1,0:T(8,128)(2,1)} %bitcast.67, bf16[1,640,128]{2,1,0:T(8,128)(2,1)S(1)} %bitcast.65, ...), kind=kOutput, calls=%fused_computation.11 | convolution fusion | flops 337444864 | bytes 3145732 | tf_op jit(solution)/shard_map/dot_general | solution.py:154
  124.2 8.5 %all-to-all-start.1 = ((bf16[16,40,512]{2,1,0:T(8,128)(2,1)}), bf16[16,40,512]{2,1,0:T(8,128)(2,1)S(1)}, u32[]{:S(2)}, u32[]{:S(2)}) async-start(bf16[16,40,512]{2,1,0:T(8,128)(2,1)} %bitcast.28), calls=%async_computation.1 | async-start | bytes 1310720 | tf_op jit(solution)/shard_map/all_to_all | solution.py:164
  133.2 0.1 copy.53
  133.4 0.1 gt.27
  133.8 0.1 reduce_sum.143
  133.9 0.1 reduce_sum.144
  134.1 0.1 squeeze.7
  134.2 0.1 copy.46
  134.5 34.0 %all-to-all-done.1 = bf16[16,40,512]{2,1,0:T(8,128)(2,1)S(1)} async-done(((bf16[16,40,512]{2,1,0:T(8,128)(2,1)}), bf16[16,40,512]{2,1,0:T(8,128)(2,1)S(1)}, u32[]{:S(2)}, u32[]{:S(2)}) %all-to-all-start.1) | async-done | bytes 655392 | tf_op jit(solution)/shard_map/all_to_all | solution.py:164
  168.5 1.2 gather_fusion
  169.7 0.9 multiply_reduce_fusion
  170.6 3.4 %collective-permute-start.9 = (bf16[128,512]{1,0:T(8,128)(2,1)S(1)}, bf16[128,512]{1,0:T(8,128)(2,1)S(1)}, u32[]{:S(2)}, u32[]{:S(2)}) collective-permute-start(bf16[128,512]{1,0:T(8,128)(2,1)S(1)} %multiply_reduce_fusion), channel_id=1, source_target_pairs={{0,128},{128,256},{256,384},{384,0},{1,129},{129,257},{257,385},{3... | collective-permute-start | bytes 393224 | tf_op jit(solution)/shard_map/ppermute | solution.py:10
  174.0 4.7 %collective-permute-done.9 = bf16[128,512]{1,0:T(8,128)(2,1)S(1)} collective-permute-done((bf16[128,512]{1,0:T(8,128)(2,1)S(1)}, bf16[128,512]{1,0:T(8,128)(2,1)S(1)}, u32[]{:S(2)}, u32[]{:S(2)}) %collective-permute-start.9) | collective-permute-done | bytes 131104 | tf_op jit(solution)/shard_map/ppermute | solution.py:10
  178.7 0.7 copy.59
  (74 shorter events, 2.4 us)
Async XLA Ops:
  0.0 119.0 %copy-start = (bf16[1,1,1024,512]{3,2,1,0:T(8,128)(2,1)S(1)}, bf16[1,1,1024,512]{3,2,1,0:T(8,128)(2,1)}, u32[]{:S(2)}) copy-start(bf16[1,1,1024,512]{3,2,1,0:T(8,128)(2,1)} %param.21) | copy-start | bytes 3145732
  58.8 31.2 %copy-start.1 = (bf16[16,40,512]{2,1,0:T(8,128)(2,1)}, bf16[16,40,512]{2,1,0:T(8,128)(2,1)S(1)}, u32[]{:S(2)}) copy-start(bf16[16,40,512]{2,1,0:T(8,128)(2,1)S(1)} %all_to_all.10) | copy-start | bytes 1966084
  58.8 15.6 %collective-permute-start = (bf16[640,512]{1,0:T(8,128)(2,1)S(1)}, bf16[640,512]{1,0:T(8,128)(2,1)S(1)}, u32[]{:S(2)}, u32[]{:S(2)}) collective-permute-start(bf16[640,512]{1,0:T(8,128)(2,1)S(1)} %bitcast.52), channel_id=1, source_target_pairs={{0,2},{1,3},{2,4},{3,5},{4,6},{5,7},{6,0},{7,1},{8,10},{9,11},{10,... | collective-permute-start | bytes 1966088 | tf_op jit(solution)/shard_map/ppermute | solution.py:42
  60.9 16.9 %collective-permute-start.1 = (bf16[640,512]{1,0:T(8,128)(2,1)S(1)}, bf16[640,512]{1,0:T(8,128)(2,1)S(1)}, u32[]{:S(2)}, u32[]{:S(2)}) collective-permute-start(bf16[640,512]{1,0:T(8,128)(2,1)S(1)} %bitcast.53), channel_id=1, source_target_pairs={{0,6},{1,7},{2,0},{3,1},{4,2},{5,3},{6,4},{7,5},{8,14},{9,15},{10,... | collective-permute-start | bytes 1966088 | tf_op jit(solution)/shard_map/ppermute | solution.py:43
  74.4 15.6 %copy-start.5 = (bf16[640,512]{1,0:T(8,128)(2,1)}, bf16[640,512]{1,0:T(8,128)(2,1)S(1)}, u32[]{:S(2)}) copy-start(bf16[640,512]{1,0:T(8,128)(2,1)S(1)} %collective-permute-done) | copy-start | bytes 1966084
  74.5 9.0 %collective-permute-start.2 = (bf16[320,512]{1,0:T(8,128)(2,1)S(1)}, bf16[320,512]{1,0:T(8,128)(2,1)S(1)}, u32[]{:S(2)}, u32[]{:S(2)}) collective-permute-start(bf16[320,512]{1,0:T(8,128)(2,1)S(1)} %slice.26), channel_id=1, source_target_pairs={{0,2},{1,3},{2,4},{3,5},{4,6},{5,7},{6,0},{7,1},{8,10},{9,11},{10,... | collective-permute-start | bytes 983048 | tf_op jit(solution)/shard_map/ppermute | solution.py:45
  77.9 12.1 %copy-start.7 = (bf16[640,512]{1,0:T(8,128)(2,1)}, bf16[640,512]{1,0:T(8,128)(2,1)S(1)}, u32[]{:S(2)}) copy-start(bf16[640,512]{1,0:T(8,128)(2,1)S(1)} %collective-permute-done.1) | copy-start | bytes 1966084
  77.9 10.2 %collective-permute-start.3 = (bf16[320,512]{1,0:T(8,128)(2,1)S(1)}, bf16[320,512]{1,0:T(8,128)(2,1)S(1)}, u32[]{:S(2)}, u32[]{:S(2)}) collective-permute-start(bf16[320,512]{1,0:T(8,128)(2,1)S(1)} %slice.27), channel_id=1, source_target_pairs={{0,6},{1,7},{2,0},{3,1},{4,2},{5,3},{6,4},{7,5},{8,14},{9,15},{10,... | collective-permute-start | bytes 983048 | tf_op jit(solution)/shard_map/ppermute | solution.py:46
  88.1 1.9 %copy-start.3 = (bf16[1,640,512]{2,1,0:T(8,128)(2,1)}, bf16[1,640,512]{2,1,0:T(8,128)(2,1)S(1)}, u32[]{:S(2)}) copy-start(bf16[1,640,512]{2,1,0:T(8,128)(2,1)S(1)} %maximum_bitcast_fusion) | copy-start | bytes 1966084
  90.0 7.2 %collective-permute-start.4 = (bf16[4,640,512]{2,1,0:T(8,128)(2,1)}, bf16[4,640,512]{2,1,0:T(8,128)(2,1)}, u32[]{:S(2)}, u32[]{:S(2)}) collective-permute-start(bf16[4,640,512]{2,1,0:T(8,128)(2,1)} %pad_maximum_fusion), channel_id=1, source_target_pairs={{0,1},{1,0},{2,3},{3,2},{4,5},{5,4},{6,7},{7,6},{8,9},{9,8},{10,11... | collective-permute-start | bytes 7864328 | tf_op jit(solution)/shard_map/ppermute | solution.py:49
  97.3 3.1 %copy-start.2 = (bf16[16,40,512]{2,1,0:T(8,128)(2,1)S(1)}, bf16[16,40,512]{2,1,0:T(8,128)(2,1)}, u32[]{:S(2)}) copy-start(bf16[16,40,512]{2,1,0:T(8,128)(2,1)} %copy-done.1) | copy-start | bytes 1966084
  97.3 3.1 %copy-start.4 = (bf16[1,640,512]{2,1,0:T(8,128)(2,1)S(1)}, bf16[1,640,512]{2,1,0:T(8,128)(2,1)}, u32[]{:S(2)}) copy-start(bf16[1,640,512]{2,1,0:T(8,128)(2,1)} %copy-done.3) | copy-start | bytes 1966084
  97.3 3.1 %copy-start.6 = (bf16[640,512]{1,0:T(8,128)(2,1)S(1)}, bf16[640,512]{1,0:T(8,128)(2,1)}, u32[]{:S(2)}) copy-start(bf16[640,512]{1,0:T(8,128)(2,1)} %copy-done.5) | copy-start | bytes 1966084
  97.3 3.1 %copy-start.8 = (bf16[640,512]{1,0:T(8,128)(2,1)S(1)}, bf16[640,512]{1,0:T(8,128)(2,1)}, u32[]{:S(2)}) copy-start(bf16[640,512]{1,0:T(8,128)(2,1)} %copy-done.7) | copy-start | bytes 1966084
  97.3 3.1 %copy-start.9 = (bf16[4,512,256]{2,1,0:T(8,128)(2,1)S(1)}, bf16[4,512,256]{2,1,0:T(8,128)(2,1)}, u32[]{:S(2)}) copy-start(bf16[4,512,256]{2,1,0:T(8,128)(2,1)} %gather_fusion.1) | copy-start | bytes 3145732
  101.5 8.9 %collective-permute-start.5 = (bf16[640,128]{1,0:T(8,128)(2,1)S(1)}, bf16[640,128]{1,0:T(8,128)(2,1)S(1)}, u32[]{:S(2)}, u32[]{:S(2)}) collective-permute-start(bf16[640,128]{1,0:T(8,128)(2,1)S(1)} %fusion.17), channel_id=1, source_target_pairs={{0,2},{1,3},{2,4},{3,5},{4,6},{5,7},{6,0},{7,1},{8,10},{9,11},{10,... | collective-permute-start | bytes 491528 | tf_op jit(solution)/shard_map/ppermute | solution.py:29
  103.4 10.1 %collective-permute-start.6 = (bf16[640,128]{1,0:T(8,128)(2,1)S(1)}, bf16[640,128]{1,0:T(8,128)(2,1)S(1)}, u32[]{:S(2)}, u32[]{:S(2)}) collective-permute-start(bf16[640,128]{1,0:T(8,128)(2,1)S(1)} %fusion.17), channel_id=1, source_target_pairs={{0,4},{1,5},{2,6},{3,7},{4,0},{5,1},{6,2},{7,3},{8,12},{9,13},{10,... | collective-permute-start | bytes 491528 | tf_op jit(solution)/shard_map/ppermute | solution.py:29
  106.7 10.2 %collective-permute-start.7 = (bf16[640,128]{1,0:T(8,128)(2,1)S(1)}, bf16[640,128]{1,0:T(8,128)(2,1)S(1)}, u32[]{:S(2)}, u32[]{:S(2)}) collective-permute-start(bf16[640,128]{1,0:T(8,128)(2,1)S(1)} %fusion.17), channel_id=1, source_target_pairs={{0,6},{1,7},{2,0},{3,1},{4,2},{5,3},{6,4},{7,5},{8,14},{9,15},{10,... | collective-permute-start | bytes 491528 | tf_op jit(solution)/shard_map/ppermute | solution.py:29
  116.9 2.1 %copy-start.10 = (bf16[640,128]{1,0:T(8,128)(2,1)}, bf16[640,128]{1,0:T(8,128)(2,1)S(1)}, u32[]{:S(2)}) copy-start(bf16[640,128]{1,0:T(8,128)(2,1)S(1)} %collective-permute-done.7) | copy-start | bytes 491524
  117.0 4.0 %collective-permute-start.8 = (bf16[4,640,128]{2,1,0:T(8,128)(2,1)S(1)}, bf16[4,640,128]{2,1,0:T(8,128)(2,1)S(1)}, u32[]{:S(2)}, u32[]{:S(2)}) collective-permute-start(bf16[4,640,128]{2,1,0:T(8,128)(2,1)S(1)} %pad_maximum_fusion.2), channel_id=1, source_target_pairs={{0,1},{1,0},{2,3},{3,2},{4,5},{5,4},{6,7},{7,6},{8,9},{9,8},{10,11... | collective-permute-start | bytes 1966088 | tf_op jit(solution)/shard_map/ppermute | solution.py:32
  121.6 11.1 %copy-start.11 = (s32[1,128,2]{1,2,0:T(2,128)S(1)}, s32[1,128,2]{1,2,0:T(2,128)}, u32[]{:S(2)}) copy-start(s32[1,128,2]{1,2,0:T(2,128)} %param.14) | copy-start | bytes 3076
  121.6 11.3 %copy-start.12 = (s32[1,16]{1,0:T(1,128)S(1)}, s32[1,16]{1,0:T(1,128)}, u32[]{:S(2)}) copy-start(s32[1,16]{1,0:T(1,128)} %param.18) | copy-start | bytes 196
  121.6 12.7 %copy-start.13 = (f32[1,128,2]{1,2,0:T(2,128)S(1)}, f32[1,128,2]{1,2,0:T(2,128)}, u32[]{:S(2)}) copy-start(f32[1,128,2]{1,2,0:T(2,128)} %param.15) | copy-start | bytes 3076
  124.2 44.3 %all-to-all-start.1 = ((bf16[16,40,512]{2,1,0:T(8,128)(2,1)}), bf16[16,40,512]{2,1,0:T(8,128)(2,1)S(1)}, u32[]{:S(2)}, u32[]{:S(2)}) async-start(bf16[16,40,512]{2,1,0:T(8,128)(2,1)} %bitcast.28), calls=%async_computation.1 | async-start | bytes 1310720 | tf_op jit(solution)/shard_map/all_to_all | solution.py:164
  170.6 8.1 %collective-permute-start.9 = (bf16[128,512]{1,0:T(8,128)(2,1)S(1)}, bf16[128,512]{1,0:T(8,128)(2,1)S(1)}, u32[]{:S(2)}, u32[]{:S(2)}) collective-permute-start(bf16[128,512]{1,0:T(8,128)(2,1)S(1)} %multiply_reduce_fusion), channel_id=1, source_target_pairs={{0,128},{128,256},{256,384},{384,0},{1,129},{129,257},{257,385},{3... | collective-permute-start | bytes 393224 | tf_op jit(solution)/shard_map/ppermute | solution.py:10

commit v11 on v10

--- a/solution.py
+++ b/solution.py
@@ -49,6 +49,31 @@
     swapped = lax.ppermute(bundle, axis, [(source, source ^ 1) for source in range(count)])
     origins = jnp.stack([me, (me - 2) % count, (me + 2) % count, (me + 4) % count])
     return bundle, swapped, origins, origins ^ 1
+
+
+def relayed_in_two_swaps(value, axis):
+    count = lax.axis_size(axis)
+    me = lax.axis_index(axis)
+    up_pairs = [(source, (source + 2) % count) for source in range(count)]
+    down_pairs = [(source, (source - 2) % count) for source in range(count)]
+    swap_pairs = [(source, source ^ 1) for source in range(count)]
+    from_below = lax.ppermute(value, axis, up_pairs)
+    from_above = lax.ppermute(value, axis, down_pairs)
+    half = value.shape[0] // 2
+    far_low = lax.ppermute(from_below[:half], axis, up_pairs)
+    far_high = lax.ppermute(from_above[half:], axis, down_pairs)
+    near = jnp.stack([value, from_below, from_above])
+    near_swapped = lax.ppermute(near, axis, swap_pairs)
+    far = jnp.concatenate([far_low, far_high], axis=0)[None]
+    far_swapped = lax.ppermute(far, axis, swap_pairs)
+    near_from = jnp.stack([me, (me - 2) % count, (me + 2) % count])
+    far_from = ((me + 4) % count)[None]
+    return [
+        (near, near_from),
+        (near_swapped, near_from ^ 1),
+        (far, far_from),
+        (far_swapped, far_from ^ 1),
+    ]
 
 
 def paired_gather(value, axis):
@@ -132,20 +157,19 @@
     ).astype(rows_local.dtype)
     arrived = lax.all_to_all(outgoing, "expert", split_axis=0, concat_axis=0, tiled=True)
     flattened = arrived.reshape(-1, feat_width)
-    own_feats, partner_feats, own_from, partner_from = relayed_chips_then_core(flattened, "rep")
+    row_pieces = relayed_in_two_swaps(flattened, "rep")
     hidden = w_gate.shape[3]
     gate_up = jnp.concatenate(
         [w_gate[0, 0].reshape(reps, feat_width, -1), w_up[0, 0].reshape(reps, feat_width, -1)],
         axis=2,
     )
     dims = (((0, 2), (0, 1)), ((), ()))
-    both = lax.dot_general(
-        own_feats, jnp.take(gate_up, own_from, axis=0), dims,
-        preferred_element_type=jnp.float32,
-    ) + lax.dot_general(
-        partner_feats, jnp.take(gate_up, partner_from, axis=0), dims,
-        preferred_element_type=jnp.float32,
-    )
+    both = None
+    for piece, origin in row_pieces:
+        term = lax.dot_general(
+            piece, jnp.take(gate_up, origin, axis=0), dims, preferred_element_type=jnp.float32
+        )
+        both = term if both is None else both + term
     gate_proj = both[:, :hidden]
     up_proj = both[:, hidden:]
     activated = (jax.nn.silu(gate_proj) * up_proj).astype(jnp.bfloat16)

time: 180 us -> 191 us (1.061)
  local copies, waits for them, and re-layouts: 9.28 us -> 14.9 us
  waiting for transfers between devices: 63.7 us -> 67.3 us
    ppermute x5 -> x6, waiting for transfers between devices: 17.5 us -> 21.5 us  [the longest x1 9.78 us: relayed_in_two_swaps(): from_below = lax.ppermute(value, axis, up_pairs)]
    gather x2, local copies, waits for them, and re-layouts: 3.25 us -> 6.22 us  [local(): jnp.take(gate_up, origin, axis=0)]
    dot_general x2 -> x4, matrix products: 4.01 us -> 6.12 us  [local(): lax.dot_general(piece, jnp.take(gate_up, origin, axis=0), dims, preferred...]
    ppermute x5 -> x6, starting transfers between devices: 13.6 us -> 15.6 us  [the longest x1 3.71 us: relayed_in_two_swaps(): from_above = lax.ppermute(value, axis, down_pairs)]
  transfers between devices with their start and end apart: 11 -> 12, of which waited for: 8 -> 9; matrix products, arithmetic and copies ran while one was open for 5% -> 9% of each run, Pallas kernels for 0% -> 0%
where the time goes in v11:
time: 191 us; the launch traced here: 189 us
  waiting for transfers between devices  67.3 us (35%)
  blocking collectives  51.4 us (27%)
  starting transfers between devices  36.6 us (19%)
  local copies, waits for them, and re-layouts  14.9 us (8%)
  other arithmetic  10.2 us (5%)
  matrix products  8.5 us (4%)
    all_to_all x1, blocking collectives, local(): lax.all_to_all(outgoing, 'expert', split_axis=0, concat_axis=0, tiled=True)  51.4 us
    all_to_all x1, waiting for transfers between devices, local(): lax.all_to_all(produced, 'expert', split_axis=0, concat_axis=0, tiled=True)  34.1 us
    ppermute x1, waiting for transfers between devices, relayed_in_two_swaps(): from_below = lax.ppermute(value, axis, up_pairs)  9.78 us
    ppermute x3, starting transfers between devices, chips_then_core(): pieces.append(lax.ppermute(value, axis, pairs))  8.31 us
    all_to_all x1, starting transfers between devices, local(): lax.all_to_all(produced, 'expert', split_axis=0, concat_axis=0, tiled=True)  7.29 us
    ppermute x3, waiting for transfers between devices, chips_then_core(): pieces.append(lax.ppermute(value, axis, pairs))  7.12 us
    gather x2, local copies, waits for them, and re-layouts, local(): jnp.take(gate_up, origin, axis=0)  6.22 us
    dot_general x4, matrix products, local(): lax.dot_general(piece, jnp.take(gate_up, origin, axis=0), dims, preferred...  6.12 us
  transfers between devices with their start and end apart: 12, of which 9 were waited for; matrix products, arithmetic and copies ran while one was open for 9% of the time, Pallas kernels for 0%

profile of v11, /device:TPU:24, one launch (start us, length us, event | category | flops | bytes accessed | tf_op | source)
XLA Modules:
  0.0 189.4 jit_solution(12143816296339514136)
XLA Ops:
  0.0 0.8 convert_reduce_fusion
  0.9 0.7 fusion.43
  1.6 1.2 multiply_reduce_fusion.1
  3.4 0.7 fusion.44
  4.2 0.7 select_reduce_fusion
  5.2 0.8 select_reduce_fusion.1
  6.1 0.4 convolution_convert_fusion
  6.5 51.4 %all_to_all.10 = bf16[16,40,512]{2,1,0:T(8,128)(2,1)S(1)} all-to-all(bf16[16,40,512]{2,1,0:T(8,128)(2,1)S(1)} %convolution_convert_fusion), channel_id=1, replica_groups=mesh['section'=4,'expert'=16,'rep'=8] {'expert'}, dimensions={0} | all-to-all | bytes 1310720 | tf_op jit(solution)/shard_map/all_to_all | solution.py:158
  57.9 2.1 %collective-permute-start = (bf16[640,512]{1,0:T(8,128)(2,1)S(1)}, bf16[640,512]{1,0:T(8,128)(2,1)S(1)}, u32[]{:S(2)}, u32[]{:S(2)}) collective-permute-start(bf16[640,512]{1,0:T(8,128)(2,1)S(1)} %bitcast.75), channel_id=1, source_target_pairs={{0,2},{1,3},{2,4},{3,5},{4,6},{5,7},{6,0},{7,1},{8,10},{9,11},{10,... | collective-permute-start | bytes 1966088 | tf_op jit(solution)/shard_map/ppermute | solution.py:60
  60.0 3.7 %collective-permute-start.1 = (bf16[640,512]{1,0:T(8,128)(2,1)S(1)}, bf16[640,512]{1,0:T(8,128)(2,1)S(1)}, u32[]{:S(2)}, u32[]{:S(2)}) collective-permute-start(bf16[640,512]{1,0:T(8,128)(2,1)S(1)} %bitcast.76), channel_id=1, source_target_pairs={{0,6},{1,7},{2,0},{3,1},{4,2},{5,3},{6,4},{7,5},{8,14},{9,15},{10,... | collective-permute-start | bytes 1966088 | tf_op jit(solution)/shard_map/ppermute | solution.py:61
  63.8 9.8 %collective-permute-done = bf16[640,512]{1,0:T(8,128)(2,1)S(1)} collective-permute-done((bf16[640,512]{1,0:T(8,128)(2,1)S(1)}, bf16[640,512]{1,0:T(8,128)(2,1)S(1)}, u32[]{:S(2)}, u32[]{:S(2)}) %collective-permute-start) | collective-permute-done | bytes 655392 | tf_op jit(solution)/shard_map/ppermute | solution.py:60
  73.5 3.1 %collective-permute-done.1 = bf16[640,512]{1,0:T(8,128)(2,1)S(1)} collective-permute-done((bf16[640,512]{1,0:T(8,128)(2,1)S(1)}, bf16[640,512]{1,0:T(8,128)(2,1)S(1)}, u32[]{:S(2)}, u32[]{:S(2)}) %collective-permute-start.1) | collective-permute-done | bytes 655392 | tf_op jit(solution)/shard_map/ppermute | solution.py:61
  76.7 1.5 pad_maximum_fusion.1
  78.2 2.0 %collective-permute-start.2 = (bf16[3,640,512]{2,1,0:T(8,128)(2,1)}, bf16[3,640,512]{2,1,0:T(8,128)(2,1)}, u32[]{:S(2)}, u32[]{:S(2)}) collective-permute-start(bf16[3,640,512]{2,1,0:T(8,128)(2,1)} %pad_maximum_fusion.1), channel_id=1, source_target_pairs={{0,1},{1,0},{2,3},{3,2},{4,5},{5,4},{6,7},{7,6},{8,9},{9,8},{10,11... | collective-permute-start | bytes 5898248 | tf_op jit(solution)/shard_map/ppermute | solution.py:66
  80.4 1.6 pad_maximum_fusion
  82.0 2.2 %collective-permute-start.3 = (bf16[320,512]{1,0:T(8,128)(2,1)S(1)}, bf16[320,512]{1,0:T(8,128)(2,1)S(1)}, u32[]{:S(2)}, u32[]{:S(2)}) collective-permute-start(bf16[320,512]{1,0:T(8,128)(2,1)S(1)} %slice.35), channel_id=1, source_target_pairs={{0,2},{1,3},{2,4},{3,5},{4,6},{5,7},{6,0},{7,1},{8,10},{9,11},{10,... | collective-permute-start | bytes 983048 | tf_op jit(solution)/shard_map/ppermute | solution.py:63
  84.3 3.6 %collective-permute-start.4 = (bf16[320,512]{1,0:T(8,128)(2,1)S(1)}, bf16[320,512]{1,0:T(8,128)(2,1)S(1)}, u32[]{:S(2)}, u32[]{:S(2)}) collective-permute-start(bf16[320,512]{1,0:T(8,128)(2,1)S(1)} %slice.36), channel_id=1, source_target_pairs={{0,6},{1,7},{2,0},{3,1},{4,2},{5,3},{6,4},{7,5},{8,14},{9,15},{10,... | collective-permute-start | bytes 983048 | tf_op jit(solution)/shard_map/ppermute | solution.py:64
  88.0 6.0 %collective-permute-done.3 = bf16[320,512]{1,0:T(8,128)(2,1)S(1)} collective-permute-done((bf16[320,512]{1,0:T(8,128)(2,1)S(1)}, bf16[320,512]{1,0:T(8,128)(2,1)S(1)}, u32[]{:S(2)}, u32[]{:S(2)}) %collective-permute-start.3) | collective-permute-done | bytes 327712 | tf_op jit(solution)/shard_map/ppermute | solution.py:63
  94.0 0.7 constant_dynamic-update-slice_fusion.1
  94.7 2.5 %collective-permute-done.4 = bf16[320,512]{1,0:T(8,128)(2,1)S(1)} collective-permute-done((bf16[320,512]{1,0:T(8,128)(2,1)S(1)}, bf16[320,512]{1,0:T(8,128)(2,1)S(1)}, u32[]{:S(2)}, u32[]{:S(2)}) %collective-permute-start.4) | collective-permute-done | bytes 327712 | tf_op jit(solution)/shard_map/ppermute | solution.py:64
  97.3 0.8 constant_dynamic-update-slice_fusion
  98.0 1.9 %collective-permute-start.5 = (bf16[1,640,512]{2,1,0:T(8,128)(2,1)}, bf16[1,640,512]{2,1,0:T(8,128)(2,1)}, u32[]{:S(2)}, u32[]{:S(2)}) collective-permute-start(bf16[1,640,512]{2,1,0:T(8,128)(2,1)} %bitcast.21), channel_id=1, source_target_pairs={{0,1},{1,0},{2,3},{3,2},{4,5},{5,4},{6,7},{7,6},{8,9},{9,8},{10,11... | collective-permute-start | bytes 1966088 | tf_op jit(solution)/shard_map/ppermute | solution.py:68
  100.0 3.1 %gather_fusion.2 = bf16[3,512,256]{2,1,0:T(8,128)(2,1)} fusion(bf16[8,512,256]{2,1,0:T(8,128)(2,1)} %pad_maximum_fusion, s32[1024]{0:T(1024)S(1)} %pad_clamp_fusion.3), kind=kCustom, calls=%fused_computation.2.clone | custom fusion | bytes 1572876 | tf_op jit(solution)/shard_map/jit(_take)/gather | solution.py:170
  103.1 3.1 %gather_fusion.1 = bf16[3,512,256]{2,1,0:T(8,128)(2,1)} fusion(bf16[8,512,256]{2,1,0:T(8,128)(2,1)} %pad_maximum_fusion, s32[1024]{0:T(1024)S(1)} %pad_clamp_fusion.4), kind=kCustom, calls=%fused_computation.clone | custom fusion | bytes 1572876 | tf_op jit(solution)/shard_map/jit(_take)/gather | solution.py:170
  106.2 1.4 fusion.25
  107.6 1.5 fusion.9
  109.2 2.4 %convolution_bitcast_fusion.2 = f32[640,256]{1,0:T(8,128)S(1)} fusion(bf16[3,640,512]{2,1,0:T(8,128)(2,1)} %collective-permute-done.2, bf16[3,512,256]{2,1,0:T(8,128)(2,1)S(1)} %copy-done.12, pred[3]{0:T(512)(128)(4,1)S(1)} %get-tuple-element.39), kind=kOutput, calls=%fused_computation.16 | convolution fusion | flops 503709696 | bytes 3407875 | tf_op jit(solution)/shard_map/dot_general | solution.py:169
  111.7 0.8 fusion.4
  112.6 2.3 %collective-permute-start.6 = (bf16[640,128]{1,0:T(8,128)(2,1)S(1)}, bf16[640,128]{1,0:T(8,128)(2,1)S(1)}, u32[]{:S(2)}, u32[]{:S(2)}) collective-permute-start(bf16[640,128]{1,0:T(8,128)(2,1)S(1)} %fusion.21), channel_id=1, source_target_pairs={{0,2},{1,3},{2,4},{3,5},{4,6},{5,7},{6,0},{7,1},{8,10},{9,11},{10,... | collective-permute-start | bytes 491528 | tf_op jit(solution)/shard_map/ppermute | solution.py:29
  114.8 4.1 %collective-permute-start.7 = (bf16[640,128]{1,0:T(8,128)(2,1)S(1)}, bf16[640,128]{1,0:T(8,128)(2,1)S(1)}, u32[]{:S(2)}, u32[]{:S(2)}) collective-permute-start(bf16[640,128]{1,0:T(8,128)(2,1)S(1)} %fusion.21), channel_id=1, source_target_pairs={{0,4},{1,5},{2,6},{3,7},{4,0},{5,1},{6,2},{7,3},{8,12},{9,13},{10,... | collective-permute-start | bytes 491528 | tf_op jit(solution)/shard_map/ppermute | solution.py:29
  119.0 1.9 %collective-permute-start.8 = (bf16[640,128]{1,0:T(8,128)(2,1)S(1)}, bf16[640,128]{1,0:T(8,128)(2,1)S(1)}, u32[]{:S(2)}, u32[]{:S(2)}) collective-permute-start(bf16[640,128]{1,0:T(8,128)(2,1)S(1)} %fusion.21), channel_id=1, source_target_pairs={{0,6},{1,7},{2,0},{3,1},{4,2},{5,3},{6,4},{7,5},{8,14},{9,15},{10,... | collective-permute-start | bytes 491528 | tf_op jit(solution)/shard_map/ppermute | solution.py:29
  121.0 0.4 collective-permute-done.6
  121.5 3.1 %collective-permute-done.7 = bf16[640,128]{1,0:T(8,128)(2,1)S(1)} collective-permute-done((bf16[640,128]{1,0:T(8,128)(2,1)S(1)}, bf16[640,128]{1,0:T(8,128)(2,1)S(1)}, u32[]{:S(2)}, u32[]{:S(2)}) %collective-permute-start.7) | collective-permute-done | bytes 163872 | tf_op jit(solution)/shard_map/ppermute | solution.py:29
  124.6 3.6 %collective-permute-done.8 = bf16[640,128]{1,0:T(8,128)(2,1)S(1)} collective-permute-done((bf16[640,128]{1,0:T(8,128)(2,1)S(1)}, bf16[640,128]{1,0:T(8,128)(2,1)S(1)}, u32[]{:S(2)}, u32[]{:S(2)}) %collective-permute-start.8) | collective-permute-done | bytes 163872 | tf_op jit(solution)/shard_map/ppermute | solution.py:29
  128.1 0.7 copy-done.14
  128.9 1.9 %collective-permute-start.9 = (bf16[4,640,128]{2,1,0:T(8,128)(2,1)S(1)}, bf16[4,640,128]{2,1,0:T(8,128)(2,1)S(1)}, u32[]{:S(2)}, u32[]{:S(2)}) collective-permute-start(bf16[4,640,128]{2,1,0:T(8,128)(2,1)S(1)} %pad_maximum_fusion.2), channel_id=1, source_target_pairs={{0,1},{1,0},{2,3},{3,2},{4,5},{5,4},{6,7},{7,6},{8,9},{9,8},{10,11... | collective-permute-start | bytes 1966088 | tf_op jit(solution)/shard_map/ppermute | solution.py:32
  131.0 0.6 gather_fusion.4
  131.5 1.4 gather_fusion.3
  132.9 0.6 convolution_bitcast_fusion
  133.5 0.5 copy-done.13
  134.0 1.4 fusion.1
  135.4 7.3 %all-to-all-start.1 = ((bf16[16,40,512]{2,1,0:T(8,128)(2,1)}), bf16[16,40,512]{2,1,0:T(8,128)(2,1)S(1)}, u32[]{:S(2)}, u32[]{:S(2)}) async-start(bf16[16,40,512]{2,1,0:T(8,128)(2,1)} %bitcast.35), calls=%async_computation.1 | async-start | bytes 1310720 | tf_op jit(solution)/shard_map/all_to_all | solution.py:188
  144.5 34.1 %all-to-all-done.1 = bf16[16,40,512]{2,1,0:T(8,128)(2,1)S(1)} async-done(((bf16[16,40,512]{2,1,0:T(8,128)(2,1)}), bf16[16,40,512]{2,1,0:T(8,128)(2,1)S(1)}, u32[]{:S(2)}, u32[]{:S(2)}) %all-to-all-start.1) | async-done | bytes 655392 | tf_op jit(solution)/shard_map/all_to_all | solution.py:188
  178.6 1.2 gather_fusion
  179.8 0.9 multiply_reduce_fusion
  180.7 3.4 %collective-permute-start.10 = (bf16[128,512]{1,0:T(8,128)(2,1)S(1)}, bf16[128,512]{1,0:T(8,128)(2,1)S(1)}, u32[]{:S(2)}, u32[]{:S(2)}) collective-permute-start(bf16[128,512]{1,0:T(8,128)(2,1)S(1)} %multiply_reduce_fusion), channel_id=1, source_target_pairs={{0,128},{128,256},{256,384},{384,0},{1,129},{129,257},{257,385},{3... | collective-permute-start | bytes 393224 | tf_op jit(solution)/shard_map/ppermute | solution.py:10
  184.1 4.7 %collective-permute-done.10 = bf16[128,512]{1,0:T(8,128)(2,1)S(1)} collective-permute-done((bf16[128,512]{1,0:T(8,128)(2,1)S(1)}, bf16[128,512]{1,0:T(8,128)(2,1)S(1)}, u32[]{:S(2)}, u32[]{:S(2)}) %collective-permute-start.10) | collective-permute-done | bytes 131104 | tf_op jit(solution)/shard_map/ppermute | solution.py:10
  188.8 0.7 copy.60
  (90 shorter events, 3.6 us)
Async XLA Ops:
  0.0 130.9 %copy-start = (bf16[1,1,1024,512]{3,2,1,0:T(8,128)(2,1)S(1)}, bf16[1,1,1024,512]{3,2,1,0:T(8,128)(2,1)}, u32[]{:S(2)}) copy-start(bf16[1,1,1024,512]{3,2,1,0:T(8,128)(2,1)} %param.23) | copy-start | bytes 3145732
  0.0 6.1 %copy-start.16 = (bf16[1,128,512]{2,1,0:T(8,128)(2,1)S(1)}, bf16[1,128,512]{2,1,0:T(8,128)(2,1)}, u32[]{:S(2)}) copy-start(bf16[1,128,512]{2,1,0:T(8,128)(2,1)} %param.15) | copy-start | bytes 393220
  57.9 20.3 %copy-start.3 = (bf16[16,40,512]{2,1,0:T(8,128)(2,1)}, bf16[16,40,512]{2,1,0:T(8,128)(2,1)S(1)}, u32[]{:S(2)}) copy-start(bf16[16,40,512]{2,1,0:T(8,128)(2,1)S(1)} %all_to_all.10) | copy-start | bytes 1966084
  57.9 15.6 %collective-permute-start = (bf16[640,512]{1,0:T(8,128)(2,1)S(1)}, bf16[640,512]{1,0:T(8,128)(2,1)S(1)}, u32[]{:S(2)}, u32[]{:S(2)}) collective-permute-start(bf16[640,512]{1,0:T(8,128)(2,1)S(1)} %bitcast.75), channel_id=1, source_target_pairs={{0,2},{1,3},{2,4},{3,5},{4,6},{5,7},{6,0},{7,1},{8,10},{9,11},{10,... | collective-permute-start | bytes 1966088 | tf_op jit(solution)/shard_map/ppermute | solution.py:60
  60.0 16.6 %collective-permute-start.1 = (bf16[640,512]{1,0:T(8,128)(2,1)S(1)}, bf16[640,512]{1,0:T(8,128)(2,1)S(1)}, u32[]{:S(2)}, u32[]{:S(2)}) collective-permute-start(bf16[640,512]{1,0:T(8,128)(2,1)S(1)} %bitcast.76), channel_id=1, source_target_pairs={{0,6},{1,7},{2,0},{3,1},{4,2},{5,3},{6,4},{7,5},{8,14},{9,15},{10,... | collective-permute-start | bytes 1966088 | tf_op jit(solution)/shard_map/ppermute | solution.py:61
  73.5 4.7 %copy-start.5 = (bf16[640,512]{1,0:T(8,128)(2,1)}, bf16[640,512]{1,0:T(8,128)(2,1)S(1)}, u32[]{:S(2)}) copy-start(bf16[640,512]{1,0:T(8,128)(2,1)S(1)} %collective-permute-done) | copy-start | bytes 1966084
  76.7 1.5 copy-start.8
  76.7 3.7 %copy-start.1 = (bf16[1,1,4096,128]{3,2,1,0:T(8,128)(2,1)S(1)}, bf16[1,1,4096,128]{3,2,1,0:T(8,128)(2,1)}, u32[]{:S(2)}) copy-start(bf16[1,1,4096,128]{3,2,1,0:T(8,128)(2,1)} %param.21) | copy-start | bytes 3145732
  76.7 3.7 %copy-start.2 = (bf16[1,1,4096,128]{3,2,1,0:T(8,128)(2,1)S(1)}, bf16[1,1,4096,128]{3,2,1,0:T(8,128)(2,1)}, u32[]{:S(2)}) copy-start(bf16[1,1,4096,128]{3,2,1,0:T(8,128)(2,1)} %param.22) | copy-start | bytes 3145732
  78.2 30.9 %collective-permute-start.2 = (bf16[3,640,512]{2,1,0:T(8,128)(2,1)}, bf16[3,640,512]{2,1,0:T(8,128)(2,1)}, u32[]{:S(2)}, u32[]{:S(2)}) collective-permute-start(bf16[3,640,512]{2,1,0:T(8,128)(2,1)} %pad_maximum_fusion.1), channel_id=1, source_target_pairs={{0,1},{1,0},{2,3},{3,2},{4,5},{5,4},{6,7},{7,6},{8,9},{9,8},{10,11... | collective-permute-start | bytes 5898248 | tf_op jit(solution)/shard_map/ppermute | solution.py:66
  80.4 1.6 copy-start.6
  80.4 3.9 %copy-start.9 = (bf16[640,512]{1,0:T(8,128)(2,1)S(1)}, bf16[640,512]{1,0:T(8,128)(2,1)}, u32[]{:S(2)}) copy-start(bf16[640,512]{1,0:T(8,128)(2,1)} %copy-done.8) | copy-start | bytes 1966084
  82.0 12.0 %collective-permute-start.3 = (bf16[320,512]{1,0:T(8,128)(2,1)S(1)}, bf16[320,512]{1,0:T(8,128)(2,1)S(1)}, u32[]{:S(2)}, u32[]{:S(2)}) collective-permute-start(bf16[320,512]{1,0:T(8,128)(2,1)S(1)} %slice.35), channel_id=1, source_target_pairs={{0,2},{1,3},{2,4},{3,5},{4,6},{5,7},{6,0},{7,1},{8,10},{9,11},{10,... | collective-permute-start | bytes 983048 | tf_op jit(solution)/shard_map/ppermute | solution.py:63
  84.3 12.9 %collective-permute-start.4 = (bf16[320,512]{1,0:T(8,128)(2,1)S(1)}, bf16[320,512]{1,0:T(8,128)(2,1)S(1)}, u32[]{:S(2)}, u32[]{:S(2)}) collective-permute-start(bf16[320,512]{1,0:T(8,128)(2,1)S(1)} %slice.36), channel_id=1, source_target_pairs={{0,6},{1,7},{2,0},{3,1},{4,2},{5,3},{6,4},{7,5},{8,14},{9,15},{10,... | collective-permute-start | bytes 983048 | tf_op jit(solution)/shard_map/ppermute | solution.py:64
  98.0 9.6 %collective-permute-start.5 = (bf16[1,640,512]{2,1,0:T(8,128)(2,1)}, bf16[1,640,512]{2,1,0:T(8,128)(2,1)}, u32[]{:S(2)}, u32[]{:S(2)}) collective-permute-start(bf16[1,640,512]{2,1,0:T(8,128)(2,1)} %bitcast.21), channel_id=1, source_target_pairs={{0,1},{1,0},{2,3},{3,2},{4,5},{5,4},{6,7},{7,6},{8,9},{9,8},{10,11... | collective-permute-start | bytes 1966088 | tf_op jit(solution)/shard_map/ppermute | solution.py:68
  107.6 1.5 copy-start.12
  109.2 2.5 %copy-start.4 = (bf16[16,40,512]{2,1,0:T(8,128)(2,1)S(1)}, bf16[16,40,512]{2,1,0:T(8,128)(2,1)}, u32[]{:S(2)}) copy-start(bf16[16,40,512]{2,1,0:T(8,128)(2,1)} %copy-done.3) | copy-start | bytes 1966084
  109.2 2.5 %copy-start.7 = (bf16[640,512]{1,0:T(8,128)(2,1)S(1)}, bf16[640,512]{1,0:T(8,128)(2,1)}, u32[]{:S(2)}) copy-start(bf16[640,512]{1,0:T(8,128)(2,1)} %copy-done.5) | copy-start | bytes 1966084
  109.2 2.5 %copy-start.10 = (bf16[640,512]{1,0:T(8,128)(2,1)S(1)}, bf16[640,512]{1,0:T(8,128)(2,1)}, u32[]{:S(2)}) copy-start(bf16[640,512]{1,0:T(8,128)(2,1)} %copy-done.8) | copy-start | bytes 1966084
  109.2 2.5 %copy-start.11 = (bf16[3,512,256]{2,1,0:T(8,128)(2,1)S(1)}, bf16[3,512,256]{2,1,0:T(8,128)(2,1)}, u32[]{:S(2)}) copy-start(bf16[3,512,256]{2,1,0:T(8,128)(2,1)} %gather_fusion.1) | copy-start | bytes 2359300
  112.6 8.9 %collective-permute-start.6 = (bf16[640,128]{1,0:T(8,128)(2,1)S(1)}, bf16[640,128]{1,0:T(8,128)(2,1)S(1)}, u32[]{:S(2)}, u32[]{:S(2)}) collective-permute-start(bf16[640,128]{1,0:T(8,128)(2,1)S(1)} %fusion.21), channel_id=1, source_target_pairs={{0,2},{1,3},{2,4},{3,5},{4,6},{5,7},{6,0},{7,1},{8,10},{9,11},{10,... | collective-permute-start | bytes 491528 | tf_op jit(solution)/shard_map/ppermute | solution.py:29
  114.8 9.7 %collective-permute-start.7 = (bf16[640,128]{1,0:T(8,128)(2,1)S(1)}, bf16[640,128]{1,0:T(8,128)(2,1)S(1)}, u32[]{:S(2)}, u32[]{:S(2)}) collective-permute-start(bf16[640,128]{1,0:T(8,128)(2,1)S(1)} %fusion.21), channel_id=1, source_target_pairs={{0,4},{1,5},{2,6},{3,7},{4,0},{5,1},{6,2},{7,3},{8,12},{9,13},{10,... | collective-permute-start | bytes 491528 | tf_op jit(solution)/shard_map/ppermute | solution.py:29
  119.0 9.2 %collective-permute-start.8 = (bf16[640,128]{1,0:T(8,128)(2,1)S(1)}, bf16[640,128]{1,0:T(8,128)(2,1)S(1)}, u32[]{:S(2)}, u32[]{:S(2)}) collective-permute-start(bf16[640,128]{1,0:T(8,128)(2,1)S(1)} %fusion.21), channel_id=1, source_target_pairs={{0,6},{1,7},{2,0},{3,1},{4,2},{5,3},{6,4},{7,5},{8,14},{9,15},{10,... | collective-permute-start | bytes 491528 | tf_op jit(solution)/shard_map/ppermute | solution.py:29
  128.1 0.7 copy-start.14
  128.9 4.0 %collective-permute-start.9 = (bf16[4,640,128]{2,1,0:T(8,128)(2,1)S(1)}, bf16[4,640,128]{2,1,0:T(8,128)(2,1)S(1)}, u32[]{:S(2)}, u32[]{:S(2)}) collective-permute-start(bf16[4,640,128]{2,1,0:T(8,128)(2,1)S(1)} %pad_maximum_fusion.2), channel_id=1, source_target_pairs={{0,1},{1,0},{2,3},{3,2},{4,5},{5,4},{6,7},{7,6},{8,9},{9,8},{10,11... | collective-permute-start | bytes 1966088 | tf_op jit(solution)/shard_map/ppermute | solution.py:32
  132.9 1.0 copy-start.13
  132.9 1.1 copy-start.15
  134.0 8.7 %copy-start.17 = (s32[1,128,2]{1,2,0:T(2,128)S(1)}, s32[1,128,2]{1,2,0:T(2,128)}, u32[]{:S(2)}) copy-start(s32[1,128,2]{1,2,0:T(2,128)} %param.16) | copy-start | bytes 3076
  134.0 8.9 %copy-start.18 = (s32[1,16]{1,0:T(1,128)S(1)}, s32[1,16]{1,0:T(1,128)}, u32[]{:S(2)}) copy-start(s32[1,16]{1,0:T(1,128)} %param.20) | copy-start | bytes 196
  135.4 9.0 %copy-start.19 = (f32[1,128,2]{1,2,0:T(2,128)S(1)}, f32[1,128,2]{1,2,0:T(2,128)}, u32[]{:S(2)}) copy-start(f32[1,128,2]{1,2,0:T(2,128)} %param.17) | copy-start | bytes 3076
  135.4 43.2 %all-to-all-start.1 = ((bf16[16,40,512]{2,1,0:T(8,128)(2,1)}), bf16[16,40,512]{2,1,0:T(8,128)(2,1)S(1)}, u32[]{:S(2)}, u32[]{:S(2)}) async-start(bf16[16,40,512]{2,1,0:T(8,128)(2,1)} %bitcast.35), calls=%async_computation.1 | async-start | bytes 1310720 | tf_op jit(solution)/shard_map/all_to_all | solution.py:188
  180.7 8.1 %collective-permute-start.10 = (bf16[128,512]{1,0:T(8,128)(2,1)S(1)}, bf16[128,512]{1,0:T(8,128)(2,1)S(1)}, u32[]{:S(2)}, u32[]{:S(2)}) collective-permute-start(bf16[128,512]{1,0:T(8,128)(2,1)S(1)} %multiply_reduce_fusion), channel_id=1, source_target_pairs={{0,128},{128,256},{256,384},{384,0},{1,129},{129,257},{257,385},{3... | collective-permute-start | bytes 393224 | tf_op jit(solution)/shard_map/ppermute | solution.py:10

commit v12 on v10

--- a/solution.py
+++ b/solution.py
@@ -34,21 +34,21 @@
     return bundle, swapped, origins, origins ^ 1
 
 
-def relayed_chips_then_core(value, axis):
+def relayed_chips_then_core(value, axis, riders):
     count = lax.axis_size(axis)
     me = lax.axis_index(axis)
     up_pairs = [(source, (source + 2) % count) for source in range(count)]
     down_pairs = [(source, (source - 2) % count) for source in range(count)]
     from_below = lax.ppermute(value, axis, up_pairs)
     from_above = lax.ppermute(value, axis, down_pairs)
+    from_below, from_above, riders = lax.optimization_barrier((from_below, from_above, riders))
     half = value.shape[0] // 2
     far_low = lax.ppermute(from_below[:half], axis, up_pairs)
     far_high = lax.ppermute(from_above[half:], axis, down_pairs)
     far = jnp.concatenate([far_low, far_high], axis=0)
     bundle = jnp.stack([value, from_below, from_above, far])
     swapped = lax.ppermute(bundle, axis, [(source, source ^ 1) for source in range(count)])
-    origins = jnp.stack([me, (me - 2) % count, (me + 2) % count, (me + 4) % count])
-    return bundle, swapped, origins, origins ^ 1
+    return bundle, swapped, riders
 
 
 def paired_gather(value, axis):
@@ -132,32 +132,34 @@
     ).astype(rows_local.dtype)
     arrived = lax.all_to_all(outgoing, "expert", split_axis=0, concat_axis=0, tiled=True)
     flattened = arrived.reshape(-1, feat_width)
-    own_feats, partner_feats, own_from, partner_from = relayed_chips_then_core(flattened, "rep")
+    me_rep = lax.axis_index("rep")
+    rows_from = jnp.stack([me_rep, (me_rep - 2) % reps, (me_rep + 2) % reps, (me_rep + 4) % reps])
+    act_from = (me_rep - 2 * jnp.arange(reps // 2, dtype=jnp.int32)) % reps
     hidden = w_gate.shape[3]
     gate_up = jnp.concatenate(
         [w_gate[0, 0].reshape(reps, feat_width, -1), w_up[0, 0].reshape(reps, feat_width, -1)],
         axis=2,
     )
+    down_all = w_down[0, 0].reshape(reps, hidden, -1)
+    riders = (
+        jnp.take(gate_up, rows_from, axis=0),
+        jnp.take(gate_up, rows_from ^ 1, axis=0),
+        jnp.take(down_all, act_from, axis=0),
+        jnp.take(down_all, act_from ^ 1, axis=0),
+    )
+    own_feats, partner_feats, riders = relayed_chips_then_core(flattened, "rep", riders)
+    gu_own, gu_partner, down_own, down_partner = riders
     dims = (((0, 2), (0, 1)), ((), ()))
     both = lax.dot_general(
-        own_feats, jnp.take(gate_up, own_from, axis=0), dims,
-        preferred_element_type=jnp.float32,
-    ) + lax.dot_general(
-        partner_feats, jnp.take(gate_up, partner_from, axis=0), dims,
-        preferred_element_type=jnp.float32,
-    )
+        own_feats, gu_own, dims, preferred_element_type=jnp.float32
+    ) + lax.dot_general(partner_feats, gu_partner, dims, preferred_element_type=jnp.float32)
     gate_proj = both[:, :hidden]
     up_proj = both[:, hidden:]
     activated = (jax.nn.silu(gate_proj) * up_proj).astype(jnp.bfloat16)
-    own_act, partner_act, act_own_from, act_partner_from = chips_then_core(activated, "rep")
-    down_all = w_down[0, 0].reshape(reps, activated.shape[1], -1)
+    own_act, partner_act, _, _ = chips_then_core(activated, "rep")
     produced = lax.dot_general(
-        own_act, jnp.take(down_all, act_own_from, axis=0), dims,
-        preferred_element_type=jnp.float32,
-    ) + lax.dot_general(
-        partner_act, jnp.take(down_all, act_partner_from, axis=0), dims,
-        preferred_element_type=jnp.float32,
-    )
+        own_act, down_own, dims, preferred_element_type=jnp.float32
+    ) + lax.dot_general(partner_act, down_partner, dims, preferred_element_type=jnp.float32)
     down_w = down_all
     out_width = down_w.shape[2]
     produced = produced.astype(jnp.bfloat16).reshape(experts, 2 * slot_depth, out_width)

time: 180 us -> 182 us (1.011)
  blocking collectives: 51.4 us -> 0 us
  waiting for transfers between devices: 63.7 us -> 90.4 us
  starting transfers between devices: 35.2 us -> 56.4 us
  other arithmetic: 10.7 us -> 14 us
  local copies, waits for them, and re-layouts: 9.28 us -> 12 us
    all_to_all x1 -> x0, blocking collectives: 51.4 us -> none  [local(): lax.all_to_all(outgoing, 'expert', split_axis=0, concat_axis=0, tiled=True)]
    all_to_all x0 -> x1, waiting for transfers between devices: none -> 25 us  [local(): lax.all_to_all(outgoing, 'expert', split_axis=0, concat_axis=0, tiled=True)]
    all_to_all x0 -> x1, starting transfers between devices: none -> 15.2 us  [local(): lax.all_to_all(outgoing, 'expert', split_axis=0, concat_axis=0, tiled=True)]
    all_to_all x1, starting transfers between devices: 8.51 us -> 13.8 us  [local(): lax.all_to_all(produced, 'expert', split_axis=0, concat_axis=0, tiled=True)]
    ppermute x1, waiting for transfers between devices: 0.01 us -> 4.88 us  [relayed_chips_then_core(): lax.ppermute(bundle, axis, [(source, source ^ 1) for source in range(coun...]
    ppermute x1, waiting for transfers between devices: 9.78 us -> 4.9 us  [relayed_chips_then_core(): from_below = lax.ppermute(value, axis, up_pairs)]
    select_n x2 -> x5, other arithmetic: 0.01 us -> 3.37 us  [the longest x2 1.96 us: local(): jnp.take(down_all, act_from ^ 1, axis=0)]
    ppermute x1, waiting for transfers between devices: 0.01 us -> 3.14 us  [relayed_chips_then_core(): from_above = lax.ppermute(value, axis, down_pairs)]
  transfers between devices with their start and end apart: 11 -> 12, of which waited for: 8 -> 12; matrix products, arithmetic and copies ran while one was open for 5% -> 8% of each run, Pallas kernels for 0% -> 0%
where the time goes in v12:
time: 182 us; the launch traced here: 180 us
  waiting for transfers between devices  90.4 us (50%)
  starting transfers between devices  56.4 us (31%)
  other arithmetic  14 us (8%)
  local copies, waits for them, and re-layouts  12 us (7%)
  matrix products  7.17 us (4%)
    all_to_all x1, waiting for transfers between devices, local(): lax.all_to_all(produced, 'expert', split_axis=0, concat_axis=0, tiled=True)  32.4 us
    all_to_all x1, waiting for transfers between devices, local(): lax.all_to_all(outgoing, 'expert', split_axis=0, concat_axis=0, tiled=True)  25 us
    all_to_all x1, starting transfers between devices, local(): lax.all_to_all(outgoing, 'expert', split_axis=0, concat_axis=0, tiled=True)  15.2 us
    all_to_all x1, starting transfers between devices, local(): lax.all_to_all(produced, 'expert', split_axis=0, concat_axis=0, tiled=True)  13.8 us
    ppermute x3, starting transfers between devices, chips_then_core(): pieces.append(lax.ppermute(value, axis, pairs))  8.45 us
    ppermute x3, waiting for transfers between devices, chips_then_core(): pieces.append(lax.ppermute(value, axis, pairs))  6.75 us
    ppermute x1, waiting for transfers between devices, relayed_chips_then_core(): from_below = lax.ppermute(value, axis, up_pairs)  4.9 us
    ppermute x1, waiting for transfers between devices, relayed_chips_then_core(): lax.ppermute(bundle, axis, [(source, source ^ 1) for source in range(coun...  4.88 us
  transfers between devices with their start and end apart: 12, of which 12 were waited for; matrix products, arithmetic and copies ran while one was open for 8% of the time, Pallas kernels for 0%

profile of v12, /device:TPU:24, one launch (start us, length us, event | category | flops | bytes accessed | tf_op | source)
XLA Modules:
  0.0 180.3 jit_solution(1892089694960772158)
XLA Ops:
  0.0 0.8 convert_reduce_fusion
  0.9 0.7 fusion.14
  1.6 1.2 multiply_reduce_fusion.1
  3.4 0.7 fusion.15
  4.2 0.7 select_reduce_fusion
  5.1 0.8 select_reduce_fusion.1
  6.1 2.1 %convolution_convert_fusion = bf16[16,40,512]{2,1,0:T(8,128)(2,1)} fusion(s32[16,40]{1,0:T(8,128)S(1)} %pad_add_fusion, bf16[1,128,512]{2,1,0:T(8,128)(2,1)} %param.13), kind=kOutput, calls=%fused_computation.10 | convolution fusion | flops 84295680 | bytes 788992 | tf_op jit(solution)/shard_map/xjt,tf->xjf/dot_general | solution.py:130
  8.2 15.2 %all-to-all-start = ((bf16[16,40,512]{2,1,0:T(8,128)(2,1)}), bf16[16,40,512]{2,1,0:T(8,128)(2,1)}, u32[]{:S(2)}, u32[]{:S(2)}) async-start(bf16[16,40,512]{2,1,0:T(8,128)(2,1)} %convolution_convert_fusion), calls=%async_computation | async-start | bytes 1310720 | tf_op jit(solution)/shard_map/all_to_all | solution.py:133
  23.6 1.8 pad_maximum_fusion.1
  25.4 1.6 gather_fusion.1
  27.1 1.6 gather_fusion.2
  28.7 1.4 gather_fusion.4
  30.1 1.9 %broadcast_select_fusion.2 = bf16[4,128,512]{2,1,0:T(8,128)(2,1)} fusion(bf16[4,128,512]{2,1,0:T(8,128)(2,1)} %gather_fusion.4, pred[4]{0:T(512)(128)(4,1)S(1)} %get-tuple-element.42), kind=kLoop, calls=%fused_computation.20 | loop fusion | flops 262144 | bytes 1048580 | tf_op jit(solution)/shard_map/jit(_take)/select_n | solution.py:148
  32.1 25.0 %all-to-all-done = bf16[16,40,512]{2,1,0:T(8,128)(2,1)} async-done(((bf16[16,40,512]{2,1,0:T(8,128)(2,1)}), bf16[16,40,512]{2,1,0:T(8,128)(2,1)}, u32[]{:S(2)}, u32[]{:S(2)}) %all-to-all-start) | async-done | bytes 655392 | tf_op jit(solution)/shard_map/all_to_all | solution.py:133
  57.1 2.1 %collective-permute-start = (bf16[640,512]{1,0:T(8,128)(2,1)}, bf16[640,512]{1,0:T(8,128)(2,1)}, u32[]{:S(2)}, u32[]{:S(2)}) collective-permute-start(bf16[640,512]{1,0:T(8,128)(2,1)} %bitcast.7), channel_id=1, source_target_pairs={{0,2},{1,3},{2,4},{3,5},{4,6},{5,7},{6,0},{7,1},{8,10},{9,11},{10,... | collective-permute-start | bytes 1966088 | tf_op jit(solution)/shard_map/ppermute | solution.py:42
  59.2 3.7 %collective-permute-start.1 = (bf16[640,512]{1,0:T(8,128)(2,1)}, bf16[640,512]{1,0:T(8,128)(2,1)}, u32[]{:S(2)}, u32[]{:S(2)}) collective-permute-start(bf16[640,512]{1,0:T(8,128)(2,1)} %bitcast.7), channel_id=1, source_target_pairs={{0,6},{1,7},{2,0},{3,1},{4,2},{5,3},{6,4},{7,5},{8,14},{9,15},{10,... | collective-permute-start | bytes 1966088 | tf_op jit(solution)/shard_map/ppermute | solution.py:43
  62.9 1.4 gather_fusion.3
  64.3 1.2 broadcast_select_fusion.3
  65.8 4.9 %collective-permute-done = bf16[640,512]{1,0:T(8,128)(2,1)} collective-permute-done((bf16[640,512]{1,0:T(8,128)(2,1)}, bf16[640,512]{1,0:T(8,128)(2,1)}, u32[]{:S(2)}, u32[]{:S(2)}) %collective-permute-start) | collective-permute-done | bytes 655392 | tf_op jit(solution)/shard_map/ppermute | solution.py:42
  70.7 3.1 %collective-permute-done.1 = bf16[640,512]{1,0:T(8,128)(2,1)} collective-permute-done((bf16[640,512]{1,0:T(8,128)(2,1)}, bf16[640,512]{1,0:T(8,128)(2,1)}, u32[]{:S(2)}, u32[]{:S(2)}) %collective-permute-start.1) | collective-permute-done | bytes 655392 | tf_op jit(solution)/shard_map/ppermute | solution.py:43
  73.8 1.0 slice.12
  74.8 2.2 %collective-permute-start.2 = (bf16[320,512]{1,0:T(8,128)(2,1)S(1)}, bf16[320,512]{1,0:T(8,128)(2,1)S(1)}, u32[]{:S(2)}, u32[]{:S(2)}) collective-permute-start(bf16[320,512]{1,0:T(8,128)(2,1)S(1)} %slice.12), channel_id=1, source_target_pairs={{0,2},{1,3},{2,4},{3,5},{4,6},{5,7},{6,0},{7,1},{8,10},{9,11},{10,... | collective-permute-start | bytes 983048 | tf_op jit(solution)/shard_map/ppermute | solution.py:46
  77.0 1.0 slice.13
  78.0 3.6 %collective-permute-start.3 = (bf16[320,512]{1,0:T(8,128)(2,1)S(1)}, bf16[320,512]{1,0:T(8,128)(2,1)S(1)}, u32[]{:S(2)}, u32[]{:S(2)}) collective-permute-start(bf16[320,512]{1,0:T(8,128)(2,1)S(1)} %slice.13), channel_id=1, source_target_pairs={{0,6},{1,7},{2,0},{3,1},{4,2},{5,3},{6,4},{7,5},{8,14},{9,15},{10,... | collective-permute-start | bytes 983048 | tf_op jit(solution)/shard_map/ppermute | solution.py:47
  81.7 2.1 %collective-permute-done.2 = bf16[320,512]{1,0:T(8,128)(2,1)S(1)} collective-permute-done((bf16[320,512]{1,0:T(8,128)(2,1)S(1)}, bf16[320,512]{1,0:T(8,128)(2,1)S(1)}, u32[]{:S(2)}, u32[]{:S(2)}) %collective-permute-start.2) | collective-permute-done | bytes 327712 | tf_op jit(solution)/shard_map/ppermute | solution.py:46
  83.8 4.4 %collective-permute-done.3 = bf16[320,512]{1,0:T(8,128)(2,1)S(1)} collective-permute-done((bf16[320,512]{1,0:T(8,128)(2,1)S(1)}, bf16[320,512]{1,0:T(8,128)(2,1)S(1)}, u32[]{:S(2)}, u32[]{:S(2)}) %collective-permute-start.3) | collective-permute-done | bytes 327712 | tf_op jit(solution)/shard_map/ppermute | solution.py:47
  88.2 1.8 %pad_maximum_fusion = bf16[4,640,512]{2,1,0:T(8,128)(2,1)S(1)} fusion(bf16[1,640,512]{2,1,0:T(8,128)(2,1)S(1)} %maximum_bitcast_fusion, bf16[1,640,512]{2,1,0:T(8,128)(2,1)} %bitcast.16, bf16[1,640,512]{2,1,0:T(8,128)(2,1)} %bitcast.15, bf16[1,640,512]{2,1,0:T(8,128)(2,1)} %bitcast.6), kind=kLoop, calls=%fused_computation.5 | loop fusion | flops 3932160 | bytes 5242880 | tf_op jit(solution)/shard_map/stack | solution.py:49
  90.1 1.9 %collective-permute-start.4 = (bf16[4,640,512]{2,1,0:T(8,128)(2,1)S(1)}, bf16[4,640,512]{2,1,0:T(8,128)(2,1)S(1)}, u32[]{:S(2)}, u32[]{:S(2)}) collective-permute-start(bf16[4,640,512]{2,1,0:T(8,128)(2,1)S(1)} %pad_maximum_fusion), channel_id=1, source_target_pairs={{0,1},{1,0},{2,3},{3,2},{4,5},{5,4},{6,7},{7,6},{8,9},{9,8},{10,11... | collective-permute-start | bytes 7864328 | tf_op jit(solution)/shard_map/ppermute | solution.py:50
  92.0 4.9 %collective-permute-done.4 = bf16[4,640,512]{2,1,0:T(8,128)(2,1)S(1)} collective-permute-done((bf16[4,640,512]{2,1,0:T(8,128)(2,1)S(1)}, bf16[4,640,512]{2,1,0:T(8,128)(2,1)S(1)}, u32[]{:S(2)}, u32[]{:S(2)}) %collective-permute-start.4) | collective-permute-done | bytes 2621472 | tf_op jit(solution)/shard_map/ppermute | solution.py:50
  96.9 0.8 convolution_bitcast_fusion.2
  97.7 2.3 %fusion.2 = f32[640,256]{1,0:T(8,128)S(1)} fusion(f32[640,256]{1,0:T(8,128)S(1)} %convolution_bitcast_fusion.2, bf16[4,512,256]{2,1,0:T(8,128)(2,1)S(1)} %get-tuple-element.15, bf16[1,640,512]{2,1,0:T(8,128)(2,1)S(1)} %maximum_bitcast_fusion, bf16[1,640,512]{2,1,0:T(8,128)(2,1)} %bitcast.16, bf16[1,640,512]{2,1,0:T(8,128)(2,1)} %bitcast.15, ...), kind=kOutput, calls=%fused_computation.14 | convolution fusion | flops 675184640 | bytes 4980736 | tf_op jit(solution)/shard_map/dot_general | solution.py:153
  100.2 2.4 %collective-permute-start.5 = (bf16[640,128]{1,0:T(8,128)(2,1)S(1)}, bf16[640,128]{1,0:T(8,128)(2,1)S(1)}, u32[]{:S(2)}, u32[]{:S(2)}) collective-permute-start(bf16[640,128]{1,0:T(8,128)(2,1)S(1)} %fusion.7), channel_id=1, source_target_pairs={{0,2},{1,3},{2,4},{3,5},{4,6},{5,7},{6,0},{7,1},{8,10},{9,11},{10,... | collective-permute-start | bytes 491528 | tf_op jit(solution)/shard_map/ppermute | solution.py:29
  102.6 4.1 %collective-permute-start.6 = (bf16[640,128]{1,0:T(8,128)(2,1)S(1)}, bf16[640,128]{1,0:T(8,128)(2,1)S(1)}, u32[]{:S(2)}, u32[]{:S(2)}) collective-permute-start(bf16[640,128]{1,0:T(8,128)(2,1)S(1)} %fusion.7), channel_id=1, source_target_pairs={{0,4},{1,5},{2,6},{3,7},{4,0},{5,1},{6,2},{7,3},{8,12},{9,13},{10,... | collective-permute-start | bytes 491528 | tf_op jit(solution)/shard_map/ppermute | solution.py:29
  106.7 1.9 %collective-permute-start.7 = (bf16[640,128]{1,0:T(8,128)(2,1)S(1)}, bf16[640,128]{1,0:T(8,128)(2,1)S(1)}, u32[]{:S(2)}, u32[]{:S(2)}) collective-permute-start(bf16[640,128]{1,0:T(8,128)(2,1)S(1)} %fusion.7), channel_id=1, source_target_pairs={{0,6},{1,7},{2,0},{3,1},{4,2},{5,3},{6,4},{7,5},{8,14},{9,15},{10,... | collective-permute-start | bytes 491528 | tf_op jit(solution)/shard_map/ppermute | solution.py:29
  108.8 0.5 collective-permute-done.5
  109.2 2.7 %collective-permute-done.6 = bf16[640,128]{1,0:T(8,128)(2,1)S(1)} collective-permute-done((bf16[640,128]{1,0:T(8,128)(2,1)S(1)}, bf16[640,128]{1,0:T(8,128)(2,1)S(1)}, u32[]{:S(2)}, u32[]{:S(2)}) %collective-permute-start.6) | collective-permute-done | bytes 163872 | tf_op jit(solution)/shard_map/ppermute | solution.py:29
  111.9 3.6 %collective-permute-done.7 = bf16[640,128]{1,0:T(8,128)(2,1)S(1)} collective-permute-done((bf16[640,128]{1,0:T(8,128)(2,1)S(1)}, bf16[640,128]{1,0:T(8,128)(2,1)S(1)}, u32[]{:S(2)}, u32[]{:S(2)}) %collective-permute-start.7) | collective-permute-done | bytes 163872 | tf_op jit(solution)/shard_map/ppermute | solution.py:29
  115.6 1.9 %collective-permute-start.8 = (bf16[4,640,128]{2,1,0:T(8,128)(2,1)S(1)}, bf16[4,640,128]{2,1,0:T(8,128)(2,1)S(1)}, u32[]{:S(2)}, u32[]{:S(2)}) collective-permute-start(bf16[4,640,128]{2,1,0:T(8,128)(2,1)S(1)} %pad_maximum_fusion.2), channel_id=1, source_target_pairs={{0,1},{1,0},{2,3},{3,2},{4,5},{5,4},{6,7},{7,6},{8,9},{9,8},{10,11... | collective-permute-start | bytes 1966088 | tf_op jit(solution)/shard_map/ppermute | solution.py:32
  117.5 2.1 %collective-permute-done.8 = bf16[4,640,128]{2,1,0:T(8,128)(2,1)S(1)} collective-permute-done((bf16[4,640,128]{2,1,0:T(8,128)(2,1)S(1)}, bf16[4,640,128]{2,1,0:T(8,128)(2,1)S(1)}, u32[]{:S(2)}, u32[]{:S(2)}) %collective-permute-start.8) | collective-permute-done | bytes 655392 | tf_op jit(solution)/shard_map/ppermute | solution.py:32
  119.6 0.5 convolution_bitcast_fusion
  120.1 1.3 fusion.1
  121.5 13.8 %all-to-all-start.1 = ((bf16[16,40,512]{2,1,0:T(8,128)(2,1)}), bf16[16,40,512]{2,1,0:T(8,128)(2,1)S(1)}, u32[]{:S(2)}, u32[]{:S(2)}) async-start(bf16[16,40,512]{2,1,0:T(8,128)(2,1)} %bitcast.26), calls=%async_computation.1 | async-start | bytes 1310720 | tf_op jit(solution)/shard_map/all_to_all | solution.py:166
  137.0 32.4 %all-to-all-done.1 = bf16[16,40,512]{2,1,0:T(8,128)(2,1)S(1)} async-done(((bf16[16,40,512]{2,1,0:T(8,128)(2,1)}), bf16[16,40,512]{2,1,0:T(8,128)(2,1)S(1)}, u32[]{:S(2)}, u32[]{:S(2)}) %all-to-all-start.1) | async-done | bytes 655392 | tf_op jit(solution)/shard_map/all_to_all | solution.py:166
  169.5 1.2 gather_fusion
  170.7 0.9 multiply_reduce_fusion
  171.6 3.4 %collective-permute-start.9 = (bf16[128,512]{1,0:T(8,128)(2,1)S(1)}, bf16[128,512]{1,0:T(8,128)(2,1)S(1)}, u32[]{:S(2)}, u32[]{:S(2)}) collective-permute-start(bf16[128,512]{1,0:T(8,128)(2,1)S(1)} %multiply_reduce_fusion), channel_id=1, source_target_pairs={{0,128},{128,256},{256,384},{384,0},{1,129},{129,257},{257,385},{3... | collective-permute-start | bytes 393224 | tf_op jit(solution)/shard_map/ppermute | solution.py:10
  175.0 4.7 %collective-permute-done.9 = bf16[128,512]{1,0:T(8,128)(2,1)S(1)} collective-permute-done((bf16[128,512]{1,0:T(8,128)(2,1)S(1)}, bf16[128,512]{1,0:T(8,128)(2,1)S(1)}, u32[]{:S(2)}, u32[]{:S(2)}) %collective-permute-start.9) | collective-permute-done | bytes 131104 | tf_op jit(solution)/shard_map/ppermute | solution.py:10
  179.7 0.7 copy.59
  (63 shorter events, 3.7 us)
Async XLA Ops:
  0.0 28.7 %copy-start = (bf16[1,1,1024,512]{3,2,1,0:T(8,128)(2,1)S(1)}, bf16[1,1,1024,512]{3,2,1,0:T(8,128)(2,1)}, u32[]{:S(2)}) copy-start(bf16[1,1,1024,512]{3,2,1,0:T(8,128)(2,1)} %param.21) | copy-start | bytes 3145732
  8.2 48.8 %all-to-all-start = ((bf16[16,40,512]{2,1,0:T(8,128)(2,1)}), bf16[16,40,512]{2,1,0:T(8,128)(2,1)}, u32[]{:S(2)}, u32[]{:S(2)}) async-start(bf16[16,40,512]{2,1,0:T(8,128)(2,1)} %convolution_convert_fusion), calls=%async_computation | async-start | bytes 1310720 | tf_op jit(solution)/shard_map/all_to_all | solution.py:133
  28.7 36.8 %copy-start.1 = (bf16[4,512,256]{2,1,0:T(8,128)(2,1)S(1)}, bf16[4,512,256]{2,1,0:T(8,128)(2,1)}, u32[]{:S(2)}) copy-start(bf16[4,512,256]{2,1,0:T(8,128)(2,1)} %gather_fusion.1) | copy-start | bytes 3145732
  28.7 36.8 %copy-start.2 = (bf16[4,512,256]{2,1,0:T(8,128)(2,1)S(1)}, bf16[4,512,256]{2,1,0:T(8,128)(2,1)}, u32[]{:S(2)}) copy-start(bf16[4,512,256]{2,1,0:T(8,128)(2,1)} %gather_fusion.2) | copy-start | bytes 3145732
  57.1 13.6 %collective-permute-start = (bf16[640,512]{1,0:T(8,128)(2,1)}, bf16[640,512]{1,0:T(8,128)(2,1)}, u32[]{:S(2)}, u32[]{:S(2)}) collective-permute-start(bf16[640,512]{1,0:T(8,128)(2,1)} %bitcast.7), channel_id=1, source_target_pairs={{0,2},{1,3},{2,4},{3,5},{4,6},{5,7},{6,0},{7,1},{8,10},{9,11},{10,... | collective-permute-start | bytes 1966088 | tf_op jit(solution)/shard_map/ppermute | solution.py:42
  59.2 14.6 %collective-permute-start.1 = (bf16[640,512]{1,0:T(8,128)(2,1)}, bf16[640,512]{1,0:T(8,128)(2,1)}, u32[]{:S(2)}, u32[]{:S(2)}) collective-permute-start(bf16[640,512]{1,0:T(8,128)(2,1)} %bitcast.7), channel_id=1, source_target_pairs={{0,6},{1,7},{2,0},{3,1},{4,2},{5,3},{6,4},{7,5},{8,14},{9,15},{10,... | collective-permute-start | bytes 1966088 | tf_op jit(solution)/shard_map/ppermute | solution.py:43
  74.8 9.0 %collective-permute-start.2 = (bf16[320,512]{1,0:T(8,128)(2,1)S(1)}, bf16[320,512]{1,0:T(8,128)(2,1)S(1)}, u32[]{:S(2)}, u32[]{:S(2)}) collective-permute-start(bf16[320,512]{1,0:T(8,128)(2,1)S(1)} %slice.12), channel_id=1, source_target_pairs={{0,2},{1,3},{2,4},{3,5},{4,6},{5,7},{6,0},{7,1},{8,10},{9,11},{10,... | collective-permute-start | bytes 983048 | tf_op jit(solution)/shard_map/ppermute | solution.py:46
  78.0 10.2 %collective-permute-start.3 = (bf16[320,512]{1,0:T(8,128)(2,1)S(1)}, bf16[320,512]{1,0:T(8,128)(2,1)S(1)}, u32[]{:S(2)}, u32[]{:S(2)}) collective-permute-start(bf16[320,512]{1,0:T(8,128)(2,1)S(1)} %slice.13), channel_id=1, source_target_pairs={{0,6},{1,7},{2,0},{3,1},{4,2},{5,3},{6,4},{7,5},{8,14},{9,15},{10,... | collective-permute-start | bytes 983048 | tf_op jit(solution)/shard_map/ppermute | solution.py:47
  90.1 6.8 %collective-permute-start.4 = (bf16[4,640,512]{2,1,0:T(8,128)(2,1)S(1)}, bf16[4,640,512]{2,1,0:T(8,128)(2,1)S(1)}, u32[]{:S(2)}, u32[]{:S(2)}) collective-permute-start(bf16[4,640,512]{2,1,0:T(8,128)(2,1)S(1)} %pad_maximum_fusion), channel_id=1, source_target_pairs={{0,1},{1,0},{2,3},{3,2},{4,5},{5,4},{6,7},{7,6},{8,9},{9,8},{10,11... | collective-permute-start | bytes 7864328 | tf_op jit(solution)/shard_map/ppermute | solution.py:50
  100.0 19.5 %copy-start.3 = (bf16[4,128,512]{2,1,0:T(8,128)(2,1)S(1)}, bf16[4,128,512]{2,1,0:T(8,128)(2,1)}, u32[]{:S(2)}) copy-start(bf16[4,128,512]{2,1,0:T(8,128)(2,1)} %broadcast_select_fusion.2) | copy-start | bytes 1572868
  100.2 9.1 %collective-permute-start.5 = (bf16[640,128]{1,0:T(8,128)(2,1)S(1)}, bf16[640,128]{1,0:T(8,128)(2,1)S(1)}, u32[]{:S(2)}, u32[]{:S(2)}) collective-permute-start(bf16[640,128]{1,0:T(8,128)(2,1)S(1)} %fusion.7), channel_id=1, source_target_pairs={{0,2},{1,3},{2,4},{3,5},{4,6},{5,7},{6,0},{7,1},{8,10},{9,11},{10,... | collective-permute-start | bytes 491528 | tf_op jit(solution)/shard_map/ppermute | solution.py:29
  102.6 9.4 %collective-permute-start.6 = (bf16[640,128]{1,0:T(8,128)(2,1)S(1)}, bf16[640,128]{1,0:T(8,128)(2,1)S(1)}, u32[]{:S(2)}, u32[]{:S(2)}) collective-permute-start(bf16[640,128]{1,0:T(8,128)(2,1)S(1)} %fusion.7), channel_id=1, source_target_pairs={{0,4},{1,5},{2,6},{3,7},{4,0},{5,1},{6,2},{7,3},{8,12},{9,13},{10,... | collective-permute-start | bytes 491528 | tf_op jit(solution)/shard_map/ppermute | solution.py:29
  106.7 8.8 %collective-permute-start.7 = (bf16[640,128]{1,0:T(8,128)(2,1)S(1)}, bf16[640,128]{1,0:T(8,128)(2,1)S(1)}, u32[]{:S(2)}, u32[]{:S(2)}) collective-permute-start(bf16[640,128]{1,0:T(8,128)(2,1)S(1)} %fusion.7), channel_id=1, source_target_pairs={{0,6},{1,7},{2,0},{3,1},{4,2},{5,3},{6,4},{7,5},{8,14},{9,15},{10,... | collective-permute-start | bytes 491528 | tf_op jit(solution)/shard_map/ppermute | solution.py:29
  115.6 4.0 %collective-permute-start.8 = (bf16[4,640,128]{2,1,0:T(8,128)(2,1)S(1)}, bf16[4,640,128]{2,1,0:T(8,128)(2,1)S(1)}, u32[]{:S(2)}, u32[]{:S(2)}) collective-permute-start(bf16[4,640,128]{2,1,0:T(8,128)(2,1)S(1)} %pad_maximum_fusion.2), channel_id=1, source_target_pairs={{0,1},{1,0},{2,3},{3,2},{4,5},{5,4},{6,7},{7,6},{8,9},{9,8},{10,11... | collective-permute-start | bytes 1966088 | tf_op jit(solution)/shard_map/ppermute | solution.py:32
  120.1 15.2 %copy-start.4 = (s32[1,128,2]{1,2,0:T(2,128)S(1)}, s32[1,128,2]{1,2,0:T(2,128)}, u32[]{:S(2)}) copy-start(s32[1,128,2]{1,2,0:T(2,128)} %param.14) | copy-start | bytes 3076
  120.1 15.3 %copy-start.5 = (s32[1,16]{1,0:T(1,128)S(1)}, s32[1,16]{1,0:T(1,128)}, u32[]{:S(2)}) copy-start(s32[1,16]{1,0:T(1,128)} %param.18) | copy-start | bytes 196
  120.1 16.8 %copy-start.6 = (f32[1,128,2]{1,2,0:T(2,128)S(1)}, f32[1,128,2]{1,2,0:T(2,128)}, u32[]{:S(2)}) copy-start(f32[1,128,2]{1,2,0:T(2,128)} %param.15) | copy-start | bytes 3076
  121.5 48.0 %all-to-all-start.1 = ((bf16[16,40,512]{2,1,0:T(8,128)(2,1)}), bf16[16,40,512]{2,1,0:T(8,128)(2,1)S(1)}, u32[]{:S(2)}, u32[]{:S(2)}) async-start(bf16[16,40,512]{2,1,0:T(8,128)(2,1)} %bitcast.26), calls=%async_computation.1 | async-start | bytes 1310720 | tf_op jit(solution)/shard_map/all_to_all | solution.py:166
  171.6 8.1 %collective-permute-start.9 = (bf16[128,512]{1,0:T(8,128)(2,1)S(1)}, bf16[128,512]{1,0:T(8,128)(2,1)S(1)}, u32[]{:S(2)}, u32[]{:S(2)}) collective-permute-start(bf16[128,512]{1,0:T(8,128)(2,1)S(1)} %multiply_reduce_fusion), channel_id=1, source_target_pairs={{0,128},{128,256},{256,384},{384,0},{1,129},{129,257},{257,385},{3... | collective-permute-start | bytes 393224 | tf_op jit(solution)/shard_map/ppermute | solution.py:10

commit v13 on v10

--- a/solution.py
+++ b/solution.py
@@ -149,7 +149,9 @@
     gate_proj = both[:, :hidden]
     up_proj = both[:, hidden:]
     activated = (jax.nn.silu(gate_proj) * up_proj).astype(jnp.bfloat16)
-    own_act, partner_act, act_own_from, act_partner_from = chips_then_core(activated, "rep")
+    own_act, partner_act, act_own_from, act_partner_from = relayed_chips_then_core(
+        activated, "rep"
+    )
     down_all = w_down[0, 0].reshape(reps, activated.shape[1], -1)
     produced = lax.dot_general(
         own_act, jnp.take(down_all, act_own_from, axis=0), dims,

time: 180 us -> 185 us (1.028)
  starting transfers between devices: 35.2 us -> 39.1 us
    ppermute x4 -> x0, starting transfers between devices: 9.72 us -> none  [the longest x3 7.76 us: chips_then_core(): pieces.append(lax.ppermute(value, axis, pairs))]
    ppermute x4 -> x0, waiting for transfers between devices: 7.55 us -> none  [the longest x3 7.55 us: chips_then_core(): pieces.append(lax.ppermute(value, axis, pairs))]
    ppermute x1 -> x2, waiting for transfers between devices: 4.68 us -> 9.34 us  [relayed_chips_then_core(): far_high = lax.ppermute(from_above[half:], axis, down_pairs)]
    ppermute x1 -> x2, starting transfers between devices: 3.71 us -> 7.63 us  [relayed_chips_then_core(): from_above = lax.ppermute(value, axis, down_pairs)]
    ppermute x1 -> x2, starting transfers between devices: 3.41 us -> 6.81 us  [relayed_chips_then_core(): far_low = lax.ppermute(from_below[:half], axis, up_pairs)]
    ppermute x1 -> x2, waiting for transfers between devices: 9.78 us -> 12.4 us  [relayed_chips_then_core(): from_below = lax.ppermute(value, axis, up_pairs)]
    ppermute x1 -> x2, starting transfers between devices: 2.43 us -> 4.86 us  [relayed_chips_then_core(): far_high = lax.ppermute(from_above[half:], axis, down_pairs)]
    ppermute x1 -> x2, starting transfers between devices: 1.92 us -> 3.84 us  [relayed_chips_then_core(): lax.ppermute(bundle, axis, [(source, source ^ 1) for source in range(coun...]
  transfers between devices with their start and end apart: 11 -> 12, of which waited for: 8 -> 8; matrix products, arithmetic and copies ran while one was open for 5% -> 5% of each run, Pallas kernels for 0% -> 0%
where the time goes in v13:
time: 185 us
  waiting for transfers between devices  63.9 us (35%)
  blocking collectives  51.4 us (28%)
  starting transfers between devices  39.1 us (21%)
  other arithmetic  11.3 us (6%)
  local copies, waits for them, and re-layouts  9.55 us (5%)
  matrix products  8.97 us (5%)
    all_to_all x1, blocking collectives, local(): lax.all_to_all(outgoing, 'expert', split_axis=0, concat_axis=0, tiled=True)  51.4 us
    all_to_all x1, waiting for transfers between devices, local(): lax.all_to_all(produced, 'expert', split_axis=0, concat_axis=0, tiled=True)  34.1 us
    ppermute x2, waiting for transfers between devices, relayed_chips_then_core(): from_below = lax.ppermute(value, axis, up_pairs)  12.4 us
    ppermute x2, waiting for transfers between devices, relayed_chips_then_core(): far_high = lax.ppermute(from_above[half:], axis, down_pairs)  9.34 us
    all_to_all x1, starting transfers between devices, local(): lax.all_to_all(produced, 'expert', split_axis=0, concat_axis=0, tiled=True)  8.51 us
    ppermute x2, starting transfers between devices, relayed_chips_then_core(): from_above = lax.ppermute(value, axis, down_pairs)  7.63 us
    ppermute x2, starting transfers between devices, relayed_chips_then_core(): far_low = lax.ppermute(from_below[:half], axis, up_pairs)  6.81 us
    ppermute x2, starting transfers between devices, relayed_chips_then_core(): far_high = lax.ppermute(from_above[half:], axis, down_pairs)  4.86 us
  transfers between devices with their start and end apart: 12, of which 8 were waited for; matrix products, arithmetic and copies ran while one was open for 5% of the time, Pallas kernels for 0%

profile of v13, /device:TPU:24, one launch (start us, length us, event | category | flops | bytes accessed | tf_op | source)
XLA Modules:
  0.0 184.7 jit_solution(3687968274449733536)
XLA Ops:
  0.0 0.8 convert_reduce_fusion
  0.9 0.7 fusion.26
  1.6 1.2 multiply_reduce_fusion.1
  2.9 0.2 reduce_window_sum.30
  3.1 0.2 reduce_window_sum.29
  3.3 0.7 fusion.32
  4.0 0.7 fusion.27
  4.9 0.7 select_reduce_fusion
  5.8 0.8 select_reduce_fusion.1
  6.7 1.3 convolution_convert_fusion
  8.0 51.4 %all_to_all.10 = bf16[16,40,512]{2,1,0:T(8,128)(2,1)S(1)} all-to-all(bf16[16,40,512]{2,1,0:T(8,128)(2,1)S(1)} %convolution_convert_fusion), channel_id=1, replica_groups=mesh['section'=4,'expert'=16,'rep'=8] {'expert'}, dimensions={0} | all-to-all | bytes 1310720 | tf_op jit(solution)/shard_map/all_to_all | solution.py:133
  59.4 2.1 %collective-permute-start = (bf16[640,512]{1,0:T(8,128)(2,1)S(1)}, bf16[640,512]{1,0:T(8,128)(2,1)S(1)}, u32[]{:S(2)}, u32[]{:S(2)}) collective-permute-start(bf16[640,512]{1,0:T(8,128)(2,1)S(1)} %bitcast.51), channel_id=1, source_target_pairs={{0,2},{1,3},{2,4},{3,5},{4,6},{5,7},{6,0},{7,1},{8,10},{9,11},{10,... | collective-permute-start | bytes 1966088 | tf_op jit(solution)/shard_map/ppermute | solution.py:42
  61.6 3.7 %collective-permute-start.1 = (bf16[640,512]{1,0:T(8,128)(2,1)S(1)}, bf16[640,512]{1,0:T(8,128)(2,1)S(1)}, u32[]{:S(2)}, u32[]{:S(2)}) collective-permute-start(bf16[640,512]{1,0:T(8,128)(2,1)S(1)} %bitcast.52), channel_id=1, source_target_pairs={{0,6},{1,7},{2,0},{3,1},{4,2},{5,3},{6,4},{7,5},{8,14},{9,15},{10,... | collective-permute-start | bytes 1966088 | tf_op jit(solution)/shard_map/ppermute | solution.py:43
  65.3 9.8 %collective-permute-done = bf16[640,512]{1,0:T(8,128)(2,1)S(1)} collective-permute-done((bf16[640,512]{1,0:T(8,128)(2,1)S(1)}, bf16[640,512]{1,0:T(8,128)(2,1)S(1)}, u32[]{:S(2)}, u32[]{:S(2)}) %collective-permute-start) | collective-permute-done | bytes 655392 | tf_op jit(solution)/shard_map/ppermute | solution.py:42
  75.1 3.4 %collective-permute-start.2 = (bf16[320,512]{1,0:T(8,128)(2,1)S(1)}, bf16[320,512]{1,0:T(8,128)(2,1)S(1)}, u32[]{:S(2)}, u32[]{:S(2)}) collective-permute-start(bf16[320,512]{1,0:T(8,128)(2,1)S(1)} %slice.34), channel_id=1, source_target_pairs={{0,2},{1,3},{2,4},{3,5},{4,6},{5,7},{6,0},{7,1},{8,10},{9,11},{10,... | collective-permute-start | bytes 983048 | tf_op jit(solution)/shard_map/ppermute | solution.py:45
  78.5 2.4 %collective-permute-start.3 = (bf16[320,512]{1,0:T(8,128)(2,1)S(1)}, bf16[320,512]{1,0:T(8,128)(2,1)S(1)}, u32[]{:S(2)}, u32[]{:S(2)}) collective-permute-start(bf16[320,512]{1,0:T(8,128)(2,1)S(1)} %slice.35), channel_id=1, source_target_pairs={{0,6},{1,7},{2,0},{3,1},{4,2},{5,3},{6,4},{7,5},{8,14},{9,15},{10,... | collective-permute-start | bytes 983048 | tf_op jit(solution)/shard_map/ppermute | solution.py:46
  81.0 3.1 %collective-permute-done.2 = bf16[320,512]{1,0:T(8,128)(2,1)S(1)} collective-permute-done((bf16[320,512]{1,0:T(8,128)(2,1)S(1)}, bf16[320,512]{1,0:T(8,128)(2,1)S(1)}, u32[]{:S(2)}, u32[]{:S(2)}) %collective-permute-start.2) | collective-permute-done | bytes 327712 | tf_op jit(solution)/shard_map/ppermute | solution.py:45
  84.0 4.7 %collective-permute-done.3 = bf16[320,512]{1,0:T(8,128)(2,1)S(1)} collective-permute-done((bf16[320,512]{1,0:T(8,128)(2,1)S(1)}, bf16[320,512]{1,0:T(8,128)(2,1)S(1)}, u32[]{:S(2)}, u32[]{:S(2)}) %collective-permute-start.3) | collective-permute-done | bytes 327712 | tf_op jit(solution)/shard_map/ppermute | solution.py:46
  88.8 1.8 pad_maximum_fusion
  90.6 1.9 %collective-permute-start.4 = (bf16[4,640,512]{2,1,0:T(8,128)(2,1)}, bf16[4,640,512]{2,1,0:T(8,128)(2,1)}, u32[]{:S(2)}, u32[]{:S(2)}) collective-permute-start(bf16[4,640,512]{2,1,0:T(8,128)(2,1)} %pad_maximum_fusion), channel_id=1, source_target_pairs={{0,1},{1,0},{2,3},{3,2},{4,5},{5,4},{6,7},{7,6},{8,9},{9,8},{10,11... | collective-permute-start | bytes 7864328 | tf_op jit(solution)/shard_map/ppermute | solution.py:49
  92.7 1.8 pad_maximum_fusion.1
  94.5 1.6 gather_fusion.2
  96.2 1.6 gather_fusion.1
  97.8 3.1 %convolution_bitcast_fusion.2 = f32[640,256]{1,0:T(8,128)S(1)} fusion(bf16[4,640,512]{2,1,0:T(8,128)(2,1)} %collective-permute-done.4, bf16[4,512,256]{2,1,0:T(8,128)(2,1)} %gather_fusion.2, pred[4]{0:T(512)(128)(4,1)S(1)} %get-tuple-element.23), kind=kOutput, calls=%fused_computation.12 | convolution fusion | flops 671612928 | bytes 4325380 | tf_op jit(solution)/shard_map/dot_general | solution.py:145
  101.0 0.9 fusion.2
  102.0 1.9 %collective-permute-start.5 = (bf16[640,128]{1,0:T(8,128)(2,1)S(1)}, bf16[640,128]{1,0:T(8,128)(2,1)S(1)}, u32[]{:S(2)}, u32[]{:S(2)}) collective-permute-start(bf16[640,128]{1,0:T(8,128)(2,1)S(1)} %fusion.17), channel_id=1, source_target_pairs={{0,2},{1,3},{2,4},{3,5},{4,6},{5,7},{6,0},{7,1},{8,10},{9,11},{10,... | collective-permute-start | bytes 491528 | tf_op jit(solution)/shard_map/ppermute | solution.py:42
  104.0 3.9 %collective-permute-start.6 = (bf16[640,128]{1,0:T(8,128)(2,1)S(1)}, bf16[640,128]{1,0:T(8,128)(2,1)S(1)}, u32[]{:S(2)}, u32[]{:S(2)}) collective-permute-start(bf16[640,128]{1,0:T(8,128)(2,1)S(1)} %fusion.17), channel_id=1, source_target_pairs={{0,6},{1,7},{2,0},{3,1},{4,2},{5,3},{6,4},{7,5},{8,14},{9,15},{10,... | collective-permute-start | bytes 491528 | tf_op jit(solution)/shard_map/ppermute | solution.py:43
  107.9 2.6 %collective-permute-done.5 = bf16[640,128]{1,0:T(8,128)(2,1)S(1)} collective-permute-done((bf16[640,128]{1,0:T(8,128)(2,1)S(1)}, bf16[640,128]{1,0:T(8,128)(2,1)S(1)}, u32[]{:S(2)}, u32[]{:S(2)}) %collective-permute-start.5) | collective-permute-done | bytes 163872 | tf_op jit(solution)/shard_map/ppermute | solution.py:42
  110.6 3.4 %collective-permute-start.7 = (bf16[320,128]{1,0:T(8,128)(2,1)S(1)}, bf16[320,128]{1,0:T(8,128)(2,1)S(1)}, u32[]{:S(2)}, u32[]{:S(2)}) collective-permute-start(bf16[320,128]{1,0:T(8,128)(2,1)S(1)} %slice.38), channel_id=1, source_target_pairs={{0,2},{1,3},{2,4},{3,5},{4,6},{5,7},{6,0},{7,1},{8,10},{9,11},{10,... | collective-permute-start | bytes 245768 | tf_op jit(solution)/shard_map/ppermute | solution.py:45
  114.0 2.4 %collective-permute-start.8 = (bf16[320,128]{1,0:T(8,128)(2,1)S(1)}, bf16[320,128]{1,0:T(8,128)(2,1)S(1)}, u32[]{:S(2)}, u32[]{:S(2)}) collective-permute-start(bf16[320,128]{1,0:T(8,128)(2,1)S(1)} %slice.39), channel_id=1, source_target_pairs={{0,6},{1,7},{2,0},{3,1},{4,2},{5,3},{6,4},{7,5},{8,14},{9,15},{10,... | collective-permute-start | bytes 245768 | tf_op jit(solution)/shard_map/ppermute | solution.py:46
  116.5 0.3 collective-permute-done.7
  116.9 4.7 %collective-permute-done.8 = bf16[320,128]{1,0:T(8,128)(2,1)S(1)} collective-permute-done((bf16[320,128]{1,0:T(8,128)(2,1)S(1)}, bf16[320,128]{1,0:T(8,128)(2,1)S(1)}, u32[]{:S(2)}, u32[]{:S(2)}) %collective-permute-start.8) | collective-permute-done | bytes 81952 | tf_op jit(solution)/shard_map/ppermute | solution.py:46
  121.6 1.9 %collective-permute-start.9 = (bf16[4,640,128]{2,1,0:T(8,128)(2,1)S(1)}, bf16[4,640,128]{2,1,0:T(8,128)(2,1)S(1)}, u32[]{:S(2)}, u32[]{:S(2)}) collective-permute-start(bf16[4,640,128]{2,1,0:T(8,128)(2,1)S(1)} %pad_maximum_fusion.2), channel_id=1, source_target_pairs={{0,1},{1,0},{2,3},{3,2},{4,5},{5,4},{6,7},{7,6},{8,9},{9,8},{10,11... | collective-permute-start | bytes 1966088 | tf_op jit(solution)/shard_map/ppermute | solution.py:49
  123.6 0.7 gather_fusion.4
  124.3 1.5 gather_fusion.3
  125.8 1.2 convolution_bitcast_fusion
  127.0 2.5 %fusion.1 = bf16[640,512]{1,0:T(8,128)(2,1)} fusion(f32[640,512]{1,0:T(8,128)S(1)} %convolution_bitcast_fusion, bf16[4,128,512]{2,1,0:T(8,128)(2,1)} %gather_fusion.3, pred[4]{0:T(512)(128)(4,1)} %copy-done.16, bf16[1,640,128]{2,1,0:T(8,128)(2,1)S(1)} %maximum_bitcast_fusion.1, bf16[1,640,128]{2,1,0:T(8,128)(2,1)S(1)} %bitcast.64, ...), kind=kOutput, calls=%fused_computation.11 | convolution fusion | flops 337444864 | bytes 3145732 | tf_op jit(solution)/shard_map/dot_general | solution.py:156
  129.5 8.5 %all-to-all-start.1 = ((bf16[16,40,512]{2,1,0:T(8,128)(2,1)}), bf16[16,40,512]{2,1,0:T(8,128)(2,1)S(1)}, u32[]{:S(2)}, u32[]{:S(2)}) async-start(bf16[16,40,512]{2,1,0:T(8,128)(2,1)} %bitcast.26), calls=%async_computation.1 | async-start | bytes 1310720 | tf_op jit(solution)/shard_map/all_to_all | solution.py:166
  138.7 0.1 gt.27
  139.1 0.1 reduce_sum.143
  139.3 0.1 reduce_sum.144
  139.4 0.1 squeeze.7
  139.8 34.1 %all-to-all-done.1 = bf16[16,40,512]{2,1,0:T(8,128)(2,1)S(1)} async-done(((bf16[16,40,512]{2,1,0:T(8,128)(2,1)}), bf16[16,40,512]{2,1,0:T(8,128)(2,1)S(1)}, u32[]{:S(2)}, u32[]{:S(2)}) %all-to-all-start.1) | async-done | bytes 655392 | tf_op jit(solution)/shard_map/all_to_all | solution.py:166
  173.9 1.2 gather_fusion
  175.1 0.9 multiply_reduce_fusion
  176.0 3.4 %collective-permute-start.10 = (bf16[128,512]{1,0:T(8,128)(2,1)S(1)}, bf16[128,512]{1,0:T(8,128)(2,1)S(1)}, u32[]{:S(2)}, u32[]{:S(2)}) collective-permute-start(bf16[128,512]{1,0:T(8,128)(2,1)S(1)} %multiply_reduce_fusion), channel_id=1, source_target_pairs={{0,128},{128,256},{256,384},{384,0},{1,129},{129,257},{257,385},{3... | collective-permute-start | bytes 393224 | tf_op jit(solution)/shard_map/ppermute | solution.py:10
  179.4 4.7 %collective-permute-done.10 = bf16[128,512]{1,0:T(8,128)(2,1)S(1)} collective-permute-done((bf16[128,512]{1,0:T(8,128)(2,1)S(1)}, bf16[128,512]{1,0:T(8,128)(2,1)S(1)}, u32[]{:S(2)}, u32[]{:S(2)}) %collective-permute-start.10) | collective-permute-done | bytes 131104 | tf_op jit(solution)/shard_map/ppermute | solution.py:10
  184.1 0.7 copy.59
  (82 shorter events, 2.5 us)
Async XLA Ops:
  0.0 123.6 %copy-start = (bf16[1,1,1024,512]{3,2,1,0:T(8,128)(2,1)S(1)}, bf16[1,1,1024,512]{3,2,1,0:T(8,128)(2,1)}, u32[]{:S(2)}) copy-start(bf16[1,1,1024,512]{3,2,1,0:T(8,128)(2,1)} %param.21) | copy-start | bytes 3145732
  59.4 31.2 %copy-start.1 = (bf16[16,40,512]{2,1,0:T(8,128)(2,1)}, bf16[16,40,512]{2,1,0:T(8,128)(2,1)S(1)}, u32[]{:S(2)}) copy-start(bf16[16,40,512]{2,1,0:T(8,128)(2,1)S(1)} %all_to_all.10) | copy-start | bytes 1966084
  59.4 15.6 %collective-permute-start = (bf16[640,512]{1,0:T(8,128)(2,1)S(1)}, bf16[640,512]{1,0:T(8,128)(2,1)S(1)}, u32[]{:S(2)}, u32[]{:S(2)}) collective-permute-start(bf16[640,512]{1,0:T(8,128)(2,1)S(1)} %bitcast.51), channel_id=1, source_target_pairs={{0,2},{1,3},{2,4},{3,5},{4,6},{5,7},{6,0},{7,1},{8,10},{9,11},{10,... | collective-permute-start | bytes 1966088 | tf_op jit(solution)/shard_map/ppermute | solution.py:42
  61.6 16.9 %collective-permute-start.1 = (bf16[640,512]{1,0:T(8,128)(2,1)S(1)}, bf16[640,512]{1,0:T(8,128)(2,1)S(1)}, u32[]{:S(2)}, u32[]{:S(2)}) collective-permute-start(bf16[640,512]{1,0:T(8,128)(2,1)S(1)} %bitcast.52), channel_id=1, source_target_pairs={{0,6},{1,7},{2,0},{3,1},{4,2},{5,3},{6,4},{7,5},{8,14},{9,15},{10,... | collective-permute-start | bytes 1966088 | tf_op jit(solution)/shard_map/ppermute | solution.py:43
  75.0 15.6 %copy-start.5 = (bf16[640,512]{1,0:T(8,128)(2,1)}, bf16[640,512]{1,0:T(8,128)(2,1)S(1)}, u32[]{:S(2)}) copy-start(bf16[640,512]{1,0:T(8,128)(2,1)S(1)} %collective-permute-done) | copy-start | bytes 1966084
  75.1 9.0 %collective-permute-start.2 = (bf16[320,512]{1,0:T(8,128)(2,1)S(1)}, bf16[320,512]{1,0:T(8,128)(2,1)S(1)}, u32[]{:S(2)}, u32[]{:S(2)}) collective-permute-start(bf16[320,512]{1,0:T(8,128)(2,1)S(1)} %slice.34), channel_id=1, source_target_pairs={{0,2},{1,3},{2,4},{3,5},{4,6},{5,7},{6,0},{7,1},{8,10},{9,11},{10,... | collective-permute-start | bytes 983048 | tf_op jit(solution)/shard_map/ppermute | solution.py:45
  78.5 12.1 %copy-start.7 = (bf16[640,512]{1,0:T(8,128)(2,1)}, bf16[640,512]{1,0:T(8,128)(2,1)S(1)}, u32[]{:S(2)}) copy-start(bf16[640,512]{1,0:T(8,128)(2,1)S(1)} %collective-permute-done.1) | copy-start | bytes 1966084
  78.5 10.2 %collective-permute-start.3 = (bf16[320,512]{1,0:T(8,128)(2,1)S(1)}, bf16[320,512]{1,0:T(8,128)(2,1)S(1)}, u32[]{:S(2)}, u32[]{:S(2)}) collective-permute-start(bf16[320,512]{1,0:T(8,128)(2,1)S(1)} %slice.35), channel_id=1, source_target_pairs={{0,6},{1,7},{2,0},{3,1},{4,2},{5,3},{6,4},{7,5},{8,14},{9,15},{10,... | collective-permute-start | bytes 983048 | tf_op jit(solution)/shard_map/ppermute | solution.py:46
  88.8 1.9 %copy-start.3 = (bf16[1,640,512]{2,1,0:T(8,128)(2,1)}, bf16[1,640,512]{2,1,0:T(8,128)(2,1)S(1)}, u32[]{:S(2)}) copy-start(bf16[1,640,512]{2,1,0:T(8,128)(2,1)S(1)} %maximum_bitcast_fusion) | copy-start | bytes 1966084
  90.6 7.2 %collective-permute-start.4 = (bf16[4,640,512]{2,1,0:T(8,128)(2,1)}, bf16[4,640,512]{2,1,0:T(8,128)(2,1)}, u32[]{:S(2)}, u32[]{:S(2)}) collective-permute-start(bf16[4,640,512]{2,1,0:T(8,128)(2,1)} %pad_maximum_fusion), channel_id=1, source_target_pairs={{0,1},{1,0},{2,3},{3,2},{4,5},{5,4},{6,7},{7,6},{8,9},{9,8},{10,11... | collective-permute-start | bytes 7864328 | tf_op jit(solution)/shard_map/ppermute | solution.py:49
  92.7 8.3 %copy-start.16 = (pred[4]{0:T(512)(128)(4,1)}, pred[4]{0:T(512)(128)(4,1)S(1)}, u32[]{:S(2)}) copy-start(pred[4]{0:T(512)(128)(4,1)S(1)} %get-tuple-element.21) | copy-start | bytes 16
  92.7 5.1 %copy-start.17 = (pred[4]{0:T(512)(128)(4,1)}, pred[4]{0:T(512)(128)(4,1)S(1)}, u32[]{:S(2)}) copy-start(pred[4]{0:T(512)(128)(4,1)S(1)} %get-tuple-element.23) | copy-start | bytes 16
  92.7 3.4 %copy-start.12 = (s32[1024]{0:T(1024)}, s32[1024]{0:T(1024)S(1)}, u32[]{:S(2)}) copy-start(s32[1024]{0:T(1024)S(1)} %pad_clamp_fusion.1) | copy-start | bytes 12292
  96.2 4.8 %copy-start.13 = (s32[1024]{0:T(1024)}, s32[1024]{0:T(1024)S(1)}, u32[]{:S(2)}) copy-start(s32[1024]{0:T(1024)S(1)} %pad_clamp_fusion.2) | copy-start | bytes 12292
  97.8 3.1 %copy-start.2 = (bf16[16,40,512]{2,1,0:T(8,128)(2,1)S(1)}, bf16[16,40,512]{2,1,0:T(8,128)(2,1)}, u32[]{:S(2)}) copy-start(bf16[16,40,512]{2,1,0:T(8,128)(2,1)} %copy-done.1) | copy-start | bytes 1966084
  97.8 3.2 %copy-start.4 = (bf16[1,640,512]{2,1,0:T(8,128)(2,1)S(1)}, bf16[1,640,512]{2,1,0:T(8,128)(2,1)}, u32[]{:S(2)}) copy-start(bf16[1,640,512]{2,1,0:T(8,128)(2,1)} %copy-done.3) | copy-start | bytes 1966084
  97.8 3.2 %copy-start.6 = (bf16[640,512]{1,0:T(8,128)(2,1)S(1)}, bf16[640,512]{1,0:T(8,128)(2,1)}, u32[]{:S(2)}) copy-start(bf16[640,512]{1,0:T(8,128)(2,1)} %copy-done.5) | copy-start | bytes 1966084
  97.8 3.2 %copy-start.8 = (bf16[640,512]{1,0:T(8,128)(2,1)S(1)}, bf16[640,512]{1,0:T(8,128)(2,1)}, u32[]{:S(2)}) copy-start(bf16[640,512]{1,0:T(8,128)(2,1)} %copy-done.7) | copy-start | bytes 1966084
  97.8 3.2 %copy-start.9 = (bf16[4,512,256]{2,1,0:T(8,128)(2,1)S(1)}, bf16[4,512,256]{2,1,0:T(8,128)(2,1)}, u32[]{:S(2)}) copy-start(bf16[4,512,256]{2,1,0:T(8,128)(2,1)} %gather_fusion.1) | copy-start | bytes 3145732
  102.0 8.5 %collective-permute-start.5 = (bf16[640,128]{1,0:T(8,128)(2,1)S(1)}, bf16[640,128]{1,0:T(8,128)(2,1)S(1)}, u32[]{:S(2)}, u32[]{:S(2)}) collective-permute-start(bf16[640,128]{1,0:T(8,128)(2,1)S(1)} %fusion.17), channel_id=1, source_target_pairs={{0,2},{1,3},{2,4},{3,5},{4,6},{5,7},{6,0},{7,1},{8,10},{9,11},{10,... | collective-permute-start | bytes 491528 | tf_op jit(solution)/shard_map/ppermute | solution.py:42
  104.0 10.0 %collective-permute-start.6 = (bf16[640,128]{1,0:T(8,128)(2,1)S(1)}, bf16[640,128]{1,0:T(8,128)(2,1)S(1)}, u32[]{:S(2)}, u32[]{:S(2)}) collective-permute-start(bf16[640,128]{1,0:T(8,128)(2,1)S(1)} %fusion.17), channel_id=1, source_target_pairs={{0,6},{1,7},{2,0},{3,1},{4,2},{5,3},{6,4},{7,5},{8,14},{9,15},{10,... | collective-permute-start | bytes 491528 | tf_op jit(solution)/shard_map/ppermute | solution.py:43
  110.6 6.3 %collective-permute-start.7 = (bf16[320,128]{1,0:T(8,128)(2,1)S(1)}, bf16[320,128]{1,0:T(8,128)(2,1)S(1)}, u32[]{:S(2)}, u32[]{:S(2)}) collective-permute-start(bf16[320,128]{1,0:T(8,128)(2,1)S(1)} %slice.38), channel_id=1, source_target_pairs={{0,2},{1,3},{2,4},{3,5},{4,6},{5,7},{6,0},{7,1},{8,10},{9,11},{10,... | collective-permute-start | bytes 245768 | tf_op jit(solution)/shard_map/ppermute | solution.py:45
  114.0 7.5 %collective-permute-start.8 = (bf16[320,128]{1,0:T(8,128)(2,1)S(1)}, bf16[320,128]{1,0:T(8,128)(2,1)S(1)}, u32[]{:S(2)}, u32[]{:S(2)}) collective-permute-start(bf16[320,128]{1,0:T(8,128)(2,1)S(1)} %slice.39), channel_id=1, source_target_pairs={{0,6},{1,7},{2,0},{3,1},{4,2},{5,3},{6,4},{7,5},{8,14},{9,15},{10,... | collective-permute-start | bytes 245768 | tf_op jit(solution)/shard_map/ppermute | solution.py:46
  121.6 4.1 %collective-permute-start.9 = (bf16[4,640,128]{2,1,0:T(8,128)(2,1)S(1)}, bf16[4,640,128]{2,1,0:T(8,128)(2,1)S(1)}, u32[]{:S(2)}, u32[]{:S(2)}) collective-permute-start(bf16[4,640,128]{2,1,0:T(8,128)(2,1)S(1)} %pad_maximum_fusion.2), channel_id=1, source_target_pairs={{0,1},{1,0},{2,3},{3,2},{4,5},{5,4},{6,7},{7,6},{8,9},{9,8},{10,11... | collective-permute-start | bytes 1966088 | tf_op jit(solution)/shard_map/ppermute | solution.py:49
  127.0 11.1 %copy-start.11 = (s32[1,128,2]{1,2,0:T(2,128)S(1)}, s32[1,128,2]{1,2,0:T(2,128)}, u32[]{:S(2)}) copy-start(s32[1,128,2]{1,2,0:T(2,128)} %param.14) | copy-start | bytes 3076
  127.0 11.2 %copy-start.10 = (s32[128,16]{1,0:T(8,128)S(1)}, s32[128,16]{1,0:T(8,128)}, u32[]{:S(2)}) copy-start(s32[128,16]{1,0:T(8,128)} %get-tuple-element.26) | copy-start | bytes 24580
  127.0 11.2 %copy-start.14 = (s32[1,16]{1,0:T(1,128)S(1)}, s32[1,16]{1,0:T(1,128)}, u32[]{:S(2)}) copy-start(s32[1,16]{1,0:T(1,128)} %param.18) | copy-start | bytes 196
  127.0 12.7 %copy-start.15 = (f32[1,128,2]{1,2,0:T(2,128)S(1)}, f32[1,128,2]{1,2,0:T(2,128)}, u32[]{:S(2)}) copy-start(f32[1,128,2]{1,2,0:T(2,128)} %param.15) | copy-start | bytes 3076
  129.5 44.4 %all-to-all-start.1 = ((bf16[16,40,512]{2,1,0:T(8,128)(2,1)}), bf16[16,40,512]{2,1,0:T(8,128)(2,1)S(1)}, u32[]{:S(2)}, u32[]{:S(2)}) async-start(bf16[16,40,512]{2,1,0:T(8,128)(2,1)} %bitcast.26), calls=%async_computation.1 | async-start | bytes 1310720 | tf_op jit(solution)/shard_map/all_to_all | solution.py:166
  176.0 8.1 %collective-permute-start.10 = (bf16[128,512]{1,0:T(8,128)(2,1)S(1)}, bf16[128,512]{1,0:T(8,128)(2,1)S(1)}, u32[]{:S(2)}, u32[]{:S(2)}) collective-permute-start(bf16[128,512]{1,0:T(8,128)(2,1)S(1)} %multiply_reduce_fusion), channel_id=1, source_target_pairs={{0,128},{128,256},{256,384},{384,0},{1,129},{129,257},{257,385},{3... | collective-permute-start | bytes 393224 | tf_op jit(solution)/shard_map/ppermute | solution.py:10

commit v14 on v10

--- a/solution.py
+++ b/solution.py
@@ -121,12 +121,12 @@
     spill_places = jnp.sum((spill_slot * spilled)[:, :, None] * spill_move[None, :, :], axis=1)
     rows_local = tokens[0]
     feat_width = rows_local.shape[1]
-    main_source = slot_sources(admitted, main_slot, slot_depth)
-    spill_source = slot_sources(spill_marks, spill_places, slot_depth)
-    sources = jnp.concatenate([main_source, spill_source], axis=1)
-    picks = (sources[:, :, None] == jnp.arange(tok_rows, dtype=jnp.int32)[None, None, :]).astype(
-        rows_local.dtype
+    slot_iota = jnp.arange(slot_depth, dtype=jnp.int32)
+    main_picks = admitted.T[:, None, :] * (main_slot.T[:, None, :] == slot_iota[None, :, None])
+    spill_picks = spill_marks.T[:, None, :] * (
+        spill_places.T[:, None, :] == slot_iota[None, :, None]
     )
+    picks = jnp.concatenate([main_picks, spill_picks], axis=1).astype(rows_local.dtype)
     outgoing = jnp.einsum(
         "xjt,tf->xjf", picks, rows_local, preferred_element_type=jnp.float32
     ).astype(rows_local.dtype)

time: 180 us -> 178 us (0.989)
  no operation moved by 1% of the time
where the time goes in v14:
time: 178 us
  waiting for transfers between devices  63.6 us (36%)
  blocking collectives  51.4 us (29%)
  starting transfers between devices  35.2 us (20%)
  local copies, waits for them, and re-layouts  9.27 us (5%)
  other arithmetic  9.19 us (5%)
  matrix products  8.44 us (5%)
    all_to_all x1, blocking collectives, local(): lax.all_to_all(outgoing, 'expert', split_axis=0, concat_axis=0, tiled=True)  51.4 us
    all_to_all x1, waiting for transfers between devices, local(): lax.all_to_all(produced, 'expert', split_axis=0, concat_axis=0, tiled=True)  33.8 us
    ppermute x1, waiting for transfers between devices, relayed_chips_then_core(): from_below = lax.ppermute(value, axis, up_pairs)  9.78 us
    all_to_all x1, starting transfers between devices, local(): lax.all_to_all(produced, 'expert', split_axis=0, concat_axis=0, tiled=True)  8.51 us
    ppermute x3, starting transfers between devices, chips_then_core(): pieces.append(lax.ppermute(value, axis, pairs))  7.76 us
    ppermute x3, waiting for transfers between devices, chips_then_core(): pieces.append(lax.ppermute(value, axis, pairs))  7.54 us
    ppermute x1, waiting for transfers between devices, relayed_chips_then_core(): far_high = lax.ppermute(from_above[half:], axis, down_pairs)  4.68 us
    ppermute x1, waiting for transfers between devices, passed_along(): return lax.ppermute(value, axis, pairs)  4.67 us
  transfers between devices with their start and end apart: 11, of which 8 were waited for; matrix products, arithmetic and copies ran while one was open for 5% of the time, Pallas kernels for 0%

profile of v14, /device:TPU:24, one launch (start us, length us, event | category | flops | bytes accessed | tf_op | source)
XLA Modules:
  0.0 177.7 jit_solution(9991882795647988969)
XLA Ops:
  0.0 0.8 convert_reduce_fusion
  0.9 0.7 fusion.26
  1.6 1.2 multiply_reduce_fusion.1
  2.9 0.2 reduce_window_sum.32
  3.1 0.7 fusion.27
  3.9 0.2 reduce_window_sum.31
  4.2 0.1 multiply_reduce_fusion.4
  4.4 1.2 convolution_convert_fusion
  5.6 51.4 %all_to_all.10 = bf16[16,40,512]{2,1,0:T(8,128)(2,1)S(1)} all-to-all(bf16[16,40,512]{2,1,0:T(8,128)(2,1)S(1)} %convolution_convert_fusion), channel_id=1, replica_groups=mesh['section'=4,'expert'=16,'rep'=8] {'expert'}, dimensions={0} | all-to-all | bytes 1310720 | tf_op jit(solution)/shard_map/all_to_all | solution.py:133
  57.0 2.1 %collective-permute-start = (bf16[640,512]{1,0:T(8,128)(2,1)S(1)}, bf16[640,512]{1,0:T(8,128)(2,1)S(1)}, u32[]{:S(2)}, u32[]{:S(2)}) collective-permute-start(bf16[640,512]{1,0:T(8,128)(2,1)S(1)} %bitcast.58), channel_id=1, source_target_pairs={{0,2},{1,3},{2,4},{3,5},{4,6},{5,7},{6,0},{7,1},{8,10},{9,11},{10,... | collective-permute-start | bytes 1966088 | tf_op jit(solution)/shard_map/ppermute | solution.py:42
  59.2 3.7 %collective-permute-start.1 = (bf16[640,512]{1,0:T(8,128)(2,1)S(1)}, bf16[640,512]{1,0:T(8,128)(2,1)S(1)}, u32[]{:S(2)}, u32[]{:S(2)}) collective-permute-start(bf16[640,512]{1,0:T(8,128)(2,1)S(1)} %bitcast.59), channel_id=1, source_target_pairs={{0,6},{1,7},{2,0},{3,1},{4,2},{5,3},{6,4},{7,5},{8,14},{9,15},{10,... | collective-permute-start | bytes 1966088 | tf_op jit(solution)/shard_map/ppermute | solution.py:43
  62.9 9.8 %collective-permute-done = bf16[640,512]{1,0:T(8,128)(2,1)S(1)} collective-permute-done((bf16[640,512]{1,0:T(8,128)(2,1)S(1)}, bf16[640,512]{1,0:T(8,128)(2,1)S(1)}, u32[]{:S(2)}, u32[]{:S(2)}) %collective-permute-start) | collective-permute-done | bytes 655392 | tf_op jit(solution)/shard_map/ppermute | solution.py:42
  72.7 3.4 %collective-permute-start.2 = (bf16[320,512]{1,0:T(8,128)(2,1)S(1)}, bf16[320,512]{1,0:T(8,128)(2,1)S(1)}, u32[]{:S(2)}, u32[]{:S(2)}) collective-permute-start(bf16[320,512]{1,0:T(8,128)(2,1)S(1)} %slice.26), channel_id=1, source_target_pairs={{0,2},{1,3},{2,4},{3,5},{4,6},{5,7},{6,0},{7,1},{8,10},{9,11},{10,... | collective-permute-start | bytes 983048 | tf_op jit(solution)/shard_map/ppermute | solution.py:45
  76.2 2.4 %collective-permute-start.3 = (bf16[320,512]{1,0:T(8,128)(2,1)S(1)}, bf16[320,512]{1,0:T(8,128)(2,1)S(1)}, u32[]{:S(2)}, u32[]{:S(2)}) collective-permute-start(bf16[320,512]{1,0:T(8,128)(2,1)S(1)} %slice.27), channel_id=1, source_target_pairs={{0,6},{1,7},{2,0},{3,1},{4,2},{5,3},{6,4},{7,5},{8,14},{9,15},{10,... | collective-permute-start | bytes 983048 | tf_op jit(solution)/shard_map/ppermute | solution.py:46
  78.6 3.1 %collective-permute-done.2 = bf16[320,512]{1,0:T(8,128)(2,1)S(1)} collective-permute-done((bf16[320,512]{1,0:T(8,128)(2,1)S(1)}, bf16[320,512]{1,0:T(8,128)(2,1)S(1)}, u32[]{:S(2)}, u32[]{:S(2)}) %collective-permute-start.2) | collective-permute-done | bytes 327712 | tf_op jit(solution)/shard_map/ppermute | solution.py:45
  81.7 4.7 %collective-permute-done.3 = bf16[320,512]{1,0:T(8,128)(2,1)S(1)} collective-permute-done((bf16[320,512]{1,0:T(8,128)(2,1)S(1)}, bf16[320,512]{1,0:T(8,128)(2,1)S(1)}, u32[]{:S(2)}, u32[]{:S(2)}) %collective-permute-start.3) | collective-permute-done | bytes 327712 | tf_op jit(solution)/shard_map/ppermute | solution.py:46
  86.4 1.8 %pad_maximum_fusion = bf16[4,640,512]{2,1,0:T(8,128)(2,1)} fusion(bf16[1,640,512]{2,1,0:T(8,128)(2,1)S(1)} %maximum_bitcast_fusion, bf16[1,640,512]{2,1,0:T(8,128)(2,1)S(1)} %bitcast.65, bf16[1,640,512]{2,1,0:T(8,128)(2,1)S(1)} %bitcast.63, bf16[1,640,512]{2,1,0:T(8,128)(2,1)S(1)} %bitcast.60), kind=kLoop, calls=%fused_computation.5 | loop fusion | flops 3932160 | bytes 5242880 | tf_op jit(solution)/shard_map/stack | solution.py:48
  88.2 1.9 %collective-permute-start.4 = (bf16[4,640,512]{2,1,0:T(8,128)(2,1)}, bf16[4,640,512]{2,1,0:T(8,128)(2,1)}, u32[]{:S(2)}, u32[]{:S(2)}) collective-permute-start(bf16[4,640,512]{2,1,0:T(8,128)(2,1)} %pad_maximum_fusion), channel_id=1, source_target_pairs={{0,1},{1,0},{2,3},{3,2},{4,5},{5,4},{6,7},{7,6},{8,9},{9,8},{10,11... | collective-permute-start | bytes 7864328 | tf_op jit(solution)/shard_map/ppermute | solution.py:49
  90.4 1.8 %pad_maximum_fusion.1 = bf16[8,512,256]{2,1,0:T(8,128)(2,1)S(1)} fusion(bf16[8,512,128]{2,1,0:T(8,128)(2,1)} %bitcast.67, bf16[8,512,128]{2,1,0:T(8,128)(2,1)} %bitcast.68), kind=kLoop, calls=%fused_computation.6 | loop fusion | flops 4194304 | bytes 4194304 | tf_op jit(solution)/shard_map/concatenate | solution.py:137
  92.1 1.6 gather_fusion.2
  93.8 1.6 gather_fusion.1
  95.5 3.1 %convolution_bitcast_fusion.2 = f32[640,256]{1,0:T(8,128)S(1)} fusion(bf16[4,640,512]{2,1,0:T(8,128)(2,1)} %collective-permute-done.4, bf16[4,512,256]{2,1,0:T(8,128)(2,1)} %gather_fusion.2, pred[4]{0:T(512)(128)(4,1)S(1)} %get-tuple-element.23), kind=kOutput, calls=%fused_computation.12 | convolution fusion | flops 671612928 | bytes 4325380 | tf_op jit(solution)/shard_map/dot_general | solution.py:145
  98.7 0.9 fusion.2
  99.7 1.9 %collective-permute-start.5 = (bf16[640,128]{1,0:T(8,128)(2,1)S(1)}, bf16[640,128]{1,0:T(8,128)(2,1)S(1)}, u32[]{:S(2)}, u32[]{:S(2)}) collective-permute-start(bf16[640,128]{1,0:T(8,128)(2,1)S(1)} %fusion.17), channel_id=1, source_target_pairs={{0,2},{1,3},{2,4},{3,5},{4,6},{5,7},{6,0},{7,1},{8,10},{9,11},{10,... | collective-permute-start | bytes 491528 | tf_op jit(solution)/shard_map/ppermute | solution.py:29
  101.7 3.3 %collective-permute-start.6 = (bf16[640,128]{1,0:T(8,128)(2,1)S(1)}, bf16[640,128]{1,0:T(8,128)(2,1)S(1)}, u32[]{:S(2)}, u32[]{:S(2)}) collective-permute-start(bf16[640,128]{1,0:T(8,128)(2,1)S(1)} %fusion.17), channel_id=1, source_target_pairs={{0,4},{1,5},{2,6},{3,7},{4,0},{5,1},{6,2},{7,3},{8,12},{9,13},{10,... | collective-permute-start | bytes 491528 | tf_op jit(solution)/shard_map/ppermute | solution.py:29
  104.9 2.6 %collective-permute-start.7 = (bf16[640,128]{1,0:T(8,128)(2,1)S(1)}, bf16[640,128]{1,0:T(8,128)(2,1)S(1)}, u32[]{:S(2)}, u32[]{:S(2)}) collective-permute-start(bf16[640,128]{1,0:T(8,128)(2,1)S(1)} %fusion.17), channel_id=1, source_target_pairs={{0,6},{1,7},{2,0},{3,1},{4,2},{5,3},{6,4},{7,5},{8,14},{9,15},{10,... | collective-permute-start | bytes 491528 | tf_op jit(solution)/shard_map/ppermute | solution.py:29
  107.6 1.0 collective-permute-done.5
  108.6 3.1 %collective-permute-done.6 = bf16[640,128]{1,0:T(8,128)(2,1)S(1)} collective-permute-done((bf16[640,128]{1,0:T(8,128)(2,1)S(1)}, bf16[640,128]{1,0:T(8,128)(2,1)S(1)}, u32[]{:S(2)}, u32[]{:S(2)}) %collective-permute-start.6) | collective-permute-done | bytes 163872 | tf_op jit(solution)/shard_map/ppermute | solution.py:29
  111.7 3.4 %collective-permute-done.7 = bf16[640,128]{1,0:T(8,128)(2,1)S(1)} collective-permute-done((bf16[640,128]{1,0:T(8,128)(2,1)S(1)}, bf16[640,128]{1,0:T(8,128)(2,1)S(1)}, u32[]{:S(2)}, u32[]{:S(2)}) %collective-permute-start.7) | collective-permute-done | bytes 163872 | tf_op jit(solution)/shard_map/ppermute | solution.py:29
  115.3 2.0 %collective-permute-start.8 = (bf16[4,640,128]{2,1,0:T(8,128)(2,1)S(1)}, bf16[4,640,128]{2,1,0:T(8,128)(2,1)S(1)}, u32[]{:S(2)}, u32[]{:S(2)}) collective-permute-start(bf16[4,640,128]{2,1,0:T(8,128)(2,1)S(1)} %pad_maximum_fusion.2), channel_id=1, source_target_pairs={{0,1},{1,0},{2,3},{3,2},{4,5},{5,4},{6,7},{7,6},{8,9},{9,8},{10,11... | collective-permute-start | bytes 1966088 | tf_op jit(solution)/shard_map/ppermute | solution.py:32
  117.3 0.6 gather_fusion.4
  117.9 1.4 gather_fusion.3
  119.3 0.6 convolution_bitcast_fusion
  119.9 2.6 %fusion.1 = bf16[640,512]{1,0:T(8,128)(2,1)} fusion(f32[640,512]{1,0:T(8,128)S(1)} %convolution_bitcast_fusion, bf16[4,128,512]{2,1,0:T(8,128)(2,1)} %gather_fusion.3, pred[4]{0:T(512)(128)(4,1)S(1)} %get-tuple-element.17, bf16[1,640,128]{2,1,0:T(8,128)(2,1)} %bitcast.74, bf16[1,640,128]{2,1,0:T(8,128)(2,1)} %bitcast.72, ...), kind=kOutput, calls=%fused_computation.11 | convolution fusion | flops 337444864 | bytes 3145732 | tf_op jit(solution)/shard_map/dot_general | solution.py:154
  122.5 8.5 %all-to-all-start.1 = ((bf16[16,40,512]{2,1,0:T(8,128)(2,1)}), bf16[16,40,512]{2,1,0:T(8,128)(2,1)S(1)}, u32[]{:S(2)}, u32[]{:S(2)}) async-start(bf16[16,40,512]{2,1,0:T(8,128)(2,1)} %bitcast.32), calls=%async_computation.1 | async-start | bytes 1310720 | tf_op jit(solution)/shard_map/all_to_all | solution.py:164
  131.7 0.1 copy.37
  131.9 0.1 gt.19
  132.1 0.1 add.115
  132.3 0.1 reduce_sum.103
  132.4 0.1 reduce_sum.104
  132.6 0.1 squeeze.7
  132.7 0.1 copy.32
  133.0 33.8 %all-to-all-done.1 = bf16[16,40,512]{2,1,0:T(8,128)(2,1)S(1)} async-done(((bf16[16,40,512]{2,1,0:T(8,128)(2,1)}), bf16[16,40,512]{2,1,0:T(8,128)(2,1)S(1)}, u32[]{:S(2)}, u32[]{:S(2)}) %all-to-all-start.1) | async-done | bytes 655392 | tf_op jit(solution)/shard_map/all_to_all | solution.py:164
  166.8 1.2 gather_fusion
  168.1 0.9 multiply_reduce_fusion
  168.9 3.4 %collective-permute-start.9 = (bf16[128,512]{1,0:T(8,128)(2,1)S(1)}, bf16[128,512]{1,0:T(8,128)(2,1)S(1)}, u32[]{:S(2)}, u32[]{:S(2)}) collective-permute-start(bf16[128,512]{1,0:T(8,128)(2,1)S(1)} %multiply_reduce_fusion), channel_id=1, source_target_pairs={{0,128},{128,256},{256,384},{384,0},{1,129},{129,257},{257,385},{3... | collective-permute-start | bytes 393224 | tf_op jit(solution)/shard_map/ppermute | solution.py:10
  172.4 4.7 %collective-permute-done.9 = bf16[128,512]{1,0:T(8,128)(2,1)S(1)} collective-permute-done((bf16[128,512]{1,0:T(8,128)(2,1)S(1)}, bf16[128,512]{1,0:T(8,128)(2,1)S(1)}, u32[]{:S(2)}, u32[]{:S(2)}) %collective-permute-start.9) | collective-permute-done | bytes 131104 | tf_op jit(solution)/shard_map/ppermute | solution.py:10
  177.0 0.7 copy.43
  (73 shorter events, 2.1 us)
Async XLA Ops:
  0.0 117.3 %copy-start = (bf16[1,1,1024,512]{3,2,1,0:T(8,128)(2,1)S(1)}, bf16[1,1,1024,512]{3,2,1,0:T(8,128)(2,1)}, u32[]{:S(2)}) copy-start(bf16[1,1,1024,512]{3,2,1,0:T(8,128)(2,1)} %param.21) | copy-start | bytes 3145732
  57.0 31.2 %copy-start.1 = (bf16[16,40,512]{2,1,0:T(8,128)(2,1)}, bf16[16,40,512]{2,1,0:T(8,128)(2,1)S(1)}, u32[]{:S(2)}) copy-start(bf16[16,40,512]{2,1,0:T(8,128)(2,1)S(1)} %all_to_all.10) | copy-start | bytes 1966084
  57.0 15.6 %collective-permute-start = (bf16[640,512]{1,0:T(8,128)(2,1)S(1)}, bf16[640,512]{1,0:T(8,128)(2,1)S(1)}, u32[]{:S(2)}, u32[]{:S(2)}) collective-permute-start(bf16[640,512]{1,0:T(8,128)(2,1)S(1)} %bitcast.58), channel_id=1, source_target_pairs={{0,2},{1,3},{2,4},{3,5},{4,6},{5,7},{6,0},{7,1},{8,10},{9,11},{10,... | collective-permute-start | bytes 1966088 | tf_op jit(solution)/shard_map/ppermute | solution.py:42
  59.2 16.9 %collective-permute-start.1 = (bf16[640,512]{1,0:T(8,128)(2,1)S(1)}, bf16[640,512]{1,0:T(8,128)(2,1)S(1)}, u32[]{:S(2)}, u32[]{:S(2)}) collective-permute-start(bf16[640,512]{1,0:T(8,128)(2,1)S(1)} %bitcast.59), channel_id=1, source_target_pairs={{0,6},{1,7},{2,0},{3,1},{4,2},{5,3},{6,4},{7,5},{8,14},{9,15},{10,... | collective-permute-start | bytes 1966088 | tf_op jit(solution)/shard_map/ppermute | solution.py:43
  72.7 15.6 %copy-start.5 = (bf16[640,512]{1,0:T(8,128)(2,1)}, bf16[640,512]{1,0:T(8,128)(2,1)S(1)}, u32[]{:S(2)}) copy-start(bf16[640,512]{1,0:T(8,128)(2,1)S(1)} %collective-permute-done) | copy-start | bytes 1966084
  72.7 9.0 %collective-permute-start.2 = (bf16[320,512]{1,0:T(8,128)(2,1)S(1)}, bf16[320,512]{1,0:T(8,128)(2,1)S(1)}, u32[]{:S(2)}, u32[]{:S(2)}) collective-permute-start(bf16[320,512]{1,0:T(8,128)(2,1)S(1)} %slice.26), channel_id=1, source_target_pairs={{0,2},{1,3},{2,4},{3,5},{4,6},{5,7},{6,0},{7,1},{8,10},{9,11},{10,... | collective-permute-start | bytes 983048 | tf_op jit(solution)/shard_map/ppermute | solution.py:45
  76.1 12.1 %copy-start.7 = (bf16[640,512]{1,0:T(8,128)(2,1)}, bf16[640,512]{1,0:T(8,128)(2,1)S(1)}, u32[]{:S(2)}) copy-start(bf16[640,512]{1,0:T(8,128)(2,1)S(1)} %collective-permute-done.1) | copy-start | bytes 1966084
  76.2 10.2 %collective-permute-start.3 = (bf16[320,512]{1,0:T(8,128)(2,1)S(1)}, bf16[320,512]{1,0:T(8,128)(2,1)S(1)}, u32[]{:S(2)}, u32[]{:S(2)}) collective-permute-start(bf16[320,512]{1,0:T(8,128)(2,1)S(1)} %slice.27), channel_id=1, source_target_pairs={{0,6},{1,7},{2,0},{3,1},{4,2},{5,3},{6,4},{7,5},{8,14},{9,15},{10,... | collective-permute-start | bytes 983048 | tf_op jit(solution)/shard_map/ppermute | solution.py:46
  86.4 1.9 %copy-start.3 = (bf16[1,640,512]{2,1,0:T(8,128)(2,1)}, bf16[1,640,512]{2,1,0:T(8,128)(2,1)S(1)}, u32[]{:S(2)}) copy-start(bf16[1,640,512]{2,1,0:T(8,128)(2,1)S(1)} %maximum_bitcast_fusion) | copy-start | bytes 1966084
  88.2 7.2 %collective-permute-start.4 = (bf16[4,640,512]{2,1,0:T(8,128)(2,1)}, bf16[4,640,512]{2,1,0:T(8,128)(2,1)}, u32[]{:S(2)}, u32[]{:S(2)}) collective-permute-start(bf16[4,640,512]{2,1,0:T(8,128)(2,1)} %pad_maximum_fusion), channel_id=1, source_target_pairs={{0,1},{1,0},{2,3},{3,2},{4,5},{5,4},{6,7},{7,6},{8,9},{9,8},{10,11... | collective-permute-start | bytes 7864328 | tf_op jit(solution)/shard_map/ppermute | solution.py:49
  95.5 3.1 %copy-start.2 = (bf16[16,40,512]{2,1,0:T(8,128)(2,1)S(1)}, bf16[16,40,512]{2,1,0:T(8,128)(2,1)}, u32[]{:S(2)}) copy-start(bf16[16,40,512]{2,1,0:T(8,128)(2,1)} %copy-done.1) | copy-start | bytes 1966084
  95.5 3.1 %copy-start.4 = (bf16[1,640,512]{2,1,0:T(8,128)(2,1)S(1)}, bf16[1,640,512]{2,1,0:T(8,128)(2,1)}, u32[]{:S(2)}) copy-start(bf16[1,640,512]{2,1,0:T(8,128)(2,1)} %copy-done.3) | copy-start | bytes 1966084
  95.5 3.1 %copy-start.6 = (bf16[640,512]{1,0:T(8,128)(2,1)S(1)}, bf16[640,512]{1,0:T(8,128)(2,1)}, u32[]{:S(2)}) copy-start(bf16[640,512]{1,0:T(8,128)(2,1)} %copy-done.5) | copy-start | bytes 1966084
  95.5 3.1 %copy-start.8 = (bf16[640,512]{1,0:T(8,128)(2,1)S(1)}, bf16[640,512]{1,0:T(8,128)(2,1)}, u32[]{:S(2)}) copy-start(bf16[640,512]{1,0:T(8,128)(2,1)} %copy-done.7) | copy-start | bytes 1966084
  95.5 3.1 %copy-start.9 = (bf16[4,512,256]{2,1,0:T(8,128)(2,1)S(1)}, bf16[4,512,256]{2,1,0:T(8,128)(2,1)}, u32[]{:S(2)}) copy-start(bf16[4,512,256]{2,1,0:T(8,128)(2,1)} %gather_fusion.1) | copy-start | bytes 3145732
  99.7 8.9 %collective-permute-start.5 = (bf16[640,128]{1,0:T(8,128)(2,1)S(1)}, bf16[640,128]{1,0:T(8,128)(2,1)S(1)}, u32[]{:S(2)}, u32[]{:S(2)}) collective-permute-start(bf16[640,128]{1,0:T(8,128)(2,1)S(1)} %fusion.17), channel_id=1, source_target_pairs={{0,2},{1,3},{2,4},{3,5},{4,6},{5,7},{6,0},{7,1},{8,10},{9,11},{10,... | collective-permute-start | bytes 491528 | tf_op jit(solution)/shard_map/ppermute | solution.py:29
  101.7 10.1 %collective-permute-start.6 = (bf16[640,128]{1,0:T(8,128)(2,1)S(1)}, bf16[640,128]{1,0:T(8,128)(2,1)S(1)}, u32[]{:S(2)}, u32[]{:S(2)}) collective-permute-start(bf16[640,128]{1,0:T(8,128)(2,1)S(1)} %fusion.17), channel_id=1, source_target_pairs={{0,4},{1,5},{2,6},{3,7},{4,0},{5,1},{6,2},{7,3},{8,12},{9,13},{10,... | collective-permute-start | bytes 491528 | tf_op jit(solution)/shard_map/ppermute | solution.py:29
  104.9 10.2 %collective-permute-start.7 = (bf16[640,128]{1,0:T(8,128)(2,1)S(1)}, bf16[640,128]{1,0:T(8,128)(2,1)S(1)}, u32[]{:S(2)}, u32[]{:S(2)}) collective-permute-start(bf16[640,128]{1,0:T(8,128)(2,1)S(1)} %fusion.17), channel_id=1, source_target_pairs={{0,6},{1,7},{2,0},{3,1},{4,2},{5,3},{6,4},{7,5},{8,14},{9,15},{10,... | collective-permute-start | bytes 491528 | tf_op jit(solution)/shard_map/ppermute | solution.py:29
  111.7 5.5 %copy-start.10 = (bf16[640,128]{1,0:T(8,128)(2,1)}, bf16[640,128]{1,0:T(8,128)(2,1)S(1)}, u32[]{:S(2)}) copy-start(bf16[640,128]{1,0:T(8,128)(2,1)S(1)} %collective-permute-done.6) | copy-start | bytes 491524
  115.2 2.1 %copy-start.11 = (bf16[640,128]{1,0:T(8,128)(2,1)}, bf16[640,128]{1,0:T(8,128)(2,1)S(1)}, u32[]{:S(2)}) copy-start(bf16[640,128]{1,0:T(8,128)(2,1)S(1)} %collective-permute-done.7) | copy-start | bytes 491524
  115.3 4.0 %collective-permute-start.8 = (bf16[4,640,128]{2,1,0:T(8,128)(2,1)S(1)}, bf16[4,640,128]{2,1,0:T(8,128)(2,1)S(1)}, u32[]{:S(2)}, u32[]{:S(2)}) collective-permute-start(bf16[4,640,128]{2,1,0:T(8,128)(2,1)S(1)} %pad_maximum_fusion.2), channel_id=1, source_target_pairs={{0,1},{1,0},{2,3},{3,2},{4,5},{5,4},{6,7},{7,6},{8,9},{9,8},{10,11... | collective-permute-start | bytes 1966088 | tf_op jit(solution)/shard_map/ppermute | solution.py:32
  119.8 11.3 %copy-start.12 = (s32[1,128,2]{1,2,0:T(2,128)S(1)}, s32[1,128,2]{1,2,0:T(2,128)}, u32[]{:S(2)}) copy-start(s32[1,128,2]{1,2,0:T(2,128)} %param.14) | copy-start | bytes 3076
  119.9 11.5 %copy-start.13 = (s32[1,16]{1,0:T(1,128)S(1)}, s32[1,16]{1,0:T(1,128)}, u32[]{:S(2)}) copy-start(s32[1,16]{1,0:T(1,128)} %param.18) | copy-start | bytes 196
  119.9 13.0 %copy-start.14 = (f32[1,128,2]{1,2,0:T(2,128)S(1)}, f32[1,128,2]{1,2,0:T(2,128)}, u32[]{:S(2)}) copy-start(f32[1,128,2]{1,2,0:T(2,128)} %param.15) | copy-start | bytes 3076
  122.5 44.3 %all-to-all-start.1 = ((bf16[16,40,512]{2,1,0:T(8,128)(2,1)}), bf16[16,40,512]{2,1,0:T(8,128)(2,1)S(1)}, u32[]{:S(2)}, u32[]{:S(2)}) async-start(bf16[16,40,512]{2,1,0:T(8,128)(2,1)} %bitcast.32), calls=%async_computation.1 | async-start | bytes 1310720 | tf_op jit(solution)/shard_map/all_to_all | solution.py:164
  168.9 8.1 %collective-permute-start.9 = (bf16[128,512]{1,0:T(8,128)(2,1)S(1)}, bf16[128,512]{1,0:T(8,128)(2,1)S(1)}, u32[]{:S(2)}, u32[]{:S(2)}) collective-permute-start(bf16[128,512]{1,0:T(8,128)(2,1)S(1)} %multiply_reduce_fusion), channel_id=1, source_target_pairs={{0,128},{128,256},{256,384},{384,0},{1,129},{129,257},{257,385},{3... | collective-permute-start | bytes 393224 | tf_op jit(solution)/shard_map/ppermute | solution.py:10

commit v15 on v14

--- a/solution.py
+++ b/solution.py
@@ -74,8 +74,18 @@
     return jnp.take(weight, origin, axis=0)
 
 
+def earlier(counts):
+    tok_rows = counts.shape[0]
+    iota = jnp.arange(tok_rows, dtype=jnp.int32)
+    before = (iota[None, :] < iota[:, None]).astype(jnp.bfloat16)
+    return jnp.dot(
+        before, counts.astype(jnp.bfloat16), preferred_element_type=jnp.float32
+    ).astype(jnp.int32)
+
+
 def admission(chosen, language, capacity, experts):
     lang_count = capacity.shape[0]
+    tok_rows = chosen.shape[0]
     hit_table = jnp.sum(
         (chosen[:, :, None] == jnp.arange(experts, dtype=jnp.int32)[None, None, :]).astype(
             jnp.int32
@@ -85,9 +95,13 @@
     lang_hot = (language[:, None] == jnp.arange(lang_count, dtype=jnp.int32)[None, :]).astype(
         jnp.int32
     )
-    lang_hits = lang_hot[:, :, None] * hit_table[:, None, :]
-    before = jnp.cumsum(lang_hits, axis=0) - lang_hits
-    place_rank = jnp.sum(before * lang_hot[:, :, None], axis=1)
+    iota = jnp.arange(tok_rows, dtype=jnp.int32)
+    same_before = ((language[None, :] == language[:, None]) & (iota[None, :] < iota[:, None])).astype(
+        jnp.bfloat16
+    )
+    place_rank = jnp.dot(
+        same_before, hit_table.astype(jnp.bfloat16), preferred_element_type=jnp.float32
+    ).astype(jnp.int32)
     allowance = jnp.sum(lang_hot[:, :, None] * capacity[None, :, :], axis=1)
     admitted = hit_table * (place_rank < allowance).astype(jnp.int32)
     return (hit_table, admitted)
@@ -114,8 +128,8 @@
     expert_iota = jnp.arange(experts, dtype=jnp.int32)
     hit_table, admitted = admission(chosen, language[0], capacity, experts)
     spilled = hit_table - admitted
-    main_slot = jnp.cumsum(admitted, axis=0) - admitted
-    spill_slot = jnp.cumsum(spilled, axis=0) - spilled
+    main_slot = earlier(admitted)
+    spill_slot = earlier(spilled)
     spill_move = (spill_row[:, None] == expert_iota[None, :]).astype(jnp.int32)
     spill_marks = jnp.sum(spilled[:, :, None] * spill_move[None, :, :], axis=1)
     spill_places = jnp.sum((spill_slot * spilled)[:, :, None] * spill_move[None, :, :], axis=1)

time: 178 us -> 182 us (1.022)
  other arithmetic: 9.19 us -> 11.2 us
  transfers between devices with their start and end apart: 11 -> 11, of which waited for: 8 -> 8; matrix products, arithmetic and copies ran while one was open for 5% -> 7% of each run, Pallas kernels for 0% -> 0%
where the time goes in v15:
time: 182 us
  waiting for transfers between devices  63.8 us (35%)
  blocking collectives  51.4 us (28%)
  starting transfers between devices  35.2 us (19%)
  other arithmetic  11.2 us (6%)
  matrix products  10.1 us (6%)
  local copies, waits for them, and re-layouts  9.41 us (5%)
    all_to_all x1, blocking collectives, local(): lax.all_to_all(outgoing, 'expert', split_axis=0, concat_axis=0, tiled=True)  51.4 us
    all_to_all x1, waiting for transfers between devices, local(): lax.all_to_all(produced, 'expert', split_axis=0, concat_axis=0, tiled=True)  34 us
    ppermute x1, waiting for transfers between devices, relayed_chips_then_core(): from_below = lax.ppermute(value, axis, up_pairs)  9.78 us
    all_to_all x1, starting transfers between devices, local(): lax.all_to_all(produced, 'expert', split_axis=0, concat_axis=0, tiled=True)  8.49 us
    ppermute x3, starting transfers between devices, chips_then_core(): pieces.append(lax.ppermute(value, axis, pairs))  7.76 us
    ppermute x3, waiting for transfers between devices, chips_then_core(): pieces.append(lax.ppermute(value, axis, pairs))  7.55 us
    ppermute x1, waiting for transfers between devices, relayed_chips_then_core(): far_high = lax.ppermute(from_above[half:], axis, down_pairs)  4.68 us
    ppermute x1, waiting for transfers between devices, passed_along(): return lax.ppermute(value, axis, pairs)  4.66 us
  transfers between devices with their start and end apart: 11, of which 8 were waited for; matrix products, arithmetic and copies ran while one was open for 7% of the time, Pallas kernels for 0%

profile of v15, /device:TPU:24, one launch (start us, length us, event | category | flops | bytes accessed | tf_op | source)
XLA Modules:
  0.0 181.6 jit_solution(10786102810433607806)
XLA Ops:
  0.0 0.7 fusion.31
  0.8 0.7 convert_reduce_fusion
  1.4 0.8 multiply_reduce_fusion.3
  2.2 0.9 fusion.37
  3.1 0.2 fusion.38
  3.3 0.8 fusion.27
  4.4 0.4 copy-done.10
  4.8 1.2 convolution_convert_fusion
  6.0 51.4 %all_to_all.10 = bf16[16,40,512]{2,1,0:T(8,128)(2,1)S(1)} all-to-all(bf16[16,40,512]{2,1,0:T(8,128)(2,1)S(1)} %convolution_convert_fusion), channel_id=1, replica_groups=mesh['section'=4,'expert'=16,'rep'=8] {'expert'}, dimensions={0} | all-to-all | bytes 1310720 | tf_op jit(solution)/shard_map/all_to_all | solution.py:147
  57.4 2.1 %collective-permute-start = (bf16[640,512]{1,0:T(8,128)(2,1)S(1)}, bf16[640,512]{1,0:T(8,128)(2,1)S(1)}, u32[]{:S(2)}, u32[]{:S(2)}) collective-permute-start(bf16[640,512]{1,0:T(8,128)(2,1)S(1)} %bitcast.56), channel_id=1, source_target_pairs={{0,2},{1,3},{2,4},{3,5},{4,6},{5,7},{6,0},{7,1},{8,10},{9,11},{10,... | collective-permute-start | bytes 1966088 | tf_op jit(solution)/shard_map/ppermute | solution.py:42
  59.6 3.7 %collective-permute-start.1 = (bf16[640,512]{1,0:T(8,128)(2,1)S(1)}, bf16[640,512]{1,0:T(8,128)(2,1)S(1)}, u32[]{:S(2)}, u32[]{:S(2)}) collective-permute-start(bf16[640,512]{1,0:T(8,128)(2,1)S(1)} %bitcast.57), channel_id=1, source_target_pairs={{0,6},{1,7},{2,0},{3,1},{4,2},{5,3},{6,4},{7,5},{8,14},{9,15},{10,... | collective-permute-start | bytes 1966088 | tf_op jit(solution)/shard_map/ppermute | solution.py:43
  63.3 9.8 %collective-permute-done = bf16[640,512]{1,0:T(8,128)(2,1)S(1)} collective-permute-done((bf16[640,512]{1,0:T(8,128)(2,1)S(1)}, bf16[640,512]{1,0:T(8,128)(2,1)S(1)}, u32[]{:S(2)}, u32[]{:S(2)}) %collective-permute-start) | collective-permute-done | bytes 655392 | tf_op jit(solution)/shard_map/ppermute | solution.py:42
  73.1 3.4 %collective-permute-start.2 = (bf16[320,512]{1,0:T(8,128)(2,1)S(1)}, bf16[320,512]{1,0:T(8,128)(2,1)S(1)}, u32[]{:S(2)}, u32[]{:S(2)}) collective-permute-start(bf16[320,512]{1,0:T(8,128)(2,1)S(1)} %slice.26), channel_id=1, source_target_pairs={{0,2},{1,3},{2,4},{3,5},{4,6},{5,7},{6,0},{7,1},{8,10},{9,11},{10,... | collective-permute-start | bytes 983048 | tf_op jit(solution)/shard_map/ppermute | solution.py:45
  76.6 2.4 %collective-permute-start.3 = (bf16[320,512]{1,0:T(8,128)(2,1)S(1)}, bf16[320,512]{1,0:T(8,128)(2,1)S(1)}, u32[]{:S(2)}, u32[]{:S(2)}) collective-permute-start(bf16[320,512]{1,0:T(8,128)(2,1)S(1)} %slice.27), channel_id=1, source_target_pairs={{0,6},{1,7},{2,0},{3,1},{4,2},{5,3},{6,4},{7,5},{8,14},{9,15},{10,... | collective-permute-start | bytes 983048 | tf_op jit(solution)/shard_map/ppermute | solution.py:46
  79.0 3.1 %collective-permute-done.2 = bf16[320,512]{1,0:T(8,128)(2,1)S(1)} collective-permute-done((bf16[320,512]{1,0:T(8,128)(2,1)S(1)}, bf16[320,512]{1,0:T(8,128)(2,1)S(1)}, u32[]{:S(2)}, u32[]{:S(2)}) %collective-permute-start.2) | collective-permute-done | bytes 327712 | tf_op jit(solution)/shard_map/ppermute | solution.py:45
  82.1 4.7 %collective-permute-done.3 = bf16[320,512]{1,0:T(8,128)(2,1)S(1)} collective-permute-done((bf16[320,512]{1,0:T(8,128)(2,1)S(1)}, bf16[320,512]{1,0:T(8,128)(2,1)S(1)}, u32[]{:S(2)}, u32[]{:S(2)}) %collective-permute-start.3) | collective-permute-done | bytes 327712 | tf_op jit(solution)/shard_map/ppermute | solution.py:46
  86.8 1.8 %pad_maximum_fusion = bf16[4,640,512]{2,1,0:T(8,128)(2,1)} fusion(bf16[1,640,512]{2,1,0:T(8,128)(2,1)S(1)} %maximum_bitcast_fusion, bf16[1,640,512]{2,1,0:T(8,128)(2,1)S(1)} %bitcast.62, bf16[1,640,512]{2,1,0:T(8,128)(2,1)S(1)} %bitcast.60, bf16[1,640,512]{2,1,0:T(8,128)(2,1)S(1)} %bitcast.58), kind=kLoop, calls=%fused_computation.5 | loop fusion | flops 3932160 | bytes 5242880 | tf_op jit(solution)/shard_map/stack | solution.py:48
  88.7 1.9 %collective-permute-start.4 = (bf16[4,640,512]{2,1,0:T(8,128)(2,1)}, bf16[4,640,512]{2,1,0:T(8,128)(2,1)}, u32[]{:S(2)}, u32[]{:S(2)}) collective-permute-start(bf16[4,640,512]{2,1,0:T(8,128)(2,1)} %pad_maximum_fusion), channel_id=1, source_target_pairs={{0,1},{1,0},{2,3},{3,2},{4,5},{5,4},{6,7},{7,6},{8,9},{9,8},{10,11... | collective-permute-start | bytes 7864328 | tf_op jit(solution)/shard_map/ppermute | solution.py:49
  90.8 1.8 pad_maximum_fusion.1
  92.6 1.6 gather_fusion.2
  94.2 1.6 gather_fusion.1
  95.8 0.6 compare_and_fusion.1
  96.5 3.1 %convolution_bitcast_fusion.2 = f32[640,256]{1,0:T(8,128)S(1)} fusion(bf16[4,640,512]{2,1,0:T(8,128)(2,1)} %collective-permute-done.4, bf16[4,512,256]{2,1,0:T(8,128)(2,1)} %gather_fusion.2, pred[4]{0:T(512)(128)(4,1)S(1)} %get-tuple-element.21), kind=kOutput, calls=%fused_computation.12 | convolution fusion | flops 671612928 | bytes 4325380 | tf_op jit(solution)/shard_map/dot_general | solution.py:159
  99.6 0.9 fusion.2
  100.6 1.9 %collective-permute-start.5 = (bf16[640,128]{1,0:T(8,128)(2,1)S(1)}, bf16[640,128]{1,0:T(8,128)(2,1)S(1)}, u32[]{:S(2)}, u32[]{:S(2)}) collective-permute-start(bf16[640,128]{1,0:T(8,128)(2,1)S(1)} %fusion.15), channel_id=1, source_target_pairs={{0,2},{1,3},{2,4},{3,5},{4,6},{5,7},{6,0},{7,1},{8,10},{9,11},{10,... | collective-permute-start | bytes 491528 | tf_op jit(solution)/shard_map/ppermute | solution.py:29
  102.6 3.3 %collective-permute-start.6 = (bf16[640,128]{1,0:T(8,128)(2,1)S(1)}, bf16[640,128]{1,0:T(8,128)(2,1)S(1)}, u32[]{:S(2)}, u32[]{:S(2)}) collective-permute-start(bf16[640,128]{1,0:T(8,128)(2,1)S(1)} %fusion.15), channel_id=1, source_target_pairs={{0,4},{1,5},{2,6},{3,7},{4,0},{5,1},{6,2},{7,3},{8,12},{9,13},{10,... | collective-permute-start | bytes 491528 | tf_op jit(solution)/shard_map/ppermute | solution.py:29
  105.8 2.6 %collective-permute-start.7 = (bf16[640,128]{1,0:T(8,128)(2,1)S(1)}, bf16[640,128]{1,0:T(8,128)(2,1)S(1)}, u32[]{:S(2)}, u32[]{:S(2)}) collective-permute-start(bf16[640,128]{1,0:T(8,128)(2,1)S(1)} %fusion.15), channel_id=1, source_target_pairs={{0,6},{1,7},{2,0},{3,1},{4,2},{5,3},{6,4},{7,5},{8,14},{9,15},{10,... | collective-permute-start | bytes 491528 | tf_op jit(solution)/shard_map/ppermute | solution.py:29
  108.5 1.0 collective-permute-done.5
  109.5 3.1 %collective-permute-done.6 = bf16[640,128]{1,0:T(8,128)(2,1)S(1)} collective-permute-done((bf16[640,128]{1,0:T(8,128)(2,1)S(1)}, bf16[640,128]{1,0:T(8,128)(2,1)S(1)}, u32[]{:S(2)}, u32[]{:S(2)}) %collective-permute-start.6) | collective-permute-done | bytes 163872 | tf_op jit(solution)/shard_map/ppermute | solution.py:29
  112.6 3.4 %collective-permute-done.7 = bf16[640,128]{1,0:T(8,128)(2,1)S(1)} collective-permute-done((bf16[640,128]{1,0:T(8,128)(2,1)S(1)}, bf16[640,128]{1,0:T(8,128)(2,1)S(1)}, u32[]{:S(2)}, u32[]{:S(2)}) %collective-permute-start.7) | collective-permute-done | bytes 163872 | tf_op jit(solution)/shard_map/ppermute | solution.py:29
  116.2 2.0 %collective-permute-start.8 = (bf16[4,640,128]{2,1,0:T(8,128)(2,1)S(1)}, bf16[4,640,128]{2,1,0:T(8,128)(2,1)S(1)}, u32[]{:S(2)}, u32[]{:S(2)}) collective-permute-start(bf16[4,640,128]{2,1,0:T(8,128)(2,1)S(1)} %pad_maximum_fusion.2), channel_id=1, source_target_pairs={{0,1},{1,0},{2,3},{3,2},{4,5},{5,4},{6,7},{7,6},{8,9},{9,8},{10,11... | collective-permute-start | bytes 1966088 | tf_op jit(solution)/shard_map/ppermute | solution.py:32
  118.1 0.5 compare_and_fusion
  118.7 0.6 pad_clamp_fusion.1
  119.3 0.7 gather_fusion.4
  120.0 0.7 compare_select_fusion.3
  120.6 0.6 pad_clamp_fusion.2
  121.2 1.5 gather_fusion.3
  122.7 1.2 convolution_bitcast_fusion
  124.0 2.5 %fusion.1 = bf16[640,512]{1,0:T(8,128)(2,1)} fusion(f32[640,512]{1,0:T(8,128)S(1)} %convolution_bitcast_fusion, bf16[4,128,512]{2,1,0:T(8,128)(2,1)} %gather_fusion.3, pred[4]{0:T(512)(128)(4,1)} %get-tuple-element.15, bf16[1,640,128]{2,1,0:T(8,128)(2,1)S(1)} %bitcast.71, bf16[1,640,128]{2,1,0:T(8,128)(2,1)S(1)} %bitcast.69, ...), kind=kOutput, calls=%fused_computation.11 | convolution fusion | flops 337444864 | bytes 3145732 | tf_op jit(solution)/shard_map/dot_general | solution.py:168
  126.5 8.5 %all-to-all-start.1 = ((bf16[16,40,512]{2,1,0:T(8,128)(2,1)}), bf16[16,40,512]{2,1,0:T(8,128)(2,1)S(1)}, u32[]{:S(2)}, u32[]{:S(2)}) async-start(bf16[16,40,512]{2,1,0:T(8,128)(2,1)} %bitcast.32), calls=%async_computation.1 | async-start | bytes 1310720 | tf_op jit(solution)/shard_map/all_to_all | solution.py:178
  135.6 0.1 gt.19
  136.0 0.1 reduce_sum.93
  136.7 34.0 %all-to-all-done.1 = bf16[16,40,512]{2,1,0:T(8,128)(2,1)S(1)} async-done(((bf16[16,40,512]{2,1,0:T(8,128)(2,1)}), bf16[16,40,512]{2,1,0:T(8,128)(2,1)S(1)}, u32[]{:S(2)}, u32[]{:S(2)}) %all-to-all-start.1) | async-done | bytes 655392 | tf_op jit(solution)/shard_map/all_to_all | solution.py:178
  170.7 1.2 gather_fusion
  172.0 0.9 multiply_reduce_fusion
  172.9 3.4 %collective-permute-start.9 = (bf16[128,512]{1,0:T(8,128)(2,1)S(1)}, bf16[128,512]{1,0:T(8,128)(2,1)S(1)}, u32[]{:S(2)}, u32[]{:S(2)}) collective-permute-start(bf16[128,512]{1,0:T(8,128)(2,1)S(1)} %multiply_reduce_fusion), channel_id=1, source_target_pairs={{0,128},{128,256},{256,384},{384,0},{1,129},{129,257},{257,385},{3... | collective-permute-start | bytes 393224 | tf_op jit(solution)/shard_map/ppermute | solution.py:10
  176.3 4.7 %collective-permute-done.9 = bf16[128,512]{1,0:T(8,128)(2,1)S(1)} collective-permute-done((bf16[128,512]{1,0:T(8,128)(2,1)S(1)}, bf16[128,512]{1,0:T(8,128)(2,1)S(1)}, u32[]{:S(2)}, u32[]{:S(2)}) %collective-permute-start.9) | collective-permute-done | bytes 131104 | tf_op jit(solution)/shard_map/ppermute | solution.py:10
  180.9 0.7 copy.39
  (64 shorter events, 2.4 us)
Async XLA Ops:
  0.0 119.3 %copy-start = (bf16[1,1,1024,512]{3,2,1,0:T(8,128)(2,1)S(1)}, bf16[1,1,1024,512]{3,2,1,0:T(8,128)(2,1)}, u32[]{:S(2)}) copy-start(bf16[1,1,1024,512]{3,2,1,0:T(8,128)(2,1)} %param.21) | copy-start | bytes 3145732
  4.2 0.6 copy-start.10
  57.4 31.2 %copy-start.1 = (bf16[16,40,512]{2,1,0:T(8,128)(2,1)}, bf16[16,40,512]{2,1,0:T(8,128)(2,1)S(1)}, u32[]{:S(2)}) copy-start(bf16[16,40,512]{2,1,0:T(8,128)(2,1)S(1)} %all_to_all.10) | copy-start | bytes 1966084
  57.4 15.6 %collective-permute-start = (bf16[640,512]{1,0:T(8,128)(2,1)S(1)}, bf16[640,512]{1,0:T(8,128)(2,1)S(1)}, u32[]{:S(2)}, u32[]{:S(2)}) collective-permute-start(bf16[640,512]{1,0:T(8,128)(2,1)S(1)} %bitcast.56), channel_id=1, source_target_pairs={{0,2},{1,3},{2,4},{3,5},{4,6},{5,7},{6,0},{7,1},{8,10},{9,11},{10,... | collective-permute-start | bytes 1966088 | tf_op jit(solution)/shard_map/ppermute | solution.py:42
  59.6 16.9 %collective-permute-start.1 = (bf16[640,512]{1,0:T(8,128)(2,1)S(1)}, bf16[640,512]{1,0:T(8,128)(2,1)S(1)}, u32[]{:S(2)}, u32[]{:S(2)}) collective-permute-start(bf16[640,512]{1,0:T(8,128)(2,1)S(1)} %bitcast.57), channel_id=1, source_target_pairs={{0,6},{1,7},{2,0},{3,1},{4,2},{5,3},{6,4},{7,5},{8,14},{9,15},{10,... | collective-permute-start | bytes 1966088 | tf_op jit(solution)/shard_map/ppermute | solution.py:43
  73.1 15.6 %copy-start.5 = (bf16[640,512]{1,0:T(8,128)(2,1)}, bf16[640,512]{1,0:T(8,128)(2,1)S(1)}, u32[]{:S(2)}) copy-start(bf16[640,512]{1,0:T(8,128)(2,1)S(1)} %collective-permute-done) | copy-start | bytes 1966084
  73.1 9.0 %collective-permute-start.2 = (bf16[320,512]{1,0:T(8,128)(2,1)S(1)}, bf16[320,512]{1,0:T(8,128)(2,1)S(1)}, u32[]{:S(2)}, u32[]{:S(2)}) collective-permute-start(bf16[320,512]{1,0:T(8,128)(2,1)S(1)} %slice.26), channel_id=1, source_target_pairs={{0,2},{1,3},{2,4},{3,5},{4,6},{5,7},{6,0},{7,1},{8,10},{9,11},{10,... | collective-permute-start | bytes 983048 | tf_op jit(solution)/shard_map/ppermute | solution.py:45
  76.5 12.1 %copy-start.7 = (bf16[640,512]{1,0:T(8,128)(2,1)}, bf16[640,512]{1,0:T(8,128)(2,1)S(1)}, u32[]{:S(2)}) copy-start(bf16[640,512]{1,0:T(8,128)(2,1)S(1)} %collective-permute-done.1) | copy-start | bytes 1966084
  76.6 10.2 %collective-permute-start.3 = (bf16[320,512]{1,0:T(8,128)(2,1)S(1)}, bf16[320,512]{1,0:T(8,128)(2,1)S(1)}, u32[]{:S(2)}, u32[]{:S(2)}) collective-permute-start(bf16[320,512]{1,0:T(8,128)(2,1)S(1)} %slice.27), channel_id=1, source_target_pairs={{0,6},{1,7},{2,0},{3,1},{4,2},{5,3},{6,4},{7,5},{8,14},{9,15},{10,... | collective-permute-start | bytes 983048 | tf_op jit(solution)/shard_map/ppermute | solution.py:46
  86.8 1.9 %copy-start.3 = (bf16[1,640,512]{2,1,0:T(8,128)(2,1)}, bf16[1,640,512]{2,1,0:T(8,128)(2,1)S(1)}, u32[]{:S(2)}) copy-start(bf16[1,640,512]{2,1,0:T(8,128)(2,1)S(1)} %maximum_bitcast_fusion) | copy-start | bytes 1966084
  88.7 7.8 %collective-permute-start.4 = (bf16[4,640,512]{2,1,0:T(8,128)(2,1)}, bf16[4,640,512]{2,1,0:T(8,128)(2,1)}, u32[]{:S(2)}, u32[]{:S(2)}) collective-permute-start(bf16[4,640,512]{2,1,0:T(8,128)(2,1)} %pad_maximum_fusion), channel_id=1, source_target_pairs={{0,1},{1,0},{2,3},{3,2},{4,5},{5,4},{6,7},{7,6},{8,9},{9,8},{10,11... | collective-permute-start | bytes 7864328 | tf_op jit(solution)/shard_map/ppermute | solution.py:49
  96.4 21.7 %copy-start.15 = (s32[4]{0:T(128)}, s32[4]{0:T(128)S(1)}, u32[]{:S(2)}) copy-start(s32[4]{0:T(128)S(1)} %get-tuple-element.16) | copy-start | bytes 52
  96.4 3.1 %copy-start.2 = (bf16[16,40,512]{2,1,0:T(8,128)(2,1)S(1)}, bf16[16,40,512]{2,1,0:T(8,128)(2,1)}, u32[]{:S(2)}) copy-start(bf16[16,40,512]{2,1,0:T(8,128)(2,1)} %copy-done.1) | copy-start | bytes 1966084
  96.4 3.1 %copy-start.4 = (bf16[1,640,512]{2,1,0:T(8,128)(2,1)S(1)}, bf16[1,640,512]{2,1,0:T(8,128)(2,1)}, u32[]{:S(2)}) copy-start(bf16[1,640,512]{2,1,0:T(8,128)(2,1)} %copy-done.3) | copy-start | bytes 1966084
  96.4 3.1 %copy-start.6 = (bf16[640,512]{1,0:T(8,128)(2,1)S(1)}, bf16[640,512]{1,0:T(8,128)(2,1)}, u32[]{:S(2)}) copy-start(bf16[640,512]{1,0:T(8,128)(2,1)} %copy-done.5) | copy-start | bytes 1966084
  96.4 3.1 %copy-start.8 = (bf16[640,512]{1,0:T(8,128)(2,1)S(1)}, bf16[640,512]{1,0:T(8,128)(2,1)}, u32[]{:S(2)}) copy-start(bf16[640,512]{1,0:T(8,128)(2,1)} %copy-done.7) | copy-start | bytes 1966084
  96.4 3.1 %copy-start.9 = (bf16[4,512,256]{2,1,0:T(8,128)(2,1)S(1)}, bf16[4,512,256]{2,1,0:T(8,128)(2,1)}, u32[]{:S(2)}) copy-start(bf16[4,512,256]{2,1,0:T(8,128)(2,1)} %gather_fusion.1) | copy-start | bytes 3145732
  100.6 8.9 %collective-permute-start.5 = (bf16[640,128]{1,0:T(8,128)(2,1)S(1)}, bf16[640,128]{1,0:T(8,128)(2,1)S(1)}, u32[]{:S(2)}, u32[]{:S(2)}) collective-permute-start(bf16[640,128]{1,0:T(8,128)(2,1)S(1)} %fusion.15), channel_id=1, source_target_pairs={{0,2},{1,3},{2,4},{3,5},{4,6},{5,7},{6,0},{7,1},{8,10},{9,11},{10,... | collective-permute-start | bytes 491528 | tf_op jit(solution)/shard_map/ppermute | solution.py:29
  102.6 10.1 %collective-permute-start.6 = (bf16[640,128]{1,0:T(8,128)(2,1)S(1)}, bf16[640,128]{1,0:T(8,128)(2,1)S(1)}, u32[]{:S(2)}, u32[]{:S(2)}) collective-permute-start(bf16[640,128]{1,0:T(8,128)(2,1)S(1)} %fusion.15), channel_id=1, source_target_pairs={{0,4},{1,5},{2,6},{3,7},{4,0},{5,1},{6,2},{7,3},{8,12},{9,13},{10,... | collective-permute-start | bytes 491528 | tf_op jit(solution)/shard_map/ppermute | solution.py:29
  105.8 10.2 %collective-permute-start.7 = (bf16[640,128]{1,0:T(8,128)(2,1)S(1)}, bf16[640,128]{1,0:T(8,128)(2,1)S(1)}, u32[]{:S(2)}, u32[]{:S(2)}) collective-permute-start(bf16[640,128]{1,0:T(8,128)(2,1)S(1)} %fusion.15), channel_id=1, source_target_pairs={{0,6},{1,7},{2,0},{3,1},{4,2},{5,3},{6,4},{7,5},{8,14},{9,15},{10,... | collective-permute-start | bytes 491528 | tf_op jit(solution)/shard_map/ppermute | solution.py:29
  116.2 6.6 %collective-permute-start.8 = (bf16[4,640,128]{2,1,0:T(8,128)(2,1)S(1)}, bf16[4,640,128]{2,1,0:T(8,128)(2,1)S(1)}, u32[]{:S(2)}, u32[]{:S(2)}) collective-permute-start(bf16[4,640,128]{2,1,0:T(8,128)(2,1)S(1)} %pad_maximum_fusion.2), channel_id=1, source_target_pairs={{0,1},{1,0},{2,3},{3,2},{4,5},{5,4},{6,7},{7,6},{8,9},{9,8},{10,11... | collective-permute-start | bytes 1966088 | tf_op jit(solution)/shard_map/ppermute | solution.py:32
  123.9 11.0 %copy-start.12 = (s32[1,128,2]{1,2,0:T(2,128)S(1)}, s32[1,128,2]{1,2,0:T(2,128)}, u32[]{:S(2)}) copy-start(s32[1,128,2]{1,2,0:T(2,128)} %param.14) | copy-start | bytes 3076
  123.9 11.1 %copy-start.11 = (s32[128,16]{0,1:T(8,128)S(1)}, s32[128,16]{0,1:T(8,128)}, u32[]{:S(2)}) copy-start(s32[128,16]{0,1:T(8,128)} %copy-done.10) | copy-start | bytes 24580
  124.0 11.1 %copy-start.13 = (s32[1,16]{1,0:T(1,128)S(1)}, s32[1,16]{1,0:T(1,128)}, u32[]{:S(2)}) copy-start(s32[1,16]{1,0:T(1,128)} %param.18) | copy-start | bytes 196
  124.0 12.6 %copy-start.14 = (f32[1,128,2]{1,2,0:T(2,128)S(1)}, f32[1,128,2]{1,2,0:T(2,128)}, u32[]{:S(2)}) copy-start(f32[1,128,2]{1,2,0:T(2,128)} %param.15) | copy-start | bytes 3076
  126.5 44.3 %all-to-all-start.1 = ((bf16[16,40,512]{2,1,0:T(8,128)(2,1)}), bf16[16,40,512]{2,1,0:T(8,128)(2,1)S(1)}, u32[]{:S(2)}, u32[]{:S(2)}) async-start(bf16[16,40,512]{2,1,0:T(8,128)(2,1)} %bitcast.32), calls=%async_computation.1 | async-start | bytes 1310720 | tf_op jit(solution)/shard_map/all_to_all | solution.py:178
  172.9 8.1 %collective-permute-start.9 = (bf16[128,512]{1,0:T(8,128)(2,1)S(1)}, bf16[128,512]{1,0:T(8,128)(2,1)S(1)}, u32[]{:S(2)}, u32[]{:S(2)}) collective-permute-start(bf16[128,512]{1,0:T(8,128)(2,1)S(1)} %multiply_reduce_fusion), channel_id=1, source_target_pairs={{0,128},{128,256},{256,384},{384,0},{1,129},{129,257},{257,385},{3... | collective-permute-start | bytes 393224 | tf_op jit(solution)/shard_map/ppermute | solution.py:10

commit v16 on v14

--- a/solution.py
+++ b/solution.py
@@ -170,12 +170,14 @@
     target = jnp.where(row_kept > 0, chosen, row_other)
     slot_pick = jnp.where(row_kept > 0, row_main, slot_depth + row_spill)
     row_index = target * (2 * slot_depth) + slot_pick
-    picked = jnp.take(returned.reshape(-1, out_width), row_index.reshape(-1), axis=0).reshape(
-        tok_rows, top_count, out_width
+    flat_returned = returned.reshape(-1, out_width)
+    row_pick = (
+        row_index[:, :, None] == jnp.arange(flat_returned.shape[0], dtype=jnp.int32)[None, None, :]
+    ).astype(flat_returned.dtype)
+    picked = jnp.einsum(
+        "tks,sf->tkf", row_pick, flat_returned, preferred_element_type=jnp.float32
     )
-    combined = jnp.sum(route_weight[0][:, :, None] * picked.astype(jnp.float32), axis=1).astype(
-        jnp.bfloat16
-    )
+    combined = jnp.sum(route_weight[0][:, :, None] * picked, axis=1).astype(jnp.bfloat16)
     forwarded = passed_along(combined, "section", 1)
     return forwarded[None]
 

time: 178 us -> 177 us (level)
  local copies, waits for them, and re-layouts: 9.27 us -> 6.47 us
  transfers between devices with their start and end apart: 11 -> 11, of which waited for: 8 -> 8; matrix products, arithmetic and copies ran while one was open for 5% -> 4% of each run, Pallas kernels for 0% -> 0%
where the time goes in v16:
time: 177 us; the launch traced here: 176 us
  waiting for transfers between devices  65.2 us (37%)
  blocking collectives  51.4 us (29%)
  starting transfers between devices  35.2 us (20%)
  matrix products  8.85 us (5%)
  other arithmetic  8.32 us (5%)
  local copies, waits for them, and re-layouts  6.47 us (4%)
    all_to_all x1, blocking collectives, local(): lax.all_to_all(outgoing, 'expert', split_axis=0, concat_axis=0, tiled=True)  51.4 us
    all_to_all x1, waiting for transfers between devices, local(): lax.all_to_all(produced, 'expert', split_axis=0, concat_axis=0, tiled=True)  35.5 us
    ppermute x1, waiting for transfers between devices, relayed_chips_then_core(): from_below = lax.ppermute(value, axis, up_pairs)  9.78 us
    all_to_all x1, starting transfers between devices, local(): lax.all_to_all(produced, 'expert', split_axis=0, concat_axis=0, tiled=True)  8.51 us
    ppermute x3, starting transfers between devices, chips_then_core(): pieces.append(lax.ppermute(value, axis, pairs))  7.76 us
    ppermute x3, waiting for transfers between devices, chips_then_core(): pieces.append(lax.ppermute(value, axis, pairs))  7.54 us
    ppermute x1, waiting for transfers between devices, relayed_chips_then_core(): far_high = lax.ppermute(from_above[half:], axis, down_pairs)  4.68 us
    ppermute x1, waiting for transfers between devices, passed_along(): return lax.ppermute(value, axis, pairs)  4.67 us
  transfers between devices with their start and end apart: 11, of which 8 were waited for; matrix products, arithmetic and copies ran while one was open for 4% of the time, Pallas kernels for 0%

profile of v16, /device:TPU:24, one launch (start us, length us, event | category | flops | bytes accessed | tf_op | source)
XLA Modules:
  0.0 176.0 jit_solution(17485451895975957702)
XLA Ops:
  0.0 0.8 convert_reduce_fusion
  0.8 0.1 copy.13
  0.9 0.7 fusion.28
  1.6 1.2 multiply_reduce_fusion
  2.9 0.2 reduce_window_sum.32
  3.1 0.7 fusion.29
  3.9 0.2 reduce_window_sum.31
  4.2 0.1 multiply_reduce_fusion.3
  4.4 1.2 convolution_convert_fusion
  5.6 51.4 %all_to_all.10 = bf16[16,40,512]{2,1,0:T(8,128)(2,1)S(1)} all-to-all(bf16[16,40,512]{2,1,0:T(8,128)(2,1)S(1)} %convolution_convert_fusion), channel_id=1, replica_groups=mesh['section'=4,'expert'=16,'rep'=8] {'expert'}, dimensions={0} | all-to-all | bytes 1310720 | tf_op jit(solution)/shard_map/all_to_all | solution.py:133
  57.0 2.1 %collective-permute-start = (bf16[640,512]{1,0:T(8,128)(2,1)S(1)}, bf16[640,512]{1,0:T(8,128)(2,1)S(1)}, u32[]{:S(2)}, u32[]{:S(2)}) collective-permute-start(bf16[640,512]{1,0:T(8,128)(2,1)S(1)} %bitcast.59), channel_id=1, source_target_pairs={{0,2},{1,3},{2,4},{3,5},{4,6},{5,7},{6,0},{7,1},{8,10},{9,11},{10,... | collective-permute-start | bytes 1966088 | tf_op jit(solution)/shard_map/ppermute | solution.py:42
  59.2 3.7 %collective-permute-start.1 = (bf16[640,512]{1,0:T(8,128)(2,1)S(1)}, bf16[640,512]{1,0:T(8,128)(2,1)S(1)}, u32[]{:S(2)}, u32[]{:S(2)}) collective-permute-start(bf16[640,512]{1,0:T(8,128)(2,1)S(1)} %bitcast.60), channel_id=1, source_target_pairs={{0,6},{1,7},{2,0},{3,1},{4,2},{5,3},{6,4},{7,5},{8,14},{9,15},{10,... | collective-permute-start | bytes 1966088 | tf_op jit(solution)/shard_map/ppermute | solution.py:43
  62.9 9.8 %collective-permute-done = bf16[640,512]{1,0:T(8,128)(2,1)S(1)} collective-permute-done((bf16[640,512]{1,0:T(8,128)(2,1)S(1)}, bf16[640,512]{1,0:T(8,128)(2,1)S(1)}, u32[]{:S(2)}, u32[]{:S(2)}) %collective-permute-start) | collective-permute-done | bytes 655392 | tf_op jit(solution)/shard_map/ppermute | solution.py:42
  72.7 3.4 %collective-permute-start.2 = (bf16[320,512]{1,0:T(8,128)(2,1)S(1)}, bf16[320,512]{1,0:T(8,128)(2,1)S(1)}, u32[]{:S(2)}, u32[]{:S(2)}) collective-permute-start(bf16[320,512]{1,0:T(8,128)(2,1)S(1)} %slice.24), channel_id=1, source_target_pairs={{0,2},{1,3},{2,4},{3,5},{4,6},{5,7},{6,0},{7,1},{8,10},{9,11},{10,... | collective-permute-start | bytes 983048 | tf_op jit(solution)/shard_map/ppermute | solution.py:45
  76.2 2.4 %collective-permute-start.3 = (bf16[320,512]{1,0:T(8,128)(2,1)S(1)}, bf16[320,512]{1,0:T(8,128)(2,1)S(1)}, u32[]{:S(2)}, u32[]{:S(2)}) collective-permute-start(bf16[320,512]{1,0:T(8,128)(2,1)S(1)} %slice.25), channel_id=1, source_target_pairs={{0,6},{1,7},{2,0},{3,1},{4,2},{5,3},{6,4},{7,5},{8,14},{9,15},{10,... | collective-permute-start | bytes 983048 | tf_op jit(solution)/shard_map/ppermute | solution.py:46
  78.6 3.1 %collective-permute-done.2 = bf16[320,512]{1,0:T(8,128)(2,1)S(1)} collective-permute-done((bf16[320,512]{1,0:T(8,128)(2,1)S(1)}, bf16[320,512]{1,0:T(8,128)(2,1)S(1)}, u32[]{:S(2)}, u32[]{:S(2)}) %collective-permute-start.2) | collective-permute-done | bytes 327712 | tf_op jit(solution)/shard_map/ppermute | solution.py:45
  81.7 4.7 %collective-permute-done.3 = bf16[320,512]{1,0:T(8,128)(2,1)S(1)} collective-permute-done((bf16[320,512]{1,0:T(8,128)(2,1)S(1)}, bf16[320,512]{1,0:T(8,128)(2,1)S(1)}, u32[]{:S(2)}, u32[]{:S(2)}) %collective-permute-start.3) | collective-permute-done | bytes 327712 | tf_op jit(solution)/shard_map/ppermute | solution.py:46
  86.4 1.8 %pad_maximum_fusion = bf16[4,640,512]{2,1,0:T(8,128)(2,1)} fusion(bf16[1,640,512]{2,1,0:T(8,128)(2,1)S(1)} %maximum_bitcast_fusion, bf16[1,640,512]{2,1,0:T(8,128)(2,1)S(1)} %bitcast.66, bf16[1,640,512]{2,1,0:T(8,128)(2,1)S(1)} %bitcast.64, bf16[1,640,512]{2,1,0:T(8,128)(2,1)S(1)} %bitcast.61), kind=kLoop, calls=%fused_computation.4 | loop fusion | flops 3932160 | bytes 5242880 | tf_op jit(solution)/shard_map/stack | solution.py:48
  88.2 1.9 %collective-permute-start.4 = (bf16[4,640,512]{2,1,0:T(8,128)(2,1)}, bf16[4,640,512]{2,1,0:T(8,128)(2,1)}, u32[]{:S(2)}, u32[]{:S(2)}) collective-permute-start(bf16[4,640,512]{2,1,0:T(8,128)(2,1)} %pad_maximum_fusion), channel_id=1, source_target_pairs={{0,1},{1,0},{2,3},{3,2},{4,5},{5,4},{6,7},{7,6},{8,9},{9,8},{10,11... | collective-permute-start | bytes 7864328 | tf_op jit(solution)/shard_map/ppermute | solution.py:49
  90.2 0.1 compare_and_fusion.3
  90.4 1.8 %pad_maximum_fusion.1 = bf16[8,512,256]{2,1,0:T(8,128)(2,1)S(1)} fusion(bf16[8,512,128]{2,1,0:T(8,128)(2,1)} %bitcast.68, bf16[8,512,128]{2,1,0:T(8,128)(2,1)} %bitcast.69), kind=kLoop, calls=%fused_computation.5 | loop fusion | flops 4194304 | bytes 4194304 | tf_op jit(solution)/shard_map/concatenate | solution.py:137
  92.1 1.6 gather_fusion.1
  93.8 1.6 gather_fusion
  95.4 0.1 compare_and_fusion.1
  95.5 3.1 %convolution_bitcast_fusion.2 = f32[640,256]{1,0:T(8,128)S(1)} fusion(bf16[4,640,512]{2,1,0:T(8,128)(2,1)} %collective-permute-done.4, bf16[4,512,256]{2,1,0:T(8,128)(2,1)} %gather_fusion.1, pred[4]{0:T(512)(128)(4,1)S(1)} %get-tuple-element.21), kind=kOutput, calls=%fused_computation.11 | convolution fusion | flops 671612928 | bytes 4325380 | tf_op jit(solution)/shard_map/dot_general | solution.py:145
  98.7 0.9 fusion.2
  99.6 0.1 fusion.18
  99.7 1.9 %collective-permute-start.5 = (bf16[640,128]{1,0:T(8,128)(2,1)S(1)}, bf16[640,128]{1,0:T(8,128)(2,1)S(1)}, u32[]{:S(2)}, u32[]{:S(2)}) collective-permute-start(bf16[640,128]{1,0:T(8,128)(2,1)S(1)} %fusion.18), channel_id=1, source_target_pairs={{0,2},{1,3},{2,4},{3,5},{4,6},{5,7},{6,0},{7,1},{8,10},{9,11},{10,... | collective-permute-start | bytes 491528 | tf_op jit(solution)/shard_map/ppermute | solution.py:29
  101.7 3.3 %collective-permute-start.6 = (bf16[640,128]{1,0:T(8,128)(2,1)S(1)}, bf16[640,128]{1,0:T(8,128)(2,1)S(1)}, u32[]{:S(2)}, u32[]{:S(2)}) collective-permute-start(bf16[640,128]{1,0:T(8,128)(2,1)S(1)} %fusion.18), channel_id=1, source_target_pairs={{0,4},{1,5},{2,6},{3,7},{4,0},{5,1},{6,2},{7,3},{8,12},{9,13},{10,... | collective-permute-start | bytes 491528 | tf_op jit(solution)/shard_map/ppermute | solution.py:29
  104.9 2.6 %collective-permute-start.7 = (bf16[640,128]{1,0:T(8,128)(2,1)S(1)}, bf16[640,128]{1,0:T(8,128)(2,1)S(1)}, u32[]{:S(2)}, u32[]{:S(2)}) collective-permute-start(bf16[640,128]{1,0:T(8,128)(2,1)S(1)} %fusion.18), channel_id=1, source_target_pairs={{0,6},{1,7},{2,0},{3,1},{4,2},{5,3},{6,4},{7,5},{8,14},{9,15},{10,... | collective-permute-start | bytes 491528 | tf_op jit(solution)/shard_map/ppermute | solution.py:29
  107.5 0.1 fusion.40
  107.6 1.0 collective-permute-done.5
  108.6 3.1 %collective-permute-done.6 = bf16[640,128]{1,0:T(8,128)(2,1)S(1)} collective-permute-done((bf16[640,128]{1,0:T(8,128)(2,1)S(1)}, bf16[640,128]{1,0:T(8,128)(2,1)S(1)}, u32[]{:S(2)}, u32[]{:S(2)}) %collective-permute-start.6) | collective-permute-done | bytes 163872 | tf_op jit(solution)/shard_map/ppermute | solution.py:29
  111.7 3.4 %collective-permute-done.7 = bf16[640,128]{1,0:T(8,128)(2,1)S(1)} collective-permute-done((bf16[640,128]{1,0:T(8,128)(2,1)S(1)}, bf16[640,128]{1,0:T(8,128)(2,1)S(1)}, u32[]{:S(2)}, u32[]{:S(2)}) %collective-permute-start.7) | collective-permute-done | bytes 163872 | tf_op jit(solution)/shard_map/ppermute | solution.py:29
  115.2 0.1 pad_maximum_fusion.2
  115.3 2.0 %collective-permute-start.8 = (bf16[4,640,128]{2,1,0:T(8,128)(2,1)S(1)}, bf16[4,640,128]{2,1,0:T(8,128)(2,1)S(1)}, u32[]{:S(2)}, u32[]{:S(2)}) collective-permute-start(bf16[4,640,128]{2,1,0:T(8,128)(2,1)S(1)} %pad_maximum_fusion.2), channel_id=1, source_target_pairs={{0,1},{1,0},{2,3},{3,2},{4,5},{5,4},{6,7},{7,6},{8,9},{9,8},{10,11... | collective-permute-start | bytes 1966088 | tf_op jit(solution)/shard_map/ppermute | solution.py:32
  117.3 0.6 gather_fusion.3
  117.9 1.4 gather_fusion.2
  119.3 0.6 convolution_bitcast_fusion
  119.9 2.6 %fusion.1 = bf16[640,512]{1,0:T(8,128)(2,1)} fusion(f32[640,512]{1,0:T(8,128)S(1)} %convolution_bitcast_fusion, bf16[4,128,512]{2,1,0:T(8,128)(2,1)} %gather_fusion.2, pred[4]{0:T(512)(128)(4,1)S(1)} %get-tuple-element.15, bf16[1,640,128]{2,1,0:T(8,128)(2,1)} %bitcast.76, bf16[1,640,128]{2,1,0:T(8,128)(2,1)} %bitcast.74, ...), kind=kOutput, calls=%fused_computation.10 | convolution fusion | flops 337444864 | bytes 3145732 | tf_op jit(solution)/shard_map/dot_general | solution.py:154
  122.5 8.5 %all-to-all-start.1 = ((bf16[16,40,512]{2,1,0:T(8,128)(2,1)}), bf16[16,40,512]{2,1,0:T(8,128)(2,1)S(1)}, u32[]{:S(2)}, u32[]{:S(2)}) async-start(bf16[16,40,512]{2,1,0:T(8,128)(2,1)} %bitcast.32), calls=%async_computation.1 | async-start | bytes 1310720 | tf_op jit(solution)/shard_map/all_to_all | solution.py:164
  131.2 0.1 copy.18
  131.3 0.1 select_reduce_fusion.3
  131.4 35.5 %all-to-all-done.1 = bf16[16,40,512]{2,1,0:T(8,128)(2,1)S(1)} async-done(((bf16[16,40,512]{2,1,0:T(8,128)(2,1)}), bf16[16,40,512]{2,1,0:T(8,128)(2,1)S(1)}, u32[]{:S(2)}, u32[]{:S(2)}) %all-to-all-start.1) | async-done | bytes 655392 | tf_op jit(solution)/shard_map/all_to_all | solution.py:164
  166.8 0.4 fusion.3
  167.2 3.4 %collective-permute-start.9 = (bf16[128,512]{1,0:T(8,128)(2,1)S(1)}, bf16[128,512]{1,0:T(8,128)(2,1)S(1)}, u32[]{:S(2)}, u32[]{:S(2)}) collective-permute-start(bf16[128,512]{1,0:T(8,128)(2,1)S(1)} %fusion.3), channel_id=1, source_target_pairs={{0,128},{128,256},{256,384},{384,0},{1,129},{129,257},{257,385},{3... | collective-permute-start | bytes 393224 | tf_op jit(solution)/shard_map/ppermute | solution.py:10
  170.6 4.7 %collective-permute-done.9 = bf16[128,512]{1,0:T(8,128)(2,1)S(1)} collective-permute-done((bf16[128,512]{1,0:T(8,128)(2,1)S(1)}, bf16[128,512]{1,0:T(8,128)(2,1)S(1)}, u32[]{:S(2)}, u32[]{:S(2)}) %collective-permute-start.9) | collective-permute-done | bytes 131104 | tf_op jit(solution)/shard_map/ppermute | solution.py:10
  175.3 0.7 copy.24
  (56 shorter events, 0.7 us)
Async XLA Ops:
  0.0 117.3 %copy-start = (bf16[1,1,1024,512]{3,2,1,0:T(8,128)(2,1)S(1)}, bf16[1,1,1024,512]{3,2,1,0:T(8,128)(2,1)}, u32[]{:S(2)}) copy-start(bf16[1,1,1024,512]{3,2,1,0:T(8,128)(2,1)} %param.21) | copy-start | bytes 3145732
  57.0 31.2 %copy-start.1 = (bf16[16,40,512]{2,1,0:T(8,128)(2,1)}, bf16[16,40,512]{2,1,0:T(8,128)(2,1)S(1)}, u32[]{:S(2)}) copy-start(bf16[16,40,512]{2,1,0:T(8,128)(2,1)S(1)} %all_to_all.10) | copy-start | bytes 1966084
  57.0 15.6 %collective-permute-start = (bf16[640,512]{1,0:T(8,128)(2,1)S(1)}, bf16[640,512]{1,0:T(8,128)(2,1)S(1)}, u32[]{:S(2)}, u32[]{:S(2)}) collective-permute-start(bf16[640,512]{1,0:T(8,128)(2,1)S(1)} %bitcast.59), channel_id=1, source_target_pairs={{0,2},{1,3},{2,4},{3,5},{4,6},{5,7},{6,0},{7,1},{8,10},{9,11},{10,... | collective-permute-start | bytes 1966088 | tf_op jit(solution)/shard_map/ppermute | solution.py:42
  59.2 16.9 %collective-permute-start.1 = (bf16[640,512]{1,0:T(8,128)(2,1)S(1)}, bf16[640,512]{1,0:T(8,128)(2,1)S(1)}, u32[]{:S(2)}, u32[]{:S(2)}) collective-permute-start(bf16[640,512]{1,0:T(8,128)(2,1)S(1)} %bitcast.60), channel_id=1, source_target_pairs={{0,6},{1,7},{2,0},{3,1},{4,2},{5,3},{6,4},{7,5},{8,14},{9,15},{10,... | collective-permute-start | bytes 1966088 | tf_op jit(solution)/shard_map/ppermute | solution.py:43
  72.7 15.6 %copy-start.5 = (bf16[640,512]{1,0:T(8,128)(2,1)}, bf16[640,512]{1,0:T(8,128)(2,1)S(1)}, u32[]{:S(2)}) copy-start(bf16[640,512]{1,0:T(8,128)(2,1)S(1)} %collective-permute-done) | copy-start | bytes 1966084
  72.7 9.0 %collective-permute-start.2 = (bf16[320,512]{1,0:T(8,128)(2,1)S(1)}, bf16[320,512]{1,0:T(8,128)(2,1)S(1)}, u32[]{:S(2)}, u32[]{:S(2)}) collective-permute-start(bf16[320,512]{1,0:T(8,128)(2,1)S(1)} %slice.24), channel_id=1, source_target_pairs={{0,2},{1,3},{2,4},{3,5},{4,6},{5,7},{6,0},{7,1},{8,10},{9,11},{10,... | collective-permute-start | bytes 983048 | tf_op jit(solution)/shard_map/ppermute | solution.py:45
  76.1 12.1 %copy-start.7 = (bf16[640,512]{1,0:T(8,128)(2,1)}, bf16[640,512]{1,0:T(8,128)(2,1)S(1)}, u32[]{:S(2)}) copy-start(bf16[640,512]{1,0:T(8,128)(2,1)S(1)} %collective-permute-done.1) | copy-start | bytes 1966084
  76.2 10.2 %collective-permute-start.3 = (bf16[320,512]{1,0:T(8,128)(2,1)S(1)}, bf16[320,512]{1,0:T(8,128)(2,1)S(1)}, u32[]{:S(2)}, u32[]{:S(2)}) collective-permute-start(bf16[320,512]{1,0:T(8,128)(2,1)S(1)} %slice.25), channel_id=1, source_target_pairs={{0,6},{1,7},{2,0},{3,1},{4,2},{5,3},{6,4},{7,5},{8,14},{9,15},{10,... | collective-permute-start | bytes 983048 | tf_op jit(solution)/shard_map/ppermute | solution.py:46
  86.4 1.9 %copy-start.3 = (bf16[1,640,512]{2,1,0:T(8,128)(2,1)}, bf16[1,640,512]{2,1,0:T(8,128)(2,1)S(1)}, u32[]{:S(2)}) copy-start(bf16[1,640,512]{2,1,0:T(8,128)(2,1)S(1)} %maximum_bitcast_fusion) | copy-start | bytes 1966084
  88.2 7.2 %collective-permute-start.4 = (bf16[4,640,512]{2,1,0:T(8,128)(2,1)}, bf16[4,640,512]{2,1,0:T(8,128)(2,1)}, u32[]{:S(2)}, u32[]{:S(2)}) collective-permute-start(bf16[4,640,512]{2,1,0:T(8,128)(2,1)} %pad_maximum_fusion), channel_id=1, source_target_pairs={{0,1},{1,0},{2,3},{3,2},{4,5},{5,4},{6,7},{7,6},{8,9},{9,8},{10,11... | collective-permute-start | bytes 7864328 | tf_op jit(solution)/shard_map/ppermute | solution.py:49
  95.5 3.1 %copy-start.2 = (bf16[16,40,512]{2,1,0:T(8,128)(2,1)S(1)}, bf16[16,40,512]{2,1,0:T(8,128)(2,1)}, u32[]{:S(2)}) copy-start(bf16[16,40,512]{2,1,0:T(8,128)(2,1)} %copy-done.1) | copy-start | bytes 1966084
  95.5 3.1 %copy-start.4 = (bf16[1,640,512]{2,1,0:T(8,128)(2,1)S(1)}, bf16[1,640,512]{2,1,0:T(8,128)(2,1)}, u32[]{:S(2)}) copy-start(bf16[1,640,512]{2,1,0:T(8,128)(2,1)} %copy-done.3) | copy-start | bytes 1966084
  95.5 3.1 %copy-start.6 = (bf16[640,512]{1,0:T(8,128)(2,1)S(1)}, bf16[640,512]{1,0:T(8,128)(2,1)}, u32[]{:S(2)}) copy-start(bf16[640,512]{1,0:T(8,128)(2,1)} %copy-done.5) | copy-start | bytes 1966084
  95.5 3.1 %copy-start.8 = (bf16[640,512]{1,0:T(8,128)(2,1)S(1)}, bf16[640,512]{1,0:T(8,128)(2,1)}, u32[]{:S(2)}) copy-start(bf16[640,512]{1,0:T(8,128)(2,1)} %copy-done.7) | copy-start | bytes 1966084
  95.5 3.1 %copy-start.9 = (bf16[4,512,256]{2,1,0:T(8,128)(2,1)S(1)}, bf16[4,512,256]{2,1,0:T(8,128)(2,1)}, u32[]{:S(2)}) copy-start(bf16[4,512,256]{2,1,0:T(8,128)(2,1)} %gather_fusion) | copy-start | bytes 3145732
  99.7 8.9 %collective-permute-start.5 = (bf16[640,128]{1,0:T(8,128)(2,1)S(1)}, bf16[640,128]{1,0:T(8,128)(2,1)S(1)}, u32[]{:S(2)}, u32[]{:S(2)}) collective-permute-start(bf16[640,128]{1,0:T(8,128)(2,1)S(1)} %fusion.18), channel_id=1, source_target_pairs={{0,2},{1,3},{2,4},{3,5},{4,6},{5,7},{6,0},{7,1},{8,10},{9,11},{10,... | collective-permute-start | bytes 491528 | tf_op jit(solution)/shard_map/ppermute | solution.py:29
  101.7 10.1 %collective-permute-start.6 = (bf16[640,128]{1,0:T(8,128)(2,1)S(1)}, bf16[640,128]{1,0:T(8,128)(2,1)S(1)}, u32[]{:S(2)}, u32[]{:S(2)}) collective-permute-start(bf16[640,128]{1,0:T(8,128)(2,1)S(1)} %fusion.18), channel_id=1, source_target_pairs={{0,4},{1,5},{2,6},{3,7},{4,0},{5,1},{6,2},{7,3},{8,12},{9,13},{10,... | collective-permute-start | bytes 491528 | tf_op jit(solution)/shard_map/ppermute | solution.py:29
  104.9 10.2 %collective-permute-start.7 = (bf16[640,128]{1,0:T(8,128)(2,1)S(1)}, bf16[640,128]{1,0:T(8,128)(2,1)S(1)}, u32[]{:S(2)}, u32[]{:S(2)}) collective-permute-start(bf16[640,128]{1,0:T(8,128)(2,1)S(1)} %fusion.18), channel_id=1, source_target_pairs={{0,6},{1,7},{2,0},{3,1},{4,2},{5,3},{6,4},{7,5},{8,14},{9,15},{10,... | collective-permute-start | bytes 491528 | tf_op jit(solution)/shard_map/ppermute | solution.py:29
  111.7 5.5 %copy-start.10 = (bf16[640,128]{1,0:T(8,128)(2,1)}, bf16[640,128]{1,0:T(8,128)(2,1)S(1)}, u32[]{:S(2)}) copy-start(bf16[640,128]{1,0:T(8,128)(2,1)S(1)} %collective-permute-done.6) | copy-start | bytes 491524
  115.2 2.1 %copy-start.11 = (bf16[640,128]{1,0:T(8,128)(2,1)}, bf16[640,128]{1,0:T(8,128)(2,1)S(1)}, u32[]{:S(2)}) copy-start(bf16[640,128]{1,0:T(8,128)(2,1)S(1)} %collective-permute-done.7) | copy-start | bytes 491524
  115.3 4.0 %collective-permute-start.8 = (bf16[4,640,128]{2,1,0:T(8,128)(2,1)S(1)}, bf16[4,640,128]{2,1,0:T(8,128)(2,1)S(1)}, u32[]{:S(2)}, u32[]{:S(2)}) collective-permute-start(bf16[4,640,128]{2,1,0:T(8,128)(2,1)S(1)} %pad_maximum_fusion.2), channel_id=1, source_target_pairs={{0,1},{1,0},{2,3},{3,2},{4,5},{5,4},{6,7},{7,6},{8,9},{9,8},{10,11... | collective-permute-start | bytes 1966088 | tf_op jit(solution)/shard_map/ppermute | solution.py:32
  119.8 11.4 %copy-start.12 = (s32[1,128,2]{1,2,0:T(2,128)S(1)}, s32[1,128,2]{1,2,0:T(2,128)}, u32[]{:S(2)}) copy-start(s32[1,128,2]{1,2,0:T(2,128)} %param.14) | copy-start | bytes 3076
  119.9 11.4 %copy-start.13 = (s32[1,16]{1,0:T(1,128)S(1)}, s32[1,16]{1,0:T(1,128)}, u32[]{:S(2)}) copy-start(s32[1,16]{1,0:T(1,128)} %param.18) | copy-start | bytes 196
  119.9 47.0 %copy-start.14 = (f32[1,128,2]{1,2,0:T(2,128)S(1)}, f32[1,128,2]{1,2,0:T(2,128)}, u32[]{:S(2)}) copy-start(f32[1,128,2]{1,2,0:T(2,128)} %param.15) | copy-start | bytes 3076
  122.5 44.3 %all-to-all-start.1 = ((bf16[16,40,512]{2,1,0:T(8,128)(2,1)}), bf16[16,40,512]{2,1,0:T(8,128)(2,1)S(1)}, u32[]{:S(2)}, u32[]{:S(2)}) async-start(bf16[16,40,512]{2,1,0:T(8,128)(2,1)} %bitcast.32), calls=%async_computation.1 | async-start | bytes 1310720 | tf_op jit(solution)/shard_map/all_to_all | solution.py:164
  167.2 8.1 %collective-permute-start.9 = (bf16[128,512]{1,0:T(8,128)(2,1)S(1)}, bf16[128,512]{1,0:T(8,128)(2,1)S(1)}, u32[]{:S(2)}, u32[]{:S(2)}) collective-permute-start(bf16[128,512]{1,0:T(8,128)(2,1)S(1)} %fusion.3), channel_id=1, source_target_pairs={{0,128},{128,256},{256,384},{384,0},{1,129},{129,257},{257,385},{3... | collective-permute-start | bytes 393224 | tf_op jit(solution)/shard_map/ppermute | solution.py:10
